TPU v7x, 256 devices: a whole 4x4x8 slice. The times are simulated.
256 devices in a mesh: seq: 32 (over y, x, core), dev: 8 (over z).
Axes of the slice: x: 4, y: 4, z: 8, core: 2. Of those that a mesh axis runs over, the one named last changes fastest.
Arguments:
- queries: bfloat16 [2048, 4096], P('seq', 'dev'), may hold values from -6 to 6
- key_vectors: bfloat16 [2048, 4096], P('seq', 'dev'), may hold values from -6 to 6
- value_vectors: bfloat16 [2048, 4096], P('seq', 'dev'), may hold values from -6 to 6
- log_decay: float32 [2048, 32], P('seq', 'dev')
- head_gain: float32 [4096], P('dev'), may hold values from 0.5 to 1.5
- gate_weight: bfloat16 [8, 4096, 4096], P('dev', None, 'seq'), may hold values from -0.09375 to 0.09375
- up_weight: bfloat16 [8, 4096, 4096], P('dev', None, 'seq'), may hold values from -0.09375 to 0.09375
- down_weight: bfloat16 [8, 4096, 4096], P('dev', 'seq'), may hold values from -0.0625 to 0.0625
- expert_ids: int32 [2048, 2], P(('seq', 'dev')), may hold values from 0 to 3, all different within a row; in each aligned block of 8 rows (0 to 7, 8 to 15, ...) at most 6 rows name the same one
- expert_weights: float32 [2048, 2], P(('seq', 'dev')), may hold values from 0.2 to 1
Outputs:
- layer_output: bfloat16 [2048, 4096], P(('seq', 'dev'))
Inputs may be any that keep to these rules, and one draw needn't show every extreme that they name: `expert_ids`: in each aligned block of 8 rows (the tokens of one device) no expert is named by more than 6 rows, a bound that some block reaches; the two experts of a row differ.
All inputs are finite; a program needn't handle non-finite values.
Results may differ from a plain program's by a relative error of at most 0.03.
Values may be sent and summed in bfloat16 or wider, within the bound.
No kernel may reach another device: no remote copies, remote signals or barrier semaphores. Data moves between devices by JAX's collectives and lax.ppermute only.
A program may use at most 128 MiB of HBM per device.

v0:
```python
import jax
import jax.numpy as jnp
from jax import lax
from jax.sharding import PartitionSpec as P

PAIR = 2
BLOCK_MAX = 512


highest = lax.Precision.HIGHEST


def carried_in(value, axis, join, neutral):
    place = lax.axis_index(axis)
    gathered = jax.tree.map(
        lambda a, kind: lax.all_gather(a.astype(kind), axis), value, (jnp.bfloat16, jnp.bfloat16)
    )
    state = jax.tree.map(lambda a, e: jnp.zeros_like(a) + jnp.asarray(e, a.dtype), value, neutral)

    def one(turn, state):
        return join(
            state,
            jax.tree.map(
                lambda a, own: lax.dynamic_index_in_dim(a, turn, 0, False).astype(own.dtype),
                gathered,
                value,
            ),
        )

    return lax.fori_loop(0, place, one, state)


def block_step(state, pieces):
    queries_blk, keys_blk, values_blk, decay_blk = pieces
    length = decay_blk.shape[0]
    running = jnp.cumsum(decay_blk)
    causal = jnp.arange(length)[:, None] >= jnp.arange(length)[None, :]
    spread = jnp.where(causal, running[:, None] - running[None, :], 0.0)
    factors = jnp.where(causal, jnp.exp(spread), 0.0)
    scores = jnp.dot(queries_blk, keys_blk.T, preferred_element_type=jnp.float32) * factors
    values_f = values_blk.astype(jnp.float32)
    keys_f = keys_blk.astype(jnp.float32)
    carried = jnp.exp(running)[:, None] * jnp.dot(
        queries_blk.astype(jnp.float32), state, precision=highest
    )
    output = jnp.dot(scores, values_f, precision=highest) + carried
    tail_decay = jnp.exp(running[-1] - running)
    state = jnp.exp(running[-1]) * state + jnp.dot(
        (keys_f * tail_decay[:, None]).T, values_f, precision=highest
    )
    return (state, output)


def run_blocks(state, queries_b, keys_b, values_b, decay_f, block):
    count = decay_f.shape[0] // block
    shaped = (
        queries_b.reshape(count, block, -1),
        keys_b.reshape(count, block, -1),
        values_b.reshape(count, block, -1),
        decay_f.reshape(count, block),
    )
    state, outputs = lax.scan(block_step, state, shaped)
    return outputs.reshape(count * block, -1)


def head_norm(attention, gain):
    square_mean = jnp.mean(attention * attention, axis=-1, keepdims=True)
    return (attention * lax.rsqrt(square_mean + 1e-06) * gain).astype(jnp.bfloat16)


def slot_ranks(flat_experts, experts):
    onehot = (flat_experts[..., None] == jnp.arange(experts, dtype=jnp.int32)).astype(jnp.int32)
    before = jnp.cumsum(onehot, axis=-2) - onehot
    return jnp.sum(before * onehot, axis=-1)


def chain_join(earlier, later):
    return (earlier[0] + later[0], jnp.exp(later[0])[:, None, None] * earlier[1] + later[1])


def per_device(
    queries,
    key_vectors,
    value_vectors,
    log_decay,
    head_gain,
    gate_weight,
    up_weight,
    down_weight,
    expert_ids,
    expert_weights,
):
    seq_len = queries.shape[0]
    heads = log_decay.shape[1]
    head_dim = queries.shape[1] // heads
    queries_h = jnp.transpose(queries.reshape(seq_len, heads, head_dim), (1, 0, 2))
    keys_h = jnp.transpose(key_vectors.reshape(seq_len, heads, head_dim), (1, 0, 2))
    values_h = jnp.transpose(value_vectors.reshape(seq_len, heads, head_dim), (1, 0, 2))
    decay_h = jnp.transpose(log_decay, (1, 0))
    running = jnp.cumsum(decay_h, axis=1)
    log_total = running[:, -1]
    tail_decay = jnp.exp(log_total[:, None] - running)
    local_state = jnp.einsum(
        "hsa,hsb->hab",
        keys_h.astype(jnp.float32) * tail_decay[:, :, None],
        values_h.astype(jnp.float32),
        precision=highest,
    )
    starting = (jnp.zeros((heads,), jnp.float32), jnp.zeros_like(local_state))
    incoming = carried_in((log_total, local_state), "seq", chain_join, starting)[1]
    block = min(BLOCK_MAX, seq_len)

    def one_head(state, head_queries, head_keys, head_values, head_decay):
        return run_blocks(state, head_queries, head_keys, head_values, head_decay, block)

    attention = jax.vmap(one_head)(incoming, queries_h, keys_h, values_h, decay_h)
    normed_h = head_norm(attention, head_gain.reshape(heads, 1, head_dim))
    normed = jnp.transpose(normed_h, (1, 0, 2)).reshape(seq_len, heads * head_dim)
    dev_count = lax.axis_size("dev")
    experts = dev_count // PAIR
    tok_count = expert_ids.shape[0]
    top_count = expert_ids.shape[1]
    capacity = max(2, (3 * tok_count * top_count + 2 * experts - 1) // (2 * experts))
    head_size = normed.shape[1]
    width = head_size * dev_count
    own_flat = expert_ids.reshape(tok_count * top_count)
    own_rank = slot_ranks(own_flat[None, :], experts)[0]
    pick_index = own_flat * capacity + own_rank
    owned_rows = lax.all_to_all(normed, "dev", split_axis=0, concat_axis=1, tiled=True)
    slot_token = (
        jnp.full((experts * capacity,), tok_count, jnp.int32)
        .at[pick_index]
        .set(jnp.arange(tok_count * top_count, dtype=jnp.int32) // top_count)
    )
    padded = jnp.concatenate([owned_rows, jnp.zeros((1, width), owned_rows.dtype)], axis=0)
    send_rows = jnp.repeat(padded[slot_token].reshape(experts, capacity, width), PAIR, axis=0)
    arrived = lax.all_to_all(send_rows, "dev", split_axis=0, concat_axis=0, tiled=True)
    local_rows = arrived.reshape(-1, width)
    piece = lax.all_gather(local_rows, "seq", axis=0, tiled=True)
    gate_part = jnp.dot(piece, gate_weight[0], preferred_element_type=jnp.float32)
    up_part = jnp.dot(piece, up_weight[0], preferred_element_type=jnp.float32)
    hidden_all = (jax.nn.silu(gate_part) * up_part).astype(jnp.bfloat16)
    piece = hidden_all
    term = jnp.dot(piece, down_weight[0], preferred_element_type=jnp.float32).astype(jnp.bfloat16)
    term = lax.optimization_barrier(term)
    summed = lax.psum_scatter(
        term.astype(jnp.float32).astype(jnp.bfloat16), "seq", scatter_dimension=0, tiled=True
    ).astype(jnp.float32)
    returned = lax.all_to_all(
        summed.reshape(dev_count, capacity, width).astype(jnp.bfloat16),
        "dev",
        split_axis=0,
        concat_axis=0,
        tiled=True,
    ).astype(jnp.float32)
    expert_out = jnp.sum(returned.reshape(experts, PAIR, capacity, width), axis=1).astype(
        jnp.bfloat16
    )
    picked = expert_out.reshape(experts * capacity, width)[pick_index].reshape(
        tok_count, top_count, width
    )
    combined = jnp.sum(picked.astype(jnp.float32) * expert_weights[:, :, None], axis=1)
    return combined.astype(jnp.bfloat16)


def solution(mesh):
    in_specs = (
        P("seq", "dev"),
        P("seq", "dev"),
        P("seq", "dev"),
        P("seq", "dev"),
        P("dev"),
        P("dev", None, "seq"),
        P("dev", None, "seq"),
        P("dev", "seq", None),
        P(("seq", "dev"), None),
        P(("seq", "dev"), None),
    )
    out_specs = P(("seq", "dev"), None)
    return jax.shard_map(
        per_device, mesh=mesh, in_specs=in_specs, out_specs=out_specs, check_vma=False
    )
```

profile of v0, /device:TPU:2, one launch (start us, length us, event | category | flops | bytes accessed | tf_op | source)
XLA Modules:
  0.0 384.8 jit_solution(10453502567396986454)
XLA Ops:
  6.5 1.0 reduce_window_sum.25
  7.5 0.2 slice_reduce_fusion
  7.7 0.1 exponential_bitcast_fusion.1
  7.8 2.0 convolution_convert_fusion.1
  9.8 1.3 dynamic-slice.8
  11.7 0.2 fusion.30
  11.9 0.2 dynamic-update-slice
  12.2 62.8 %all-reduce.1 = bf16[128]{0:T(256)(128)(2,1)S(1)} all-reduce(bf16[128]{0:T(256)(128)(2,1)S(1)} %dynamic-update-slice), channel_id=2, replica_groups=mesh['seq'=32,'dev'=8] {'seq'}, use_global_device_ids=true, to_apply=%add.1 | all-reduce | flops 128 | bytes 512
  75.0 0.1 reshape.263
  75.1 0.8 copy.29
  75.9 0.1 eq.27
  75.9 0.1 fusion.29
  76.0 0.7 broadcast_multiply_fusion
  76.7 0.1 copy.28
  76.8 0.1 mul.129
  76.9 0.2 select_reduce_fusion
  77.1 0.6 scatter_custom_fusion
  77.7 1.0 convolution_multiply_fusion.1
  78.8 0.0 all-gather.7.cloned.1.call-done
  78.8 2.2 while.3
  78.9 1.1 convert_add_fusion.2
  80.0 1.0 convert_add_fusion.2
  81.1 1.1 fusion.21
  82.2 1.1 fusion.13
  83.3 0.8 fusion.17
  84.1 0.1 copy.27
  84.2 0.7 all_to_all.20
  84.9 8.2 %all-to-all-start = ((bf16[8,8,512]{2,1,0:T(8,128)(2,1)}), bf16[8,8,512]{2,1,0:T(8,128)(2,1)S(1)}, u32[]{:S(2)}, u32[]{:S(2)}) async-start(bf16[8,8,512]{2,1,0:T(8,128)(2,1)} %all_to_all.20), calls=%async_computation | async-start | bytes 131072 | tf_op jit(solution)/shard_map/all_to_all | solution.py:129
  93.1 0.0 all-gather.5.cloned.1.call-start
  93.1 8.3 %all-to-all-done = bf16[8,8,512]{2,1,0:T(8,128)(2,1)S(1)} async-done(((bf16[8,8,512]{2,1,0:T(8,128)(2,1)}), bf16[8,8,512]{2,1,0:T(8,128)(2,1)S(1)}, u32[]{:S(2)}, u32[]{:S(2)}) %all-to-all-start) | async-done | bytes 65568 | tf_op jit(solution)/shard_map/all_to_all | solution.py:129
  101.4 0.7 gather_fusion
  102.1 0.1 reshape.232
  102.2 15.7 %all_to_all.29 = bf16[8,6,4096]{2,1,0:T(8,128)(2,1)S(1)} all-to-all(bf16[8,6,4096]{2,1,0:T(8,128)(2,1)S(1)} %bitcast.114), channel_id=1, replica_groups=mesh['seq'=32,'dev'=8] {'dev'}, dimensions={0} | all-to-all | bytes 786432 | tf_op jit(solution)/shard_map/all_to_all | solution.py:137
  117.9 0.9 reshape.234
  118.9 0.0 reduce-scatter.2.cloned.1.call-start
  118.9 95.2 %all-gather.5.cloned.1.call-done = bf16[1536,4096]{1,0:T(8,128)(2,1)} async-done(((bf16[48,4096]{1,0:T(8,128)(2,1)}), bf16[1536,4096]{1,0:T(8,128)(2,1)}) %all-gather.5.cloned.1.call-update) | async-done | bytes 12582928 | tf_op jit(solution)/shard_map/all_gather | solution.py:139
  214.2 6.7 %fusion.4 = f32[1536,128]{1,0:T(8,128)S(1)} fusion(bf16[1536,4096]{1,0:T(8,128)(2,1)} %all-gather.5.cloned.1.call-done, bf16[1,4096,128]{2,1,0:T(8,128)(2,1)} %param.17), kind=kOutput, calls=%fused_computation.12 | convolution fusion | flops 1610612736 | bytes 14417920 | tf_op jit(solution)/shard_map/dot_general | solution.py:140
  220.9 18.6 %convolution_convert_fusion = bf16[1536,4096]{1,0:T(8,128)(2,1)} fusion(bf16[1536,4096]{1,0:T(8,128)(2,1)} %all-gather.5.cloned.1.call-done, bf16[1,128,4096]{2,1,0:T(8,128)(2,1)S(1)} %copy-done, bf16[1,4096,128]{2,1,0:T(8,128)(2,1)S(1)} %copy-done.1, f32[1536,128]{1,0:T(8,128)S(1)} %fusion.4), kind=kOutput, calls=%fused_computation.5 | convolution fusion | flops 3228696576 | bytes 28049408 | tf_op jit(solution)/shard_map/dot_general | solution.py:144
  239.5 111.4 %reduce-scatter.2.cloned.1.call-done = bf16[48,4096]{1,0:T(8,128)(2,1)} async-done(((bf16[1536,4096]{1,0:T(8,128)(2,1)}), bf16[48,4096]{1,0:T(8,128)(2,1)}) %reduce-scatter.2.cloned.1.call-update) | async-done | bytes 393232 | tf_op jit(solution)/shard_map/reduce_scatter | solution.py:146
  350.9 1.9 convert_element_type.99
  352.8 7.0 %all-to-all-start.2 = ((bf16[8,6,4096]{2,1,0:T(8,128)(2,1)}), bf16[8,6,4096]{2,1,0:T(8,128)(2,1)S(1)}, u32[]{:S(2)}, u32[]{:S(2)}) async-start(bf16[8,6,4096]{2,1,0:T(8,128)(2,1)} %convert_element_type.99), calls=%async_computation.3 | async-start | bytes 1048576 | tf_op jit(solution)/shard_map/all_to_all | solution.py:149
  359.9 0.1 copy.30
  360.0 16.3 %all-to-all-done.2 = bf16[8,6,4096]{2,1,0:T(8,128)(2,1)S(1)} async-done(((bf16[8,6,4096]{2,1,0:T(8,128)(2,1)}), bf16[8,6,4096]{2,1,0:T(8,128)(2,1)S(1)}, u32[]{:S(2)}, u32[]{:S(2)}) %all-to-all-start.2) | async-done | bytes 393248 | tf_op jit(solution)/shard_map/all_to_all | solution.py:149
  376.3 0.1 bitcast_reduce_fusion
  376.4 0.1 convert_element_type.101
  376.5 0.6 gather_fusion.1
  377.1 0.2 reshape.238
  377.3 1.0 multiply_reduce_fusion
  (24 shorter events, 0.2 us)
Async XLA Ops:
  6.5 214.3 %copy-start = (bf16[1,128,4096]{2,1,0:T(8,128)(2,1)S(1)}, bf16[1,128,4096]{2,1,0:T(8,128)(2,1)}, u32[]{:S(2)}) copy-start(bf16[1,128,4096]{2,1,0:T(8,128)(2,1)} %param.19) | copy-start | bytes 3145732
  6.5 72.3 %all-gather.7.cloned.1.call-start = ((), (), s32[]{:S(2)}) async-start(), calls=%async_computation.6 | async-start | bytes 4325376 | tf_op jit(solution)/shard_map/all_gather | solution.py:16
  78.8 142.0 %copy-start.1 = (bf16[1,4096,128]{2,1,0:T(8,128)(2,1)S(1)}, bf16[1,4096,128]{2,1,0:T(8,128)(2,1)}, u32[]{:S(2)}) copy-start(bf16[1,4096,128]{2,1,0:T(8,128)(2,1)} %param.18) | copy-start | bytes 3145732
  84.9 16.6 %all-to-all-start = ((bf16[8,8,512]{2,1,0:T(8,128)(2,1)}), bf16[8,8,512]{2,1,0:T(8,128)(2,1)S(1)}, u32[]{:S(2)}, u32[]{:S(2)}) async-start(bf16[8,8,512]{2,1,0:T(8,128)(2,1)} %all_to_all.20), calls=%async_computation | async-start | bytes 131072 | tf_op jit(solution)/shard_map/all_to_all | solution.py:129
  93.1 121.1 %all-gather.5.cloned.1.call-start = ((), (), s32[]{:S(2)}) async-start(), calls=%async_computation.4 | async-start | bytes 12976128 | tf_op jit(solution)/shard_map/all_gather | solution.py:139
  118.9 232.0 %reduce-scatter.2.cloned.1.call-start = ((), (), s32[]{:S(2)}) async-start(), calls=%async_computation.5 | async-start | bytes 12976128 | tf_op jit(solution)/shard_map/reduce_scatter | solution.py:146
  239.5 120.4 %copy-start.2 = (f32[8,2]{0,1:T(2,128)S(1)}, f32[8,2]{0,1:T(2,128)}, u32[]{:S(2)}) copy-start(f32[8,2]{0,1:T(2,128)} %param.21) | copy-start | bytes 196
  352.8 23.4 %all-to-all-start.2 = ((bf16[8,6,4096]{2,1,0:T(8,128)(2,1)}), bf16[8,6,4096]{2,1,0:T(8,128)(2,1)S(1)}, u32[]{:S(2)}, u32[]{:S(2)}) async-start(bf16[8,6,4096]{2,1,0:T(8,128)(2,1)} %convert_element_type.99), calls=%async_computation.3 | async-start | bytes 1048576 | tf_op jit(solution)/shard_map/all_to_all | solution.py:149
Sparse Core Ops, SparseCore 0:
  9.9 53.7 all-gather.6
  119.0 95.1 all-gather.4
  239.6 111.2 reduce-scatter.1
where the time goes:
time: 386 us; the launch traced here: 385 us
  waiting for transfers between devices  231 us (60%)
  blocking collectives  78.5 us (20%)
  matrix products  30.5 us (8%)
  starting transfers between devices  15.3 us (4%)
  between operations  14 us (4%)
  local copies, waits for them, and re-layouts  8.93 us (2%)
  other arithmetic  6.19 us (2%)
    reduce_scatter x1, waiting for transfers between devices, per_device(): lax.psum_scatter(term.astype(jnp.float32).astype(jnp.bfloat16), 'seq', sc...  111 us
    all_gather x1, waiting for transfers between devices, per_device(): piece = lax.all_gather(local_rows, 'seq', axis=0, tiled=True)  95.2 us
    unnamed x1, blocking collectives  62.8 us
    dot_general x1, matrix products, per_device(): jnp.dot(piece, down_weight[0], preferred_element_type=jnp.float32)  18.6 us
    all_to_all x1, waiting for transfers between devices, per_device(): lax.all_to_all(summed.reshape(dev_count, capacity, width).astype(jnp.bflo...  16.3 us
    all_to_all x1, blocking collectives, per_device(): lax.all_to_all(send_rows, 'dev', split_axis=0, concat_axis=0, tiled=True)  15.7 us
    all_to_all x1, waiting for transfers between devices, per_device(): lax.all_to_all(normed, 'dev', split_axis=0, concat_axis=1, tiled=True)  8.31 us
    all_to_all x1, starting transfers between devices, per_device(): lax.all_to_all(normed, 'dev', split_axis=0, concat_axis=1, tiled=True)  8.19 us
  transfers between devices with their start and end apart: 5, of which 4 were waited for; matrix products, arithmetic and copies ran while one was open for 1% of the time, Pallas kernels for 0%

commit v1 on v0

v1 whole, which is shorter than its diff:
```python
import jax
import jax.numpy as jnp
import numpy as np
from jax import lax
from jax.sharding import Mesh
from jax.sharding import PartitionSpec as P

PAIR = 2

highest = lax.Precision.HIGHEST

SEQ_AXES = ("y", "x", "c")
TOK_AXES = ("y", "x")


def chain_join(earlier, later):
    return (earlier[0] + later[0], jnp.exp(later[0])[:, None, None] * earlier[1] + later[1])


def shifted(value, shift, count):
    pairs = [(i, i + shift) for i in range(count - shift)]
    return lax.ppermute(value, SEQ_AXES, pairs)


def carried_in(log_total, local_state, count):
    state = shifted((log_total, local_state), 1, count)
    shift = 1
    while shift < count - 1:
        state = chain_join(shifted(state, shift, count), state)
        shift *= 2
    return state[1]


def head_norm(attention, gain):
    square_mean = jnp.mean(attention * attention, axis=-1, keepdims=True)
    return (attention * lax.rsqrt(square_mean + 1e-06) * gain).astype(jnp.bfloat16)


def slot_ranks(flat_experts, experts):
    onehot = (flat_experts[..., None] == jnp.arange(experts, dtype=jnp.int32)).astype(jnp.int32)
    before = jnp.cumsum(onehot, axis=-2) - onehot
    return jnp.sum(before * onehot, axis=-1)


def per_device(
    queries,
    key_vectors,
    value_vectors,
    log_decay,
    head_gain,
    gate_weight,
    up_weight,
    down_weight,
    expert_ids,
    expert_weights,
):
    count = 1
    for name in SEQ_AXES:
        count *= lax.axis_size(name)
    dev_count = lax.axis_size("dev")
    experts = dev_count // PAIR

    gate_both = lax.all_gather(gate_weight[0], "c", axis=1, tiled=True)
    up_both = lax.all_gather(up_weight[0], "c", axis=1, tiled=True)
    down_both = lax.all_gather(down_weight[0], "c", axis=0, tiled=True)

    tok_count = expert_ids.shape[0]
    top_count = expert_ids.shape[1]
    capacity = max(2, (3 * tok_count * top_count + 2 * experts - 1) // (2 * experts))
    ids_all = lax.all_gather(expert_ids, "dev", axis=0, tiled=False)

    seq_len = queries.shape[0]
    heads = log_decay.shape[1]
    head_dim = queries.shape[1] // heads
    queries_h = jnp.transpose(queries.reshape(seq_len, heads, head_dim), (1, 0, 2))
    keys_h = jnp.transpose(key_vectors.reshape(seq_len, heads, head_dim), (1, 0, 2))
    values_h = jnp.transpose(value_vectors.reshape(seq_len, heads, head_dim), (1, 0, 2))
    decay_h = jnp.transpose(log_decay, (1, 0))
    running = jnp.cumsum(decay_h, axis=1)
    log_total = running[:, -1]
    tail_decay = jnp.exp(log_total[:, None] - running)
    keys_f = keys_h.astype(jnp.float32)
    values_f = values_h.astype(jnp.float32)
    local_state = jnp.einsum(
        "hsa,hsb->hab", keys_f * tail_decay[:, :, None], values_f, precision=highest
    )
    incoming = carried_in(log_total, local_state, count)

    causal = jnp.arange(seq_len)[:, None] >= jnp.arange(seq_len)[None, :]
    spread = jnp.where(causal[None], running[:, :, None] - running[:, None, :], 0.0)
    factors = jnp.where(causal[None], jnp.exp(spread), 0.0)
    scores = (
        jnp.einsum("hta,hsa->hts", queries_h, keys_h, preferred_element_type=jnp.float32) * factors
    )
    carried = jnp.exp(running)[:, :, None] * jnp.einsum(
        "hta,hab->htb", queries_h.astype(jnp.float32), incoming, precision=highest
    )
    attention = jnp.einsum("hts,hsb->htb", scores, values_f, precision=highest) + carried
    normed_h = head_norm(attention, head_gain.reshape(heads, 1, head_dim))
    normed = jnp.transpose(normed_h, (1, 0, 2)).reshape(seq_len, heads * head_dim)

    per_expert = dev_count * capacity
    flat = ids_all.reshape(dev_count, tok_count * top_count)
    rank = slot_ranks(flat, experts)
    source = jnp.arange(dev_count, dtype=jnp.int32)[:, None]
    slot_index = flat * per_expert + source * capacity + rank
    token_local = source * tok_count + jnp.arange(tok_count * top_count, dtype=jnp.int32)[None, :] // top_count
    slot_token = (
        jnp.full((experts * per_expert,), seq_len, jnp.int32)
        .at[slot_index.reshape(-1)]
        .set(token_local.reshape(-1))
    )
    padded = jnp.concatenate([normed, jnp.zeros((1, normed.shape[1]), normed.dtype)], axis=0)
    send_rows = jnp.repeat(padded[slot_token].reshape(experts, per_expert, -1), PAIR, axis=0)
    arrived = lax.all_to_all(send_rows, "dev", split_axis=0, concat_axis=0, tiled=True)
    local_rows = jnp.transpose(arrived.reshape(dev_count, per_expert, -1), (1, 0, 2)).reshape(
        per_expert, -1
    )
    width = local_rows.shape[1]

    piece = lax.all_gather(local_rows, TOK_AXES, axis=0, tiled=True)
    gate_part = jnp.dot(piece, gate_both, preferred_element_type=jnp.float32)
    up_part = jnp.dot(piece, up_both, preferred_element_type=jnp.float32)
    hidden_all = (jax.nn.silu(gate_part) * up_part).astype(jnp.bfloat16)
    term = jnp.dot(hidden_all, down_both, preferred_element_type=jnp.float32).astype(jnp.bfloat16)
    summed = lax.psum_scatter(term, TOK_AXES, scatter_dimension=0, tiled=True)
    returned = lax.all_to_all(
        summed.reshape(dev_count, capacity, width),
        "dev",
        split_axis=0,
        concat_axis=0,
        tiled=True,
    ).astype(jnp.float32)
    expert_out = jnp.sum(returned.reshape(experts, PAIR, capacity, width), axis=1).astype(
        jnp.bfloat16
    )
    own = lax.axis_index("dev")
    own_flat = lax.dynamic_index_in_dim(flat, own, 0, False)
    own_rank = lax.dynamic_index_in_dim(rank, own, 0, False)
    pick_index = own_flat * capacity + own_rank
    picked = expert_out.reshape(experts * capacity, width)[pick_index].reshape(
        tok_count, top_count, width
    )
    combined = jnp.sum(picked.astype(jnp.float32) * expert_weights[:, :, None], axis=1)
    return combined.astype(jnp.bfloat16)


def split_mesh(mesh):
    devices = mesh.devices
    seq_count, dev_count = devices.shape
    cores = 2
    xs = 4
    flat = devices.reshape(-1)
    if hasattr(flat[0], "coords"):
        cores = len({int(getattr(d, "core_on_chip", 0)) for d in flat})
        xs = len({int(d.coords[0]) for d in flat})
    ys = seq_count // (xs * cores)
    return Mesh(devices.reshape(ys, xs, cores, dev_count), ("y", "x", "c", "dev"))


def solution(mesh):
    fine = split_mesh(mesh)
    seq = SEQ_AXES
    in_specs = (
        P(seq, "dev"),
        P(seq, "dev"),
        P(seq, "dev"),
        P(seq, "dev"),
        P("dev"),
        P("dev", None, seq),
        P("dev", None, seq),
        P("dev", seq, None),
        P(seq + ("dev",), None),
        P(seq + ("dev",), None),
    )
    out_specs = P(seq + ("dev",), None)
    return jax.shard_map(
        per_device, mesh=fine, in_specs=in_specs, out_specs=out_specs, check_vma=False
    )
```

time: 386 us -> 337 us (0.87)
  blocking collectives: 78.5 us -> 34.7 us
  starting transfers between devices: 15.3 us -> 45.8 us
  waiting for transfers between devices: 231 us -> 212 us
  matrix products: 30.5 us -> 20.6 us
    unnamed x1 -> x0, blocking collectives: 62.8 us -> none
    ppermute x0 -> x11, starting transfers between devices: none -> 38.6 us  [shifted(): return lax.ppermute(value, SEQ_AXES, pairs)]
    reduce_scatter x1, waiting for transfers between devices: 111 us -> 87.5 us  [per_device(): summed = lax.psum_scatter(term, TOK_AXES, scatter_dimension=0, tiled=True)]
    all_gather x0 -> x1, blocking collectives: none -> 19.4 us  [per_device(): ids_all = lax.all_gather(expert_ids, 'dev', axis=0, tiled=False)]
    ppermute x0 -> x11, waiting for transfers between devices: none -> 12.8 us  [shifted(): return lax.ppermute(value, SEQ_AXES, pairs)]
    dot_general x6, matrix products: 30.5 us -> 20.6 us  [the longest x1 13.2 us: per_device(): jnp.dot(hidden_all, down_both, preferred_element_type=jnp.float32)]
    all_to_all x2 -> x1, waiting for transfers between devices: 24.6 us -> 16.1 us  [per_device(): lax.all_to_all(summed.reshape(dev_count, capacity, width), 'dev', split_a...]
    all_to_all x2 -> x1, starting transfers between devices: 15.2 us -> 7.01 us  [per_device(): lax.all_to_all(summed.reshape(dev_count, capacity, width), 'dev', split_a...]
  transfers between devices with their start and end apart: 5 -> 17, of which waited for: 4 -> 10; matrix products, arithmetic and copies ran while one was open for 1% -> 4% of each run, Pallas kernels for 0% -> 0%
where the time goes in v1:
time: 337 us
  waiting for transfers between devices  212 us (63%)
  starting transfers between devices  45.8 us (14%)
  blocking collectives  34.7 us (10%)
  matrix products  20.6 us (6%)
  between operations  13.5 us (4%)
  local copies, waits for them, and re-layouts  6.65 us (2%)
  other arithmetic  3.39 us (1%)
    reduce_scatter x1, waiting for transfers between devices, per_device(): summed = lax.psum_scatter(term, TOK_AXES, scatter_dimension=0, tiled=True)  87.5 us
    all_gather x1, waiting for transfers between devices, per_device(): piece = lax.all_gather(local_rows, TOK_AXES, axis=0, tiled=True)  62.8 us
    ppermute x11, starting transfers between devices, shifted(): return lax.ppermute(value, SEQ_AXES, pairs)  38.6 us
    all_gather x1, blocking collectives, per_device(): ids_all = lax.all_gather(expert_ids, 'dev', axis=0, tiled=False)  19.4 us
    all_gather x1, waiting for transfers between devices, per_device(): down_both = lax.all_gather(down_weight[0], 'c', axis=0, tiled=True)  18.9 us
    all_to_all x1, waiting for transfers between devices, per_device(): lax.all_to_all(summed.reshape(dev_count, capacity, width), 'dev', split_a...  16.1 us
    all_to_all x1, blocking collectives, per_device(): lax.all_to_all(send_rows, 'dev', split_axis=0, concat_axis=0, tiled=True)  15.3 us
    dot_general x1, matrix products, per_device(): jnp.dot(hidden_all, down_both, preferred_element_type=jnp.float32)  13.2 us
  transfers between devices with their start and end apart: 17, of which 10 were waited for; matrix products, arithmetic and copies ran while one was open for 4% of the time, Pallas kernels for 0%

profile of v1, /device:TPU:2, one launch (start us, length us, event | category | flops | bytes accessed | tf_op | source)
XLA Modules:
  0.0 336.8 jit_solution(2649230358285028791)
XLA Ops:
  6.5 0.7 all-gather.12.cloned.1.call-update
  7.3 0.9 reduce_window_sum.22
  8.2 0.2 slice_reduce_fusion
  8.4 1.9 collective-permute-start
  10.4 1.3 fusion.29
  11.7 3.5 %collective-permute-start.5 = (f32[4,128,128]{2,1,0:T(8,128)S(1)}, f32[4,128,128]{2,1,0:T(8,128)S(1)}, u32[]{:S(2)}, u32[]{:S(2)}) collective-permute-start(f32[4,128,128]{2,1,0:T(8,128)S(1)} %fusion.29), channel_id=1, source_target_pairs={{0,8},{8,16},{16,24},{24,32},{32,40},{40,48},{48,56},{56,64},{64,7... | collective-permute-start | bytes 786440 | tf_op jit(solution)/shard_map/ppermute | solution.py:22
  15.3 19.4 %all-gather.4 = s32[8,8,2]{1,2,0:T(2,128)S(1)} all-gather(s32[1,8,2]{1,2,0:T(2,128)} %bitcast.130), channel_id=2, replica_groups=mesh['y'=4,'x'=4,'c'=2,'dev'=8] {'dev'}, dimensions={0}, use_global_device_ids=true | all-gather | bytes 576 | tf_op jit(solution)/shard_map/all_gather | solution.py:70
  34.8 0.4 fusion.52
  35.2 1.9 collective-permute-start.6
  37.2 3.2 collective-permute-start.1
  40.4 2.6 collective-permute-done.1
  43.1 3.1 collective-permute-start.7
  46.5 0.1 copy.41
  46.7 0.1 mul.178
  46.8 0.2 convolution_multiply_fusion
  47.0 5.0 %collective-permute-done.7 = f32[4,128,128]{2,1,0:T(8,128)S(1)} collective-permute-done((f32[4,128,128]{2,1,0:T(8,128)S(1)}, f32[4,128,128]{2,1,0:T(8,128)S(1)}, u32[]{:S(2)}, u32[]{:S(2)}) %collective-permute-start.7) | collective-permute-done | bytes 262176 | tf_op jit(solution)/shard_map/ppermute | solution.py:22
  52.1 4.5 %collective-permute-start.8 = (f32[4,128,128]{2,1,0:T(8,128)S(1)}, f32[4,128,128]{2,1,0:T(8,128)S(1)}, u32[]{:S(2)}, u32[]{:S(2)}) collective-permute-start(f32[4,128,128]{2,1,0:T(8,128)S(1)} %multiply_add_fusion.2), channel_id=1, source_target_pairs={{0,32},{8,40},{16,48},{24,56},{32,64},{40,72},{48,80},{56,88},{64,... | collective-permute-start | bytes 786440 | tf_op jit(solution)/shard_map/ppermute | solution.py:22
  56.7 1.0 scatter_custom_fusion
  57.7 5.9 %collective-permute-start.2 = (f32[4]{0:T(128)S(1)}, f32[4]{0:T(128)S(1)}, u32[]{:S(2)}, u32[]{:S(2)}) collective-permute-start(f32[4]{0:T(128)S(1)} %get-tuple-element.10), channel_id=1, source_target_pairs={{0,16},{8,24},{16,32},{24,40},{32,48},{40,56},{48,64},{56,72},{64,... | collective-permute-start | bytes 56 | tf_op jit(solution)/shard_map/ppermute | solution.py:22
  63.6 1.3 collective-permute-done.2
  65.0 3.5 %collective-permute-start.9 = (f32[4,128,128]{2,1,0:T(8,128)S(1)}, f32[4,128,128]{2,1,0:T(8,128)S(1)}, u32[]{:S(2)}, u32[]{:S(2)}) collective-permute-start(f32[4,128,128]{2,1,0:T(8,128)S(1)} %multiply_add_fusion.1), channel_id=1, source_target_pairs={{0,64},{8,72},{16,80},{24,88},{32,96},{40,104},{48,112},{56,120},{... | collective-permute-start | bytes 786440 | tf_op jit(solution)/shard_map/ppermute | solution.py:22
  68.5 3.6 %collective-permute-start.3 = (f32[4]{0:T(128)S(1)}, f32[4]{0:T(128)S(1)}, u32[]{:S(2)}, u32[]{:S(2)}) collective-permute-start(f32[4]{0:T(128)S(1)} %get-tuple-element.8), channel_id=1, source_target_pairs={{0,32},{8,40},{16,48},{24,56},{32,64},{40,72},{48,80},{56,88},{64,... | collective-permute-start | bytes 56 | tf_op jit(solution)/shard_map/ppermute | solution.py:22
  72.1 1.3 collective-permute-done.3
  73.5 6.2 %collective-permute-start.10 = (f32[4,128,128]{2,1,0:T(8,128)S(1)}, f32[4,128,128]{2,1,0:T(8,128)S(1)}, u32[]{:S(2)}, u32[]{:S(2)}) collective-permute-start(f32[4,128,128]{2,1,0:T(8,128)S(1)} %multiply_add_fusion), channel_id=1, source_target_pairs={{0,128},{8,136},{16,144},{24,152},{32,160},{40,168},{48,176},{56,1... | collective-permute-start | bytes 786440 | tf_op jit(solution)/shard_map/ppermute | solution.py:22
  79.7 1.3 collective-permute-start.4
  81.0 2.6 collective-permute-done.4
  83.6 0.3 fusion.20
  84.0 0.3 fusion.24
  84.3 0.1 copy_bitcast_fusion
  84.5 1.0 gather_fusion
  85.5 15.3 %all_to_all.10 = bf16[8,48,512]{2,1,0:T(8,128)(2,1)S(1)} all-to-all(bf16[8,48,512]{2,1,0:T(8,128)(2,1)S(1)} %bitcast.123), channel_id=1, replica_groups=mesh['y'=4,'x'=4,'c'=2,'dev'=8] {'dev'}, dimensions={0} | all-to-all | bytes 786432 | tf_op jit(solution)/shard_map/all_to_all | solution.py:115
  100.8 0.8 copy.50
  101.7 0.7 all-gather.14.cloned.1.call-update
  102.4 0.5 all-gather.16.cloned.1.call-update
  103.0 62.8 %all-gather.10.cloned.1.call-done = bf16[768,4096]{1,0:T(8,128)(2,1)} async-done(((bf16[48,4096]{1,0:T(8,128)(2,1)}), bf16[768,4096]{1,0:T(8,128)(2,1)}) %all-gather.10.cloned.1.call-update) | async-done | bytes 6291472 | tf_op jit(solution)/shard_map/all_gather | solution.py:121
  165.9 5.2 %fusion.3 = f32[768,256]{1,0:T(8,128)S(1)} fusion(bf16[768,4096]{1,0:T(8,128)(2,1)} %all-gather.10.cloned.1.call-done, bf16[1,4096,256]{2,1,0:T(8,128)(2,1)} %all-gather.12.cloned.1.call-done), kind=kOutput, calls=%fused_computation.7 | convolution fusion | flops 1610612736 | bytes 9175040 | tf_op jit(solution)/shard_map/dot_general | solution.py:122
  171.1 12.0 %all-gather.14.cloned.1.call-done = bf16[1,4096,256]{2,1,0:T(8,128)(2,1)} async-done(((bf16[1,4096,128]{2,1,0:T(8,128)(2,1)}), bf16[1,4096,256]{2,1,0:T(8,128)(2,1)}) %all-gather.14.cloned.1.call-update) | async-done | bytes 2097168 | tf_op jit(solution)/shard_map/all_gather | solution.py:64
  183.1 18.9 %all-gather.16.cloned.1.call-done = bf16[1,256,4096]{2,1,0:T(8,128)(2,1)} async-done(((bf16[1,128,4096]{2,1,0:T(8,128)(2,1)}), bf16[1,256,4096]{2,1,0:T(8,128)(2,1)}) %all-gather.16.cloned.1.call-update) | async-done | bytes 2097168 | tf_op jit(solution)/shard_map/all_gather | solution.py:65
  202.0 13.2 %convolution_convert_fusion = bf16[768,4096]{1,0:T(8,128)(2,1)} fusion(bf16[1,256,4096]{2,1,0:T(8,128)(2,1)} %all-gather.16.cloned.1.call-done, bf16[768,4096]{1,0:T(8,128)(2,1)} %all-gather.10.cloned.1.call-done, bf16[1,4096,256]{2,1,0:T(8,128)(2,1)} %all-gather.14.cloned.1.call-done, f32[768,256]{1,0:T(8,128)S(1)} %fusion.3), kind=kOutput, calls=%fused_computation.3 | convolution fusion | flops 3225550848 | bytes 17563648 | tf_op jit(solution)/shard_map/dot_general | solution.py:125
  215.3 87.5 %reduce-scatter.2.cloned.1.call-done = bf16[48,4096]{1,0:T(8,128)(2,1)} async-done(((bf16[768,4096]{1,0:T(8,128)(2,1)}), bf16[48,4096]{1,0:T(8,128)(2,1)}) %reduce-scatter.2.cloned.1.call-update) | async-done | bytes 393232 | tf_op jit(solution)/shard_map/reduce_scatter | solution.py:126
  302.8 1.9 reshape.226
  304.8 7.0 %all-to-all-start.1 = ((bf16[8,6,4096]{2,1,0:T(8,128)(2,1)}), bf16[8,6,4096]{2,1,0:T(8,128)(2,1)S(1)}, u32[]{:S(2)}, u32[]{:S(2)}) async-start(bf16[8,6,4096]{2,1,0:T(8,128)(2,1)} %reshape.226), calls=%async_computation.2 | async-start | bytes 1048576 | tf_op jit(solution)/shard_map/all_to_all | solution.py:127
  311.9 0.2 add_reduce_fusion
  312.1 16.1 %all-to-all-done.1 = bf16[8,6,4096]{2,1,0:T(8,128)(2,1)S(1)} async-done(((bf16[8,6,4096]{2,1,0:T(8,128)(2,1)}), bf16[8,6,4096]{2,1,0:T(8,128)(2,1)S(1)}, u32[]{:S(2)}, u32[]{:S(2)}) %all-to-all-start.1) | async-done | bytes 393248 | tf_op jit(solution)/shard_map/all_to_all | solution.py:127
  328.2 0.1 bitcast_reduce_fusion
  328.4 0.6 gather_fusion.1
  329.0 0.2 reshape.229
  329.2 1.0 multiply_reduce_fusion
  (55 shorter events, 1.5 us)
Async XLA Ops:
  6.5 3.9 %copy-start = (bf16[64,512]{1,0:T(8,128)(2,1)S(1)}, bf16[64,512]{1,0:T(8,128)(2,1)}, u32[]{:S(2)}) copy-start(bf16[64,512]{1,0:T(8,128)(2,1)} %param.12) | copy-start | bytes 196612
  6.5 40.3 %copy-start.2 = (bf16[64,512]{1,0:T(8,128)(2,1)S(1)}, bf16[64,512]{1,0:T(8,128)(2,1)}, u32[]{:S(2)}) copy-start(bf16[64,512]{1,0:T(8,128)(2,1)} %param.11) | copy-start | bytes 196612
  6.5 40.3 %copy-start.1 = (bf16[64,512]{1,0:T(8,128)(2,1)S(1)}, bf16[64,512]{1,0:T(8,128)(2,1)}, u32[]{:S(2)}) copy-start(bf16[64,512]{1,0:T(8,128)(2,1)} %param.10) | copy-start | bytes 196612
  6.5 96.5 %all-gather.12.cloned.1.call-start = ((), (), s32[]{:S(2)}) async-start(), calls=%async_computation.5 | async-start | bytes 3145728 | tf_op jit(solution)/shard_map/all_gather | solution.py:63
  7.3 158.6 %all-gather.10.cloned.1.call-start = ((), (), s32[]{:S(2)}) async-start(), calls=%async_computation.3 | async-start | bytes 6684672 | tf_op jit(solution)/shard_map/all_gather | solution.py:121
  8.4 28.8 %collective-permute-start = (f32[4]{0:T(128)S(1)}, f32[4]{0:T(128)S(1)}, u32[]{:S(2)}, u32[]{:S(2)}) collective-permute-start(f32[4]{0:T(128)S(1)} %slice_reduce_fusion), channel_id=1, source_target_pairs={{0,8},{8,16},{16,24},{24,32},{32,40},{40,48},{48,56},{56,64},{64,7... | collective-permute-start | bytes 56 | tf_op jit(solution)/shard_map/ppermute | solution.py:22
  11.7 23.5 %collective-permute-start.5 = (f32[4,128,128]{2,1,0:T(8,128)S(1)}, f32[4,128,128]{2,1,0:T(8,128)S(1)}, u32[]{:S(2)}, u32[]{:S(2)}) collective-permute-start(f32[4,128,128]{2,1,0:T(8,128)S(1)} %fusion.29), channel_id=1, source_target_pairs={{0,8},{8,16},{16,24},{24,32},{32,40},{40,48},{48,56},{56,64},{64,7... | collective-permute-start | bytes 786440 | tf_op jit(solution)/shard_map/ppermute | solution.py:22
  35.2 7.8 %collective-permute-start.6 = (f32[4,128,128]{2,1,0:T(8,128)S(1)}, f32[4,128,128]{2,1,0:T(8,128)S(1)}, u32[]{:S(2)}, u32[]{:S(2)}) collective-permute-start(f32[4,128,128]{2,1,0:T(8,128)S(1)} %collective-permute-done.5), channel_id=1, source_target_pairs={{0,8},{8,16},{16,24},{24,32},{32,40},{40,48},{48,56},{56,64},{64,7... | collective-permute-start | bytes 786440 | tf_op jit(solution)/shard_map/ppermute | solution.py:22
  37.2 5.8 %collective-permute-start.1 = (f32[4]{0:T(128)S(1)}, f32[4]{0:T(128)S(1)}, u32[]{:S(2)}, u32[]{:S(2)}) collective-permute-start(f32[4]{0:T(128)S(1)} %collective-permute-done), channel_id=1, source_target_pairs={{0,8},{8,16},{16,24},{24,32},{32,40},{40,48},{48,56},{56,64},{64,7... | collective-permute-start | bytes 56 | tf_op jit(solution)/shard_map/ppermute | solution.py:22
  43.1 41.2 %copy-start.3 = (f32[512]{0:T(512)S(1)}, f32[512]{0:T(512)}, u32[]{:S(2)}) copy-start(f32[512]{0:T(512)} %param.14) | copy-start | bytes 6148
  43.1 8.9 %collective-permute-start.7 = (f32[4,128,128]{2,1,0:T(8,128)S(1)}, f32[4,128,128]{2,1,0:T(8,128)S(1)}, u32[]{:S(2)}, u32[]{:S(2)}) collective-permute-start(f32[4,128,128]{2,1,0:T(8,128)S(1)} %multiply_add_fusion.3), channel_id=1, source_target_pairs={{0,16},{8,24},{16,32},{24,40},{32,48},{40,56},{48,64},{56,72},{64,... | collective-permute-start | bytes 786440 | tf_op jit(solution)/shard_map/ppermute | solution.py:22
  52.1 12.8 %collective-permute-start.8 = (f32[4,128,128]{2,1,0:T(8,128)S(1)}, f32[4,128,128]{2,1,0:T(8,128)S(1)}, u32[]{:S(2)}, u32[]{:S(2)}) collective-permute-start(f32[4,128,128]{2,1,0:T(8,128)S(1)} %multiply_add_fusion.2), channel_id=1, source_target_pairs={{0,32},{8,40},{16,48},{24,56},{32,64},{40,72},{48,80},{56,88},{64,... | collective-permute-start | bytes 786440 | tf_op jit(solution)/shard_map/ppermute | solution.py:22
  57.7 7.2 %collective-permute-start.2 = (f32[4]{0:T(128)S(1)}, f32[4]{0:T(128)S(1)}, u32[]{:S(2)}, u32[]{:S(2)}) collective-permute-start(f32[4]{0:T(128)S(1)} %get-tuple-element.10), channel_id=1, source_target_pairs={{0,16},{8,24},{16,32},{24,40},{32,48},{40,56},{48,64},{56,72},{64,... | collective-permute-start | bytes 56 | tf_op jit(solution)/shard_map/ppermute | solution.py:22
  65.0 8.4 %collective-permute-start.9 = (f32[4,128,128]{2,1,0:T(8,128)S(1)}, f32[4,128,128]{2,1,0:T(8,128)S(1)}, u32[]{:S(2)}, u32[]{:S(2)}) collective-permute-start(f32[4,128,128]{2,1,0:T(8,128)S(1)} %multiply_add_fusion.1), channel_id=1, source_target_pairs={{0,64},{8,72},{16,80},{24,88},{32,96},{40,104},{48,112},{56,120},{... | collective-permute-start | bytes 786440 | tf_op jit(solution)/shard_map/ppermute | solution.py:22
  68.5 4.9 %collective-permute-start.3 = (f32[4]{0:T(128)S(1)}, f32[4]{0:T(128)S(1)}, u32[]{:S(2)}, u32[]{:S(2)}) collective-permute-start(f32[4]{0:T(128)S(1)} %get-tuple-element.8), channel_id=1, source_target_pairs={{0,32},{8,40},{16,48},{24,56},{32,64},{40,72},{48,80},{56,88},{64,... | collective-permute-start | bytes 56 | tf_op jit(solution)/shard_map/ppermute | solution.py:22
  73.5 10.1 %collective-permute-start.10 = (f32[4,128,128]{2,1,0:T(8,128)S(1)}, f32[4,128,128]{2,1,0:T(8,128)S(1)}, u32[]{:S(2)}, u32[]{:S(2)}) collective-permute-start(f32[4,128,128]{2,1,0:T(8,128)S(1)} %multiply_add_fusion), channel_id=1, source_target_pairs={{0,128},{8,136},{16,144},{24,152},{32,160},{40,168},{48,176},{56,1... | collective-permute-start | bytes 786440 | tf_op jit(solution)/shard_map/ppermute | solution.py:22
  79.7 3.9 %collective-permute-start.4 = (f32[4]{0:T(128)S(1)}, f32[4]{0:T(128)S(1)}, u32[]{:S(2)}, u32[]{:S(2)}) collective-permute-start(f32[4]{0:T(128)S(1)} %get-tuple-element.6), channel_id=1, source_target_pairs={{0,64},{8,72},{16,80},{24,88},{32,96},{40,104},{48,112},{56,120},{... | collective-permute-start | bytes 56 | tf_op jit(solution)/shard_map/ppermute | solution.py:22
  101.7 81.5 %all-gather.14.cloned.1.call-start = ((), (), s32[]{:S(2)}) async-start(), calls=%async_computation.6 | async-start | bytes 3145728 | tf_op jit(solution)/shard_map/all_gather | solution.py:64
  102.4 99.6 %all-gather.16.cloned.1.call-start = ((), (), s32[]{:S(2)}) async-start(), calls=%async_computation.7 | async-start | bytes 3145728 | tf_op jit(solution)/shard_map/all_gather | solution.py:65
  103.0 199.9 %reduce-scatter.2.cloned.1.call-start = ((), (), s32[]{:S(2)}) async-start(), calls=%async_computation.4 | async-start | bytes 6684672 | tf_op jit(solution)/shard_map/reduce_scatter | solution.py:126
  215.3 96.5 %copy-start.4 = (f32[8,2]{0,1:T(2,128)S(1)}, f32[8,2]{0,1:T(2,128)}, u32[]{:S(2)}) copy-start(f32[8,2]{0,1:T(2,128)} %param.19) | copy-start | bytes 196
  304.8 23.4 %all-to-all-start.1 = ((bf16[8,6,4096]{2,1,0:T(8,128)(2,1)}), bf16[8,6,4096]{2,1,0:T(8,128)(2,1)S(1)}, u32[]{:S(2)}, u32[]{:S(2)}) async-start(bf16[8,6,4096]{2,1,0:T(8,128)(2,1)} %reshape.226), calls=%async_computation.2 | async-start | bytes 1048576 | tf_op jit(solution)/shard_map/all_to_all | solution.py:127
Sparse Core Ops, SparseCore 0:
  9.2 18.6 all-gather.11
  101.8 64.0 all-gather.9
  167.7 15.4 all-gather.13
  184.8 17.1 all-gather.15
  215.4 87.3 reduce-scatter.1

commit v2 on v1

--- a/solution.py
+++ b/solution.py
@@ -11,10 +11,14 @@
 
 SEQ_AXES = ("y", "x", "c")
 TOK_AXES = ("y", "x")
+DEV_AXES = ("e", "p")
+BLOCK_AXES = ("c", "p")
 
 
 def chain_join(earlier, later):
-    return (earlier[0] + later[0], jnp.exp(later[0])[:, None, None] * earlier[1] + later[1])
+    scale = jnp.exp(later[:, -1:, :])
+    state = scale * earlier[:, :-1, :] + later[:, :-1, :]
+    return jnp.concatenate([state, earlier[:, -1:, :] + later[:, -1:, :]], axis=1)
 
 
 def shifted(value, shift, count):
@@ -23,12 +27,17 @@
 
 
 def carried_in(log_total, local_state, count):
-    state = shifted((log_total, local_state), 1, count)
+    width = local_state.shape[-1]
+    packed = jnp.concatenate(
+        [local_state, jnp.broadcast_to(log_total[:, None, None], (log_total.shape[0], 1, width))],
+        axis=1,
+    )
+    state = shifted(packed, 1, count)
     shift = 1
     while shift < count - 1:
         state = chain_join(shifted(state, shift, count), state)
         shift *= 2
-    return state[1]
+    return state[:, :-1, :]
 
 
 def head_norm(attention, gain):
@@ -57,17 +66,19 @@
     count = 1
     for name in SEQ_AXES:
         count *= lax.axis_size(name)
-    dev_count = lax.axis_size("dev")
+    dev_count = lax.axis_size("e") * lax.axis_size("p")
     experts = dev_count // PAIR
 
-    gate_both = lax.all_gather(gate_weight[0], "c", axis=1, tiled=True)
-    up_both = lax.all_gather(up_weight[0], "c", axis=1, tiled=True)
-    down_both = lax.all_gather(down_weight[0], "c", axis=0, tiled=True)
+    gate_up = jnp.stack([gate_weight[0], up_weight[0]])
+    gate_up = lax.all_gather(gate_up, BLOCK_AXES, axis=2, tiled=True)
+    down_all = lax.all_gather(down_weight[0], BLOCK_AXES, axis=0, tiled=True)
 
     tok_count = expert_ids.shape[0]
     top_count = expert_ids.shape[1]
     capacity = max(2, (3 * tok_count * top_count + 2 * experts - 1) // (2 * experts))
-    ids_all = lax.all_gather(expert_ids, "dev", axis=0, tiled=False)
+    capacity = -(-capacity // PAIR) * PAIR
+    half = capacity // PAIR
+    ids_all = lax.all_gather(expert_ids, DEV_AXES, axis=0, tiled=False)
 
     seq_len = queries.shape[0]
     heads = log_decay.shape[1]
@@ -99,46 +110,42 @@
     normed_h = head_norm(attention, head_gain.reshape(heads, 1, head_dim))
     normed = jnp.transpose(normed_h, (1, 0, 2)).reshape(seq_len, heads * head_dim)
 
-    per_expert = dev_count * capacity
+    per_dev = dev_count * half
     flat = ids_all.reshape(dev_count, tok_count * top_count)
     rank = slot_ranks(flat, experts)
     source = jnp.arange(dev_count, dtype=jnp.int32)[:, None]
-    slot_index = flat * per_expert + source * capacity + rank
+    slot_index = (flat * PAIR + rank // half) * per_dev + source * half + rank % half
     token_local = source * tok_count + jnp.arange(tok_count * top_count, dtype=jnp.int32)[None, :] // top_count
     slot_token = (
-        jnp.full((experts * per_expert,), seq_len, jnp.int32)
+        jnp.full((dev_count * per_dev,), seq_len, jnp.int32)
         .at[slot_index.reshape(-1)]
         .set(token_local.reshape(-1))
     )
     padded = jnp.concatenate([normed, jnp.zeros((1, normed.shape[1]), normed.dtype)], axis=0)
-    send_rows = jnp.repeat(padded[slot_token].reshape(experts, per_expert, -1), PAIR, axis=0)
-    arrived = lax.all_to_all(send_rows, "dev", split_axis=0, concat_axis=0, tiled=True)
-    local_rows = jnp.transpose(arrived.reshape(dev_count, per_expert, -1), (1, 0, 2)).reshape(
-        per_expert, -1
-    )
+    send_rows = padded[slot_token].reshape(dev_count, per_dev, -1)
+    arrived = lax.all_to_all(send_rows, DEV_AXES, split_axis=0, concat_axis=0, tiled=True)
+    local_rows = jnp.transpose(arrived, (1, 0, 2)).reshape(per_dev, -1)
     width = local_rows.shape[1]
+    gate_up, down_all, local_rows = lax.optimization_barrier((gate_up, down_all, local_rows))
 
     piece = lax.all_gather(local_rows, TOK_AXES, axis=0, tiled=True)
-    gate_part = jnp.dot(piece, gate_both, preferred_element_type=jnp.float32)
-    up_part = jnp.dot(piece, up_both, preferred_element_type=jnp.float32)
+    gate_part = jnp.dot(piece, gate_up[0], preferred_element_type=jnp.float32)
+    up_part = jnp.dot(piece, gate_up[1], preferred_element_type=jnp.float32)
     hidden_all = (jax.nn.silu(gate_part) * up_part).astype(jnp.bfloat16)
-    term = jnp.dot(hidden_all, down_both, preferred_element_type=jnp.float32).astype(jnp.bfloat16)
+    term = jnp.dot(hidden_all, down_all, preferred_element_type=jnp.float32).astype(jnp.bfloat16)
     summed = lax.psum_scatter(term, TOK_AXES, scatter_dimension=0, tiled=True)
     returned = lax.all_to_all(
-        summed.reshape(dev_count, capacity, width),
-        "dev",
+        summed.reshape(dev_count, half, width),
+        DEV_AXES,
         split_axis=0,
         concat_axis=0,
         tiled=True,
-    ).astype(jnp.float32)
-    expert_out = jnp.sum(returned.reshape(experts, PAIR, capacity, width), axis=1).astype(
-        jnp.bfloat16
     )
-    own = lax.axis_index("dev")
+    own = lax.axis_index(DEV_AXES)
     own_flat = lax.dynamic_index_in_dim(flat, own, 0, False)
     own_rank = lax.dynamic_index_in_dim(rank, own, 0, False)
     pick_index = own_flat * capacity + own_rank
-    picked = expert_out.reshape(experts * capacity, width)[pick_index].reshape(
+    picked = returned.reshape(dev_count * half, width)[pick_index].reshape(
         tok_count, top_count, width
     )
     combined = jnp.sum(picked.astype(jnp.float32) * expert_weights[:, :, None], axis=1)
@@ -155,25 +162,26 @@
         cores = len({int(getattr(d, "core_on_chip", 0)) for d in flat})
         xs = len({int(d.coords[0]) for d in flat})
     ys = seq_count // (xs * cores)
-    return Mesh(devices.reshape(ys, xs, cores, dev_count), ("y", "x", "c", "dev"))
+    shape = (ys, xs, cores, dev_count // PAIR, PAIR)
+    return Mesh(devices.reshape(shape), ("y", "x", "c", "e", "p"))
 
 
 def solution(mesh):
     fine = split_mesh(mesh)
     seq = SEQ_AXES
     in_specs = (
-        P(seq, "dev"),
-        P(seq, "dev"),
-        P(seq, "dev"),
-        P(seq, "dev"),
-        P("dev"),
-        P("dev", None, seq),
-        P("dev", None, seq),
-        P("dev", seq, None),
-        P(seq + ("dev",), None),
-        P(seq + ("dev",), None),
+        P(seq, DEV_AXES),
+        P(seq, DEV_AXES),
+        P(seq, DEV_AXES),
+        P(seq, DEV_AXES),
+        P(DEV_AXES),
+        P(DEV_AXES, None, seq),
+        P(DEV_AXES, None, seq),
+        P(DEV_AXES, seq, None),
+        P(seq + DEV_AXES, None),
+        P(seq + DEV_AXES, None),
     )
-    out_specs = P(seq + ("dev",), None)
+    out_specs = P(seq + DEV_AXES, None)
     return jax.shard_map(
         per_device, mesh=fine, in_specs=in_specs, out_specs=out_specs, check_vma=False
     )

time: 337 us -> 432 us (1.28)
  waiting for transfers between devices: 212 us -> 325 us
  starting transfers between devices: 45.8 us -> 30.4 us
  matrix products: 20.6 us -> 16.1 us
    all_gather x3 -> x2, waiting for transfers between devices: 31 us -> 156 us  [the longest x1 154 us: per_device(): gate_up = lax.all_gather(gate_up, BLOCK_AXES, axis=2, tiled=True)]
    reduce_scatter x1 -> x0, waiting for transfers between devices: 87.5 us -> none  [per_device(): summed = lax.psum_scatter(term, TOK_AXES, scatter_dimension=0, tiled=True)]
    unnamed x5, waiting for transfers between devices: 1.94 us -> 81 us
    ppermute x11 -> x6, starting transfers between devices: 38.6 us -> 23.2 us  [shifted(): return lax.ppermute(value, SEQ_AXES, pairs)]
    ppermute x11 -> x6, waiting for transfers between devices: 12.8 us -> 22.4 us  [shifted(): return lax.ppermute(value, SEQ_AXES, pairs)]
    all_gather x1, waiting for transfers between devices: 62.8 us -> 55 us  [per_device(): piece = lax.all_gather(local_rows, TOK_AXES, axis=0, tiled=True)]
    all_to_all x1, waiting for transfers between devices: 16.1 us -> 10.2 us  [per_device(): lax.all_to_all(summed.reshape(dev_count, half, width), DEV_AXES, split_ax...]
  transfers between devices with their start and end apart: 17 -> 11, of which waited for: 10 -> 10; matrix products, arithmetic and copies ran while one was open for 4% -> 2% of each run, Pallas kernels for 0% -> 0%
where the time goes in v2:
time: 432 us
  waiting for transfers between devices  325 us (75%)
  blocking collectives  34.4 us (8%)
  starting transfers between devices  30.4 us (7%)
  matrix products  16.1 us (4%)
  between operations  13.4 us (3%)
  local copies, waits for them, and re-layouts  6.66 us (2%)
  other arithmetic  5.62 us (1%)
    all_gather x1, waiting for transfers between devices, per_device(): gate_up = lax.all_gather(gate_up, BLOCK_AXES, axis=2, tiled=True)  154 us
    unnamed x5, waiting for transfers between devices  81 us
    all_gather x1, waiting for transfers between devices, per_device(): piece = lax.all_gather(local_rows, TOK_AXES, axis=0, tiled=True)  55 us
    ppermute x6, starting transfers between devices, shifted(): return lax.ppermute(value, SEQ_AXES, pairs)  23.2 us
    ppermute x6, waiting for transfers between devices, shifted(): return lax.ppermute(value, SEQ_AXES, pairs)  22.4 us
    all_gather x1, blocking collectives, per_device(): ids_all = lax.all_gather(expert_ids, DEV_AXES, axis=0, tiled=False)  19.1 us
    all_to_all x1, blocking collectives, per_device(): lax.all_to_all(send_rows, DEV_AXES, split_axis=0, concat_axis=0, tiled=True)  15.3 us
    all_to_all x1, waiting for transfers between devices, per_device(): lax.all_to_all(summed.reshape(dev_count, half, width), DEV_AXES, split_ax...  10.2 us
  transfers between devices with their start and end apart: 11, of which 10 were waited for; matrix products, arithmetic and copies ran while one was open for 2% of the time, Pallas kernels for 0%

profile of v2, /device:TPU:2, one launch (start us, length us, event | category | flops | bytes accessed | tf_op | source)
XLA Modules:
  0.0 431.8 jit_solution(68248489855559855)
XLA Ops:
  6.6 0.7 all-gather.11.cloned.1.call-update
  7.3 3.1 pad_maximum_fusion
  10.5 0.2 reduce_window_sum.22
  10.7 0.2 slice_reduce_fusion
  11.0 0.5 fusion.29
  11.6 1.9 collective-permute-start
  13.5 19.1 %all-gather.2 = s32[8,8,2]{1,2,0:T(2,128)S(1)} all-gather(s32[1,8,2]{1,2,0:T(2,128)S(1)} %bitcast.136), channel_id=3, replica_groups=mesh['y'=4,'x'=4,'c'=2,'e'=4,'p'=2] {'e','p'}, dimensions={0}, use_global_device_ids=true | all-gather | bytes 576 | tf_op jit(solution)/shard_map/all_gather | solution.py:81
  32.6 0.1 copy.58
  32.7 0.4 fusion.53
  33.3 1.9 collective-permute-start.1
  35.2 5.9 %collective-permute-done.1 = f32[4,129,128]{2,1,0:T(8,128)S(1)} collective-permute-done((f32[4,129,128]{2,1,0:T(8,128)S(1)}, f32[4,129,128]{2,1,0:T(8,128)S(1)}, u32[]{:S(2)}, u32[]{:S(2)}) %collective-permute-start.1) | collective-permute-done | bytes 264224 | tf_op jit(solution)/shard_map/ppermute | solution.py:26
  41.2 3.4 collective-permute-start.2
  44.7 0.1 add.205
  44.8 0.1 ne.75
  45.0 0.1 rem.35
  45.0 0.1 copy.57
  45.2 0.1 mul.210
  45.3 5.5 %collective-permute-done.2 = f32[4,129,128]{2,1,0:T(8,128)S(1)} collective-permute-done((f32[4,129,128]{2,1,0:T(8,128)S(1)}, f32[4,129,128]{2,1,0:T(8,128)S(1)}, u32[]{:S(2)}, u32[]{:S(2)}) %collective-permute-start.2) | collective-permute-done | bytes 264224 | tf_op jit(solution)/shard_map/ppermute | solution.py:26
  50.9 4.0 collective-permute-start.3
  55.0 4.3 collective-permute-done.3
  59.4 5.9 %collective-permute-start.4 = (f32[4,129,128]{2,1,0:T(8,128)S(1)}, f32[4,129,128]{2,1,0:T(8,128)S(1)}, u32[]{:S(2)}, u32[]{:S(2)}) collective-permute-start(f32[4,129,128]{2,1,0:T(8,128)S(1)} %pad_maximum_fusion.4), channel_id=1, source_target_pairs={{0,64},{8,72},{16,80},{24,88},{32,96},{40,104},{48,112},{56,120},{... | collective-permute-start | bytes 792584 | tf_op jit(solution)/shard_map/ppermute | solution.py:26
  65.3 0.1 reshape.298
  65.4 1.0 scatter_custom_fusion
  66.4 2.9 collective-permute-done.4
  69.4 6.0 %collective-permute-start.5 = (f32[4,129,128]{2,1,0:T(8,128)S(1)}, f32[4,129,128]{2,1,0:T(8,128)S(1)}, u32[]{:S(2)}, u32[]{:S(2)}) collective-permute-start(f32[4,129,128]{2,1,0:T(8,128)S(1)} %pad_maximum_fusion.5), channel_id=1, source_target_pairs={{0,128},{8,136},{16,144},{24,152},{32,160},{40,168},{48,176},{56,1... | collective-permute-start | bytes 792584 | tf_op jit(solution)/shard_map/ppermute | solution.py:26
  75.5 0.2 convolution_multiply_fusion
  75.7 3.8 collective-permute-done.5
  79.5 0.3 fusion.17
  79.8 0.3 fusion.23
  80.1 0.1 copy_bitcast_fusion
  80.2 1.0 gather_fusion
  81.2 15.3 %all_to_all.10 = bf16[8,24,512]{2,1,0:T(8,128)(2,1)S(1)} all-to-all(bf16[8,24,512]{2,1,0:T(8,128)(2,1)S(1)} %bitcast.124), channel_id=1, replica_groups=mesh['y'=4,'x'=4,'c'=2,'e'=4,'p'=2] {'e','p'}, dimensions={0} | all-to-all | bytes 393216 | tf_op jit(solution)/shard_map/all_to_all | solution.py:126
  96.5 0.7 copy.68
  97.2 2.5 all-gather.11.cloned.1.call-done
  99.7 154.0 %all-gather.7.cloned.1.call-done = bf16[2,4096,512]{2,1,0:T(8,128)(2,1)} async-done(((bf16[2,4096,128]{2,1,0:T(8,128)(2,1)}), bf16[2,4096,512]{2,1,0:T(8,128)(2,1)}) %all-gather.7.cloned.1.call-update) | async-done | bytes 8388624 | tf_op jit(solution)/shard_map/all_gather | solution.py:73
  253.8 55.0 %all-gather.9.cloned.1.call-done = bf16[384,4096]{1,0:T(8,128)(2,1)} async-done(((bf16[24,4096]{1,0:T(8,128)(2,1)}), bf16[384,4096]{1,0:T(8,128)(2,1)}) %all-gather.9.cloned.1.call-update) | async-done | bytes 3145744 | tf_op jit(solution)/shard_map/all_gather | solution.py:131
  308.8 6.0 %fusion.2 = f32[384,512]{1,0:T(8,128)} fusion(bf16[384,4096]{1,0:T(8,128)(2,1)} %all-gather.9.cloned.1.call-done, bf16[2,4096,512]{2,1,0:T(8,128)(2,1)} %all-gather.7.cloned.1.call-done), kind=kOutput, calls=%fused_computation.6 | convolution fusion | flops 1610612736 | bytes 8126464 | tf_op jit(solution)/shard_map/dot_general | solution.py:132
  314.7 8.9 %convolution_convert_fusion = bf16[384,4096]{1,0:T(8,128)(2,1)} fusion(bf16[512,4096]{1,0:T(8,128)(2,1)} %bitcast.137, bf16[384,4096]{1,0:T(8,128)(2,1)S(1)} %copy-done.7, bf16[2,4096,512]{2,1,0:T(8,128)(2,1)} %all-gather.7.cloned.1.call-done, f32[384,512]{1,0:T(8,128)} %fusion.2), kind=kOutput, calls=%fused_computation.3 | convolution fusion | flops 3223977984 | bytes 15466496 | tf_op jit(solution)/shard_map/dot_general | solution.py:135
  323.7 80.3 %reduce-scatter.4.cloned.1.call-done = bf16[24,4096]{1,0:T(8,128)(2,1)} async-done(((bf16[384,4096]{1,0:T(8,128)(2,1)}), bf16[24,4096]{1,0:T(8,128)(2,1)}) %reduce-scatter.4.cloned.1.call-update) | async-done | bytes 196624
  404.0 1.8 reshape.275
  405.7 7.0 %all-to-all-start.1 = ((bf16[8,3,4096]{2,1,0:T(4,128)(2,1)}), bf16[8,3,4096]{2,1,0:T(4,128)(2,1)S(1)}, u32[]{:S(2)}, u32[]{:S(2)}) async-start(bf16[8,3,4096]{2,1,0:T(4,128)(2,1)} %reshape.275), calls=%async_computation.1 | async-start | bytes 524288 | tf_op jit(solution)/shard_map/all_to_all | solution.py:137
  412.8 0.1 copy.63
  412.8 0.2 add_reduce_fusion
  413.0 10.2 %all-to-all-done.1 = bf16[8,3,4096]{2,1,0:T(4,128)(2,1)S(1)} async-done(((bf16[8,3,4096]{2,1,0:T(4,128)(2,1)}), bf16[8,3,4096]{2,1,0:T(4,128)(2,1)S(1)}, u32[]{:S(2)}, u32[]{:S(2)}) %all-to-all-start.1) | async-done | bytes 196640 | tf_op jit(solution)/shard_map/all_to_all | solution.py:137
  423.2 0.2 reshape.276
  423.4 0.6 gather_fusion.1
  424.0 0.2 reshape.277
  424.2 1.0 multiply_reduce_fusion
  (57 shorter events, 1.1 us)
Async XLA Ops:
  6.5 4.5 %copy-start = (bf16[64,512]{1,0:T(8,128)(2,1)S(1)}, bf16[64,512]{1,0:T(8,128)(2,1)}, u32[]{:S(2)}) copy-start(bf16[64,512]{1,0:T(8,128)(2,1)} %param.12) | copy-start | bytes 196612
  6.5 3.9 copy-start.4
  6.5 4.4 %copy-start.1 = (bf16[64,512]{1,0:T(8,128)(2,1)S(1)}, bf16[64,512]{1,0:T(8,128)(2,1)}, u32[]{:S(2)}) copy-start(bf16[64,512]{1,0:T(8,128)(2,1)} %param.11) | copy-start | bytes 196612
  6.5 7.0 %copy-start.5 = (s32[8,2]{0,1:T(2,128)S(1)}, s32[8,2]{0,1:T(2,128)}, u32[]{:S(2)}) copy-start(s32[8,2]{0,1:T(2,128)} %param.18) | copy-start | bytes 196
  6.5 93.1 %all-gather.11.cloned.1.call-start = ((), (), s32[]{:S(2)}) async-start(), calls=%async_computation.5 | async-start | bytes 5242880 | tf_op jit(solution)/shard_map/all_gather | solution.py:74
  7.3 246.4 %all-gather.7.cloned.1.call-start = ((), (), s32[]{:S(2)}) async-start(), calls=%async_computation.3 | async-start | bytes 10485760 | tf_op jit(solution)/shard_map/all_gather | solution.py:73
  10.4 65.1 %copy-start.2 = (bf16[64,512]{1,0:T(8,128)(2,1)S(1)}, bf16[64,512]{1,0:T(8,128)(2,1)}, u32[]{:S(2)}) copy-start(bf16[64,512]{1,0:T(8,128)(2,1)} %param.10) | copy-start | bytes 196612
  10.4 69.7 %copy-start.3 = (f32[512]{0:T(512)S(1)}, f32[512]{0:T(512)}, u32[]{:S(2)}) copy-start(f32[512]{0:T(512)} %param.14) | copy-start | bytes 6148
  10.4 298.3 %all-gather.9.cloned.1.call-start = ((), (), s32[]{:S(2)}) async-start(), calls=%async_computation.4 | async-start | bytes 3342336 | tf_op jit(solution)/shard_map/all_gather | solution.py:131
  11.6 21.7 %collective-permute-start = (f32[4,129,128]{2,1,0:T(8,128)S(1)}, f32[4,129,128]{2,1,0:T(8,128)S(1)}, u32[]{:S(2)}, u32[]{:S(2)}) collective-permute-start(f32[4,129,128]{2,1,0:T(8,128)S(1)} %pad_maximum_fusion.1), channel_id=1, source_target_pairs={{0,8},{8,16},{16,24},{24,32},{32,40},{40,48},{48,56},{56,64},{64,7... | collective-permute-start | bytes 792584 | tf_op jit(solution)/shard_map/ppermute | solution.py:26
  33.3 7.9 %collective-permute-start.1 = (f32[4,129,128]{2,1,0:T(8,128)S(1)}, f32[4,129,128]{2,1,0:T(8,128)S(1)}, u32[]{:S(2)}, u32[]{:S(2)}) collective-permute-start(f32[4,129,128]{2,1,0:T(8,128)S(1)} %collective-permute-done), channel_id=1, source_target_pairs={{0,8},{8,16},{16,24},{24,32},{32,40},{40,48},{48,56},{56,64},{64,7... | collective-permute-start | bytes 792584 | tf_op jit(solution)/shard_map/ppermute | solution.py:26
  41.2 9.6 %collective-permute-start.2 = (f32[4,129,128]{2,1,0:T(8,128)S(1)}, f32[4,129,128]{2,1,0:T(8,128)S(1)}, u32[]{:S(2)}, u32[]{:S(2)}) collective-permute-start(f32[4,129,128]{2,1,0:T(8,128)S(1)} %pad_maximum_fusion.2), channel_id=1, source_target_pairs={{0,16},{8,24},{16,32},{24,40},{32,48},{40,56},{48,64},{56,72},{64,... | collective-permute-start | bytes 792584 | tf_op jit(solution)/shard_map/ppermute | solution.py:26
  50.9 8.4 %collective-permute-start.3 = (f32[4,129,128]{2,1,0:T(8,128)S(1)}, f32[4,129,128]{2,1,0:T(8,128)S(1)}, u32[]{:S(2)}, u32[]{:S(2)}) collective-permute-start(f32[4,129,128]{2,1,0:T(8,128)S(1)} %pad_maximum_fusion.3), channel_id=1, source_target_pairs={{0,32},{8,40},{16,48},{24,56},{32,64},{40,72},{48,80},{56,88},{64,... | collective-permute-start | bytes 792584 | tf_op jit(solution)/shard_map/ppermute | solution.py:26
  59.4 10.0 %collective-permute-start.4 = (f32[4,129,128]{2,1,0:T(8,128)S(1)}, f32[4,129,128]{2,1,0:T(8,128)S(1)}, u32[]{:S(2)}, u32[]{:S(2)}) collective-permute-start(f32[4,129,128]{2,1,0:T(8,128)S(1)} %pad_maximum_fusion.4), channel_id=1, source_target_pairs={{0,64},{8,72},{16,80},{24,88},{32,96},{40,104},{48,112},{56,120},{... | collective-permute-start | bytes 792584 | tf_op jit(solution)/shard_map/ppermute | solution.py:26
  69.4 10.1 %collective-permute-start.5 = (f32[4,129,128]{2,1,0:T(8,128)S(1)}, f32[4,129,128]{2,1,0:T(8,128)S(1)}, u32[]{:S(2)}, u32[]{:S(2)}) collective-permute-start(f32[4,129,128]{2,1,0:T(8,128)S(1)} %pad_maximum_fusion.5), channel_id=1, source_target_pairs={{0,128},{8,136},{16,144},{24,152},{32,160},{40,168},{48,176},{56,1... | collective-permute-start | bytes 792584 | tf_op jit(solution)/shard_map/ppermute | solution.py:26
  253.7 150.3 %reduce-scatter.4.cloned.1.call-start = ((), (), s32[]{:S(2)}) async-start(), calls=%async_computation.6 | async-start | bytes 3342336
  308.8 6.0 %copy-start.7 = (bf16[384,4096]{1,0:T(8,128)(2,1)S(1)}, bf16[384,4096]{1,0:T(8,128)(2,1)}, u32[]{:S(2)}) copy-start(bf16[384,4096]{1,0:T(8,128)(2,1)} %all-gather.9.cloned.1.call-done) | copy-start | bytes 9437188
  314.7 98.0 %copy-start.6 = (f32[8,2]{0,1:T(2,128)S(1)}, f32[8,2]{0,1:T(2,128)}, u32[]{:S(2)}) copy-start(f32[8,2]{0,1:T(2,128)} %param.19) | copy-start | bytes 196
  405.7 17.5 %all-to-all-start.1 = ((bf16[8,3,4096]{2,1,0:T(4,128)(2,1)}), bf16[8,3,4096]{2,1,0:T(4,128)(2,1)S(1)}, u32[]{:S(2)}, u32[]{:S(2)}) async-start(bf16[8,3,4096]{2,1,0:T(4,128)(2,1)} %reshape.275), calls=%async_computation.1 | async-start | bytes 524288 | tf_op jit(solution)/shard_map/all_to_all | solution.py:137
Sparse Core Ops, SparseCore 0:
  9.2 90.4 all-gather.10
  101.5 152.1 all-gather.6
  256.1 52.6 all-gather.8
  323.8 80.1 reduce-scatter.3

commit v3 on v1

--- a/solution.py
+++ b/solution.py
@@ -14,7 +14,9 @@
 
 
 def chain_join(earlier, later):
-    return (earlier[0] + later[0], jnp.exp(later[0])[:, None, None] * earlier[1] + later[1])
+    scale = jnp.exp(later[:, -1:, :])
+    state = scale * earlier[:, :-1, :] + later[:, :-1, :]
+    return jnp.concatenate([state, earlier[:, -1:, :] + later[:, -1:, :]], axis=1)
 
 
 def shifted(value, shift, count):
@@ -23,12 +25,17 @@
 
 
 def carried_in(log_total, local_state, count):
-    state = shifted((log_total, local_state), 1, count)
+    width = local_state.shape[-1]
+    packed = jnp.concatenate(
+        [local_state, jnp.broadcast_to(log_total[:, None, None], (log_total.shape[0], 1, width))],
+        axis=1,
+    )
+    state = shifted(packed, 1, count)
     shift = 1
     while shift < count - 1:
         state = chain_join(shifted(state, shift, count), state)
         shift *= 2
-    return state[1]
+    return state[:, :-1, :]
 
 
 def head_norm(attention, gain):
@@ -117,13 +124,27 @@
         per_expert, -1
     )
     width = local_rows.shape[1]
-
-    piece = lax.all_gather(local_rows, TOK_AXES, axis=0, tiled=True)
+    gate_both, up_both, down_both, local_rows = lax.optimization_barrier(
+        (gate_both, up_both, down_both, local_rows)
+    )
+    groups = 1
+    for name in TOK_AXES:
+        groups *= lax.axis_size(name)
+    piece = lax.all_to_all(
+        jnp.broadcast_to(local_rows[None], (groups,) + local_rows.shape),
+        TOK_AXES,
+        split_axis=0,
+        concat_axis=0,
+        tiled=True,
+    ).reshape(groups * per_expert, width)
     gate_part = jnp.dot(piece, gate_both, preferred_element_type=jnp.float32)
     up_part = jnp.dot(piece, up_both, preferred_element_type=jnp.float32)
     hidden_all = (jax.nn.silu(gate_part) * up_part).astype(jnp.bfloat16)
     term = jnp.dot(hidden_all, down_both, preferred_element_type=jnp.float32).astype(jnp.bfloat16)
-    summed = lax.psum_scatter(term, TOK_AXES, scatter_dimension=0, tiled=True)
+    parts = lax.all_to_all(
+        term.reshape(groups, per_expert, width), TOK_AXES, split_axis=0, concat_axis=0, tiled=True
+    )
+    summed = jnp.sum(parts.astype(jnp.float32), axis=0).astype(jnp.bfloat16)
     returned = lax.all_to_all(
         summed.reshape(dev_count, capacity, width),
         "dev",

time: 337 us -> 286 us (0.85)
  waiting for transfers between devices: 212 us -> 36.3 us
  blocking collectives: 34.7 us -> 177 us
  starting transfers between devices: 45.8 us -> 26.9 us
  matrix products: 20.6 us -> 16.5 us
  other arithmetic: 3.39 us -> 7.31 us
    all_to_all x0 -> x2, blocking collectives: none -> 142 us  [the longest x1 72.9 us: per_device(): lax.all_to_all(jnp.broadcast_to(local_rows[None], (groups,) + local_rows....]
    reduce_scatter x1 -> x0, waiting for transfers between devices: 87.5 us -> none  [per_device(): summed = lax.psum_scatter(term, TOK_AXES, scatter_dimension=0, tiled=True)]
    all_gather x1 -> x0, waiting for transfers between devices: 62.8 us -> none  [per_device(): piece = lax.all_gather(local_rows, TOK_AXES, axis=0, tiled=True)]
    all_gather x1, waiting for transfers between devices: 18.9 us -> 0.02 us  [per_device(): down_both = lax.all_gather(down_weight[0], 'c', axis=0, tiled=True)]
    ppermute x11 -> x6, starting transfers between devices: 38.6 us -> 23.3 us  [shifted(): return lax.ppermute(value, SEQ_AXES, pairs)]
    all_gather x1, waiting for transfers between devices: 12 us -> 0.02 us  [per_device(): up_both = lax.all_gather(up_weight[0], 'c', axis=1, tiled=True)]
    ppermute x11 -> x6, waiting for transfers between devices: 12.8 us -> 21.9 us  [shifted(): return lax.ppermute(value, SEQ_AXES, pairs)]
    reduce_sum x0 -> x1, other arithmetic: none -> 4.02 us  [per_device(): summed = jnp.sum(parts.astype(jnp.float32), axis=0).astype(jnp.bfloat16)]
  transfers between devices with their start and end apart: 17 -> 10, of which waited for: 10 -> 6; matrix products, arithmetic and copies ran while one was open for 4% -> 3% of each run, Pallas kernels for 0% -> 0%
where the time goes in v3:
time: 286 us
  blocking collectives  177 us (62%)
  waiting for transfers between devices  36.3 us (13%)
  starting transfers between devices  26.9 us (9%)
  matrix products  16.5 us (6%)
  between operations  13.5 us (5%)
  local copies, waits for them, and re-layouts  8.54 us (3%)
  other arithmetic  7.31 us (3%)
    all_to_all x1, blocking collectives, per_device(): lax.all_to_all(jnp.broadcast_to(local_rows[None], (groups,) + local_rows....  72.9 us
    all_to_all x1, blocking collectives, per_device(): lax.all_to_all(term.reshape(groups, per_expert, width), TOK_AXES, split_a...  69.2 us
    ppermute x6, starting transfers between devices, shifted(): return lax.ppermute(value, SEQ_AXES, pairs)  23.3 us
    ppermute x6, waiting for transfers between devices, shifted(): return lax.ppermute(value, SEQ_AXES, pairs)  21.9 us
    all_gather x1, blocking collectives, per_device(): ids_all = lax.all_gather(expert_ids, 'dev', axis=0, tiled=False)  19.4 us
    all_to_all x1, blocking collectives, per_device(): lax.all_to_all(send_rows, 'dev', split_axis=0, concat_axis=0, tiled=True)  15.3 us
    all_to_all x1, waiting for transfers between devices, per_device(): lax.all_to_all(summed.reshape(dev_count, capacity, width), 'dev', split_a...  12.9 us
    dot_general x1, matrix products, per_device(): jnp.dot(hidden_all, down_both, preferred_element_type=jnp.float32)  12.7 us
  transfers between devices with their start and end apart: 10, of which 6 were waited for; matrix products, arithmetic and copies ran while one was open for 3% of the time, Pallas kernels for 0%

profile of v3, /device:TPU:2, one launch (start us, length us, event | category | flops | bytes accessed | tf_op | source)
XLA Modules:
  0.0 285.9 jit_solution(16269387369030982537)
XLA Ops:
  6.6 0.7 all-gather.9.cloned.1.call-update
  7.3 0.7 all-gather.11.cloned.1.call-update
  8.1 0.9 reduce_window_sum.22
  9.0 0.2 slice_reduce_fusion
  9.2 1.3 fusion.21
  10.7 1.9 collective-permute-start
  12.6 19.4 %all-gather.4 = s32[8,8,2]{1,2,0:T(2,128)S(1)} all-gather(s32[1,8,2]{1,2,0:T(2,128)} %bitcast.136), channel_id=5, replica_groups=mesh['y'=4,'x'=4,'c'=2,'dev'=8] {'dev'}, dimensions={0}, use_global_device_ids=true | all-gather | bytes 576 | tf_op jit(solution)/shard_map/all_gather | solution.py:77
  32.0 1.9 collective-permute-start.1
  33.9 0.1 copy.42
  34.0 0.4 fusion.44
  34.5 5.4 %collective-permute-done.1 = f32[4,129,128]{2,1,0:T(8,128)S(1)} collective-permute-done((f32[4,129,128]{2,1,0:T(8,128)S(1)}, f32[4,129,128]{2,1,0:T(8,128)S(1)}, u32[]{:S(2)}, u32[]{:S(2)}) %collective-permute-start.1) | collective-permute-done | bytes 264224 | tf_op jit(solution)/shard_map/ppermute | solution.py:24
  40.0 3.4 %collective-permute-start.2 = (f32[4,129,128]{2,1,0:T(8,128)S(1)}, f32[4,129,128]{2,1,0:T(8,128)S(1)}, u32[]{:S(2)}, u32[]{:S(2)}) collective-permute-start(f32[4,129,128]{2,1,0:T(8,128)S(1)} %pad_maximum_fusion.1), channel_id=1, source_target_pairs={{0,16},{8,24},{16,32},{24,40},{32,48},{40,56},{48,64},{56,72},{64,... | collective-permute-start | bytes 792584 | tf_op jit(solution)/shard_map/ppermute | solution.py:24
  43.4 0.1 add.165
  43.6 0.1 reduce_sum.52
  43.7 0.1 copy.41
  43.8 0.1 mul.193
  44.0 5.6 %collective-permute-done.2 = f32[4,129,128]{2,1,0:T(8,128)S(1)} collective-permute-done((f32[4,129,128]{2,1,0:T(8,128)S(1)}, f32[4,129,128]{2,1,0:T(8,128)S(1)}, u32[]{:S(2)}, u32[]{:S(2)}) %collective-permute-start.2) | collective-permute-done | bytes 264224 | tf_op jit(solution)/shard_map/ppermute | solution.py:24
  49.6 4.0 %collective-permute-start.3 = (f32[4,129,128]{2,1,0:T(8,128)S(1)}, f32[4,129,128]{2,1,0:T(8,128)S(1)}, u32[]{:S(2)}, u32[]{:S(2)}) collective-permute-start(f32[4,129,128]{2,1,0:T(8,128)S(1)} %pad_maximum_fusion.2), channel_id=1, source_target_pairs={{0,32},{8,40},{16,48},{24,56},{32,64},{40,72},{48,80},{56,88},{64,... | collective-permute-start | bytes 792584 | tf_op jit(solution)/shard_map/ppermute | solution.py:24
  53.7 0.1 broadcast_add_fusion
  53.8 4.2 %collective-permute-done.3 = f32[4,129,128]{2,1,0:T(8,128)S(1)} collective-permute-done((f32[4,129,128]{2,1,0:T(8,128)S(1)}, f32[4,129,128]{2,1,0:T(8,128)S(1)}, u32[]{:S(2)}, u32[]{:S(2)}) %collective-permute-start.3) | collective-permute-done | bytes 264224 | tf_op jit(solution)/shard_map/ppermute | solution.py:24
  58.0 6.0 %collective-permute-start.4 = (f32[4,129,128]{2,1,0:T(8,128)S(1)}, f32[4,129,128]{2,1,0:T(8,128)S(1)}, u32[]{:S(2)}, u32[]{:S(2)}) collective-permute-start(f32[4,129,128]{2,1,0:T(8,128)S(1)} %pad_maximum_fusion.3), channel_id=1, source_target_pairs={{0,64},{8,72},{16,80},{24,88},{32,96},{40,104},{48,112},{56,120},{... | collective-permute-start | bytes 792584 | tf_op jit(solution)/shard_map/ppermute | solution.py:24
  64.1 0.1 reshape.257
  64.1 1.0 scatter_custom_fusion
  65.1 2.9 %collective-permute-done.4 = f32[4,129,128]{2,1,0:T(8,128)S(1)} collective-permute-done((f32[4,129,128]{2,1,0:T(8,128)S(1)}, f32[4,129,128]{2,1,0:T(8,128)S(1)}, u32[]{:S(2)}, u32[]{:S(2)}) %collective-permute-start.4) | collective-permute-done | bytes 264224 | tf_op jit(solution)/shard_map/ppermute | solution.py:24
  68.2 6.0 %collective-permute-start.5 = (f32[4,129,128]{2,1,0:T(8,128)S(1)}, f32[4,129,128]{2,1,0:T(8,128)S(1)}, u32[]{:S(2)}, u32[]{:S(2)}) collective-permute-start(f32[4,129,128]{2,1,0:T(8,128)S(1)} %pad_maximum_fusion.4), channel_id=1, source_target_pairs={{0,128},{8,136},{16,144},{24,152},{32,160},{40,168},{48,176},{56,1... | collective-permute-start | bytes 792584 | tf_op jit(solution)/shard_map/ppermute | solution.py:24
  74.2 0.2 convolution_multiply_fusion.1
  74.4 3.8 %collective-permute-done.5 = f32[4,129,128]{2,1,0:T(8,128)S(1)} collective-permute-done((f32[4,129,128]{2,1,0:T(8,128)S(1)}, f32[4,129,128]{2,1,0:T(8,128)S(1)}, u32[]{:S(2)}, u32[]{:S(2)}) %collective-permute-start.5) | collective-permute-done | bytes 264224 | tf_op jit(solution)/shard_map/ppermute | solution.py:24
  78.2 0.3 fusion.9
  78.5 0.3 fusion.15
  78.8 0.1 copy_bitcast_fusion
  79.0 1.0 gather_fusion
  80.0 15.3 %all_to_all.20 = bf16[8,48,512]{2,1,0:T(8,128)(2,1)S(1)} all-to-all(bf16[8,48,512]{2,1,0:T(8,128)(2,1)S(1)} %bitcast.124), channel_id=1, replica_groups=mesh['y'=4,'x'=4,'c'=2,'dev'=8] {'dev'}, dimensions={0} | all-to-all | bytes 786432 | tf_op jit(solution)/shard_map/all_to_all | solution.py:122
  95.4 0.8 broadcast_in_dim.60
  96.2 72.9 %all_to_all.21 = bf16[16,48,4096]{2,1,0:T(8,128)(2,1)S(1)} all-to-all(bf16[16,48,4096]{2,1,0:T(8,128)(2,1)S(1)} %broadcast_in_dim.60), channel_id=1, replica_groups=mesh['y'=4,'x'=4,'c'=2,'dev'=8] {'y','x'}, dimensions={0} | all-to-all | bytes 12582912 | tf_op jit(solution)/shard_map/all_to_all | solution.py:133
  169.1 2.8 copy-done.1
  172.0 1.8 fusion.45
  173.8 12.7 %convolution_convert_fusion = bf16[768,4096]{1,0:T(8,128)(2,1)} fusion(bf16[256,4096]{1,0:T(8,128)(2,1)} %bitcast.139, bf16[768,4096]{1,0:T(8,128)(2,1)} %bitcast.121, bf16[4096,256]{1,0:T(8,128)(2,1)S(1)} %bitcast.138, f32[768,256]{1,0:T(8,128)S(1)} %fusion.45), kind=kOutput, calls=%fused_computation.3 | convolution fusion | flops 3225550848 | bytes 17563648 | tf_op jit(solution)/shard_map/dot_general | solution.py:143
  186.5 69.2 %all_to_all.22 = bf16[16,48,4096]{2,1,0:T(8,128)(2,1)} all-to-all(bf16[16,48,4096]{2,1,0:T(8,128)(2,1)} %bitcast.122), channel_id=1, replica_groups=mesh['y'=4,'x'=4,'c'=2,'dev'=8] {'y','x'}, dimensions={0} | all-to-all | bytes 12582912 | tf_op jit(solution)/shard_map/all_to_all | solution.py:144
  255.7 4.0 %reduce_sum.53 = bf16[48,4096]{1,0:T(8,128)(2,1)S(1)} reduce(bf16[16,48,4096]{2,1,0:T(8,128)(2,1)} %all_to_all.22, bf16[]{:T(256)} %constant.52.clone.1), dimensions={0}, to_apply=%region_5.6 | reduce | flops 2949120 | bytes 6684674 | tf_op jit(solution)/shard_map/reduce_sum | solution.py:147
  259.7 0.9 reshape.233
  260.7 3.5 %all-to-all-start.3 = ((bf16[8,6,4096]{2,1,0:T(8,128)(2,1)}), bf16[8,6,4096]{2,1,0:T(8,128)(2,1)S(1)}, u32[]{:S(2)}, u32[]{:S(2)}) async-start(bf16[8,6,4096]{2,1,0:T(8,128)(2,1)} %reshape.233), calls=%async_computation.3 | async-start | bytes 1048576 | tf_op jit(solution)/shard_map/all_to_all | solution.py:148
  264.2 0.1 copy.45
  264.3 0.2 add_reduce_fusion
  264.5 12.9 %all-to-all-done.3 = bf16[8,6,4096]{2,1,0:T(8,128)(2,1)S(1)} async-done(((bf16[8,6,4096]{2,1,0:T(8,128)(2,1)}), bf16[8,6,4096]{2,1,0:T(8,128)(2,1)S(1)}, u32[]{:S(2)}, u32[]{:S(2)}) %all-to-all-start.3) | async-done | bytes 393248 | tf_op jit(solution)/shard_map/all_to_all | solution.py:148
  277.4 0.1 bitcast_reduce_fusion
  277.6 0.6 gather_fusion.1
  278.2 0.2 reshape.236
  278.4 1.0 multiply_reduce_fusion
  (55 shorter events, 1.0 us)
Async XLA Ops:
  6.5 2.7 copy-start
  6.5 67.7 %copy-start.2 = (bf16[64,512]{1,0:T(8,128)(2,1)S(1)}, bf16[64,512]{1,0:T(8,128)(2,1)}, u32[]{:S(2)}) copy-start(bf16[64,512]{1,0:T(8,128)(2,1)} %param.11) | copy-start | bytes 196612
  6.5 67.7 %copy-start.3 = (bf16[64,512]{1,0:T(8,128)(2,1)S(1)}, bf16[64,512]{1,0:T(8,128)(2,1)}, u32[]{:S(2)}) copy-start(bf16[64,512]{1,0:T(8,128)(2,1)} %param.10) | copy-start | bytes 196612
  6.5 72.3 %copy-start.4 = (f32[512]{0:T(512)S(1)}, f32[512]{0:T(512)}, u32[]{:S(2)}) copy-start(f32[512]{0:T(512)} %param.14) | copy-start | bytes 6148
  6.5 88.8 %all-gather.9.cloned.1.call-start = ((), (), s32[]{:S(2)}) async-start(), calls=%async_computation.4 | async-start | bytes 3145728 | tf_op jit(solution)/shard_map/all_gather | solution.py:70
  7.3 88.1 %all-gather.11.cloned.1.call-start = ((), (), s32[]{:S(2)}) async-start(), calls=%async_computation.5 | async-start | bytes 3145728 | tf_op jit(solution)/shard_map/all_gather | solution.py:71
  8.0 87.4 %all-gather.13.cloned.1.call-start = ((), (), s32[]{:S(2)}) async-start(), calls=%async_computation.6 | async-start | bytes 3145728 | tf_op jit(solution)/shard_map/all_gather | solution.py:72
  10.7 21.4 %collective-permute-start = (f32[4,129,128]{2,1,0:T(8,128)S(1)}, f32[4,129,128]{2,1,0:T(8,128)S(1)}, u32[]{:S(2)}, u32[]{:S(2)}) collective-permute-start(f32[4,129,128]{2,1,0:T(8,128)S(1)} %pad_maximum_fusion), channel_id=1, source_target_pairs={{0,8},{8,16},{16,24},{24,32},{32,40},{40,48},{48,56},{56,64},{64,7... | collective-permute-start | bytes 792584 | tf_op jit(solution)/shard_map/ppermute | solution.py:24
  32.0 7.9 %collective-permute-start.1 = (f32[4,129,128]{2,1,0:T(8,128)S(1)}, f32[4,129,128]{2,1,0:T(8,128)S(1)}, u32[]{:S(2)}, u32[]{:S(2)}) collective-permute-start(f32[4,129,128]{2,1,0:T(8,128)S(1)} %collective-permute-done), channel_id=1, source_target_pairs={{0,8},{8,16},{16,24},{24,32},{32,40},{40,48},{48,56},{56,64},{64,7... | collective-permute-start | bytes 792584 | tf_op jit(solution)/shard_map/ppermute | solution.py:24
  40.0 9.6 %collective-permute-start.2 = (f32[4,129,128]{2,1,0:T(8,128)S(1)}, f32[4,129,128]{2,1,0:T(8,128)S(1)}, u32[]{:S(2)}, u32[]{:S(2)}) collective-permute-start(f32[4,129,128]{2,1,0:T(8,128)S(1)} %pad_maximum_fusion.1), channel_id=1, source_target_pairs={{0,16},{8,24},{16,32},{24,40},{32,48},{40,56},{48,64},{56,72},{64,... | collective-permute-start | bytes 792584 | tf_op jit(solution)/shard_map/ppermute | solution.py:24
  49.6 8.3 %collective-permute-start.3 = (f32[4,129,128]{2,1,0:T(8,128)S(1)}, f32[4,129,128]{2,1,0:T(8,128)S(1)}, u32[]{:S(2)}, u32[]{:S(2)}) collective-permute-start(f32[4,129,128]{2,1,0:T(8,128)S(1)} %pad_maximum_fusion.2), channel_id=1, source_target_pairs={{0,32},{8,40},{16,48},{24,56},{32,64},{40,72},{48,80},{56,88},{64,... | collective-permute-start | bytes 792584 | tf_op jit(solution)/shard_map/ppermute | solution.py:24
  58.0 10.1 %collective-permute-start.4 = (f32[4,129,128]{2,1,0:T(8,128)S(1)}, f32[4,129,128]{2,1,0:T(8,128)S(1)}, u32[]{:S(2)}, u32[]{:S(2)}) collective-permute-start(f32[4,129,128]{2,1,0:T(8,128)S(1)} %pad_maximum_fusion.3), channel_id=1, source_target_pairs={{0,64},{8,72},{16,80},{24,88},{32,96},{40,104},{48,112},{56,120},{... | collective-permute-start | bytes 792584 | tf_op jit(solution)/shard_map/ppermute | solution.py:24
  68.2 10.1 %collective-permute-start.5 = (f32[4,129,128]{2,1,0:T(8,128)S(1)}, f32[4,129,128]{2,1,0:T(8,128)S(1)}, u32[]{:S(2)}, u32[]{:S(2)}) collective-permute-start(f32[4,129,128]{2,1,0:T(8,128)S(1)} %pad_maximum_fusion.4), channel_id=1, source_target_pairs={{0,128},{8,136},{16,144},{24,152},{32,160},{40,168},{48,176},{56,1... | collective-permute-start | bytes 792584 | tf_op jit(solution)/shard_map/ppermute | solution.py:24
  96.2 75.8 %copy-start.6 = (bf16[1,4096,256]{2,1,0:T(8,128)(2,1)S(1)}, bf16[1,4096,256]{2,1,0:T(8,128)(2,1)}, u32[]{:S(2)}) copy-start(bf16[1,4096,256]{2,1,0:T(8,128)(2,1)} %all-gather.9.cloned.1.call-done) | copy-start | bytes 6291460
  169.1 2.8 copy-start.1
  169.1 4.6 %copy-start.7 = (bf16[1,4096,256]{2,1,0:T(8,128)(2,1)S(1)}, bf16[1,4096,256]{2,1,0:T(8,128)(2,1)}, u32[]{:S(2)}) copy-start(bf16[1,4096,256]{2,1,0:T(8,128)(2,1)} %all-gather.11.cloned.1.call-done) | copy-start | bytes 6291460
  255.7 8.5 %copy-start.5 = (f32[8,2]{0,1:T(2,128)S(1)}, f32[8,2]{0,1:T(2,128)}, u32[]{:S(2)}) copy-start(f32[8,2]{0,1:T(2,128)} %param.19) | copy-start | bytes 196
  260.7 16.7 %all-to-all-start.3 = ((bf16[8,6,4096]{2,1,0:T(8,128)(2,1)}), bf16[8,6,4096]{2,1,0:T(8,128)(2,1)S(1)}, u32[]{:S(2)}, u32[]{:S(2)}) async-start(bf16[8,6,4096]{2,1,0:T(8,128)(2,1)} %reshape.233), calls=%async_computation.3 | async-start | bytes 1048576 | tf_op jit(solution)/shard_map/all_to_all | solution.py:148
Sparse Core Ops, SparseCore 0:
  9.2 18.6 all-gather.8
  29.6 16.9 all-gather.10
  48.4 17.1 all-gather.12

commit v4 on v2

--- a/solution.py
+++ b/solution.py
@@ -12,7 +12,6 @@
 SEQ_AXES = ("y", "x", "c")
 TOK_AXES = ("y", "x")
 DEV_AXES = ("e", "p")
-BLOCK_AXES = ("c", "p")
 
 
 def chain_join(earlier, later):
@@ -69,9 +68,10 @@
     dev_count = lax.axis_size("e") * lax.axis_size("p")
     experts = dev_count // PAIR
 
+    partner = [(0, 1), (1, 0)]
     gate_up = jnp.stack([gate_weight[0], up_weight[0]])
-    gate_up = lax.all_gather(gate_up, BLOCK_AXES, axis=2, tiled=True)
-    down_all = lax.all_gather(down_weight[0], BLOCK_AXES, axis=0, tiled=True)
+    gate_up = jnp.concatenate([gate_up, lax.ppermute(gate_up, "p", partner)], axis=2)
+    down_all = jnp.concatenate([down_weight[0], lax.ppermute(down_weight[0], "p", partner)], axis=0)
 
     tok_count = expert_ids.shape[0]
     top_count = expert_ids.shape[1]
@@ -123,17 +123,30 @@
     )
     padded = jnp.concatenate([normed, jnp.zeros((1, normed.shape[1]), normed.dtype)], axis=0)
     send_rows = padded[slot_token].reshape(dev_count, per_dev, -1)
+    gate_up, down_all, send_rows = lax.optimization_barrier((gate_up, down_all, send_rows))
+    gate_up = lax.all_gather(gate_up, "c", axis=2, tiled=True)
+    down_all = lax.all_gather(down_all, "c", axis=0, tiled=True)
     arrived = lax.all_to_all(send_rows, DEV_AXES, split_axis=0, concat_axis=0, tiled=True)
     local_rows = jnp.transpose(arrived, (1, 0, 2)).reshape(per_dev, -1)
     width = local_rows.shape[1]
-    gate_up, down_all, local_rows = lax.optimization_barrier((gate_up, down_all, local_rows))
-
-    piece = lax.all_gather(local_rows, TOK_AXES, axis=0, tiled=True)
+    groups = 1
+    for name in TOK_AXES:
+        groups *= lax.axis_size(name)
+    piece = lax.all_to_all(
+        jnp.broadcast_to(local_rows[None], (groups,) + local_rows.shape),
+        TOK_AXES,
+        split_axis=0,
+        concat_axis=0,
+        tiled=True,
+    ).reshape(groups * per_dev, width)
     gate_part = jnp.dot(piece, gate_up[0], preferred_element_type=jnp.float32)
     up_part = jnp.dot(piece, gate_up[1], preferred_element_type=jnp.float32)
     hidden_all = (jax.nn.silu(gate_part) * up_part).astype(jnp.bfloat16)
     term = jnp.dot(hidden_all, down_all, preferred_element_type=jnp.float32).astype(jnp.bfloat16)
-    summed = lax.psum_scatter(term, TOK_AXES, scatter_dimension=0, tiled=True)
+    parts = lax.all_to_all(
+        term.reshape(groups, per_dev, width), TOK_AXES, split_axis=0, concat_axis=0, tiled=True
+    )
+    summed = jnp.sum(parts.astype(jnp.float32), axis=0).astype(jnp.bfloat16)
     returned = lax.all_to_all(
         summed.reshape(dev_count, half, width),
         DEV_AXES,

time: 432 us -> 289 us (0.67)
  waiting for transfers between devices: 325 us -> 25.1 us
  blocking collectives: 34.4 us -> 166 us
  other arithmetic: 5.62 us -> 21.5 us
    all_gather x3 -> x2, waiting for transfers between devices: 211 us -> 0.01 us  [the longest x1 0.01 us: per_device(): gate_up = lax.all_gather(gate_up, 'c', axis=2, tiled=True)]
    unnamed x5 -> x2, waiting for transfers between devices: 81 us -> 0.71 us
    all_to_all x0 -> x2, blocking collectives: none -> 73.4 us  [the longest x1 38.7 us: per_device(): lax.all_to_all(jnp.broadcast_to(local_rows[None], (groups,) + local_rows....]
    all_gather x1, blocking collectives: 19.1 us -> 79.6 us  [per_device(): ids_all = lax.all_gather(expert_ids, DEV_AXES, axis=0, tiled=False)]
    ppermute x6, waiting for transfers between devices: 22.4 us -> 14.2 us  [shifted(): return lax.ppermute(value, SEQ_AXES, pairs)]
    concatenate x0 -> x2, other arithmetic: none -> 6.74 us  [the longest x1 3.99 us: per_device(): jnp.concatenate([gate_up, lax.ppermute(gate_up, 'p', partner)], axis=2)]
  transfers between devices with their start and end apart: 11 -> 11, of which waited for: 10 -> 5; matrix products, arithmetic and copies ran while one was open for 2% -> 11% of each run, Pallas kernels for 0% -> 0%
where the time goes in v4:
time: 289 us; the launch traced here: 288 us
  blocking collectives  166 us (57%)
  starting transfers between devices  31.8 us (11%)
  waiting for transfers between devices  25.1 us (9%)
  other arithmetic  21.5 us (7%)
  matrix products  19.1 us (7%)
  between operations  13.6 us (5%)
  local copies, waits for them, and re-layouts  10.8 us (4%)
    all_gather x1, blocking collectives, per_device(): ids_all = lax.all_gather(expert_ids, DEV_AXES, axis=0, tiled=False)  79.6 us
    all_to_all x1, blocking collectives, per_device(): lax.all_to_all(jnp.broadcast_to(local_rows[None], (groups,) + local_rows....  38.7 us
    all_to_all x1, blocking collectives, per_device(): lax.all_to_all(term.reshape(groups, per_dev, width), TOK_AXES, split_axis...  34.6 us
    ppermute x6, starting transfers between devices, shifted(): return lax.ppermute(value, SEQ_AXES, pairs)  23.5 us
    ppermute x6, waiting for transfers between devices, shifted(): return lax.ppermute(value, SEQ_AXES, pairs)  14.2 us
    all_to_all x1, blocking collectives, per_device(): lax.all_to_all(send_rows, DEV_AXES, split_axis=0, concat_axis=0, tiled=True)  13.2 us
    all_to_all x1, waiting for transfers between devices, per_device(): lax.all_to_all(summed.reshape(dev_count, half, width), DEV_AXES, split_ax...  10.2 us
    dot_general x1, matrix products, per_device(): jnp.dot(hidden_all, down_all, preferred_element_type=jnp.float32)  8.88 us
  transfers between devices with their start and end apart: 11, of which 5 were waited for; matrix products, arithmetic and copies ran while one was open for 11% of the time, Pallas kernels for 0%

profile of v4, /device:TPU:2, one launch (start us, length us, event | category | flops | bytes accessed | tf_op | source)
XLA Modules:
  0.0 288.1 jit_solution(14320500044229852291)
XLA Ops:
  6.5 1.0 reduce_window_sum.22
  8.3 1.3 fusion.19
  9.7 0.7 pad_maximum_fusion.2
  10.4 1.9 collective-permute-start.2
  12.3 2.0 collective-permute-start.1
  14.3 1.3 constant_dynamic-update-slice_fusion.1
  15.6 1.4 constant_dynamic-update-slice_fusion
  17.3 79.6 %all-gather.1 = s32[8,8,2]{1,2,0:T(2,128)S(1)} all-gather(s32[1,8,2]{1,2,0:T(2,128)S(1)} %bitcast.142), channel_id=2, replica_groups=mesh['y'=4,'x'=4,'c'=2,'e'=4,'p'=2] {'e','p'}, dimensions={0}, use_global_device_ids=true | all-gather | bytes 576 | tf_op jit(solution)/shard_map/all_gather | solution.py:81
  97.5 1.9 collective-permute-start.3
  100.6 5.0 %collective-permute-done.3 = f32[4,129,128]{2,1,0:T(8,128)} collective-permute-done((f32[4,129,128]{2,1,0:T(8,128)}, f32[4,129,128]{2,1,0:T(8,128)}, u32[]{:S(2)}, u32[]{:S(2)}) %collective-permute-start.3) | collective-permute-done | bytes 264224 | tf_op jit(solution)/shard_map/ppermute | solution.py:25
  105.6 0.7 fusion.42
  106.4 1.1 slice_add_fusion
  107.5 3.6 %collective-permute-start.4 = (f32[4,129,128]{2,1,0:T(8,128)S(1)}, f32[4,129,128]{2,1,0:T(8,128)S(1)}, u32[]{:S(2)}, u32[]{:S(2)}) collective-permute-start(f32[4,129,128]{2,1,0:T(8,128)S(1)} %pad_maximum_fusion.3), channel_id=1, source_target_pairs={{0,16},{8,24},{16,32},{24,40},{32,48},{40,56},{48,64},{56,72},{64,... | collective-permute-start | bytes 792584 | tf_op jit(solution)/shard_map/ppermute | solution.py:25
  111.1 0.7 broadcast_add_fusion
  111.8 5.5 %collective-permute-done.4 = f32[4,129,128]{2,1,0:T(8,128)S(1)} collective-permute-done((f32[4,129,128]{2,1,0:T(8,128)S(1)}, f32[4,129,128]{2,1,0:T(8,128)S(1)}, u32[]{:S(2)}, u32[]{:S(2)}) %collective-permute-start.4) | collective-permute-done | bytes 264224 | tf_op jit(solution)/shard_map/ppermute | solution.py:25
  118.5 0.7 pad_maximum_fusion.4
  119.2 4.5 %collective-permute-start.5 = (f32[4,129,128]{2,1,0:T(8,128)}, f32[4,129,128]{2,1,0:T(8,128)}, u32[]{:S(2)}, u32[]{:S(2)}) collective-permute-start(f32[4,129,128]{2,1,0:T(8,128)} %pad_maximum_fusion.4), channel_id=1, source_target_pairs={{0,32},{8,40},{16,48},{24,56},{32,64},{40,72},{48,80},{56,88},{64,... | collective-permute-start | bytes 792584 | tf_op jit(solution)/shard_map/ppermute | solution.py:25
  123.7 0.6 iota_compare_fusion.2
  124.3 1.4 reshape.303
  125.7 1.7 scatter_custom_fusion
  127.3 1.7 convolution_multiply_fusion
  129.0 1.0 fusion.10
  130.0 0.8 fusion.40
  130.8 4.9 %collective-permute-start.6 = (f32[4,129,128]{2,1,0:T(8,128)S(1)}, f32[4,129,128]{2,1,0:T(8,128)S(1)}, u32[]{:S(2)}, u32[]{:S(2)}) collective-permute-start(f32[4,129,128]{2,1,0:T(8,128)S(1)} %pad_maximum_fusion.5), channel_id=1, source_target_pairs={{0,64},{8,72},{16,80},{24,88},{32,96},{40,104},{48,112},{56,120},{... | collective-permute-start | bytes 792584 | tf_op jit(solution)/shard_map/ppermute | solution.py:25
  135.7 0.7 compare_select_fusion
  136.3 0.6 pad_clamp_fusion.1
  136.9 2.8 collective-permute-done.6
  139.7 0.6 fusion.39
  140.3 0.7 pad_maximum_fusion.6
  141.0 6.7 %collective-permute-start.7 = (f32[4,129,128]{2,1,0:T(8,128)}, f32[4,129,128]{2,1,0:T(8,128)}, u32[]{:S(2)}, u32[]{:S(2)}) collective-permute-start(f32[4,129,128]{2,1,0:T(8,128)} %pad_maximum_fusion.6), channel_id=1, source_target_pairs={{0,128},{8,136},{16,144},{24,152},{32,160},{40,168},{48,176},{56,1... | collective-permute-start | bytes 792584 | tf_op jit(solution)/shard_map/ppermute | solution.py:25
  147.8 2.8 pad_maximum_fusion.1
  150.5 0.9 collective-permute-done.7
  151.4 1.2 fusion.7
  152.6 1.2 fusion.13
  153.8 0.8 copy_bitcast_fusion
  154.7 1.1 gather_fusion
  155.8 4.0 %pad_maximum_fusion = bf16[2,4096,256]{2,1,0:T(8,128)(2,1)} fusion(bf16[2,4096,128]{2,1,0:T(8,128)(2,1)} %collective-permute-done, bf16[2,4096,128]{2,1,0:T(8,128)(2,1)S(1)} %constant_dynamic-update-slice_fusion), kind=kLoop, calls=%fused_computation.8 | loop fusion | flops 8388608 | bytes 8388608 | tf_op jit(solution)/shard_map/concatenate | solution.py:73
  159.9 0.7 all-gather.7.cloned.1.call-update
  160.6 13.2 %all_to_all.20 = bf16[8,24,512]{2,1,0:T(8,128)(2,1)S(1)} all-to-all(bf16[8,24,512]{2,1,0:T(8,128)(2,1)S(1)} %bitcast.130), channel_id=1, replica_groups=mesh['y'=4,'x'=4,'c'=2,'e'=4,'p'=2] {'e','p'}, dimensions={0} | all-to-all | bytes 393216 | tf_op jit(solution)/shard_map/all_to_all | solution.py:129
  174.2 38.7 %all_to_all.21 = bf16[16,24,4096]{2,1,0:T(8,128)(2,1)S(1)} all-to-all(bf16[16,24,4096]{2,1,0:T(8,128)(2,1)S(1)} %broadcast_in_dim.58), channel_id=1, replica_groups=mesh['y'=4,'x'=4,'c'=2,'e'=4,'p'=2] {'y','x'}, dimensions={0} | all-to-all | bytes 6291456 | tf_op jit(solution)/shard_map/all_to_all | solution.py:135
  212.9 4.9 %fusion.1 = f32[384,512]{1,0:T(8,128)} fusion(bf16[384,4096]{1,0:T(8,128)(2,1)S(1)} %bitcast.125, bf16[2,4096,512]{2,1,0:T(8,128)(2,1)} %all-gather.5.cloned.1.call-done), kind=kOutput, calls=%fused_computation.7 | convolution fusion | flops 1610612736 | bytes 8126464 | tf_op jit(solution)/shard_map/dot_general | solution.py:142
  217.8 8.9 %convolution_convert_fusion = bf16[384,4096]{1,0:T(8,128)(2,1)} fusion(bf16[512,4096]{1,0:T(8,128)(2,1)} %all-gather.7.cloned.1.call-done, bf16[384,4096]{1,0:T(8,128)(2,1)S(1)} %bitcast.126, bf16[2,4096,512]{2,1,0:T(8,128)(2,1)} %all-gather.5.cloned.1.call-done, f32[384,512]{1,0:T(8,128)} %fusion.1), kind=kOutput, calls=%fused_computation.3 | convolution fusion | flops 3223977984 | bytes 15466496 | tf_op jit(solution)/shard_map/dot_general | solution.py:145
  226.7 34.6 %all_to_all.22 = bf16[16,24,4096]{2,1,0:T(8,128)(2,1)S(1)} all-to-all(bf16[16,24,4096]{2,1,0:T(8,128)(2,1)} %bitcast.127), channel_id=1, replica_groups=mesh['y'=4,'x'=4,'c'=2,'e'=4,'p'=2] {'y','x'}, dimensions={0} | all-to-all | bytes 6291456 | tf_op jit(solution)/shard_map/all_to_all | solution.py:146
  261.9 0.8 reshape.280
  262.7 6.1 %all-to-all-start.3 = ((bf16[8,3,4096]{2,1,0:T(4,128)(2,1)}), bf16[8,3,4096]{2,1,0:T(4,128)(2,1)S(1)}, u32[]{:S(2)}, u32[]{:S(2)}) async-start(bf16[8,3,4096]{2,1,0:T(4,128)(2,1)} %reshape.280), calls=%async_computation.3 | async-start | bytes 524288 | tf_op jit(solution)/shard_map/all_to_all | solution.py:150
  269.1 10.2 %all-to-all-done.3 = bf16[8,3,4096]{2,1,0:T(4,128)(2,1)S(1)} async-done(((bf16[8,3,4096]{2,1,0:T(4,128)(2,1)}), bf16[8,3,4096]{2,1,0:T(4,128)(2,1)S(1)}, u32[]{:S(2)}, u32[]{:S(2)}) %all-to-all-start.3) | async-done | bytes 196640 | tf_op jit(solution)/shard_map/all_to_all | solution.py:150
  279.5 0.6 gather_fusion.1
  280.3 1.0 multiply_reduce_fusion
  (62 shorter events, 5.8 us)
Async XLA Ops:
  6.5 1.7 copy-start
  6.5 120.8 %copy-start.2 = (bf16[64,512]{1,0:T(8,128)(2,1)S(1)}, bf16[64,512]{1,0:T(8,128)(2,1)}, u32[]{:S(2)}) copy-start(bf16[64,512]{1,0:T(8,128)(2,1)} %param.11) | copy-start | bytes 196612
  6.5 10.7 %copy-start.6 = (s32[8,2]{0,1:T(2,128)S(1)}, s32[8,2]{0,1:T(2,128)}, u32[]{:S(2)}) copy-start(s32[8,2]{0,1:T(2,128)} %param.18) | copy-start | bytes 196
  6.5 206.4 %all-gather.5.cloned.1.call-start = ((), (), s32[]{:S(2)}) async-start(), calls=%async_computation.4 | async-start | bytes 12582912 | tf_op jit(solution)/shard_map/all_gather | solution.py:127
  7.5 9.7 %copy-start.5 = (f32[4,64]{1,0:T(4,128)}, f32[4,64]{1,0:T(4,128)S(1)}, u32[]{:S(2)}) copy-start(f32[4,64]{1,0:T(4,128)S(1)} %reduce_window_sum.22) | copy-start | bytes 3076
  10.4 87.1 %collective-permute-start.2 = (f32[4,129,128]{2,1,0:T(8,128)}, f32[4,129,128]{2,1,0:T(8,128)}, u32[]{:S(2)}, u32[]{:S(2)}) collective-permute-start(f32[4,129,128]{2,1,0:T(8,128)} %pad_maximum_fusion.2), channel_id=1, source_target_pairs={{0,8},{8,16},{16,24},{24,32},{32,40},{40,48},{48,56},{56,64},{64,7... | collective-permute-start | bytes 792584 | tf_op jit(solution)/shard_map/ppermute | solution.py:25
  12.3 135.5 %collective-permute-start.1 = (bf16[128,4096]{1,0:T(8,128)(2,1)}, bf16[128,4096]{1,0:T(8,128)(2,1)}, u32[]{:S(2)}, u32[]{:S(2)}) collective-permute-start(bf16[128,4096]{1,0:T(8,128)(2,1)} %bitcast.128), channel_id=1, source_target_pairs={{0,1},{1,0},{2,3},{3,2},{4,5},{5,4},{6,7},{7,6},{8,9},{9,8},{10,11... | collective-permute-start | bytes 3145736 | tf_op jit(solution)/shard_map/ppermute | solution.py:74
  15.6 132.2 %copy-start.1 = (bf16[1,128,4096]{2,1,0:T(8,128)(2,1)S(1)}, bf16[1,128,4096]{2,1,0:T(8,128)(2,1)}, u32[]{:S(2)}) copy-start(bf16[1,128,4096]{2,1,0:T(8,128)(2,1)} %param.17) | copy-start | bytes 3145732
  17.1 138.8 %collective-permute-start = (bf16[2,4096,128]{2,1,0:T(8,128)(2,1)S(1)}, bf16[2,4096,128]{2,1,0:T(8,128)(2,1)}, u32[]{:S(2)}, u32[]{:S(2)}) collective-permute-start(bf16[2,4096,128]{2,1,0:T(8,128)(2,1)S(1)} %constant_dynamic-update-slice_fusion), channel_id=1, source_target_pairs={{0,1},{1,0},{2,3},{3,2},{4,5},{5,4},{6,7},{7,6},{8,9},{9,8},{10,11... | collective-permute-start | bytes 6291464 | tf_op jit(solution)/shard_map/ppermute | solution.py:73
  97.5 8.2 %collective-permute-start.3 = (f32[4,129,128]{2,1,0:T(8,128)}, f32[4,129,128]{2,1,0:T(8,128)}, u32[]{:S(2)}, u32[]{:S(2)}) collective-permute-start(f32[4,129,128]{2,1,0:T(8,128)} %collective-permute-done.2), channel_id=1, source_target_pairs={{0,8},{8,16},{16,24},{24,32},{32,40},{40,48},{48,56},{56,64},{64,7... | collective-permute-start | bytes 792584 | tf_op jit(solution)/shard_map/ppermute | solution.py:25
  107.5 9.8 %collective-permute-start.4 = (f32[4,129,128]{2,1,0:T(8,128)S(1)}, f32[4,129,128]{2,1,0:T(8,128)S(1)}, u32[]{:S(2)}, u32[]{:S(2)}) collective-permute-start(f32[4,129,128]{2,1,0:T(8,128)S(1)} %pad_maximum_fusion.3), channel_id=1, source_target_pairs={{0,16},{8,24},{16,32},{24,40},{32,48},{40,56},{48,64},{56,72},{64,... | collective-permute-start | bytes 792584 | tf_op jit(solution)/shard_map/ppermute | solution.py:25
  117.9 0.6 copy-start.4
  119.2 9.8 %collective-permute-start.5 = (f32[4,129,128]{2,1,0:T(8,128)}, f32[4,129,128]{2,1,0:T(8,128)}, u32[]{:S(2)}, u32[]{:S(2)}) collective-permute-start(f32[4,129,128]{2,1,0:T(8,128)} %pad_maximum_fusion.4), channel_id=1, source_target_pairs={{0,32},{8,40},{16,48},{24,56},{32,64},{40,72},{48,80},{56,88},{64,... | collective-permute-start | bytes 792584 | tf_op jit(solution)/shard_map/ppermute | solution.py:25
  130.0 21.4 %copy-start.3 = (bf16[64,512]{1,0:T(8,128)(2,1)S(1)}, bf16[64,512]{1,0:T(8,128)(2,1)}, u32[]{:S(2)}) copy-start(bf16[64,512]{1,0:T(8,128)(2,1)} %param.10) | copy-start | bytes 196612
  130.8 8.9 %collective-permute-start.6 = (f32[4,129,128]{2,1,0:T(8,128)S(1)}, f32[4,129,128]{2,1,0:T(8,128)S(1)}, u32[]{:S(2)}, u32[]{:S(2)}) collective-permute-start(f32[4,129,128]{2,1,0:T(8,128)S(1)} %pad_maximum_fusion.5), channel_id=1, source_target_pairs={{0,64},{8,72},{16,80},{24,88},{32,96},{40,104},{48,112},{56,120},{... | collective-permute-start | bytes 792584 | tf_op jit(solution)/shard_map/ppermute | solution.py:25
  141.0 10.4 %collective-permute-start.7 = (f32[4,129,128]{2,1,0:T(8,128)}, f32[4,129,128]{2,1,0:T(8,128)}, u32[]{:S(2)}, u32[]{:S(2)}) collective-permute-start(f32[4,129,128]{2,1,0:T(8,128)} %pad_maximum_fusion.6), channel_id=1, source_target_pairs={{0,128},{8,136},{16,144},{24,152},{32,160},{40,168},{48,176},{56,1... | collective-permute-start | bytes 792584 | tf_op jit(solution)/shard_map/ppermute | solution.py:25
  159.9 57.9 %all-gather.7.cloned.1.call-start = ((), (), s32[]{:S(2)}) async-start(), calls=%async_computation.5 | async-start | bytes 6291456 | tf_op jit(solution)/shard_map/all_gather | solution.py:128
  226.7 42.1 %copy-start.7 = (f32[8,2]{0,1:T(2,128)S(1)}, f32[8,2]{0,1:T(2,128)}, u32[]{:S(2)}) copy-start(f32[8,2]{0,1:T(2,128)} %param.19) | copy-start | bytes 196
  262.7 16.6 %all-to-all-start.3 = ((bf16[8,3,4096]{2,1,0:T(4,128)(2,1)}), bf16[8,3,4096]{2,1,0:T(4,128)(2,1)S(1)}, u32[]{:S(2)}, u32[]{:S(2)}) async-start(bf16[8,3,4096]{2,1,0:T(4,128)(2,1)} %reshape.280), calls=%async_computation.3 | async-start | bytes 524288 | tf_op jit(solution)/shard_map/all_to_all | solution.py:150
Sparse Core Ops, SparseCore 0:
  160.0 22.9 all-gather.4
  184.8 20.2 all-gather.6

commit v5 on v3

--- a/solution.py
+++ b/solution.py
@@ -9,8 +9,8 @@
 
 highest = lax.Precision.HIGHEST
 
-SEQ_AXES = ("y", "x", "c")
-TOK_AXES = ("y", "x")
+SEQ_AXES = ("y", "xh", "xl", "c")
+TOK_AXES = ("y", "xh")
 
 
 def chain_join(earlier, later):
@@ -67,9 +67,10 @@
     dev_count = lax.axis_size("dev")
     experts = dev_count // PAIR
 
-    gate_both = lax.all_gather(gate_weight[0], "c", axis=1, tiled=True)
-    up_both = lax.all_gather(up_weight[0], "c", axis=1, tiled=True)
-    down_both = lax.all_gather(down_weight[0], "c", axis=0, tiled=True)
+    partner = [(0, 1), (1, 0)]
+    gate_up = jnp.stack([gate_weight[0], up_weight[0]])
+    gate_up = jnp.concatenate([gate_up, lax.ppermute(gate_up, "xl", partner)], axis=2)
+    down_all = jnp.concatenate([down_weight[0], lax.ppermute(down_weight[0], "xl", partner)], axis=0)
 
     tok_count = expert_ids.shape[0]
     top_count = expert_ids.shape[1]
@@ -124,9 +125,8 @@
         per_expert, -1
     )
     width = local_rows.shape[1]
-    gate_both, up_both, down_both, local_rows = lax.optimization_barrier(
-        (gate_both, up_both, down_both, local_rows)
-    )
+    gate_up = lax.all_gather(gate_up, "c", axis=2, tiled=True)
+    down_all = lax.all_gather(down_all, "c", axis=0, tiled=True)
     groups = 1
     for name in TOK_AXES:
         groups *= lax.axis_size(name)
@@ -137,10 +137,10 @@
         concat_axis=0,
         tiled=True,
     ).reshape(groups * per_expert, width)
-    gate_part = jnp.dot(piece, gate_both, preferred_element_type=jnp.float32)
-    up_part = jnp.dot(piece, up_both, preferred_element_type=jnp.float32)
+    gate_part = jnp.dot(piece, gate_up[0], preferred_element_type=jnp.float32)
+    up_part = jnp.dot(piece, gate_up[1], preferred_element_type=jnp.float32)
     hidden_all = (jax.nn.silu(gate_part) * up_part).astype(jnp.bfloat16)
-    term = jnp.dot(hidden_all, down_both, preferred_element_type=jnp.float32).astype(jnp.bfloat16)
+    term = jnp.dot(hidden_all, down_all, preferred_element_type=jnp.float32).astype(jnp.bfloat16)
     parts = lax.all_to_all(
         term.reshape(groups, per_expert, width), TOK_AXES, split_axis=0, concat_axis=0, tiled=True
     )
@@ -176,7 +176,8 @@
         cores = len({int(getattr(d, "core_on_chip", 0)) for d in flat})
         xs = len({int(d.coords[0]) for d in flat})
     ys = seq_count // (xs * cores)
-    return Mesh(devices.reshape(ys, xs, cores, dev_count), ("y", "x", "c", "dev"))
+    shape = (ys, xs // 2, 2, cores, dev_count)
+    return Mesh(devices.reshape(shape), ("y", "xh", "xl", "c", "dev"))
 
 
 def solution(mesh):

time: 286 us -> 280 us (0.979); the launches traced: 286 us -> 276 us
  blocking collectives: 177 us -> 118 us
  waiting for transfers between devices: 36.3 us -> 83 us
    ppermute x0 -> x2, waiting for transfers between devices: none -> 45.1 us  [the longest x1 45.1 us: per_device(): lax.ppermute(gate_up, 'xl', partner)]
    all_to_all x1, blocking collectives: 72.9 us -> 40.7 us  [per_device(): lax.all_to_all(jnp.broadcast_to(local_rows[None], (groups,) + local_rows....]
    all_to_all x1, blocking collectives: 69.2 us -> 37.9 us  [per_device(): lax.all_to_all(term.reshape(groups, per_expert, width), TOK_AXES, split_a...]
    all_to_all x1, blocking collectives: 15.3 us -> 20.2 us  [per_device(): lax.all_to_all(send_rows, 'dev', split_axis=0, concat_axis=0, tiled=True)]
    concatenate x0 -> x2, other arithmetic: none -> 3.88 us  [the longest x1 2.4 us: per_device(): jnp.concatenate([gate_up, lax.ppermute(gate_up, 'xl', partner)], axis=2)]
    ppermute x6, waiting for transfers between devices: 21.9 us -> 25.6 us  [shifted(): return lax.ppermute(value, SEQ_AXES, pairs)]
  transfers between devices with their start and end apart: 10 -> 11, of which waited for: 6 -> 7; matrix products, arithmetic and copies ran while one was open for 3% -> 5% of each run, Pallas kernels for 0% -> 0%
where the time goes in v5:
time: 280 us; the launch traced here: 276 us
  blocking collectives  118 us (42%)
  waiting for transfers between devices  83 us (30%)
  starting transfers between devices  29.1 us (10%)
  matrix products  15 us (5%)
  between operations  13.8 us (5%)
  local copies, waits for them, and re-layouts  9.56 us (3%)
  other arithmetic  7.8 us (3%)
    ppermute x1, waiting for transfers between devices, per_device(): lax.ppermute(gate_up, 'xl', partner)  45.1 us
    all_to_all x1, blocking collectives, per_device(): lax.all_to_all(jnp.broadcast_to(local_rows[None], (groups,) + local_rows....  40.7 us
    all_to_all x1, blocking collectives, per_device(): lax.all_to_all(term.reshape(groups, per_expert, width), TOK_AXES, split_a...  37.9 us
    ppermute x6, waiting for transfers between devices, shifted(): return lax.ppermute(value, SEQ_AXES, pairs)  25.6 us
    ppermute x6, starting transfers between devices, shifted(): return lax.ppermute(value, SEQ_AXES, pairs)  23.1 us
    all_to_all x1, blocking collectives, per_device(): lax.all_to_all(send_rows, 'dev', split_axis=0, concat_axis=0, tiled=True)  20.2 us
    all_gather x1, blocking collectives, per_device(): ids_all = lax.all_gather(expert_ids, 'dev', axis=0, tiled=False)  19.1 us
    all_to_all x1, waiting for transfers between devices, per_device(): lax.all_to_all(summed.reshape(dev_count, capacity, width), 'dev', split_a...  12.2 us
  transfers between devices with their start and end apart: 11, of which 7 were waited for; matrix products, arithmetic and copies ran while one was open for 5% of the time, Pallas kernels for 0%

profile of v5, /device:TPU:2, one launch (start us, length us, event | category | flops | bytes accessed | tf_op | source)
XLA Modules:
  0.0 276.1 jit_solution(8728059597793792246)
XLA Ops:
  6.5 1.3 constant_dynamic-update-slice_fusion.1
  7.9 1.4 constant_dynamic-update-slice_fusion
  9.2 2.4 collective-permute-start.6
  11.6 45.1 %collective-permute-done.6 = bf16[2,4096,128]{2,1,0:T(8,128)(2,1)S(1)} collective-permute-done((bf16[2,4096,128]{2,1,0:T(8,128)(2,1)S(1)}, bf16[2,4096,128]{2,1,0:T(8,128)(2,1)S(1)}, u32[]{:S(2)}, u32[]{:S(2)}) %collective-permute-start.6) | collective-permute-done | bytes 2097184 | tf_op jit(solution)/shard_map/ppermute | solution.py:72
  56.7 2.4 pad_maximum_fusion
  59.2 0.6 copy-done.5
  59.8 0.2 reduce_window_sum.22
  60.0 0.2 slice_reduce_fusion
  60.3 0.5 fusion.17
  60.9 1.9 collective-permute-start
  62.8 0.1 collective-permute-start.7
  62.9 19.1 %all-gather.1 = s32[8,8,2]{1,2,0:T(2,128)S(1)} all-gather(s32[1,8,2]{1,2,0:T(2,128)S(1)} %bitcast.144), channel_id=2, replica_groups=mesh['y'=4,'xh'=2,'xl'=2,'c'=2,'dev'=8] {'dev'}, dimensions={0}, use_global_device_ids=true | all-gather | bytes 576 | tf_op jit(solution)/shard_map/all_gather | solution.py:78
  82.1 0.4 fusion.40
  82.6 1.9 collective-permute-start.1
  84.8 0.1 copy.41
  84.9 0.1 mul.193
  85.1 9.1 %collective-permute-done.1 = f32[4,129,128]{2,1,0:T(8,128)S(1)} collective-permute-done((f32[4,129,128]{2,1,0:T(8,128)S(1)}, f32[4,129,128]{2,1,0:T(8,128)S(1)}, u32[]{:S(2)}, u32[]{:S(2)}) %collective-permute-start.1) | collective-permute-done | bytes 264224 | tf_op jit(solution)/shard_map/ppermute | solution.py:24
  94.3 1.9 collective-permute-start.2
  96.3 6.4 %collective-permute-done.2 = f32[4,129,128]{2,1,0:T(8,128)S(1)} collective-permute-done((f32[4,129,128]{2,1,0:T(8,128)S(1)}, f32[4,129,128]{2,1,0:T(8,128)S(1)}, u32[]{:S(2)}, u32[]{:S(2)}) %collective-permute-start.2) | collective-permute-done | bytes 264224 | tf_op jit(solution)/shard_map/ppermute | solution.py:24
  102.8 4.2 %collective-permute-start.3 = (f32[4,129,128]{2,1,0:T(8,128)S(1)}, f32[4,129,128]{2,1,0:T(8,128)S(1)}, u32[]{:S(2)}, u32[]{:S(2)}) collective-permute-start(f32[4,129,128]{2,1,0:T(8,128)S(1)} %pad_maximum_fusion.4), channel_id=1, source_target_pairs={{0,32},{8,40},{16,48},{24,56},{32,64},{40,72},{48,80},{56,88},{64,... | collective-permute-start | bytes 792584 | tf_op jit(solution)/shard_map/ppermute | solution.py:24
  107.1 1.0 scatter_custom_fusion
  108.1 3.3 %collective-permute-done.3 = f32[4,129,128]{2,1,0:T(8,128)S(1)} collective-permute-done((f32[4,129,128]{2,1,0:T(8,128)S(1)}, f32[4,129,128]{2,1,0:T(8,128)S(1)}, u32[]{:S(2)}, u32[]{:S(2)}) %collective-permute-start.3) | collective-permute-done | bytes 264224 | tf_op jit(solution)/shard_map/ppermute | solution.py:24
  111.5 7.1 %collective-permute-start.4 = (f32[4,129,128]{2,1,0:T(8,128)S(1)}, f32[4,129,128]{2,1,0:T(8,128)S(1)}, u32[]{:S(2)}, u32[]{:S(2)}) collective-permute-start(f32[4,129,128]{2,1,0:T(8,128)S(1)} %pad_maximum_fusion.5), channel_id=1, source_target_pairs={{0,64},{8,72},{16,80},{24,88},{32,96},{40,104},{48,112},{56,120},{... | collective-permute-start | bytes 792584 | tf_op jit(solution)/shard_map/ppermute | solution.py:24
  118.6 0.2 convolution_multiply_fusion
  118.8 4.3 %collective-permute-done.4 = f32[4,129,128]{2,1,0:T(8,128)S(1)} collective-permute-done((f32[4,129,128]{2,1,0:T(8,128)S(1)}, f32[4,129,128]{2,1,0:T(8,128)S(1)}, u32[]{:S(2)}, u32[]{:S(2)}) %collective-permute-start.4) | collective-permute-done | bytes 264224 | tf_op jit(solution)/shard_map/ppermute | solution.py:24
  123.2 6.0 %collective-permute-start.5 = (f32[4,129,128]{2,1,0:T(8,128)S(1)}, f32[4,129,128]{2,1,0:T(8,128)S(1)}, u32[]{:S(2)}, u32[]{:S(2)}) collective-permute-start(f32[4,129,128]{2,1,0:T(8,128)S(1)} %pad_maximum_fusion.6), channel_id=1, source_target_pairs={{0,128},{8,136},{16,144},{24,152},{32,160},{40,168},{48,176},{56,1... | collective-permute-start | bytes 792584 | tf_op jit(solution)/shard_map/ppermute | solution.py:24
  129.2 1.5 pad_maximum_fusion.1
  130.7 2.5 collective-permute-done.5
  133.2 0.3 fusion.5
  133.5 0.3 fusion.11
  133.8 0.1 copy_bitcast_fusion
  134.0 1.0 gather_fusion
  135.0 20.2 %all_to_all.20 = bf16[8,48,512]{2,1,0:T(8,128)(2,1)S(1)} all-to-all(bf16[8,48,512]{2,1,0:T(8,128)(2,1)S(1)} %bitcast.129), channel_id=1, replica_groups=mesh['y'=4,'xh'=2,'xl'=2,'c'=2,'dev'=8] {'dev'}, dimensions={0} | all-to-all | bytes 786432 | tf_op jit(solution)/shard_map/all_to_all | solution.py:123
  155.2 0.4 broadcast_in_dim.62
  155.6 40.7 %all_to_all.21 = bf16[8,48,4096]{2,1,0:T(8,128)(2,1)S(1)} all-to-all(bf16[8,48,4096]{2,1,0:T(8,128)(2,1)S(1)} %broadcast_in_dim.62), channel_id=1, replica_groups=mesh['y'=4,'xh'=2,'xl'=2,'c'=2,'dev'=8] {'y','xh'}, dimensions={0} | all-to-all | bytes 6291456 | tf_op jit(solution)/shard_map/all_to_all | solution.py:133
  196.3 4.9 %fusion = f32[384,512]{1,0:T(8,128)} fusion(bf16[384,4096]{1,0:T(8,128)(2,1)S(1)} %bitcast.126, bf16[2,4096,512]{2,1,0:T(8,128)(2,1)} %all-gather.5.cloned.1.call-done), kind=kOutput, calls=%fused_computation.5 | convolution fusion | flops 1610612736 | bytes 8126464 | tf_op jit(solution)/shard_map/dot_general | solution.py:141
  201.2 8.9 %convolution_convert_fusion = bf16[384,4096]{1,0:T(8,128)(2,1)} fusion(bf16[512,4096]{1,0:T(8,128)(2,1)} %all-gather.7.cloned.1.call-done, f32[384,512]{1,0:T(8,128)} %fusion, bf16[384,4096]{1,0:T(8,128)(2,1)S(1)} %bitcast.127, bf16[2,4096,512]{2,1,0:T(8,128)(2,1)} %all-gather.5.cloned.1.call-done), kind=kOutput, calls=%fused_computation.3 | convolution fusion | flops 3223977984 | bytes 15466496 | tf_op jit(solution)/shard_map/dot_general | solution.py:143
  210.1 37.9 %all_to_all.22 = bf16[8,48,4096]{2,1,0:T(8,128)(2,1)S(1)} all-to-all(bf16[8,48,4096]{2,1,0:T(8,128)(2,1)} %bitcast.128), channel_id=1, replica_groups=mesh['y'=4,'xh'=2,'xl'=2,'c'=2,'dev'=8] {'y','xh'}, dimensions={0} | all-to-all | bytes 6291456 | tf_op jit(solution)/shard_map/all_to_all | solution.py:144
  248.0 1.3 reduce_sum.53
  249.4 1.9 reshape.229
  251.3 3.5 %all-to-all-start.3 = ((bf16[8,6,4096]{2,1,0:T(8,128)(2,1)}), bf16[8,6,4096]{2,1,0:T(8,128)(2,1)S(1)}, u32[]{:S(2)}, u32[]{:S(2)}) async-start(bf16[8,6,4096]{2,1,0:T(8,128)(2,1)} %reshape.229), calls=%async_computation.3 | async-start | bytes 1048576 | tf_op jit(solution)/shard_map/all_to_all | solution.py:148
  254.8 0.1 copy.45
  254.9 0.2 add_reduce_fusion
  255.1 12.2 %all-to-all-done.3 = bf16[8,6,4096]{2,1,0:T(8,128)(2,1)S(1)} async-done(((bf16[8,6,4096]{2,1,0:T(8,128)(2,1)}), bf16[8,6,4096]{2,1,0:T(8,128)(2,1)S(1)}, u32[]{:S(2)}, u32[]{:S(2)}) %all-to-all-start.3) | async-done | bytes 393248 | tf_op jit(solution)/shard_map/all_to_all | solution.py:148
  267.3 0.1 bitcast_reduce_fusion
  267.5 0.6 gather_fusion.1
  268.1 0.2 reshape.232
  268.3 1.0 multiply_reduce_fusion
  (60 shorter events, 1.3 us)
Async XLA Ops:
  6.5 53.7 %copy-start = (bf16[64,512]{1,0:T(8,128)(2,1)S(1)}, bf16[64,512]{1,0:T(8,128)(2,1)}, u32[]{:S(2)}) copy-start(bf16[64,512]{1,0:T(8,128)(2,1)} %param.12) | copy-start | bytes 196612
  6.5 189.8 %all-gather.5.cloned.1.call-start = ((), (), s32[]{:S(2)}) async-start(), calls=%async_computation.4 | async-start | bytes 12582912 | tf_op jit(solution)/shard_map/all_gather | solution.py:128
  9.2 47.5 %collective-permute-start.6 = (bf16[2,4096,128]{2,1,0:T(8,128)(2,1)S(1)}, bf16[2,4096,128]{2,1,0:T(8,128)(2,1)S(1)}, u32[]{:S(2)}, u32[]{:S(2)}) collective-permute-start(bf16[2,4096,128]{2,1,0:T(8,128)(2,1)S(1)} %constant_dynamic-update-slice_fusion), channel_id=1, source_target_pairs={{0,16},{16,0},{1,17},{17,1},{2,18},{18,2},{3,19},{19,3},{4,20},{20... | collective-permute-start | bytes 6291464 | tf_op jit(solution)/shard_map/ppermute | solution.py:72
  59.1 0.7 copy-start.5
  59.1 1.2 copy-start.2
  59.1 3.7 %copy-start.1 = (bf16[1,128,4096]{2,1,0:T(8,128)(2,1)S(1)}, bf16[1,128,4096]{2,1,0:T(8,128)(2,1)}, u32[]{:S(2)}) copy-start(bf16[1,128,4096]{2,1,0:T(8,128)(2,1)} %param.17) | copy-start | bytes 3145732
  59.1 3.8 %copy-start.6 = (s32[8,2]{0,1:T(2,128)S(1)}, s32[8,2]{0,1:T(2,128)}, u32[]{:S(2)}) copy-start(s32[8,2]{0,1:T(2,128)} %param.18) | copy-start | bytes 196
  59.1 59.5 %copy-start.3 = (bf16[64,512]{1,0:T(8,128)(2,1)S(1)}, bf16[64,512]{1,0:T(8,128)(2,1)}, u32[]{:S(2)}) copy-start(bf16[64,512]{1,0:T(8,128)(2,1)} %param.10) | copy-start | bytes 196612
  59.1 142.0 %all-gather.7.cloned.1.call-start = ((), (), s32[]{:S(2)}) async-start(), calls=%async_computation.5 | async-start | bytes 6291456 | tf_op jit(solution)/shard_map/all_gather | solution.py:129
  60.9 21.7 %collective-permute-start = (f32[4,129,128]{2,1,0:T(8,128)S(1)}, f32[4,129,128]{2,1,0:T(8,128)S(1)}, u32[]{:S(2)}, u32[]{:S(2)}) collective-permute-start(f32[4,129,128]{2,1,0:T(8,128)S(1)} %pad_maximum_fusion.2), channel_id=1, source_target_pairs={{0,8},{8,16},{16,24},{24,32},{32,40},{40,48},{48,56},{56,64},{64,7... | collective-permute-start | bytes 792584 | tf_op jit(solution)/shard_map/ppermute | solution.py:24
  62.8 66.4 %collective-permute-start.7 = (bf16[128,4096]{1,0:T(8,128)(2,1)S(1)}, bf16[128,4096]{1,0:T(8,128)(2,1)S(1)}, u32[]{:S(2)}, u32[]{:S(2)}) collective-permute-start(bf16[128,4096]{1,0:T(8,128)(2,1)S(1)} %bitcast.132), channel_id=1, source_target_pairs={{0,16},{16,0},{1,17},{17,1},{2,18},{18,2},{3,19},{19,3},{4,20},{20... | collective-permute-start | bytes 3145736 | tf_op jit(solution)/shard_map/ppermute | solution.py:73
  82.6 11.6 %collective-permute-start.1 = (f32[4,129,128]{2,1,0:T(8,128)S(1)}, f32[4,129,128]{2,1,0:T(8,128)S(1)}, u32[]{:S(2)}, u32[]{:S(2)}) collective-permute-start(f32[4,129,128]{2,1,0:T(8,128)S(1)} %collective-permute-done), channel_id=1, source_target_pairs={{0,8},{8,16},{16,24},{24,32},{32,40},{40,48},{48,56},{56,64},{64,7... | collective-permute-start | bytes 792584 | tf_op jit(solution)/shard_map/ppermute | solution.py:24
  94.3 8.4 %collective-permute-start.2 = (f32[4,129,128]{2,1,0:T(8,128)S(1)}, f32[4,129,128]{2,1,0:T(8,128)S(1)}, u32[]{:S(2)}, u32[]{:S(2)}) collective-permute-start(f32[4,129,128]{2,1,0:T(8,128)S(1)} %pad_maximum_fusion.3), channel_id=1, source_target_pairs={{0,16},{8,24},{16,32},{24,40},{32,48},{40,56},{48,64},{56,72},{64,... | collective-permute-start | bytes 792584 | tf_op jit(solution)/shard_map/ppermute | solution.py:24
  102.8 8.6 %collective-permute-start.3 = (f32[4,129,128]{2,1,0:T(8,128)S(1)}, f32[4,129,128]{2,1,0:T(8,128)S(1)}, u32[]{:S(2)}, u32[]{:S(2)}) collective-permute-start(f32[4,129,128]{2,1,0:T(8,128)S(1)} %pad_maximum_fusion.4), channel_id=1, source_target_pairs={{0,32},{8,40},{16,48},{24,56},{32,64},{40,72},{48,80},{56,88},{64,... | collective-permute-start | bytes 792584 | tf_op jit(solution)/shard_map/ppermute | solution.py:24
  111.5 11.6 %collective-permute-start.4 = (f32[4,129,128]{2,1,0:T(8,128)S(1)}, f32[4,129,128]{2,1,0:T(8,128)S(1)}, u32[]{:S(2)}, u32[]{:S(2)}) collective-permute-start(f32[4,129,128]{2,1,0:T(8,128)S(1)} %pad_maximum_fusion.5), channel_id=1, source_target_pairs={{0,64},{8,72},{16,80},{24,88},{32,96},{40,104},{48,112},{56,120},{... | collective-permute-start | bytes 792584 | tf_op jit(solution)/shard_map/ppermute | solution.py:24
  123.1 10.7 %copy-start.4 = (f32[512]{0:T(512)S(1)}, f32[512]{0:T(512)}, u32[]{:S(2)}) copy-start(f32[512]{0:T(512)} %param.14) | copy-start | bytes 6148
  123.2 10.1 %collective-permute-start.5 = (f32[4,129,128]{2,1,0:T(8,128)S(1)}, f32[4,129,128]{2,1,0:T(8,128)S(1)}, u32[]{:S(2)}, u32[]{:S(2)}) collective-permute-start(f32[4,129,128]{2,1,0:T(8,128)S(1)} %pad_maximum_fusion.6), channel_id=1, source_target_pairs={{0,128},{8,136},{16,144},{24,152},{32,160},{40,168},{48,176},{56,1... | collective-permute-start | bytes 792584 | tf_op jit(solution)/shard_map/ppermute | solution.py:24
  248.0 6.7 %copy-start.7 = (f32[8,2]{0,1:T(2,128)S(1)}, f32[8,2]{0,1:T(2,128)}, u32[]{:S(2)}) copy-start(f32[8,2]{0,1:T(2,128)} %param.19) | copy-start | bytes 196
  251.3 16.0 %all-to-all-start.3 = ((bf16[8,6,4096]{2,1,0:T(8,128)(2,1)}), bf16[8,6,4096]{2,1,0:T(8,128)(2,1)S(1)}, u32[]{:S(2)}, u32[]{:S(2)}) async-start(bf16[8,6,4096]{2,1,0:T(8,128)(2,1)} %reshape.229), calls=%async_computation.3 | async-start | bytes 1048576 | tf_op jit(solution)/shard_map/all_to_all | solution.py:148
Sparse Core Ops, SparseCore 0:
  59.3 27.0 all-gather.4
  130.8 21.1 all-gather.6

commit v6 on v5

--- a/solution.py
+++ b/solution.py
@@ -120,13 +120,14 @@
     )
     padded = jnp.concatenate([normed, jnp.zeros((1, normed.shape[1]), normed.dtype)], axis=0)
     send_rows = jnp.repeat(padded[slot_token].reshape(experts, per_expert, -1), PAIR, axis=0)
+    gate_up, down_all, send_rows = lax.optimization_barrier((gate_up, down_all, send_rows))
+    gate_up = lax.all_gather(gate_up, "c", axis=2, tiled=True)
+    down_all = lax.all_gather(down_all, "c", axis=0, tiled=True)
     arrived = lax.all_to_all(send_rows, "dev", split_axis=0, concat_axis=0, tiled=True)
     local_rows = jnp.transpose(arrived.reshape(dev_count, per_expert, -1), (1, 0, 2)).reshape(
         per_expert, -1
     )
     width = local_rows.shape[1]
-    gate_up = lax.all_gather(gate_up, "c", axis=2, tiled=True)
-    down_all = lax.all_gather(down_all, "c", axis=0, tiled=True)
     groups = 1
     for name in TOK_AXES:
         groups *= lax.axis_size(name)

time: 280 us -> 290 us (1.036)
  other arithmetic: 7.8 us -> 22.4 us
  waiting for transfers between devices: 83 us -> 72.2 us
  matrix products: 15 us -> 19.2 us
    ppermute x1, waiting for transfers between devices: 45.1 us -> 0.01 us  [per_device(): lax.ppermute(gate_up, 'xl', partner)]
    ppermute x6, waiting for transfers between devices: 25.6 us -> 59.2 us  [shifted(): return lax.ppermute(value, SEQ_AXES, pairs)]
  transfers between devices with their start and end apart: 11 -> 11, of which waited for: 7 -> 6; matrix products, arithmetic and copies ran while one was open for 5% -> 11% of each run, Pallas kernels for 0% -> 0%
where the time goes in v6:
time: 290 us; the launch traced here: 286 us
  blocking collectives  118 us (41%)
  waiting for transfers between devices  72.2 us (25%)
  starting transfers between devices  29 us (10%)
  other arithmetic  22.4 us (8%)
  matrix products  19.2 us (7%)
  between operations  13.7 us (5%)
  local copies, waits for them, and re-layouts  11.5 us (4%)
    ppermute x6, waiting for transfers between devices, shifted(): return lax.ppermute(value, SEQ_AXES, pairs)  59.2 us
    all_to_all x1, blocking collectives, per_device(): lax.all_to_all(jnp.broadcast_to(local_rows[None], (groups,) + local_rows....  40.7 us
    all_to_all x1, blocking collectives, per_device(): lax.all_to_all(term.reshape(groups, per_expert, width), TOK_AXES, split_a...  37.9 us
    ppermute x6, starting transfers between devices, shifted(): return lax.ppermute(value, SEQ_AXES, pairs)  23 us
    all_to_all x1, blocking collectives, per_device(): lax.all_to_all(send_rows, 'dev', split_axis=0, concat_axis=0, tiled=True)  20.2 us
    all_gather x1, blocking collectives, per_device(): ids_all = lax.all_gather(expert_ids, 'dev', axis=0, tiled=False)  18.9 us
    all_to_all x1, waiting for transfers between devices, per_device(): lax.all_to_all(summed.reshape(dev_count, capacity, width), 'dev', split_a...  12.2 us
    dot_general x1, matrix products, per_device(): jnp.dot(hidden_all, down_all, preferred_element_type=jnp.float32)  8.91 us
  transfers between devices with their start and end apart: 11, of which 6 were waited for; matrix products, arithmetic and copies ran while one was open for 11% of the time, Pallas kernels for 0%

profile of v6, /device:TPU:2, one launch (start us, length us, event | category | flops | bytes accessed | tf_op | source)
XLA Modules:
  0.0 285.5 jit_solution(12104189778408012138)
XLA Ops:
  6.5 1.0 reduce_window_sum.22
  8.3 1.3 fusion.19
  9.7 0.7 pad_maximum_fusion.2
  10.4 1.9 collective-permute-start.2
  12.3 2.4 collective-permute-start.1
  14.7 1.3 constant_dynamic-update-slice_fusion.1
  16.0 1.4 constant_dynamic-update-slice_fusion
  17.5 18.9 %all-gather.1 = s32[8,8,2]{1,2,0:T(2,128)S(1)} all-gather(s32[1,8,2]{1,2,0:T(2,128)S(1)} %bitcast.146), channel_id=2, replica_groups=mesh['y'=4,'xh'=2,'xl'=2,'c'=2,'dev'=8] {'dev'}, dimensions={0}, use_global_device_ids=true | all-gather | bytes 576 | tf_op jit(solution)/shard_map/all_gather | solution.py:78
  36.9 1.9 collective-permute-start.3
  40.1 48.9 %collective-permute-done.3 = f32[4,129,128]{2,1,0:T(8,128)} collective-permute-done((f32[4,129,128]{2,1,0:T(8,128)}, f32[4,129,128]{2,1,0:T(8,128)}, u32[]{:S(2)}, u32[]{:S(2)}) %collective-permute-start.3) | collective-permute-done | bytes 264224 | tf_op jit(solution)/shard_map/ppermute | solution.py:24
  89.0 0.7 fusion.41
  89.7 1.1 slice_add_fusion
  90.8 1.9 collective-permute-start.4
  92.8 0.7 broadcast_add_fusion
  93.4 5.8 %collective-permute-done.4 = f32[4,129,128]{2,1,0:T(8,128)S(1)} collective-permute-done((f32[4,129,128]{2,1,0:T(8,128)S(1)}, f32[4,129,128]{2,1,0:T(8,128)S(1)}, u32[]{:S(2)}, u32[]{:S(2)}) %collective-permute-start.4) | collective-permute-done | bytes 264224 | tf_op jit(solution)/shard_map/ppermute | solution.py:24
  100.4 0.7 pad_maximum_fusion.4
  101.2 4.9 %collective-permute-start.5 = (f32[4,129,128]{2,1,0:T(8,128)}, f32[4,129,128]{2,1,0:T(8,128)}, u32[]{:S(2)}, u32[]{:S(2)}) collective-permute-start(f32[4,129,128]{2,1,0:T(8,128)} %pad_maximum_fusion.4), channel_id=1, source_target_pairs={{0,32},{8,40},{16,48},{24,56},{32,64},{40,72},{48,80},{56,88},{64,... | collective-permute-start | bytes 792584 | tf_op jit(solution)/shard_map/ppermute | solution.py:24
  106.1 0.6 iota_compare_fusion.2
  106.7 1.2 reshape.253
  107.9 1.6 scatter_custom_fusion
  109.5 1.7 convolution_multiply_fusion
  111.6 1.0 fusion.10
  112.6 0.8 fusion.39
  113.3 5.6 %collective-permute-start.6 = (f32[4,129,128]{2,1,0:T(8,128)S(1)}, f32[4,129,128]{2,1,0:T(8,128)S(1)}, u32[]{:S(2)}, u32[]{:S(2)}) collective-permute-start(f32[4,129,128]{2,1,0:T(8,128)S(1)} %pad_maximum_fusion.5), channel_id=1, source_target_pairs={{0,64},{8,72},{16,80},{24,88},{32,96},{40,104},{48,112},{56,120},{... | collective-permute-start | bytes 792584 | tf_op jit(solution)/shard_map/ppermute | solution.py:24
  119.0 0.6 compare_select_fusion
  120.2 3.2 %collective-permute-done.6 = f32[4,129,128]{2,1,0:T(8,128)S(1)} collective-permute-done((f32[4,129,128]{2,1,0:T(8,128)S(1)}, f32[4,129,128]{2,1,0:T(8,128)S(1)}, u32[]{:S(2)}, u32[]{:S(2)}) %collective-permute-start.6) | collective-permute-done | bytes 264224 | tf_op jit(solution)/shard_map/ppermute | solution.py:24
  123.5 0.6 fusion.38
  124.1 0.7 pad_maximum_fusion.6
  124.8 6.7 %collective-permute-start.7 = (f32[4,129,128]{2,1,0:T(8,128)}, f32[4,129,128]{2,1,0:T(8,128)}, u32[]{:S(2)}, u32[]{:S(2)}) collective-permute-start(f32[4,129,128]{2,1,0:T(8,128)} %pad_maximum_fusion.6), channel_id=1, source_target_pairs={{0,128},{8,136},{16,144},{24,152},{32,160},{40,168},{48,176},{56,1... | collective-permute-start | bytes 792584 | tf_op jit(solution)/shard_map/ppermute | solution.py:24
  131.6 2.8 pad_maximum_fusion.1
  134.3 0.9 collective-permute-done.7
  135.2 1.2 fusion.7
  136.4 1.2 fusion.13
  137.6 0.8 copy_bitcast_fusion
  138.5 1.1 gather_fusion
  139.6 4.0 %pad_maximum_fusion = bf16[2,4096,256]{2,1,0:T(8,128)(2,1)} fusion(bf16[2,4096,128]{2,1,0:T(8,128)(2,1)} %collective-permute-done, bf16[2,4096,128]{2,1,0:T(8,128)(2,1)S(1)} %constant_dynamic-update-slice_fusion), kind=kLoop, calls=%fused_computation.8 | loop fusion | flops 8388608 | bytes 8388608 | tf_op jit(solution)/shard_map/concatenate | solution.py:72
  143.7 0.7 all-gather.7.cloned.1.call-update
  144.4 20.2 %all_to_all.20 = bf16[8,48,512]{2,1,0:T(8,128)(2,1)S(1)} all-to-all(bf16[8,48,512]{2,1,0:T(8,128)(2,1)S(1)} %bitcast.131), channel_id=1, replica_groups=mesh['y'=4,'xh'=2,'xl'=2,'c'=2,'dev'=8] {'dev'}, dimensions={0} | all-to-all | bytes 786432 | tf_op jit(solution)/shard_map/all_to_all | solution.py:126
  165.0 40.7 %all_to_all.21 = bf16[8,48,4096]{2,1,0:T(8,128)(2,1)S(1)} all-to-all(bf16[8,48,4096]{2,1,0:T(8,128)(2,1)S(1)} %broadcast_in_dim.62), channel_id=1, replica_groups=mesh['y'=4,'xh'=2,'xl'=2,'c'=2,'dev'=8] {'y','xh'}, dimensions={0} | all-to-all | bytes 6291456 | tf_op jit(solution)/shard_map/all_to_all | solution.py:134
  205.7 4.9 %fusion.1 = f32[384,512]{1,0:T(8,128)} fusion(bf16[384,4096]{1,0:T(8,128)(2,1)S(1)} %bitcast.128, bf16[2,4096,512]{2,1,0:T(8,128)(2,1)} %all-gather.5.cloned.1.call-done), kind=kOutput, calls=%fused_computation.7 | convolution fusion | flops 1610612736 | bytes 8126464 | tf_op jit(solution)/shard_map/dot_general | solution.py:141
  210.6 8.9 %convolution_convert_fusion = bf16[384,4096]{1,0:T(8,128)(2,1)} fusion(bf16[512,4096]{1,0:T(8,128)(2,1)} %all-gather.7.cloned.1.call-done, bf16[384,4096]{1,0:T(8,128)(2,1)S(1)} %bitcast.129, bf16[2,4096,512]{2,1,0:T(8,128)(2,1)} %all-gather.5.cloned.1.call-done, f32[384,512]{1,0:T(8,128)} %fusion.1), kind=kOutput, calls=%fused_computation.3 | convolution fusion | flops 3223977984 | bytes 15466496 | tf_op jit(solution)/shard_map/dot_general | solution.py:144
  219.5 37.9 %all_to_all.22 = bf16[8,48,4096]{2,1,0:T(8,128)(2,1)S(1)} all-to-all(bf16[8,48,4096]{2,1,0:T(8,128)(2,1)} %bitcast.130), channel_id=1, replica_groups=mesh['y'=4,'xh'=2,'xl'=2,'c'=2,'dev'=8] {'y','xh'}, dimensions={0} | all-to-all | bytes 6291456 | tf_op jit(solution)/shard_map/all_to_all | solution.py:145
  257.4 1.3 reduce_sum.53
  258.8 1.9 reshape.229
  260.7 3.5 %all-to-all-start.3 = ((bf16[8,6,4096]{2,1,0:T(8,128)(2,1)}), bf16[8,6,4096]{2,1,0:T(8,128)(2,1)S(1)}, u32[]{:S(2)}, u32[]{:S(2)}) async-start(bf16[8,6,4096]{2,1,0:T(8,128)(2,1)} %reshape.229), calls=%async_computation.3 | async-start | bytes 1048576 | tf_op jit(solution)/shard_map/all_to_all | solution.py:149
  264.5 12.2 %all-to-all-done.3 = bf16[8,6,4096]{2,1,0:T(8,128)(2,1)S(1)} async-done(((bf16[8,6,4096]{2,1,0:T(8,128)(2,1)}), bf16[8,6,4096]{2,1,0:T(8,128)(2,1)S(1)}, u32[]{:S(2)}, u32[]{:S(2)}) %all-to-all-start.3) | async-done | bytes 393248 | tf_op jit(solution)/shard_map/all_to_all | solution.py:149
  276.9 0.6 gather_fusion.1
  277.7 1.0 multiply_reduce_fusion
  (60 shorter events, 6.0 us)
Async XLA Ops:
  6.5 1.8 copy-start
  6.5 103.0 %copy-start.2 = (bf16[64,512]{1,0:T(8,128)(2,1)S(1)}, bf16[64,512]{1,0:T(8,128)(2,1)}, u32[]{:S(2)}) copy-start(bf16[64,512]{1,0:T(8,128)(2,1)} %param.11) | copy-start | bytes 196612
  6.5 11.0 %copy-start.6 = (s32[8,2]{0,1:T(2,128)S(1)}, s32[8,2]{0,1:T(2,128)}, u32[]{:S(2)}) copy-start(s32[8,2]{0,1:T(2,128)} %param.18) | copy-start | bytes 196
  6.5 199.2 %all-gather.5.cloned.1.call-start = ((), (), s32[]{:S(2)}) async-start(), calls=%async_computation.4 | async-start | bytes 12582912 | tf_op jit(solution)/shard_map/all_gather | solution.py:124
  7.5 28.9 %copy-start.5 = (f32[4,64]{1,0:T(4,128)}, f32[4,64]{1,0:T(4,128)S(1)}, u32[]{:S(2)}) copy-start(f32[4,64]{1,0:T(4,128)S(1)} %reduce_window_sum.22) | copy-start | bytes 3076
  10.4 26.5 %collective-permute-start.2 = (f32[4,129,128]{2,1,0:T(8,128)}, f32[4,129,128]{2,1,0:T(8,128)}, u32[]{:S(2)}, u32[]{:S(2)}) collective-permute-start(f32[4,129,128]{2,1,0:T(8,128)} %pad_maximum_fusion.2), channel_id=1, source_target_pairs={{0,8},{8,16},{16,24},{24,32},{32,40},{40,48},{48,56},{56,64},{64,7... | collective-permute-start | bytes 792584 | tf_op jit(solution)/shard_map/ppermute | solution.py:24
  12.3 119.2 %collective-permute-start.1 = (bf16[128,4096]{1,0:T(8,128)(2,1)}, bf16[128,4096]{1,0:T(8,128)(2,1)}, u32[]{:S(2)}, u32[]{:S(2)}) collective-permute-start(bf16[128,4096]{1,0:T(8,128)(2,1)} %bitcast.134), channel_id=1, source_target_pairs={{0,16},{16,0},{1,17},{17,1},{2,18},{18,2},{3,19},{19,3},{4,20},{20... | collective-permute-start | bytes 3145736 | tf_op jit(solution)/shard_map/ppermute | solution.py:73
  16.0 115.6 %copy-start.1 = (bf16[1,128,4096]{2,1,0:T(8,128)(2,1)S(1)}, bf16[1,128,4096]{2,1,0:T(8,128)(2,1)}, u32[]{:S(2)}) copy-start(bf16[1,128,4096]{2,1,0:T(8,128)(2,1)} %param.17) | copy-start | bytes 3145732
  17.4 122.2 %collective-permute-start = (bf16[2,4096,128]{2,1,0:T(8,128)(2,1)S(1)}, bf16[2,4096,128]{2,1,0:T(8,128)(2,1)}, u32[]{:S(2)}, u32[]{:S(2)}) collective-permute-start(bf16[2,4096,128]{2,1,0:T(8,128)(2,1)S(1)} %constant_dynamic-update-slice_fusion), channel_id=1, source_target_pairs={{0,16},{16,0},{1,17},{17,1},{2,18},{18,2},{3,19},{19,3},{4,20},{20... | collective-permute-start | bytes 6291464 | tf_op jit(solution)/shard_map/ppermute | solution.py:72
  36.9 52.0 %collective-permute-start.3 = (f32[4,129,128]{2,1,0:T(8,128)}, f32[4,129,128]{2,1,0:T(8,128)}, u32[]{:S(2)}, u32[]{:S(2)}) collective-permute-start(f32[4,129,128]{2,1,0:T(8,128)} %collective-permute-done.2), channel_id=1, source_target_pairs={{0,8},{8,16},{16,24},{24,32},{32,40},{40,48},{48,56},{56,64},{64,7... | collective-permute-start | bytes 792584 | tf_op jit(solution)/shard_map/ppermute | solution.py:24
  90.8 8.4 %collective-permute-start.4 = (f32[4,129,128]{2,1,0:T(8,128)S(1)}, f32[4,129,128]{2,1,0:T(8,128)S(1)}, u32[]{:S(2)}, u32[]{:S(2)}) collective-permute-start(f32[4,129,128]{2,1,0:T(8,128)S(1)} %pad_maximum_fusion.3), channel_id=1, source_target_pairs={{0,16},{8,24},{16,32},{24,40},{32,48},{40,56},{48,64},{56,72},{64,... | collective-permute-start | bytes 792584 | tf_op jit(solution)/shard_map/ppermute | solution.py:24
  99.9 0.6 copy-start.4
  101.2 10.4 %collective-permute-start.5 = (f32[4,129,128]{2,1,0:T(8,128)}, f32[4,129,128]{2,1,0:T(8,128)}, u32[]{:S(2)}, u32[]{:S(2)}) collective-permute-start(f32[4,129,128]{2,1,0:T(8,128)} %pad_maximum_fusion.4), channel_id=1, source_target_pairs={{0,32},{8,40},{16,48},{24,56},{32,64},{40,72},{48,80},{56,88},{64,... | collective-permute-start | bytes 792584 | tf_op jit(solution)/shard_map/ppermute | solution.py:24
  112.5 22.7 %copy-start.3 = (bf16[64,512]{1,0:T(8,128)(2,1)S(1)}, bf16[64,512]{1,0:T(8,128)(2,1)}, u32[]{:S(2)}) copy-start(bf16[64,512]{1,0:T(8,128)(2,1)} %param.10) | copy-start | bytes 196612
  113.3 10.1 %collective-permute-start.6 = (f32[4,129,128]{2,1,0:T(8,128)S(1)}, f32[4,129,128]{2,1,0:T(8,128)S(1)}, u32[]{:S(2)}, u32[]{:S(2)}) collective-permute-start(f32[4,129,128]{2,1,0:T(8,128)S(1)} %pad_maximum_fusion.5), channel_id=1, source_target_pairs={{0,64},{8,72},{16,80},{24,88},{32,96},{40,104},{48,112},{56,120},{... | collective-permute-start | bytes 792584 | tf_op jit(solution)/shard_map/ppermute | solution.py:24
  124.8 10.4 %collective-permute-start.7 = (f32[4,129,128]{2,1,0:T(8,128)}, f32[4,129,128]{2,1,0:T(8,128)}, u32[]{:S(2)}, u32[]{:S(2)}) collective-permute-start(f32[4,129,128]{2,1,0:T(8,128)} %pad_maximum_fusion.6), channel_id=1, source_target_pairs={{0,128},{8,136},{16,144},{24,152},{32,160},{40,168},{48,176},{56,1... | collective-permute-start | bytes 792584 | tf_op jit(solution)/shard_map/ppermute | solution.py:24
  143.7 66.9 %all-gather.7.cloned.1.call-start = ((), (), s32[]{:S(2)}) async-start(), calls=%async_computation.5 | async-start | bytes 6291456 | tf_op jit(solution)/shard_map/all_gather | solution.py:125
  257.4 6.7 %copy-start.7 = (f32[8,2]{0,1:T(2,128)S(1)}, f32[8,2]{0,1:T(2,128)}, u32[]{:S(2)}) copy-start(f32[8,2]{0,1:T(2,128)} %param.19) | copy-start | bytes 196
  260.7 16.0 %all-to-all-start.3 = ((bf16[8,6,4096]{2,1,0:T(8,128)(2,1)}), bf16[8,6,4096]{2,1,0:T(8,128)(2,1)S(1)}, u32[]{:S(2)}, u32[]{:S(2)}) async-start(bf16[8,6,4096]{2,1,0:T(8,128)(2,1)} %reshape.229), calls=%async_computation.3 | async-start | bytes 1048576 | tf_op jit(solution)/shard_map/all_to_all | solution.py:149
Sparse Core Ops, SparseCore 0:
  143.8 29.2 all-gather.4
  174.9 20.2 all-gather.6

commit v7 on v5

--- a/solution.py
+++ b/solution.py
@@ -11,6 +11,7 @@
 
 SEQ_AXES = ("y", "xh", "xl", "c")
 TOK_AXES = ("y", "xh")
+ROUTE_AXES = ("y", "xh", "dev")
 
 
 def chain_join(earlier, later):
@@ -71,6 +72,8 @@
     gate_up = jnp.stack([gate_weight[0], up_weight[0]])
     gate_up = jnp.concatenate([gate_up, lax.ppermute(gate_up, "xl", partner)], axis=2)
     down_all = jnp.concatenate([down_weight[0], lax.ppermute(down_weight[0], "xl", partner)], axis=0)
+    gate_up = lax.all_gather(gate_up, "c", axis=2, tiled=True)
+    down_all = lax.all_gather(down_all, "c", axis=0, tiled=True)
 
     tok_count = expert_ids.shape[0]
     top_count = expert_ids.shape[1]
@@ -119,42 +122,37 @@
         .set(token_local.reshape(-1))
     )
     padded = jnp.concatenate([normed, jnp.zeros((1, normed.shape[1]), normed.dtype)], axis=0)
-    send_rows = jnp.repeat(padded[slot_token].reshape(experts, per_expert, -1), PAIR, axis=0)
-    arrived = lax.all_to_all(send_rows, "dev", split_axis=0, concat_axis=0, tiled=True)
-    local_rows = jnp.transpose(arrived.reshape(dev_count, per_expert, -1), (1, 0, 2)).reshape(
-        per_expert, -1
-    )
-    width = local_rows.shape[1]
-    gate_up = lax.all_gather(gate_up, "c", axis=2, tiled=True)
-    down_all = lax.all_gather(down_all, "c", axis=0, tiled=True)
     groups = 1
     for name in TOK_AXES:
         groups *= lax.axis_size(name)
-    piece = lax.all_to_all(
-        jnp.broadcast_to(local_rows[None], (groups,) + local_rows.shape),
-        TOK_AXES,
+    send_rows = jnp.repeat(padded[slot_token].reshape(experts, per_expert, -1), PAIR, axis=0)
+    send_rows = jnp.broadcast_to(send_rows[None], (groups,) + send_rows.shape)
+    arrived = lax.all_to_all(
+        send_rows.reshape((groups * dev_count,) + send_rows.shape[2:]),
+        ROUTE_AXES,
         split_axis=0,
         concat_axis=0,
         tiled=True,
-    ).reshape(groups * per_expert, width)
+    )
+    head_width = arrived.shape[-1]
+    piece = jnp.transpose(
+        arrived.reshape(groups, dev_count, per_expert, head_width), (0, 2, 1, 3)
+    ).reshape(groups * per_expert, dev_count * head_width)
+    width = piece.shape[1]
     gate_part = jnp.dot(piece, gate_up[0], preferred_element_type=jnp.float32)
     up_part = jnp.dot(piece, gate_up[1], preferred_element_type=jnp.float32)
     hidden_all = (jax.nn.silu(gate_part) * up_part).astype(jnp.bfloat16)
     term = jnp.dot(hidden_all, down_all, preferred_element_type=jnp.float32).astype(jnp.bfloat16)
     parts = lax.all_to_all(
-        term.reshape(groups, per_expert, width), TOK_AXES, split_axis=0, concat_axis=0, tiled=True
-    )
-    summed = jnp.sum(parts.astype(jnp.float32), axis=0).astype(jnp.bfloat16)
-    returned = lax.all_to_all(
-        summed.reshape(dev_count, capacity, width),
-        "dev",
+        term.reshape(groups * dev_count, capacity, width),
+        ROUTE_AXES,
         split_axis=0,
         concat_axis=0,
         tiled=True,
     ).astype(jnp.float32)
-    expert_out = jnp.sum(returned.reshape(experts, PAIR, capacity, width), axis=1).astype(
-        jnp.bfloat16
-    )
+    expert_out = jnp.sum(
+        parts.reshape(groups, experts, PAIR, capacity, width), axis=(0, 2)
+    ).astype(jnp.bfloat16)
     own = lax.axis_index("dev")
     own_flat = lax.dynamic_index_in_dim(flat, own, 0, False)
     own_rank = lax.dynamic_index_in_dim(rank, own, 0, False)

time: 280 us -> 344 us (1.23)
  waiting for transfers between devices: 83 us -> 221 us
  blocking collectives: 118 us -> 19.1 us
  starting transfers between devices: 29.1 us -> 45.5 us
  local copies, waits for them, and re-layouts: 9.56 us -> 15.6 us
  other arithmetic: 7.8 us -> 12.5 us
    all_to_all x1 -> x2, waiting for transfers between devices: 12.2 us -> 116 us  [the longest x1 91.1 us: per_device(): lax.all_to_all(term.reshape(groups * dev_count, capacity, width), ROUTE_A...]
    all_to_all x3 -> x0, blocking collectives: 98.8 us -> none  [the longest x1 40.7 us: per_device(): lax.all_to_all(jnp.broadcast_to(local_rows[None], (groups,) + local_rows....]
    ppermute x1, waiting for transfers between devices: 0.01 us -> 37.3 us  [per_device(): lax.ppermute(down_weight[0], 'xl', partner)]
    all_to_all x1 -> x2, starting transfers between devices: 3.49 us -> 16.1 us  [the longest x1 8.43 us: per_device(): lax.all_to_all(send_rows.reshape((groups * dev_count,) + send_rows.shape[...]
    ppermute x1, starting transfers between devices: 0.09 us -> 3.59 us  [per_device(): lax.ppermute(down_weight[0], 'xl', partner)]
  transfers between devices with their start and end apart: 11 -> 12, of which waited for: 7 -> 9; matrix products, arithmetic and copies ran while one was open for 5% -> 6% of each run, Pallas kernels for 0% -> 0%
where the time goes in v7:
time: 344 us; the launch traced here: 343 us
  waiting for transfers between devices  221 us (64%)
  starting transfers between devices  45.5 us (13%)
  blocking collectives  19.1 us (6%)
  local copies, waits for them, and re-layouts  15.6 us (5%)
  matrix products  15.4 us (4%)
  between operations  13.8 us (4%)
  other arithmetic  12.5 us (4%)
    all_to_all x1, waiting for transfers between devices, per_device(): lax.all_to_all(term.reshape(groups * dev_count, capacity, width), ROUTE_A...  91.1 us
    ppermute x1, waiting for transfers between devices, per_device(): lax.ppermute(gate_up, 'xl', partner)  44.8 us
    ppermute x1, waiting for transfers between devices, per_device(): lax.ppermute(down_weight[0], 'xl', partner)  37.3 us
    all_to_all x1, waiting for transfers between devices, per_device(): lax.all_to_all(send_rows.reshape((groups * dev_count,) + send_rows.shape[...  25 us
    ppermute x6, starting transfers between devices, shifted(): return lax.ppermute(value, SEQ_AXES, pairs)  23.3 us
    ppermute x6, waiting for transfers between devices, shifted(): return lax.ppermute(value, SEQ_AXES, pairs)  22.4 us
    all_gather x1, blocking collectives, per_device(): ids_all = lax.all_gather(expert_ids, 'dev', axis=0, tiled=False)  19.1 us
    all_to_all x1, starting transfers between devices, per_device(): lax.all_to_all(send_rows.reshape((groups * dev_count,) + send_rows.shape[...  8.43 us
  transfers between devices with their start and end apart: 12, of which 9 were waited for; matrix products, arithmetic and copies ran while one was open for 6% of the time, Pallas kernels for 0%

profile of v7, /device:TPU:2, one launch (start us, length us, event | category | flops | bytes accessed | tf_op | source)
XLA Modules:
  0.0 342.6 jit_solution(2955041800374853195)
XLA Ops:
  6.5 1.3 constant_dynamic-update-slice_fusion.1
  7.9 1.4 constant_dynamic-update-slice_fusion
  9.2 2.4 collective-permute-start.6
  11.6 0.2 reduce_window_sum.22
  11.8 0.2 slice_reduce_fusion
  12.0 44.8 %collective-permute-done.6 = bf16[2,4096,128]{2,1,0:T(8,128)(2,1)} collective-permute-done((bf16[2,4096,128]{2,1,0:T(8,128)(2,1)S(1)}, bf16[2,4096,128]{2,1,0:T(8,128)(2,1)}, u32[]{:S(2)}, u32[]{:S(2)}) %collective-permute-start.6) | collective-permute-done | bytes 2097184 | tf_op jit(solution)/shard_map/ppermute | solution.py:73
  56.8 4.0 %pad_maximum_fusion = bf16[2,4096,256]{2,1,0:T(8,128)(2,1)} fusion(bf16[2,4096,128]{2,1,0:T(8,128)(2,1)} %collective-permute-done.6, bf16[2,4096,128]{2,1,0:T(8,128)(2,1)S(1)} %constant_dynamic-update-slice_fusion), kind=kLoop, calls=%fused_computation.8 | loop fusion | flops 8388608 | bytes 8388608 | tf_op jit(solution)/shard_map/concatenate | solution.py:73
  60.9 0.7 copy-done.2
  61.7 0.5 fusion.17
  62.2 1.9 collective-permute-start
  64.2 19.1 %all-gather.1 = s32[8,8,2]{1,2,0:T(2,128)S(1)} all-gather(s32[1,8,2]{1,2,0:T(2,128)S(1)} %bitcast.144), channel_id=2, replica_groups=mesh['y'=4,'xh'=2,'xl'=2,'c'=2,'dev'=8] {'dev'}, dimensions={0}, use_global_device_ids=true | all-gather | bytes 576 | tf_op jit(solution)/shard_map/all_gather | solution.py:81
  83.4 0.4 fusion.40
  83.8 0.2 add_reduce_fusion
  84.0 1.9 collective-permute-start.1
  86.0 5.9 %collective-permute-done.1 = f32[4,129,128]{2,1,0:T(8,128)S(1)} collective-permute-done((f32[4,129,128]{2,1,0:T(8,128)S(1)}, f32[4,129,128]{2,1,0:T(8,128)S(1)}, u32[]{:S(2)}, u32[]{:S(2)}) %collective-permute-start.1) | collective-permute-done | bytes 264224 | tf_op jit(solution)/shard_map/ppermute | solution.py:25
  92.0 3.4 collective-permute-start.2
  95.5 0.1 copy.49
  95.7 0.1 mul.193
  96.0 5.6 %collective-permute-done.2 = f32[4,129,128]{2,1,0:T(8,128)S(1)} collective-permute-done((f32[4,129,128]{2,1,0:T(8,128)S(1)}, f32[4,129,128]{2,1,0:T(8,128)S(1)}, u32[]{:S(2)}, u32[]{:S(2)}) %collective-permute-start.2) | collective-permute-done | bytes 264224 | tf_op jit(solution)/shard_map/ppermute | solution.py:25
  101.6 4.0 %collective-permute-start.3 = (f32[4,129,128]{2,1,0:T(8,128)S(1)}, f32[4,129,128]{2,1,0:T(8,128)S(1)}, u32[]{:S(2)}, u32[]{:S(2)}) collective-permute-start(f32[4,129,128]{2,1,0:T(8,128)S(1)} %pad_maximum_fusion.4), channel_id=1, source_target_pairs={{0,32},{8,40},{16,48},{24,56},{32,64},{40,72},{48,80},{56,88},{64,... | collective-permute-start | bytes 792584 | tf_op jit(solution)/shard_map/ppermute | solution.py:25
  105.8 4.2 %collective-permute-done.3 = f32[4,129,128]{2,1,0:T(8,128)S(1)} collective-permute-done((f32[4,129,128]{2,1,0:T(8,128)S(1)}, f32[4,129,128]{2,1,0:T(8,128)S(1)}, u32[]{:S(2)}, u32[]{:S(2)}) %collective-permute-start.3) | collective-permute-done | bytes 264224 | tf_op jit(solution)/shard_map/ppermute | solution.py:25
  110.0 6.0 %collective-permute-start.4 = (f32[4,129,128]{2,1,0:T(8,128)S(1)}, f32[4,129,128]{2,1,0:T(8,128)S(1)}, u32[]{:S(2)}, u32[]{:S(2)}) collective-permute-start(f32[4,129,128]{2,1,0:T(8,128)S(1)} %pad_maximum_fusion.5), channel_id=1, source_target_pairs={{0,64},{8,72},{16,80},{24,88},{32,96},{40,104},{48,112},{56,120},{... | collective-permute-start | bytes 792584 | tf_op jit(solution)/shard_map/ppermute | solution.py:25
  116.2 1.0 scatter_custom_fusion
  117.2 2.9 collective-permute-done.4
  120.2 6.0 %collective-permute-start.5 = (f32[4,129,128]{2,1,0:T(8,128)S(1)}, f32[4,129,128]{2,1,0:T(8,128)S(1)}, u32[]{:S(2)}, u32[]{:S(2)}) collective-permute-start(f32[4,129,128]{2,1,0:T(8,128)S(1)} %pad_maximum_fusion.6), channel_id=1, source_target_pairs={{0,128},{8,136},{16,144},{24,152},{32,160},{40,168},{48,176},{56,1... | collective-permute-start | bytes 792584 | tf_op jit(solution)/shard_map/ppermute | solution.py:25
  126.2 0.2 convolution_multiply_fusion
  126.4 3.8 %collective-permute-done.5 = f32[4,129,128]{2,1,0:T(8,128)S(1)} collective-permute-done((f32[4,129,128]{2,1,0:T(8,128)S(1)}, f32[4,129,128]{2,1,0:T(8,128)S(1)}, u32[]{:S(2)}, u32[]{:S(2)}) %collective-permute-start.5) | collective-permute-done | bytes 264224 | tf_op jit(solution)/shard_map/ppermute | solution.py:25
  130.2 0.3 fusion.5
  130.5 0.3 fusion.11
  130.8 0.1 copy_bitcast_fusion
  131.0 1.0 gather_fusion
  132.0 2.0 broadcast_in_dim.62
  134.1 8.4 %all-to-all-start = ((bf16[64,48,512]{2,1,0:T(8,128)(2,1)}), bf16[64,48,512]{2,1,0:T(8,128)(2,1)S(1)}, u32[]{:S(2)}, u32[]{:S(2)}) async-start(bf16[64,48,512]{2,1,0:T(8,128)(2,1)} %bitcast.127), calls=%async_computation | async-start | bytes 6291456 | tf_op jit(solution)/shard_map/all_to_all | solution.py:130
  142.5 3.6 %collective-permute-start.7 = (bf16[128,4096]{1,0:T(8,128)(2,1)}, bf16[128,4096]{1,0:T(8,128)(2,1)S(1)}, u32[]{:S(2)}, u32[]{:S(2)}) collective-permute-start(bf16[128,4096]{1,0:T(8,128)(2,1)} %bitcast.132), channel_id=1, source_target_pairs={{0,16},{16,0},{1,17},{17,1},{2,18},{18,2},{3,19},{19,3},{4,20},{20... | collective-permute-start | bytes 3145736 | tf_op jit(solution)/shard_map/ppermute | solution.py:74
  146.1 37.3 %collective-permute-done.7 = bf16[128,4096]{1,0:T(8,128)(2,1)S(1)} collective-permute-done((bf16[128,4096]{1,0:T(8,128)(2,1)}, bf16[128,4096]{1,0:T(8,128)(2,1)S(1)}, u32[]{:S(2)}, u32[]{:S(2)}) %collective-permute-start.7) | collective-permute-done | bytes 1048608 | tf_op jit(solution)/shard_map/ppermute | solution.py:74
  183.4 2.8 pad_maximum_fusion.1
  186.2 25.0 %all-to-all-done = bf16[64,48,512]{2,1,0:T(8,128)(2,1)S(1)} async-done(((bf16[64,48,512]{2,1,0:T(8,128)(2,1)}), bf16[64,48,512]{2,1,0:T(8,128)(2,1)S(1)}, u32[]{:S(2)}, u32[]{:S(2)}) %all-to-all-start) | async-done | bytes 3145760 | tf_op jit(solution)/shard_map/all_to_all | solution.py:130
  211.2 1.9 copy.52
  213.1 1.4 copy.58
  214.6 6.0 %fusion = f32[384,512]{1,0:T(8,128)} fusion(bf16[384,4096]{1,0:T(8,128)(2,1)S(1)} %bitcast.129, bf16[2,4096,512]{2,1,0:T(8,128)(2,1)} %all-gather.5.cloned.1.call-done), kind=kOutput, calls=%fused_computation.5 | convolution fusion | flops 1610612736 | bytes 8126464 | tf_op jit(solution)/shard_map/dot_general | solution.py:143
  220.6 8.2 %convolution_convert_fusion = bf16[384,4096]{1,0:T(8,128)(2,1)S(1)} fusion(bf16[512,4096]{1,0:T(8,128)(2,1)} %all-gather.7.cloned.1.call-done, f32[384,512]{1,0:T(8,128)} %fusion, bf16[384,4096]{1,0:T(8,128)(2,1)} %bitcast.130, bf16[2,4096,512]{2,1,0:T(8,128)(2,1)} %all-gather.5.cloned.1.call-done), kind=kOutput, calls=%fused_computation.3 | convolution fusion | flops 3223977984 | bytes 15466496 | tf_op jit(solution)/shard_map/dot_general | solution.py:145
  228.8 2.9 reshape.229
  231.7 7.7 %all-to-all-start.1 = ((bf16[64,6,4096]{2,1,0:T(8,128)(2,1)}), bf16[64,6,4096]{2,1,0:T(8,128)(2,1)}, u32[]{:S(2)}, u32[]{:S(2)}) async-start(bf16[64,6,4096]{2,1,0:T(8,128)(2,1)} %reshape.229), calls=%async_computation.1 | async-start | bytes 8388608 | tf_op jit(solution)/shard_map/all_to_all | solution.py:146
  239.5 91.1 %all-to-all-done.1 = bf16[64,6,4096]{2,1,0:T(8,128)(2,1)} async-done(((bf16[64,6,4096]{2,1,0:T(8,128)(2,1)}), bf16[64,6,4096]{2,1,0:T(8,128)(2,1)}, u32[]{:S(2)}, u32[]{:S(2)}) %all-to-all-start.1) | async-done | bytes 3145760 | tf_op jit(solution)/shard_map/all_to_all | solution.py:146
  330.6 3.2 reduce
  333.9 0.6 gather_fusion.1
  334.5 0.2 reshape.232
  334.7 1.0 multiply_reduce_fusion
  (58 shorter events, 1.3 us)
Async XLA Ops:
  6.5 54.4 %copy-start = (bf16[64,512]{1,0:T(8,128)(2,1)S(1)}, bf16[64,512]{1,0:T(8,128)(2,1)}, u32[]{:S(2)}) copy-start(bf16[64,512]{1,0:T(8,128)(2,1)} %param.12) | copy-start | bytes 196612
  6.5 5.1 %copy-start.5 = (f32[64,4]{0,1:T(4,128)S(1)}, f32[64,4]{0,1:T(4,128)}, u32[]{:S(2)}) copy-start(f32[64,4]{0,1:T(4,128)} %param.13) | copy-start | bytes 3076
  6.5 208.0 %all-gather.5.cloned.1.call-start = ((), (), s32[]{:S(2)}) async-start(), calls=%async_computation.2 | async-start | bytes 12582912 | tf_op jit(solution)/shard_map/all_gather | solution.py:75
  9.2 47.6 %collective-permute-start.6 = (bf16[2,4096,128]{2,1,0:T(8,128)(2,1)S(1)}, bf16[2,4096,128]{2,1,0:T(8,128)(2,1)}, u32[]{:S(2)}, u32[]{:S(2)}) collective-permute-start(bf16[2,4096,128]{2,1,0:T(8,128)(2,1)S(1)} %constant_dynamic-update-slice_fusion), channel_id=1, source_target_pairs={{0,16},{16,0},{1,17},{17,1},{2,18},{18,2},{3,19},{19,3},{4,20},{20... | collective-permute-start | bytes 6291464 | tf_op jit(solution)/shard_map/ppermute | solution.py:73
  60.8 0.8 copy-start.2
  60.8 3.3 copy-start.6
  60.8 65.4 %copy-start.3 = (bf16[64,512]{1,0:T(8,128)(2,1)S(1)}, bf16[64,512]{1,0:T(8,128)(2,1)}, u32[]{:S(2)}) copy-start(bf16[64,512]{1,0:T(8,128)(2,1)} %param.10) | copy-start | bytes 196612
  60.9 70.0 %copy-start.4 = (f32[512]{0:T(512)S(1)}, f32[512]{0:T(512)}, u32[]{:S(2)}) copy-start(f32[512]{0:T(512)} %param.14) | copy-start | bytes 6148
  62.2 21.8 %collective-permute-start = (f32[4,129,128]{2,1,0:T(8,128)S(1)}, f32[4,129,128]{2,1,0:T(8,128)S(1)}, u32[]{:S(2)}, u32[]{:S(2)}) collective-permute-start(f32[4,129,128]{2,1,0:T(8,128)S(1)} %pad_maximum_fusion.2), channel_id=1, source_target_pairs={{0,8},{8,16},{16,24},{24,32},{32,40},{40,48},{48,56},{56,64},{64,7... | collective-permute-start | bytes 792584 | tf_op jit(solution)/shard_map/ppermute | solution.py:25
  84.0 7.9 %collective-permute-start.1 = (f32[4,129,128]{2,1,0:T(8,128)S(1)}, f32[4,129,128]{2,1,0:T(8,128)S(1)}, u32[]{:S(2)}, u32[]{:S(2)}) collective-permute-start(f32[4,129,128]{2,1,0:T(8,128)S(1)} %collective-permute-done), channel_id=1, source_target_pairs={{0,8},{8,16},{16,24},{24,32},{32,40},{40,48},{48,56},{56,64},{64,7... | collective-permute-start | bytes 792584 | tf_op jit(solution)/shard_map/ppermute | solution.py:25
  92.0 9.6 %collective-permute-start.2 = (f32[4,129,128]{2,1,0:T(8,128)S(1)}, f32[4,129,128]{2,1,0:T(8,128)S(1)}, u32[]{:S(2)}, u32[]{:S(2)}) collective-permute-start(f32[4,129,128]{2,1,0:T(8,128)S(1)} %pad_maximum_fusion.3), channel_id=1, source_target_pairs={{0,16},{8,24},{16,32},{24,40},{32,48},{40,56},{48,64},{56,72},{64,... | collective-permute-start | bytes 792584 | tf_op jit(solution)/shard_map/ppermute | solution.py:25
  101.6 8.3 %collective-permute-start.3 = (f32[4,129,128]{2,1,0:T(8,128)S(1)}, f32[4,129,128]{2,1,0:T(8,128)S(1)}, u32[]{:S(2)}, u32[]{:S(2)}) collective-permute-start(f32[4,129,128]{2,1,0:T(8,128)S(1)} %pad_maximum_fusion.4), channel_id=1, source_target_pairs={{0,32},{8,40},{16,48},{24,56},{32,64},{40,72},{48,80},{56,88},{64,... | collective-permute-start | bytes 792584 | tf_op jit(solution)/shard_map/ppermute | solution.py:25
  110.0 10.1 %collective-permute-start.4 = (f32[4,129,128]{2,1,0:T(8,128)S(1)}, f32[4,129,128]{2,1,0:T(8,128)S(1)}, u32[]{:S(2)}, u32[]{:S(2)}) collective-permute-start(f32[4,129,128]{2,1,0:T(8,128)S(1)} %pad_maximum_fusion.5), channel_id=1, source_target_pairs={{0,64},{8,72},{16,80},{24,88},{32,96},{40,104},{48,112},{56,120},{... | collective-permute-start | bytes 792584 | tf_op jit(solution)/shard_map/ppermute | solution.py:25
  120.2 10.1 %collective-permute-start.5 = (f32[4,129,128]{2,1,0:T(8,128)S(1)}, f32[4,129,128]{2,1,0:T(8,128)S(1)}, u32[]{:S(2)}, u32[]{:S(2)}) collective-permute-start(f32[4,129,128]{2,1,0:T(8,128)S(1)} %pad_maximum_fusion.6), channel_id=1, source_target_pairs={{0,128},{8,136},{16,144},{24,152},{32,160},{40,168},{48,176},{56,1... | collective-permute-start | bytes 792584 | tf_op jit(solution)/shard_map/ppermute | solution.py:25
  134.1 77.2 %all-to-all-start = ((bf16[64,48,512]{2,1,0:T(8,128)(2,1)}), bf16[64,48,512]{2,1,0:T(8,128)(2,1)S(1)}, u32[]{:S(2)}, u32[]{:S(2)}) async-start(bf16[64,48,512]{2,1,0:T(8,128)(2,1)} %bitcast.127), calls=%async_computation | async-start | bytes 6291456 | tf_op jit(solution)/shard_map/all_to_all | solution.py:130
  142.5 78.1 %all-gather.7.cloned.1.call-start = ((), (), s32[]{:S(2)}) async-start(), calls=%async_computation.3 | async-start | bytes 6291456 | tf_op jit(solution)/shard_map/all_gather | solution.py:76
  142.5 40.9 %collective-permute-start.7 = (bf16[128,4096]{1,0:T(8,128)(2,1)}, bf16[128,4096]{1,0:T(8,128)(2,1)S(1)}, u32[]{:S(2)}, u32[]{:S(2)}) collective-permute-start(bf16[128,4096]{1,0:T(8,128)(2,1)} %bitcast.132), channel_id=1, source_target_pairs={{0,16},{16,0},{1,17},{17,1},{2,18},{18,2},{3,19},{19,3},{4,20},{20... | collective-permute-start | bytes 3145736 | tf_op jit(solution)/shard_map/ppermute | solution.py:74
  214.6 6.1 %copy-start.1 = (bf16[48,8,8,512]{3,1,2,0:T(8,128)(2,1)}, bf16[48,8,8,512]{3,1,2,0:T(8,128)(2,1)S(1)}, u32[]{:S(2)}) copy-start(bf16[48,8,8,512]{3,1,2,0:T(8,128)(2,1)S(1)} %copy.58) | copy-start | bytes 9437188
  231.7 7.7 %copy-start.7 = (f32[8,2]{0,1:T(2,128)S(1)}, f32[8,2]{0,1:T(2,128)}, u32[]{:S(2)}) copy-start(f32[8,2]{0,1:T(2,128)} %param.19) | copy-start | bytes 196
  231.7 98.9 %all-to-all-start.1 = ((bf16[64,6,4096]{2,1,0:T(8,128)(2,1)}), bf16[64,6,4096]{2,1,0:T(8,128)(2,1)}, u32[]{:S(2)}, u32[]{:S(2)}) async-start(bf16[64,6,4096]{2,1,0:T(8,128)(2,1)} %reshape.229), calls=%async_computation.1 | async-start | bytes 8388608 | tf_op jit(solution)/shard_map/all_to_all | solution.py:146
Sparse Core Ops, SparseCore 0:
  61.0 27.0 all-gather.4
  186.4 23.4 all-gather.6

commit v8 on v5

--- a/solution.py
+++ b/solution.py
@@ -76,6 +76,7 @@
     top_count = expert_ids.shape[1]
     capacity = max(2, (3 * tok_count * top_count + 2 * experts - 1) // (2 * experts))
     ids_all = lax.all_gather(expert_ids, "dev", axis=0, tiled=False)
+    gate_up, down_all, ids_all = lax.optimization_barrier((gate_up, down_all, ids_all))
 
     seq_len = queries.shape[0]
     heads = log_decay.shape[1]

time: 280 us -> 295 us (1.054); the launches traced: 276 us -> 295 us
  waiting for transfers between devices: 83 us -> 93 us
  blocking collectives: 118 us -> 122 us
    ppermute x1, waiting for transfers between devices: 0.01 us -> 48.7 us  [per_device(): lax.ppermute(down_weight[0], 'xl', partner)]
    ppermute x1, waiting for transfers between devices: 45.1 us -> 0.01 us  [per_device(): lax.ppermute(gate_up, 'xl', partner)]
    ppermute x6, waiting for transfers between devices: 25.6 us -> 31.3 us  [shifted(): return lax.ppermute(value, SEQ_AXES, pairs)]
    all_to_all x1, blocking collectives: 40.7 us -> 45.2 us  [per_device(): lax.all_to_all(jnp.broadcast_to(local_rows[None], (groups,) + local_rows....]
  transfers between devices with their start and end apart: 11 -> 11, of which waited for: 7 -> 8; matrix products, arithmetic and copies ran while one was open for 5% -> 4% of each run, Pallas kernels for 0% -> 0%
where the time goes in v8:
time: 295 us
  blocking collectives  122 us (41%)
  waiting for transfers between devices  93 us (32%)
  starting transfers between devices  31.2 us (11%)
  matrix products  15 us (5%)
  between operations  13.7 us (5%)
  other arithmetic  9.81 us (3%)
  local copies, waits for them, and re-layouts  9.61 us (3%)
    ppermute x1, waiting for transfers between devices, per_device(): lax.ppermute(down_weight[0], 'xl', partner)  48.7 us
    all_to_all x1, blocking collectives, per_device(): lax.all_to_all(jnp.broadcast_to(local_rows[None], (groups,) + local_rows....  45.2 us
    all_to_all x1, blocking collectives, per_device(): lax.all_to_all(term.reshape(groups, per_expert, width), TOK_AXES, split_a...  38.1 us
    ppermute x6, waiting for transfers between devices, shifted(): return lax.ppermute(value, SEQ_AXES, pairs)  31.3 us
    ppermute x6, starting transfers between devices, shifted(): return lax.ppermute(value, SEQ_AXES, pairs)  24.3 us
    all_to_all x1, blocking collectives, per_device(): lax.all_to_all(send_rows, 'dev', split_axis=0, concat_axis=0, tiled=True)  20.2 us
    all_gather x1, blocking collectives, per_device(): ids_all = lax.all_gather(expert_ids, 'dev', axis=0, tiled=False)  18.8 us
    all_to_all x1, waiting for transfers between devices, per_device(): lax.all_to_all(summed.reshape(dev_count, capacity, width), 'dev', split_a...  13 us
  transfers between devices with their start and end apart: 11, of which 8 were waited for; matrix products, arithmetic and copies ran while one was open for 4% of the time, Pallas kernels for 0%

profile of v8, /device:TPU:2, one launch (start us, length us, event | category | flops | bytes accessed | tf_op | source)
XLA Modules:
  0.0 294.6 jit_solution(15733714182065670350)
XLA Ops:
  6.5 1.4 constant_dynamic-update-slice_fusion.1
  7.9 1.4 constant_dynamic-update-slice_fusion
  9.3 2.4 collective-permute-start.6
  11.7 0.1 collective-permute-start.7
  11.8 18.8 %all-gather.1 = s32[8,8,2]{1,2,0:T(2,128)S(1)} all-gather(s32[1,8,2]{1,2,0:T(2,128)S(1)} %bitcast.146), channel_id=2, replica_groups=mesh['y'=4,'xh'=2,'xl'=2,'c'=2,'dev'=8] {'dev'}, dimensions={0}, use_global_device_ids=true | all-gather | bytes 576 | tf_op jit(solution)/shard_map/all_gather | solution.py:78
  30.6 48.7 %collective-permute-done.7 = bf16[128,4096]{1,0:T(8,128)(2,1)S(1)} collective-permute-done((bf16[128,4096]{1,0:T(8,128)(2,1)S(1)}, bf16[128,4096]{1,0:T(8,128)(2,1)S(1)}, u32[]{:S(2)}, u32[]{:S(2)}) %collective-permute-start.7) | collective-permute-done | bytes 1048608 | tf_op jit(solution)/shard_map/ppermute | solution.py:73
  79.2 1.5 pad_maximum_fusion.1
  80.8 4.4 %pad_maximum_fusion = bf16[2,4096,256]{2,1,0:T(8,128)(2,1)} fusion(bf16[2,4096,128]{2,1,0:T(8,128)(2,1)} %collective-permute-done.6, bf16[2,4096,128]{2,1,0:T(8,128)(2,1)S(1)} %constant_dynamic-update-slice_fusion), kind=kLoop, calls=%fused_computation.8 | loop fusion | flops 8388608 | bytes 8388608 | tf_op jit(solution)/shard_map/concatenate | solution.py:72
  85.2 0.6 copy-done.5
  85.8 0.2 reduce_window_sum.22
  86.0 0.2 slice_reduce_fusion
  86.3 0.5 fusion.19
  86.9 1.9 collective-permute-start
  88.8 5.9 %collective-permute-done = f32[4,129,128]{2,1,0:T(8,128)S(1)} collective-permute-done((f32[4,129,128]{2,1,0:T(8,128)S(1)}, f32[4,129,128]{2,1,0:T(8,128)S(1)}, u32[]{:S(2)}, u32[]{:S(2)}) %collective-permute-start) | collective-permute-done | bytes 264224 | tf_op jit(solution)/shard_map/ppermute | solution.py:24
  94.7 1.9 collective-permute-start.1
  96.7 5.9 %collective-permute-done.1 = f32[4,129,128]{2,1,0:T(8,128)S(1)} collective-permute-done((f32[4,129,128]{2,1,0:T(8,128)S(1)}, f32[4,129,128]{2,1,0:T(8,128)S(1)}, u32[]{:S(2)}, u32[]{:S(2)}) %collective-permute-start.1) | collective-permute-done | bytes 264224 | tf_op jit(solution)/shard_map/ppermute | solution.py:24
  102.7 3.4 %collective-permute-start.2 = (f32[4,129,128]{2,1,0:T(8,128)S(1)}, f32[4,129,128]{2,1,0:T(8,128)S(1)}, u32[]{:S(2)}, u32[]{:S(2)}) collective-permute-start(f32[4,129,128]{2,1,0:T(8,128)S(1)} %pad_maximum_fusion.3), channel_id=1, source_target_pairs={{0,16},{8,24},{16,32},{24,40},{32,48},{40,56},{48,64},{56,72},{64,... | collective-permute-start | bytes 792584 | tf_op jit(solution)/shard_map/ppermute | solution.py:24
  106.1 6.2 %collective-permute-done.2 = f32[4,129,128]{2,1,0:T(8,128)S(1)} collective-permute-done((f32[4,129,128]{2,1,0:T(8,128)S(1)}, f32[4,129,128]{2,1,0:T(8,128)S(1)}, u32[]{:S(2)}, u32[]{:S(2)}) %collective-permute-start.2) | collective-permute-done | bytes 264224 | tf_op jit(solution)/shard_map/ppermute | solution.py:24
  112.3 6.1 %collective-permute-start.3 = (f32[4,129,128]{2,1,0:T(8,128)S(1)}, f32[4,129,128]{2,1,0:T(8,128)S(1)}, u32[]{:S(2)}, u32[]{:S(2)}) collective-permute-start(f32[4,129,128]{2,1,0:T(8,128)S(1)} %pad_maximum_fusion.4), channel_id=1, source_target_pairs={{0,32},{8,40},{16,48},{24,56},{32,64},{40,72},{48,80},{56,88},{64,... | collective-permute-start | bytes 792584 | tf_op jit(solution)/shard_map/ppermute | solution.py:24
  118.5 5.6 %collective-permute-done.3 = f32[4,129,128]{2,1,0:T(8,128)S(1)} collective-permute-done((f32[4,129,128]{2,1,0:T(8,128)S(1)}, f32[4,129,128]{2,1,0:T(8,128)S(1)}, u32[]{:S(2)}, u32[]{:S(2)}) %collective-permute-start.3) | collective-permute-done | bytes 264224 | tf_op jit(solution)/shard_map/ppermute | solution.py:24
  124.2 4.2 %collective-permute-start.4 = (f32[4,129,128]{2,1,0:T(8,128)S(1)}, f32[4,129,128]{2,1,0:T(8,128)S(1)}, u32[]{:S(2)}, u32[]{:S(2)}) collective-permute-start(f32[4,129,128]{2,1,0:T(8,128)S(1)} %pad_maximum_fusion.5), channel_id=1, source_target_pairs={{0,64},{8,72},{16,80},{24,88},{32,96},{40,104},{48,112},{56,120},{... | collective-permute-start | bytes 792584 | tf_op jit(solution)/shard_map/ppermute | solution.py:24
  128.5 4.0 %collective-permute-done.4 = f32[4,129,128]{2,1,0:T(8,128)S(1)} collective-permute-done((f32[4,129,128]{2,1,0:T(8,128)S(1)}, f32[4,129,128]{2,1,0:T(8,128)S(1)}, u32[]{:S(2)}, u32[]{:S(2)}) %collective-permute-start.4) | collective-permute-done | bytes 264224 | tf_op jit(solution)/shard_map/ppermute | solution.py:24
  132.5 6.8 %collective-permute-start.5 = (f32[4,129,128]{2,1,0:T(8,128)S(1)}, f32[4,129,128]{2,1,0:T(8,128)S(1)}, u32[]{:S(2)}, u32[]{:S(2)}) collective-permute-start(f32[4,129,128]{2,1,0:T(8,128)S(1)} %pad_maximum_fusion.6), channel_id=1, source_target_pairs={{0,128},{8,136},{16,144},{24,152},{32,160},{40,168},{48,176},{56,1... | collective-permute-start | bytes 792584 | tf_op jit(solution)/shard_map/ppermute | solution.py:24
  139.6 0.2 convolution_multiply_fusion
  139.7 3.6 %collective-permute-done.5 = f32[4,129,128]{2,1,0:T(8,128)S(1)} collective-permute-done((f32[4,129,128]{2,1,0:T(8,128)S(1)}, f32[4,129,128]{2,1,0:T(8,128)S(1)}, u32[]{:S(2)}, u32[]{:S(2)}) %collective-permute-start.5) | collective-permute-done | bytes 264224 | tf_op jit(solution)/shard_map/ppermute | solution.py:24
  143.4 0.3 fusion.7
  143.6 0.3 fusion.13
  144.0 0.1 copy_bitcast_fusion
  144.2 0.4 fusion.42
  144.8 0.1 copy.31
  144.9 0.1 mul.193
  145.1 1.0 scatter_custom_fusion
  146.1 1.0 gather_fusion
  147.1 20.2 %all_to_all.20 = bf16[8,48,512]{2,1,0:T(8,128)(2,1)S(1)} all-to-all(bf16[8,48,512]{2,1,0:T(8,128)(2,1)S(1)} %bitcast.131), channel_id=1, replica_groups=mesh['y'=4,'xh'=2,'xl'=2,'c'=2,'dev'=8] {'dev'}, dimensions={0} | all-to-all | bytes 786432 | tf_op jit(solution)/shard_map/all_to_all | solution.py:124
  167.4 0.4 broadcast_in_dim.62
  167.8 45.2 %all_to_all.21 = bf16[8,48,4096]{2,1,0:T(8,128)(2,1)S(1)} all-to-all(bf16[8,48,4096]{2,1,0:T(8,128)(2,1)S(1)} %broadcast_in_dim.62), channel_id=1, replica_groups=mesh['y'=4,'xh'=2,'xl'=2,'c'=2,'dev'=8] {'y','xh'}, dimensions={0} | all-to-all | bytes 6291456 | tf_op jit(solution)/shard_map/all_to_all | solution.py:134
  212.9 4.9 %fusion.1 = f32[384,512]{1,0:T(8,128)} fusion(bf16[384,4096]{1,0:T(8,128)(2,1)S(1)} %bitcast.128, bf16[2,4096,512]{2,1,0:T(8,128)(2,1)} %all-gather.5.cloned.1.call-done), kind=kOutput, calls=%fused_computation.7 | convolution fusion | flops 1610612736 | bytes 8126464 | tf_op jit(solution)/shard_map/dot_general | solution.py:141
  217.8 8.9 %convolution_convert_fusion = bf16[384,4096]{1,0:T(8,128)(2,1)} fusion(bf16[512,4096]{1,0:T(8,128)(2,1)} %all-gather.7.cloned.1.call-done, bf16[384,4096]{1,0:T(8,128)(2,1)S(1)} %bitcast.129, bf16[2,4096,512]{2,1,0:T(8,128)(2,1)} %all-gather.5.cloned.1.call-done, f32[384,512]{1,0:T(8,128)} %fusion.1), kind=kOutput, calls=%fused_computation.3 | convolution fusion | flops 3223977984 | bytes 15466496 | tf_op jit(solution)/shard_map/dot_general | solution.py:144
  226.7 38.1 %all_to_all.22 = bf16[8,48,4096]{2,1,0:T(8,128)(2,1)S(1)} all-to-all(bf16[8,48,4096]{2,1,0:T(8,128)(2,1)} %bitcast.130), channel_id=1, replica_groups=mesh['y'=4,'xh'=2,'xl'=2,'c'=2,'dev'=8] {'y','xh'}, dimensions={0} | all-to-all | bytes 6291456 | tf_op jit(solution)/shard_map/all_to_all | solution.py:145
  264.8 1.3 reduce_sum.53
  266.1 1.9 reshape.229
  268.0 4.4 %all-to-all-start.3 = ((bf16[8,6,4096]{2,1,0:T(8,128)(2,1)}), bf16[8,6,4096]{2,1,0:T(8,128)(2,1)S(1)}, u32[]{:S(2)}, u32[]{:S(2)}) async-start(bf16[8,6,4096]{2,1,0:T(8,128)(2,1)} %reshape.229), calls=%async_computation.3 | async-start | bytes 1048576 | tf_op jit(solution)/shard_map/all_to_all | solution.py:149
  272.5 0.2 add_reduce_fusion
  272.7 13.0 %all-to-all-done.3 = bf16[8,6,4096]{2,1,0:T(8,128)(2,1)S(1)} async-done(((bf16[8,6,4096]{2,1,0:T(8,128)(2,1)}), bf16[8,6,4096]{2,1,0:T(8,128)(2,1)S(1)}, u32[]{:S(2)}, u32[]{:S(2)}) %all-to-all-start.3) | async-done | bytes 393248 | tf_op jit(solution)/shard_map/all_to_all | solution.py:149
  285.7 0.1 bitcast_reduce_fusion
  285.9 0.6 gather_fusion.1
  286.5 0.2 reshape.232
  286.7 1.0 multiply_reduce_fusion
  (60 shorter events, 1.4 us)
Async XLA Ops:
  6.5 79.8 %copy-start = (bf16[64,512]{1,0:T(8,128)(2,1)S(1)}, bf16[64,512]{1,0:T(8,128)(2,1)}, u32[]{:S(2)}) copy-start(bf16[64,512]{1,0:T(8,128)(2,1)} %param.12) | copy-start | bytes 196612
  6.5 5.1 %copy-start.1 = (bf16[1,128,4096]{2,1,0:T(8,128)(2,1)S(1)}, bf16[1,128,4096]{2,1,0:T(8,128)(2,1)}, u32[]{:S(2)}) copy-start(bf16[1,128,4096]{2,1,0:T(8,128)(2,1)} %param.17) | copy-start | bytes 3145732
  6.5 5.2 %copy-start.6 = (s32[8,2]{0,1:T(2,128)S(1)}, s32[8,2]{0,1:T(2,128)}, u32[]{:S(2)}) copy-start(s32[8,2]{0,1:T(2,128)} %param.18) | copy-start | bytes 196
  6.5 206.4 %all-gather.5.cloned.1.call-start = ((), (), s32[]{:S(2)}) async-start(), calls=%async_computation.4 | async-start | bytes 12582912 | tf_op jit(solution)/shard_map/all_gather | solution.py:129
  9.3 71.5 %collective-permute-start.6 = (bf16[2,4096,128]{2,1,0:T(8,128)(2,1)S(1)}, bf16[2,4096,128]{2,1,0:T(8,128)(2,1)}, u32[]{:S(2)}, u32[]{:S(2)}) collective-permute-start(bf16[2,4096,128]{2,1,0:T(8,128)(2,1)S(1)} %constant_dynamic-update-slice_fusion), channel_id=1, source_target_pairs={{0,16},{16,0},{1,17},{17,1},{2,18},{18,2},{3,19},{19,3},{4,20},{20... | collective-permute-start | bytes 6291464 | tf_op jit(solution)/shard_map/ppermute | solution.py:72
  11.7 67.6 %collective-permute-start.7 = (bf16[128,4096]{1,0:T(8,128)(2,1)S(1)}, bf16[128,4096]{1,0:T(8,128)(2,1)S(1)}, u32[]{:S(2)}, u32[]{:S(2)}) collective-permute-start(bf16[128,4096]{1,0:T(8,128)(2,1)S(1)} %bitcast.134), channel_id=1, source_target_pairs={{0,16},{16,0},{1,17},{17,1},{2,18},{18,2},{3,19},{19,3},{4,20},{20... | collective-permute-start | bytes 3145736 | tf_op jit(solution)/shard_map/ppermute | solution.py:73
  85.1 0.7 copy-start.5
  85.1 1.2 copy-start.2
  85.1 54.4 %copy-start.3 = (bf16[64,512]{1,0:T(8,128)(2,1)S(1)}, bf16[64,512]{1,0:T(8,128)(2,1)}, u32[]{:S(2)}) copy-start(bf16[64,512]{1,0:T(8,128)(2,1)} %param.10) | copy-start | bytes 196612
  85.2 58.8 %copy-start.4 = (f32[512]{0:T(512)S(1)}, f32[512]{0:T(512)}, u32[]{:S(2)}) copy-start(f32[512]{0:T(512)} %param.14) | copy-start | bytes 6148
  85.2 132.7 %all-gather.7.cloned.1.call-start = ((), (), s32[]{:S(2)}) async-start(), calls=%async_computation.5 | async-start | bytes 6291456 | tf_op jit(solution)/shard_map/all_gather | solution.py:130
  86.9 7.9 %collective-permute-start = (f32[4,129,128]{2,1,0:T(8,128)S(1)}, f32[4,129,128]{2,1,0:T(8,128)S(1)}, u32[]{:S(2)}, u32[]{:S(2)}) collective-permute-start(f32[4,129,128]{2,1,0:T(8,128)S(1)} %pad_maximum_fusion.2), channel_id=1, source_target_pairs={{0,8},{8,16},{16,24},{24,32},{32,40},{40,48},{48,56},{56,64},{64,7... | collective-permute-start | bytes 792584 | tf_op jit(solution)/shard_map/ppermute | solution.py:24
  94.7 7.9 %collective-permute-start.1 = (f32[4,129,128]{2,1,0:T(8,128)S(1)}, f32[4,129,128]{2,1,0:T(8,128)S(1)}, u32[]{:S(2)}, u32[]{:S(2)}) collective-permute-start(f32[4,129,128]{2,1,0:T(8,128)S(1)} %collective-permute-done), channel_id=1, source_target_pairs={{0,8},{8,16},{16,24},{24,32},{32,40},{40,48},{48,56},{56,64},{64,7... | collective-permute-start | bytes 792584 | tf_op jit(solution)/shard_map/ppermute | solution.py:24
  102.7 9.6 %collective-permute-start.2 = (f32[4,129,128]{2,1,0:T(8,128)S(1)}, f32[4,129,128]{2,1,0:T(8,128)S(1)}, u32[]{:S(2)}, u32[]{:S(2)}) collective-permute-start(f32[4,129,128]{2,1,0:T(8,128)S(1)} %pad_maximum_fusion.3), channel_id=1, source_target_pairs={{0,16},{8,24},{16,32},{24,40},{32,48},{40,56},{48,64},{56,72},{64,... | collective-permute-start | bytes 792584 | tf_op jit(solution)/shard_map/ppermute | solution.py:24
  112.3 11.8 %collective-permute-start.3 = (f32[4,129,128]{2,1,0:T(8,128)S(1)}, f32[4,129,128]{2,1,0:T(8,128)S(1)}, u32[]{:S(2)}, u32[]{:S(2)}) collective-permute-start(f32[4,129,128]{2,1,0:T(8,128)S(1)} %pad_maximum_fusion.4), channel_id=1, source_target_pairs={{0,32},{8,40},{16,48},{24,56},{32,64},{40,72},{48,80},{56,88},{64,... | collective-permute-start | bytes 792584 | tf_op jit(solution)/shard_map/ppermute | solution.py:24
  124.2 8.2 %collective-permute-start.4 = (f32[4,129,128]{2,1,0:T(8,128)S(1)}, f32[4,129,128]{2,1,0:T(8,128)S(1)}, u32[]{:S(2)}, u32[]{:S(2)}) collective-permute-start(f32[4,129,128]{2,1,0:T(8,128)S(1)} %pad_maximum_fusion.5), channel_id=1, source_target_pairs={{0,64},{8,72},{16,80},{24,88},{32,96},{40,104},{48,112},{56,120},{... | collective-permute-start | bytes 792584 | tf_op jit(solution)/shard_map/ppermute | solution.py:24
  132.5 10.8 %collective-permute-start.5 = (f32[4,129,128]{2,1,0:T(8,128)S(1)}, f32[4,129,128]{2,1,0:T(8,128)S(1)}, u32[]{:S(2)}, u32[]{:S(2)}) collective-permute-start(f32[4,129,128]{2,1,0:T(8,128)S(1)} %pad_maximum_fusion.6), channel_id=1, source_target_pairs={{0,128},{8,136},{16,144},{24,152},{32,160},{40,168},{48,176},{56,1... | collective-permute-start | bytes 792584 | tf_op jit(solution)/shard_map/ppermute | solution.py:24
  264.8 7.6 %copy-start.7 = (f32[8,2]{0,1:T(2,128)S(1)}, f32[8,2]{0,1:T(2,128)}, u32[]{:S(2)}) copy-start(f32[8,2]{0,1:T(2,128)} %param.19) | copy-start | bytes 196
  268.0 17.7 %all-to-all-start.3 = ((bf16[8,6,4096]{2,1,0:T(8,128)(2,1)}), bf16[8,6,4096]{2,1,0:T(8,128)(2,1)S(1)}, u32[]{:S(2)}, u32[]{:S(2)}) async-start(bf16[8,6,4096]{2,1,0:T(8,128)(2,1)} %reshape.229), calls=%async_computation.3 | async-start | bytes 1048576 | tf_op jit(solution)/shard_map/all_to_all | solution.py:149
Sparse Core Ops, SparseCore 0:
  85.3 26.6 all-gather.4
  145.2 24.6 all-gather.6

commit v9 on v4

--- a/solution.py
+++ b/solution.py
@@ -68,17 +68,18 @@
     dev_count = lax.axis_size("e") * lax.axis_size("p")
     experts = dev_count // PAIR
 
+    ids_all = lax.all_gather(expert_ids, DEV_AXES, axis=0, tiled=False)
     partner = [(0, 1), (1, 0)]
     gate_up = jnp.stack([gate_weight[0], up_weight[0]])
+    gate_up, down_own, ids_all = lax.optimization_barrier((gate_up, down_weight[0], ids_all))
     gate_up = jnp.concatenate([gate_up, lax.ppermute(gate_up, "p", partner)], axis=2)
-    down_all = jnp.concatenate([down_weight[0], lax.ppermute(down_weight[0], "p", partner)], axis=0)
+    down_all = jnp.concatenate([down_own, lax.ppermute(down_own, "p", partner)], axis=0)
 
     tok_count = expert_ids.shape[0]
     top_count = expert_ids.shape[1]
     capacity = max(2, (3 * tok_count * top_count + 2 * experts - 1) // (2 * experts))
     capacity = -(-capacity // PAIR) * PAIR
     half = capacity // PAIR
-    ids_all = lax.all_gather(expert_ids, DEV_AXES, axis=0, tiled=False)
 
     seq_len = queries.shape[0]
     heads = log_decay.shape[1]

time: 289 us -> 238 us (0.82)
  blocking collectives: 166 us -> 112 us
  waiting for transfers between devices: 25.1 us -> 32.2 us
    all_gather x1, blocking collectives: 79.6 us -> 19.4 us  [per_device(): ids_all = lax.all_gather(expert_ids, DEV_AXES, axis=0, tiled=False)]
    ppermute x1, waiting for transfers between devices: 0.01 us -> 7.19 us  [per_device(): lax.ppermute(gate_up, 'p', partner)]
    all_to_all x1, blocking collectives: 34.6 us -> 38.1 us  [per_device(): lax.all_to_all(term.reshape(groups, per_dev, width), TOK_AXES, split_axis...]
  transfers between devices with their start and end apart: 11 -> 11, of which waited for: 5 -> 6; matrix products, arithmetic and copies ran while one was open for 11% -> 12% of each run, Pallas kernels for 0% -> 0%
where the time goes in v9:
time: 238 us; the launch traced here: 237 us
  blocking collectives  112 us (47%)
  waiting for transfers between devices  32.2 us (14%)
  starting transfers between devices  29 us (12%)
  other arithmetic  23.2 us (10%)
  matrix products  19.1 us (8%)
  between operations  13.7 us (6%)
  local copies, waits for them, and re-layouts  7.94 us (3%)
    all_to_all x1, blocking collectives, per_device(): lax.all_to_all(jnp.broadcast_to(local_rows[None], (groups,) + local_rows....  40.9 us
    all_to_all x1, blocking collectives, per_device(): lax.all_to_all(term.reshape(groups, per_dev, width), TOK_AXES, split_axis...  38.1 us
    ppermute x6, starting transfers between devices, shifted(): return lax.ppermute(value, SEQ_AXES, pairs)  23.4 us
    all_gather x1, blocking collectives, per_device(): ids_all = lax.all_gather(expert_ids, DEV_AXES, axis=0, tiled=False)  19.4 us
    ppermute x6, waiting for transfers between devices, shifted(): return lax.ppermute(value, SEQ_AXES, pairs)  14.2 us
    all_to_all x1, blocking collectives, per_device(): lax.all_to_all(send_rows, DEV_AXES, split_axis=0, concat_axis=0, tiled=True)  13.2 us
    all_to_all x1, waiting for transfers between devices, per_device(): lax.all_to_all(summed.reshape(dev_count, half, width), DEV_AXES, split_ax...  10.1 us
    dot_general x1, matrix products, per_device(): jnp.dot(hidden_all, down_all, preferred_element_type=jnp.float32)  8.88 us
  transfers between devices with their start and end apart: 11, of which 6 were waited for; matrix products, arithmetic and copies ran while one was open for 12% of the time, Pallas kernels for 0%

profile of v9, /device:TPU:2, one launch (start us, length us, event | category | flops | bytes accessed | tf_op | source)
XLA Modules:
  0.0 236.7 jit_solution(11899924621867713789)
XLA Ops:
  6.5 1.0 reduce_window_sum.22
  7.7 0.6 exponential_bitcast_fusion
  8.4 1.3 fusion.19
  9.7 0.7 pad_maximum_fusion.3
  10.4 1.9 collective-permute-start.2
  12.4 19.4 %all-gather.1 = s32[8,8,2]{1,2,0:T(2,128)S(1)} all-gather(s32[1,8,2]{1,2,0:T(2,128)} %bitcast.142), channel_id=2, replica_groups=mesh['y'=4,'x'=4,'c'=2,'e'=4,'p'=2] {'e','p'}, dimensions={0}, use_global_device_ids=true | all-gather | bytes 576 | tf_op jit(solution)/shard_map/all_gather | solution.py:71
  31.8 1.7 pad_maximum_fusion.1
  33.6 2.0 collective-permute-start
  36.3 1.9 collective-permute-start.3
  39.5 5.0 %collective-permute-done.3 = f32[4,129,128]{2,1,0:T(8,128)} collective-permute-done((f32[4,129,128]{2,1,0:T(8,128)}, f32[4,129,128]{2,1,0:T(8,128)}, u32[]{:S(2)}, u32[]{:S(2)}) %collective-permute-start.3) | collective-permute-done | bytes 264224 | tf_op jit(solution)/shard_map/ppermute | solution.py:25
  44.4 0.7 fusion.42
  45.2 1.1 slice_add_fusion
  46.3 3.4 %collective-permute-start.4 = (f32[4,129,128]{2,1,0:T(8,128)S(1)}, f32[4,129,128]{2,1,0:T(8,128)S(1)}, u32[]{:S(2)}, u32[]{:S(2)}) collective-permute-start(f32[4,129,128]{2,1,0:T(8,128)S(1)} %pad_maximum_fusion.4), channel_id=1, source_target_pairs={{0,16},{8,24},{16,32},{24,40},{32,48},{40,56},{48,64},{56,72},{64,... | collective-permute-start | bytes 792584 | tf_op jit(solution)/shard_map/ppermute | solution.py:25
  49.7 0.7 broadcast_add_fusion
  50.4 5.5 %collective-permute-done.4 = f32[4,129,128]{2,1,0:T(8,128)S(1)} collective-permute-done((f32[4,129,128]{2,1,0:T(8,128)S(1)}, f32[4,129,128]{2,1,0:T(8,128)S(1)}, u32[]{:S(2)}, u32[]{:S(2)}) %collective-permute-start.4) | collective-permute-done | bytes 264224 | tf_op jit(solution)/shard_map/ppermute | solution.py:25
  55.9 0.6 fusion.41
  57.1 0.7 pad_maximum_fusion.5
  57.8 4.7 %collective-permute-start.5 = (f32[4,129,128]{2,1,0:T(8,128)}, f32[4,129,128]{2,1,0:T(8,128)}, u32[]{:S(2)}, u32[]{:S(2)}) collective-permute-start(f32[4,129,128]{2,1,0:T(8,128)} %pad_maximum_fusion.5), channel_id=1, source_target_pairs={{0,32},{8,40},{16,48},{24,56},{32,64},{40,72},{48,80},{56,88},{64,... | collective-permute-start | bytes 792584 | tf_op jit(solution)/shard_map/ppermute | solution.py:25
  62.5 0.6 iota_compare_fusion.2
  63.1 1.3 reshape.303
  64.4 1.6 scatter_custom_fusion
  66.0 1.7 convolution_multiply_fusion
  67.7 1.0 fusion.10
  68.7 0.8 fusion.40
  69.5 4.7 %collective-permute-start.6 = (f32[4,129,128]{2,1,0:T(8,128)S(1)}, f32[4,129,128]{2,1,0:T(8,128)S(1)}, u32[]{:S(2)}, u32[]{:S(2)}) collective-permute-start(f32[4,129,128]{2,1,0:T(8,128)S(1)} %pad_maximum_fusion.6), channel_id=1, source_target_pairs={{0,64},{8,72},{16,80},{24,88},{32,96},{40,104},{48,112},{56,120},{... | collective-permute-start | bytes 792584 | tf_op jit(solution)/shard_map/ppermute | solution.py:25
  74.2 0.6 compare_select_fusion
  75.4 2.8 %collective-permute-done.6 = f32[4,129,128]{2,1,0:T(8,128)S(1)} collective-permute-done((f32[4,129,128]{2,1,0:T(8,128)S(1)}, f32[4,129,128]{2,1,0:T(8,128)S(1)}, u32[]{:S(2)}, u32[]{:S(2)}) %collective-permute-start.6) | collective-permute-done | bytes 264224 | tf_op jit(solution)/shard_map/ppermute | solution.py:25
  78.8 0.7 pad_maximum_fusion.7
  79.5 6.7 %collective-permute-start.7 = (f32[4,129,128]{2,1,0:T(8,128)}, f32[4,129,128]{2,1,0:T(8,128)}, u32[]{:S(2)}, u32[]{:S(2)}) collective-permute-start(f32[4,129,128]{2,1,0:T(8,128)} %pad_maximum_fusion.7), channel_id=1, source_target_pairs={{0,128},{8,136},{16,144},{24,152},{32,160},{40,168},{48,176},{56,1... | collective-permute-start | bytes 792584 | tf_op jit(solution)/shard_map/ppermute | solution.py:25
  86.3 2.7 %pad_maximum_fusion.2 = bf16[256,4096]{1,0:T(8,128)(2,1)} fusion(bf16[128,4096]{1,0:T(8,128)(2,1)} %collective-permute-done.1, bf16[128,4096]{1,0:T(8,128)(2,1)S(1)} %bitcast.129), kind=kLoop, calls=%fused_computation.10 | loop fusion | flops 4194304 | bytes 4194304 | tf_op jit(solution)/shard_map/concatenate | solution.py:76
  89.0 0.9 collective-permute-done.7
  89.9 1.2 fusion.7
  91.1 1.2 fusion.13
  92.4 0.8 copy_bitcast_fusion
  93.2 1.1 gather_fusion
  94.3 7.2 %collective-permute-done = bf16[2,4096,128]{2,1,0:T(8,128)(2,1)} collective-permute-done((bf16[2,4096,128]{2,1,0:T(8,128)(2,1)S(1)}, bf16[2,4096,128]{2,1,0:T(8,128)(2,1)}, u32[]{:S(2)}, u32[]{:S(2)}) %collective-permute-start) | collective-permute-done | bytes 2097184 | tf_op jit(solution)/shard_map/ppermute | solution.py:75
  101.5 4.0 %pad_maximum_fusion = bf16[2,4096,256]{2,1,0:T(8,128)(2,1)} fusion(bf16[2,4096,128]{2,1,0:T(8,128)(2,1)} %collective-permute-done, bf16[2,4096,128]{2,1,0:T(8,128)(2,1)S(1)} %pad_maximum_fusion.1), kind=kLoop, calls=%fused_computation.8 | loop fusion | flops 8388608 | bytes 8388608 | tf_op jit(solution)/shard_map/concatenate | solution.py:75
  105.6 0.7 all-gather.7.cloned.1.call-update
  106.3 13.2 %all_to_all.20 = bf16[8,24,512]{2,1,0:T(8,128)(2,1)S(1)} all-to-all(bf16[8,24,512]{2,1,0:T(8,128)(2,1)S(1)} %bitcast.130), channel_id=1, replica_groups=mesh['y'=4,'x'=4,'c'=2,'e'=4,'p'=2] {'e','p'}, dimensions={0} | all-to-all | bytes 393216 | tf_op jit(solution)/shard_map/all_to_all | solution.py:130
  119.9 40.9 %all_to_all.21 = bf16[16,24,4096]{2,1,0:T(8,128)(2,1)S(1)} all-to-all(bf16[16,24,4096]{2,1,0:T(8,128)(2,1)S(1)} %broadcast_in_dim.58), channel_id=1, replica_groups=mesh['y'=4,'x'=4,'c'=2,'e'=4,'p'=2] {'y','x'}, dimensions={0} | all-to-all | bytes 6291456 | tf_op jit(solution)/shard_map/all_to_all | solution.py:136
  160.8 4.9 %fusion.1 = f32[384,512]{1,0:T(8,128)} fusion(bf16[384,4096]{1,0:T(8,128)(2,1)S(1)} %bitcast.125, bf16[2,4096,512]{2,1,0:T(8,128)(2,1)} %all-gather.5.cloned.1.call-done), kind=kOutput, calls=%fused_computation.7 | convolution fusion | flops 1610612736 | bytes 8126464 | tf_op jit(solution)/shard_map/dot_general | solution.py:143
  165.7 8.9 %convolution_convert_fusion = bf16[384,4096]{1,0:T(8,128)(2,1)} fusion(bf16[512,4096]{1,0:T(8,128)(2,1)} %all-gather.7.cloned.1.call-done, bf16[384,4096]{1,0:T(8,128)(2,1)S(1)} %bitcast.126, bf16[2,4096,512]{2,1,0:T(8,128)(2,1)} %all-gather.5.cloned.1.call-done, f32[384,512]{1,0:T(8,128)} %fusion.1), kind=kOutput, calls=%fused_computation.3 | convolution fusion | flops 3223977984 | bytes 15466496 | tf_op jit(solution)/shard_map/dot_general | solution.py:146
  174.6 38.1 %all_to_all.22 = bf16[16,24,4096]{2,1,0:T(8,128)(2,1)S(1)} all-to-all(bf16[16,24,4096]{2,1,0:T(8,128)(2,1)} %bitcast.127), channel_id=1, replica_groups=mesh['y'=4,'x'=4,'c'=2,'e'=4,'p'=2] {'y','x'}, dimensions={0} | all-to-all | bytes 6291456 | tf_op jit(solution)/shard_map/all_to_all | solution.py:147
  213.2 0.8 reshape.280
  214.1 3.4 %all-to-all-start.3 = ((bf16[8,3,4096]{2,1,0:T(4,128)(2,1)}), bf16[8,3,4096]{2,1,0:T(4,128)(2,1)S(1)}, u32[]{:S(2)}, u32[]{:S(2)}) async-start(bf16[8,3,4096]{2,1,0:T(4,128)(2,1)} %reshape.280), calls=%async_computation.3 | async-start | bytes 524288 | tf_op jit(solution)/shard_map/all_to_all | solution.py:151
  217.8 10.1 %all-to-all-done.3 = bf16[8,3,4096]{2,1,0:T(4,128)(2,1)S(1)} async-done(((bf16[8,3,4096]{2,1,0:T(4,128)(2,1)}), bf16[8,3,4096]{2,1,0:T(4,128)(2,1)S(1)}, u32[]{:S(2)}, u32[]{:S(2)}) %all-to-all-start.3) | async-done | bytes 196640 | tf_op jit(solution)/shard_map/all_to_all | solution.py:151
  228.0 0.6 gather_fusion.1
  228.8 1.0 multiply_reduce_fusion
  (59 shorter events, 5.7 us)
Async XLA Ops:
  6.5 1.8 copy-start
  6.5 59.5 %copy-start.2 = (bf16[64,512]{1,0:T(8,128)(2,1)S(1)}, bf16[64,512]{1,0:T(8,128)(2,1)}, u32[]{:S(2)}) copy-start(bf16[64,512]{1,0:T(8,128)(2,1)} %param.11) | copy-start | bytes 196612
  6.5 27.0 %copy-start.1 = (bf16[1,128,4096]{2,1,0:T(8,128)(2,1)S(1)}, bf16[1,128,4096]{2,1,0:T(8,128)(2,1)}, u32[]{:S(2)}) copy-start(bf16[1,128,4096]{2,1,0:T(8,128)(2,1)} %param.17) | copy-start | bytes 3145732
  6.5 154.3 %all-gather.5.cloned.1.call-start = ((), (), s32[]{:S(2)}) async-start(), calls=%async_computation.4 | async-start | bytes 12582912 | tf_op jit(solution)/shard_map/all_gather | solution.py:128
  7.6 26.0 %copy-start.5 = (f32[4,64]{1,0:T(4,128)}, f32[4,64]{1,0:T(4,128)S(1)}, u32[]{:S(2)}) copy-start(f32[4,64]{1,0:T(4,128)S(1)} %reduce_window_sum.22) | copy-start | bytes 3076
  10.4 25.8 %collective-permute-start.2 = (f32[4,129,128]{2,1,0:T(8,128)}, f32[4,129,128]{2,1,0:T(8,128)}, u32[]{:S(2)}, u32[]{:S(2)}) collective-permute-start(f32[4,129,128]{2,1,0:T(8,128)} %pad_maximum_fusion.3), channel_id=1, source_target_pairs={{0,8},{8,16},{16,24},{24,32},{32,40},{40,48},{48,56},{56,64},{64,7... | collective-permute-start | bytes 792584 | tf_op jit(solution)/shard_map/ppermute | solution.py:25
  33.5 52.8 %collective-permute-start.1 = (bf16[128,4096]{1,0:T(8,128)(2,1)S(1)}, bf16[128,4096]{1,0:T(8,128)(2,1)}, u32[]{:S(2)}, u32[]{:S(2)}) collective-permute-start(bf16[128,4096]{1,0:T(8,128)(2,1)S(1)} %bitcast.128), channel_id=1, source_target_pairs={{0,1},{1,0},{2,3},{3,2},{4,5},{5,4},{6,7},{7,6},{8,9},{9,8},{10,11... | collective-permute-start | bytes 3145736 | tf_op jit(solution)/shard_map/ppermute | solution.py:76
  33.6 67.9 %collective-permute-start = (bf16[2,4096,128]{2,1,0:T(8,128)(2,1)S(1)}, bf16[2,4096,128]{2,1,0:T(8,128)(2,1)}, u32[]{:S(2)}, u32[]{:S(2)}) collective-permute-start(bf16[2,4096,128]{2,1,0:T(8,128)(2,1)S(1)} %pad_maximum_fusion.1), channel_id=1, source_target_pairs={{0,1},{1,0},{2,3},{3,2},{4,5},{5,4},{6,7},{7,6},{8,9},{9,8},{10,11... | collective-permute-start | bytes 6291464 | tf_op jit(solution)/shard_map/ppermute | solution.py:75
  36.3 8.2 %collective-permute-start.3 = (f32[4,129,128]{2,1,0:T(8,128)}, f32[4,129,128]{2,1,0:T(8,128)}, u32[]{:S(2)}, u32[]{:S(2)}) collective-permute-start(f32[4,129,128]{2,1,0:T(8,128)} %collective-permute-done.2), channel_id=1, source_target_pairs={{0,8},{8,16},{16,24},{24,32},{32,40},{40,48},{48,56},{56,64},{64,7... | collective-permute-start | bytes 792584 | tf_op jit(solution)/shard_map/ppermute | solution.py:25
  46.3 9.6 %collective-permute-start.4 = (f32[4,129,128]{2,1,0:T(8,128)S(1)}, f32[4,129,128]{2,1,0:T(8,128)S(1)}, u32[]{:S(2)}, u32[]{:S(2)}) collective-permute-start(f32[4,129,128]{2,1,0:T(8,128)S(1)} %pad_maximum_fusion.4), channel_id=1, source_target_pairs={{0,16},{8,24},{16,32},{24,40},{32,48},{40,56},{48,64},{56,72},{64,... | collective-permute-start | bytes 792584 | tf_op jit(solution)/shard_map/ppermute | solution.py:25
  56.5 0.6 copy-start.4
  57.8 9.9 %collective-permute-start.5 = (f32[4,129,128]{2,1,0:T(8,128)}, f32[4,129,128]{2,1,0:T(8,128)}, u32[]{:S(2)}, u32[]{:S(2)}) collective-permute-start(f32[4,129,128]{2,1,0:T(8,128)} %pad_maximum_fusion.5), channel_id=1, source_target_pairs={{0,32},{8,40},{16,48},{24,56},{32,64},{40,72},{48,80},{56,88},{64,... | collective-permute-start | bytes 792584 | tf_op jit(solution)/shard_map/ppermute | solution.py:25
  68.7 21.3 %copy-start.3 = (bf16[64,512]{1,0:T(8,128)(2,1)S(1)}, bf16[64,512]{1,0:T(8,128)(2,1)}, u32[]{:S(2)}) copy-start(bf16[64,512]{1,0:T(8,128)(2,1)} %param.10) | copy-start | bytes 196612
  69.5 8.8 %collective-permute-start.6 = (f32[4,129,128]{2,1,0:T(8,128)S(1)}, f32[4,129,128]{2,1,0:T(8,128)S(1)}, u32[]{:S(2)}, u32[]{:S(2)}) collective-permute-start(f32[4,129,128]{2,1,0:T(8,128)S(1)} %pad_maximum_fusion.6), channel_id=1, source_target_pairs={{0,64},{8,72},{16,80},{24,88},{32,96},{40,104},{48,112},{56,120},{... | collective-permute-start | bytes 792584 | tf_op jit(solution)/shard_map/ppermute | solution.py:25
  79.5 10.4 %collective-permute-start.7 = (f32[4,129,128]{2,1,0:T(8,128)}, f32[4,129,128]{2,1,0:T(8,128)}, u32[]{:S(2)}, u32[]{:S(2)}) collective-permute-start(f32[4,129,128]{2,1,0:T(8,128)} %pad_maximum_fusion.7), channel_id=1, source_target_pairs={{0,128},{8,136},{16,144},{24,152},{32,160},{40,168},{48,176},{56,1... | collective-permute-start | bytes 792584 | tf_op jit(solution)/shard_map/ppermute | solution.py:25
  105.5 60.1 %all-gather.7.cloned.1.call-start = ((), (), s32[]{:S(2)}) async-start(), calls=%async_computation.5 | async-start | bytes 6291456 | tf_op jit(solution)/shard_map/all_gather | solution.py:129
  174.6 42.9 %copy-start.6 = (f32[8,2]{0,1:T(2,128)S(1)}, f32[8,2]{0,1:T(2,128)}, u32[]{:S(2)}) copy-start(f32[8,2]{0,1:T(2,128)} %param.19) | copy-start | bytes 196
  214.1 13.8 %all-to-all-start.3 = ((bf16[8,3,4096]{2,1,0:T(4,128)(2,1)}), bf16[8,3,4096]{2,1,0:T(4,128)(2,1)S(1)}, u32[]{:S(2)}, u32[]{:S(2)}) async-start(bf16[8,3,4096]{2,1,0:T(4,128)(2,1)} %reshape.280), calls=%async_computation.3 | async-start | bytes 524288 | tf_op jit(solution)/shard_map/all_to_all | solution.py:151
Sparse Core Ops, SparseCore 0:
  105.7 21.4 all-gather.4
  129.0 20.2 all-gather.6

commit v10 on v9

--- a/solution.py
+++ b/solution.py
@@ -27,16 +27,19 @@
 
 def carried_in(log_total, local_state, count):
     width = local_state.shape[-1]
-    packed = jnp.concatenate(
+    window = jnp.concatenate(
         [local_state, jnp.broadcast_to(log_total[:, None, None], (log_total.shape[0], 1, width))],
         axis=1,
     )
-    state = shifted(packed, 1, count)
+    earlier = None
     shift = 1
-    while shift < count - 1:
-        state = chain_join(shifted(state, shift, count), state)
+    while shift < count:
+        arrived = shifted(window, shift, count)
+        earlier = arrived if earlier is None else chain_join(arrived, earlier)
+        if 2 * shift < count:
+            window = chain_join(arrived, window)
         shift *= 2
-    return state[:, :-1, :]
+    return earlier[:, :-1, :]
 
 
 def head_norm(attention, gain):

time: 238 us -> 238 us (level)
    ppermute x1, waiting for transfers between devices: 7.19 us -> 14.2 us  [per_device(): lax.ppermute(gate_up, 'p', partner)]
    ppermute x6 -> x5, waiting for transfers between devices: 14.2 us -> 9.35 us  [shifted(): return lax.ppermute(value, SEQ_AXES, pairs)]
    ppermute x6 -> x5, starting transfers between devices: 23.4 us -> 23.1 us  [shifted(): return lax.ppermute(value, SEQ_AXES, pairs)]
  transfers between devices with their start and end apart: 11 -> 10, of which waited for: 6 -> 6; matrix products, arithmetic and copies ran while one was open for 12% -> 12% of each run, Pallas kernels for 0% -> 0%
where the time goes in v10:
time: 238 us; the launch traced here: 237 us
  blocking collectives  112 us (47%)
  waiting for transfers between devices  34.4 us (14%)
  starting transfers between devices  28.7 us (12%)
  other arithmetic  21.3 us (9%)
  matrix products  19.5 us (8%)
  between operations  13.7 us (6%)
  local copies, waits for them, and re-layouts  7.57 us (3%)
    all_to_all x1, blocking collectives, per_device(): lax.all_to_all(jnp.broadcast_to(local_rows[None], (groups,) + local_rows....  40.9 us
    all_to_all x1, blocking collectives, per_device(): lax.all_to_all(term.reshape(groups, per_dev, width), TOK_AXES, split_axis...  38.1 us
    ppermute x5, starting transfers between devices, shifted(): return lax.ppermute(value, SEQ_AXES, pairs)  23.1 us
    all_gather x1, blocking collectives, per_device(): ids_all = lax.all_gather(expert_ids, DEV_AXES, axis=0, tiled=False)  19.4 us
    ppermute x1, waiting for transfers between devices, per_device(): lax.ppermute(gate_up, 'p', partner)  14.2 us
    all_to_all x1, blocking collectives, per_device(): lax.all_to_all(send_rows, DEV_AXES, split_axis=0, concat_axis=0, tiled=True)  13.2 us
    all_to_all x1, waiting for transfers between devices, per_device(): lax.all_to_all(summed.reshape(dev_count, half, width), DEV_AXES, split_ax...  10.1 us
    ppermute x5, waiting for transfers between devices, shifted(): return lax.ppermute(value, SEQ_AXES, pairs)  9.35 us
  transfers between devices with their start and end apart: 10, of which 6 were waited for; matrix products, arithmetic and copies ran while one was open for 12% of the time, Pallas kernels for 0%

profile of v10, /device:TPU:2, one launch (start us, length us, event | category | flops | bytes accessed | tf_op | source)
XLA Modules:
  0.0 236.7 jit_solution(10873836926282492394)
XLA Ops:
  6.5 1.0 reduce_window_sum.22
  7.6 0.7 exponential_reduce_fusion
  8.3 1.3 fusion.29
  9.7 0.7 pad_maximum_fusion.3
  10.4 1.9 collective-permute-start.2
  12.4 19.4 %all-gather.1 = s32[8,8,2]{1,2,0:T(2,128)S(1)} all-gather(s32[1,8,2]{1,2,0:T(2,128)} %bitcast.146), channel_id=2, replica_groups=mesh['y'=4,'x'=4,'c'=2,'e'=4,'p'=2] {'e','p'}, dimensions={0}, use_global_device_ids=true | all-gather | bytes 576 | tf_op jit(solution)/shard_map/all_gather | solution.py:74
  31.7 1.7 pad_maximum_fusion.1
  33.6 2.0 collective-permute-start
  36.2 0.6 iota_multiply_fusion
  37.0 0.6 ne.75
  38.5 0.6 fusion.44
  39.1 0.8 fusion.52
  39.9 1.0 multiply_add_fusion.3
  41.0 3.4 %collective-permute-start.3 = (f32[4,129,128]{2,1,0:T(8,128)S(1)}, f32[4,129,128]{2,1,0:T(8,128)S(1)}, u32[]{:S(2)}, u32[]{:S(2)}) collective-permute-start(f32[4,129,128]{2,1,0:T(8,128)S(1)} %pad_maximum_fusion.4), channel_id=1, source_target_pairs={{0,16},{8,24},{16,32},{24,40},{32,48},{40,56},{48,64},{56,72},{64,... | collective-permute-start | bytes 792584 | tf_op jit(solution)/shard_map/ppermute | solution.py:25
  44.4 0.8 broadcast_add_fusion
  45.1 4.3 %collective-permute-done.3 = f32[4,129,128]{2,1,0:T(8,128)S(1)} collective-permute-done((f32[4,129,128]{2,1,0:T(8,128)S(1)}, f32[4,129,128]{2,1,0:T(8,128)S(1)}, u32[]{:S(2)}, u32[]{:S(2)}) %collective-permute-start.3) | collective-permute-done | bytes 264224 | tf_op jit(solution)/shard_map/ppermute | solution.py:25
  49.5 0.6 copy-done.2
  50.1 0.7 pad_maximum_fusion.5
  50.8 4.7 %collective-permute-start.4 = (f32[4,129,128]{2,1,0:T(8,128)}, f32[4,129,128]{2,1,0:T(8,128)}, u32[]{:S(2)}, u32[]{:S(2)}) collective-permute-start(f32[4,129,128]{2,1,0:T(8,128)} %pad_maximum_fusion.5), channel_id=1, source_target_pairs={{0,32},{8,40},{16,48},{24,56},{32,64},{40,72},{48,80},{56,88},{64,... | collective-permute-start | bytes 792584 | tf_op jit(solution)/shard_map/ppermute | solution.py:25
  55.7 1.0 scatter_custom_fusion
  56.7 2.6 %collective-permute-done.4 = f32[4,129,128]{2,1,0:T(8,128)} collective-permute-done((f32[4,129,128]{2,1,0:T(8,128)}, f32[4,129,128]{2,1,0:T(8,128)}, u32[]{:S(2)}, u32[]{:S(2)}) %collective-permute-start.4) | collective-permute-done | bytes 264224 | tf_op jit(solution)/shard_map/ppermute | solution.py:25
  59.2 0.7 fusion.50
  60.0 1.0 multiply_add_fusion.1
  61.0 6.4 %collective-permute-start.5 = (f32[4,129,128]{2,1,0:T(8,128)S(1)}, f32[4,129,128]{2,1,0:T(8,128)S(1)}, u32[]{:S(2)}, u32[]{:S(2)}) collective-permute-start(f32[4,129,128]{2,1,0:T(8,128)S(1)} %pad_maximum_fusion.6), channel_id=1, source_target_pairs={{0,64},{8,72},{16,80},{24,88},{32,96},{40,104},{48,112},{56,120},{... | collective-permute-start | bytes 792584 | tf_op jit(solution)/shard_map/ppermute | solution.py:25
  67.4 1.7 convolution_multiply_fusion
  69.1 2.3 collective-permute-done.5
  71.4 0.8 add_exponential_fusion
  72.3 0.7 pad_maximum_fusion.7
  73.1 6.7 %collective-permute-start.6 = (f32[4,129,128]{2,1,0:T(8,128)}, f32[4,129,128]{2,1,0:T(8,128)}, u32[]{:S(2)}, u32[]{:S(2)}) collective-permute-start(f32[4,129,128]{2,1,0:T(8,128)} %pad_maximum_fusion.7), channel_id=1, source_target_pairs={{0,128},{8,136},{16,144},{24,152},{32,160},{40,168},{48,176},{56,1... | collective-permute-start | bytes 792584 | tf_op jit(solution)/shard_map/ppermute | solution.py:25
  79.8 2.7 %pad_maximum_fusion.2 = bf16[256,4096]{1,0:T(8,128)(2,1)} fusion(bf16[128,4096]{1,0:T(8,128)(2,1)} %collective-permute-done.1, bf16[128,4096]{1,0:T(8,128)(2,1)S(1)} %bitcast.131), kind=kLoop, calls=%fused_computation.10 | loop fusion | flops 4194304 | bytes 4194304 | tf_op jit(solution)/shard_map/concatenate | solution.py:79
  82.5 0.7 fusion.49
  83.4 1.5 fusion.7
  84.9 1.2 fusion.20
  86.3 1.0 gather_fusion
  87.3 14.2 %collective-permute-done = bf16[2,4096,128]{2,1,0:T(8,128)(2,1)} collective-permute-done((bf16[2,4096,128]{2,1,0:T(8,128)(2,1)S(1)}, bf16[2,4096,128]{2,1,0:T(8,128)(2,1)}, u32[]{:S(2)}, u32[]{:S(2)}) %collective-permute-start) | collective-permute-done | bytes 2097184 | tf_op jit(solution)/shard_map/ppermute | solution.py:78
  101.5 4.0 %pad_maximum_fusion = bf16[2,4096,256]{2,1,0:T(8,128)(2,1)} fusion(bf16[2,4096,128]{2,1,0:T(8,128)(2,1)} %collective-permute-done, bf16[2,4096,128]{2,1,0:T(8,128)(2,1)S(1)} %pad_maximum_fusion.1), kind=kLoop, calls=%fused_computation.8 | loop fusion | flops 8388608 | bytes 8388608 | tf_op jit(solution)/shard_map/concatenate | solution.py:78
  105.6 0.7 all-gather.7.cloned.1.call-update
  106.3 13.2 %all_to_all.20 = bf16[8,24,512]{2,1,0:T(8,128)(2,1)S(1)} all-to-all(bf16[8,24,512]{2,1,0:T(8,128)(2,1)S(1)} %bitcast.132), channel_id=1, replica_groups=mesh['y'=4,'x'=4,'c'=2,'e'=4,'p'=2] {'e','p'}, dimensions={0} | all-to-all | bytes 393216 | tf_op jit(solution)/shard_map/all_to_all | solution.py:133
  119.9 40.9 %all_to_all.21 = bf16[16,24,4096]{2,1,0:T(8,128)(2,1)S(1)} all-to-all(bf16[16,24,4096]{2,1,0:T(8,128)(2,1)S(1)} %broadcast_in_dim.58), channel_id=1, replica_groups=mesh['y'=4,'x'=4,'c'=2,'e'=4,'p'=2] {'y','x'}, dimensions={0} | all-to-all | bytes 6291456 | tf_op jit(solution)/shard_map/all_to_all | solution.py:139
  160.8 4.9 %fusion.1 = f32[384,512]{1,0:T(8,128)} fusion(bf16[384,4096]{1,0:T(8,128)(2,1)S(1)} %bitcast.127, bf16[2,4096,512]{2,1,0:T(8,128)(2,1)} %all-gather.5.cloned.1.call-done), kind=kOutput, calls=%fused_computation.7 | convolution fusion | flops 1610612736 | bytes 8126464 | tf_op jit(solution)/shard_map/dot_general | solution.py:146
  165.7 8.9 %convolution_convert_fusion = bf16[384,4096]{1,0:T(8,128)(2,1)} fusion(bf16[512,4096]{1,0:T(8,128)(2,1)} %all-gather.7.cloned.1.call-done, bf16[384,4096]{1,0:T(8,128)(2,1)S(1)} %bitcast.128, bf16[2,4096,512]{2,1,0:T(8,128)(2,1)} %all-gather.5.cloned.1.call-done, f32[384,512]{1,0:T(8,128)} %fusion.1), kind=kOutput, calls=%fused_computation.3 | convolution fusion | flops 3223977984 | bytes 15466496 | tf_op jit(solution)/shard_map/dot_general | solution.py:149
  174.6 38.1 %all_to_all.22 = bf16[16,24,4096]{2,1,0:T(8,128)(2,1)S(1)} all-to-all(bf16[16,24,4096]{2,1,0:T(8,128)(2,1)} %bitcast.129), channel_id=1, replica_groups=mesh['y'=4,'x'=4,'c'=2,'e'=4,'p'=2] {'y','x'}, dimensions={0} | all-to-all | bytes 6291456 | tf_op jit(solution)/shard_map/all_to_all | solution.py:150
  212.7 0.6 reduce_sum.41
  213.3 0.8 reshape.284
  214.1 3.4 %all-to-all-start.3 = ((bf16[8,3,4096]{2,1,0:T(4,128)(2,1)}), bf16[8,3,4096]{2,1,0:T(4,128)(2,1)S(1)}, u32[]{:S(2)}, u32[]{:S(2)}) async-start(bf16[8,3,4096]{2,1,0:T(4,128)(2,1)} %reshape.284), calls=%async_computation.3 | async-start | bytes 524288 | tf_op jit(solution)/shard_map/all_to_all | solution.py:154
  217.8 10.1 %all-to-all-done.3 = bf16[8,3,4096]{2,1,0:T(4,128)(2,1)S(1)} async-done(((bf16[8,3,4096]{2,1,0:T(4,128)(2,1)}), bf16[8,3,4096]{2,1,0:T(4,128)(2,1)S(1)}, u32[]{:S(2)}, u32[]{:S(2)}) %all-to-all-start.3) | async-done | bytes 196640 | tf_op jit(solution)/shard_map/all_to_all | solution.py:154
  228.1 0.6 gather_fusion.1
  228.9 1.0 multiply_reduce_fusion
  (58 shorter events, 3.5 us)
Async XLA Ops:
  6.5 1.8 copy-start
  6.5 26.9 %copy-start.1 = (bf16[1,128,4096]{2,1,0:T(8,128)(2,1)S(1)}, bf16[1,128,4096]{2,1,0:T(8,128)(2,1)}, u32[]{:S(2)}) copy-start(bf16[1,128,4096]{2,1,0:T(8,128)(2,1)} %param.17) | copy-start | bytes 3145732
  6.5 154.3 %all-gather.5.cloned.1.call-start = ((), (), s32[]{:S(2)}) async-start(), calls=%async_computation.4 | async-start | bytes 12582912 | tf_op jit(solution)/shard_map/all_gather | solution.py:131
  10.4 28.7 %collective-permute-start.2 = (f32[4,129,128]{2,1,0:T(8,128)}, f32[4,129,128]{2,1,0:T(8,128)}, u32[]{:S(2)}, u32[]{:S(2)}) collective-permute-start(f32[4,129,128]{2,1,0:T(8,128)} %pad_maximum_fusion.3), channel_id=1, source_target_pairs={{0,8},{8,16},{16,24},{24,32},{32,40},{40,48},{48,56},{56,64},{64,7... | collective-permute-start | bytes 792584 | tf_op jit(solution)/shard_map/ppermute | solution.py:25
  33.5 46.3 %collective-permute-start.1 = (bf16[128,4096]{1,0:T(8,128)(2,1)S(1)}, bf16[128,4096]{1,0:T(8,128)(2,1)}, u32[]{:S(2)}, u32[]{:S(2)}) collective-permute-start(bf16[128,4096]{1,0:T(8,128)(2,1)S(1)} %bitcast.130), channel_id=1, source_target_pairs={{0,1},{1,0},{2,3},{3,2},{4,5},{5,4},{6,7},{7,6},{8,9},{9,8},{10,11... | collective-permute-start | bytes 3145736 | tf_op jit(solution)/shard_map/ppermute | solution.py:79
  33.6 67.9 %collective-permute-start = (bf16[2,4096,128]{2,1,0:T(8,128)(2,1)S(1)}, bf16[2,4096,128]{2,1,0:T(8,128)(2,1)}, u32[]{:S(2)}, u32[]{:S(2)}) collective-permute-start(bf16[2,4096,128]{2,1,0:T(8,128)(2,1)S(1)} %pad_maximum_fusion.1), channel_id=1, source_target_pairs={{0,1},{1,0},{2,3},{3,2},{4,5},{5,4},{6,7},{7,6},{8,9},{9,8},{10,11... | collective-permute-start | bytes 6291464 | tf_op jit(solution)/shard_map/ppermute | solution.py:78
  41.0 8.4 %collective-permute-start.3 = (f32[4,129,128]{2,1,0:T(8,128)S(1)}, f32[4,129,128]{2,1,0:T(8,128)S(1)}, u32[]{:S(2)}, u32[]{:S(2)}) collective-permute-start(f32[4,129,128]{2,1,0:T(8,128)S(1)} %pad_maximum_fusion.4), channel_id=1, source_target_pairs={{0,16},{8,24},{16,32},{24,40},{32,48},{40,56},{48,64},{56,72},{64,... | collective-permute-start | bytes 792584 | tf_op jit(solution)/shard_map/ppermute | solution.py:25
  49.4 0.7 copy-start.2
  50.8 8.4 %collective-permute-start.4 = (f32[4,129,128]{2,1,0:T(8,128)}, f32[4,129,128]{2,1,0:T(8,128)}, u32[]{:S(2)}, u32[]{:S(2)}) collective-permute-start(f32[4,129,128]{2,1,0:T(8,128)} %pad_maximum_fusion.5), channel_id=1, source_target_pairs={{0,32},{8,40},{16,48},{24,56},{32,64},{40,72},{48,80},{56,88},{64,... | collective-permute-start | bytes 792584 | tf_op jit(solution)/shard_map/ppermute | solution.py:25
  60.9 22.5 %copy-start.3 = (f32[4,129,128]{2,1,0:T(8,128)S(1)}, f32[4,129,128]{2,1,0:T(8,128)}, u32[]{:S(2)}) copy-start(f32[4,129,128]{2,1,0:T(8,128)} %copy-done.2) | copy-start | bytes 792580
  60.9 25.2 %copy-start.5 = (f32[512]{0:T(512)S(1)}, f32[512]{0:T(512)}, u32[]{:S(2)}) copy-start(f32[512]{0:T(512)} %param.14) | copy-start | bytes 6148
  61.0 10.4 %collective-permute-start.5 = (f32[4,129,128]{2,1,0:T(8,128)S(1)}, f32[4,129,128]{2,1,0:T(8,128)S(1)}, u32[]{:S(2)}, u32[]{:S(2)}) collective-permute-start(f32[4,129,128]{2,1,0:T(8,128)S(1)} %pad_maximum_fusion.6), channel_id=1, source_target_pairs={{0,64},{8,72},{16,80},{24,88},{32,96},{40,104},{48,112},{56,120},{... | collective-permute-start | bytes 792584 | tf_op jit(solution)/shard_map/ppermute | solution.py:25
  71.4 1.6 copy-start.4
  73.1 10.4 %collective-permute-start.6 = (f32[4,129,128]{2,1,0:T(8,128)}, f32[4,129,128]{2,1,0:T(8,128)}, u32[]{:S(2)}, u32[]{:S(2)}) collective-permute-start(f32[4,129,128]{2,1,0:T(8,128)} %pad_maximum_fusion.7), channel_id=1, source_target_pairs={{0,128},{8,136},{16,144},{24,152},{32,160},{40,168},{48,176},{56,1... | collective-permute-start | bytes 792584 | tf_op jit(solution)/shard_map/ppermute | solution.py:25
  105.5 60.1 %all-gather.7.cloned.1.call-start = ((), (), s32[]{:S(2)}) async-start(), calls=%async_computation.5 | async-start | bytes 6291456 | tf_op jit(solution)/shard_map/all_gather | solution.py:132
  174.6 42.9 %copy-start.6 = (f32[8,2]{0,1:T(2,128)S(1)}, f32[8,2]{0,1:T(2,128)}, u32[]{:S(2)}) copy-start(f32[8,2]{0,1:T(2,128)} %param.19) | copy-start | bytes 196
  214.1 13.8 %all-to-all-start.3 = ((bf16[8,3,4096]{2,1,0:T(4,128)(2,1)}), bf16[8,3,4096]{2,1,0:T(4,128)(2,1)S(1)}, u32[]{:S(2)}, u32[]{:S(2)}) async-start(bf16[8,3,4096]{2,1,0:T(4,128)(2,1)} %reshape.284), calls=%async_computation.3 | async-start | bytes 524288 | tf_op jit(solution)/shard_map/all_to_all | solution.py:154
Sparse Core Ops, SparseCore 0:
  105.7 21.4 all-gather.4
  129.0 20.2 all-gather.6

commit v11 on v10

--- a/solution.py
+++ b/solution.py
@@ -74,9 +74,9 @@
     ids_all = lax.all_gather(expert_ids, DEV_AXES, axis=0, tiled=False)
     partner = [(0, 1), (1, 0)]
     gate_up = jnp.stack([gate_weight[0], up_weight[0]])
-    gate_up, down_own, ids_all = lax.optimization_barrier((gate_up, down_weight[0], ids_all))
+    gate_up, ids_all = lax.optimization_barrier((gate_up, ids_all))
+    down_core = lax.all_gather(down_weight[0], "c", axis=0, tiled=True)
     gate_up = jnp.concatenate([gate_up, lax.ppermute(gate_up, "p", partner)], axis=2)
-    down_all = jnp.concatenate([down_own, lax.ppermute(down_own, "p", partner)], axis=0)
 
     tok_count = expert_ids.shape[0]
     top_count = expert_ids.shape[1]
@@ -127,10 +127,11 @@
     )
     padded = jnp.concatenate([normed, jnp.zeros((1, normed.shape[1]), normed.dtype)], axis=0)
     send_rows = padded[slot_token].reshape(dev_count, per_dev, -1)
-    gate_up, down_all, send_rows = lax.optimization_barrier((gate_up, down_all, send_rows))
+    gate_up, send_rows = lax.optimization_barrier((gate_up, send_rows))
     gate_up = lax.all_gather(gate_up, "c", axis=2, tiled=True)
-    down_all = lax.all_gather(down_all, "c", axis=0, tiled=True)
     arrived = lax.all_to_all(send_rows, DEV_AXES, split_axis=0, concat_axis=0, tiled=True)
+    down_core, arrived = lax.optimization_barrier((down_core, arrived))
+    down_far = lax.ppermute(down_core, "p", partner)
     local_rows = jnp.transpose(arrived, (1, 0, 2)).reshape(per_dev, -1)
     width = local_rows.shape[1]
     groups = 1
@@ -143,6 +144,11 @@
         concat_axis=0,
         tiled=True,
     ).reshape(groups * per_dev, width)
+    down_far, piece = lax.optimization_barrier((down_far, piece))
+    cores = down_far.shape[0] // down_weight.shape[1]
+    down_all = jnp.stack(
+        [down_core.reshape(cores, -1, width), down_far.reshape(cores, -1, width)], axis=1
+    ).reshape(-1, width)
     gate_part = jnp.dot(piece, gate_up[0], preferred_element_type=jnp.float32)
     up_part = jnp.dot(piece, gate_up[1], preferred_element_type=jnp.float32)
     hidden_all = (jax.nn.silu(gate_part) * up_part).astype(jnp.bfloat16)

time: 238 us -> 230 us (0.966)
  blocking collectives: 112 us -> 56.4 us
  waiting for transfers between devices: 34.4 us -> 70.6 us
  starting transfers between devices: 28.7 us -> 39.2 us
  local copies, waits for them, and re-layouts: 7.57 us -> 10.5 us
    all_to_all x2 -> x0, blocking collectives: 54.1 us -> none  [the longest x1 40.9 us: per_device(): lax.all_to_all(jnp.broadcast_to(local_rows[None], (groups,) + local_rows....]
    ppermute x1, waiting for transfers between devices: 0.01 us -> 39.1 us  [per_device(): down_far = lax.ppermute(down_core, 'p', partner)]
    ppermute x1, waiting for transfers between devices: 14.2 us -> 0.01 us  [per_device(): lax.ppermute(gate_up, 'p', partner)]
    all_to_all x0 -> x2, starting transfers between devices: none -> 12.7 us  [the longest x1 8.13 us: per_device(): lax.all_to_all(jnp.broadcast_to(local_rows[None], (groups,) + local_rows....]
    all_to_all x0 -> x2, waiting for transfers between devices: none -> 9.76 us  [the longest x1 9.76 us: per_device(): lax.all_to_all(send_rows, DEV_AXES, split_axis=0, concat_axis=0, tiled=True)]
    another operation x0 -> x1, other arithmetic: none -> 4.54 us  [per_device(): jnp.stack([down_core.reshape(cores, -1, width), down_far.reshape(cores, -...]
    concatenate x1 -> x0, other arithmetic: 2.75 us -> none  [per_device(): jnp.concatenate([down_own, lax.ppermute(down_own, 'p', partner)], axis=0)]
  transfers between devices with their start and end apart: 10 -> 12, of which waited for: 6 -> 7; matrix products, arithmetic and copies ran while one was open for 12% -> 14% of each run, Pallas kernels for 0% -> 0%
where the time goes in v11:
time: 230 us; the launch traced here: 229 us
  waiting for transfers between devices  70.6 us (31%)
  blocking collectives  56.4 us (25%)
  starting transfers between devices  39.2 us (17%)
  other arithmetic  20.4 us (9%)
  matrix products  18.5 us (8%)
  between operations  13.7 us (6%)
  local copies, waits for them, and re-layouts  10.5 us (5%)
    ppermute x1, waiting for transfers between devices, per_device(): down_far = lax.ppermute(down_core, 'p', partner)  39.1 us
    all_to_all x1, blocking collectives, per_device(): lax.all_to_all(term.reshape(groups, per_dev, width), TOK_AXES, split_axis...  37 us
    ppermute x5, starting transfers between devices, shifted(): return lax.ppermute(value, SEQ_AXES, pairs)  22.2 us
    all_gather x1, blocking collectives, per_device(): ids_all = lax.all_gather(expert_ids, DEV_AXES, axis=0, tiled=False)  19.4 us
    ppermute x5, waiting for transfers between devices, shifted(): return lax.ppermute(value, SEQ_AXES, pairs)  11 us
    all_to_all x1, waiting for transfers between devices, per_device(): lax.all_to_all(summed.reshape(dev_count, half, width), DEV_AXES, split_ax...  10.1 us
    all_to_all x1, waiting for transfers between devices, per_device(): lax.all_to_all(send_rows, DEV_AXES, split_axis=0, concat_axis=0, tiled=True)  9.76 us
    dot_general x1, matrix products, per_device(): jnp.dot(hidden_all, down_all, preferred_element_type=jnp.float32)  9.02 us
  transfers between devices with their start and end apart: 12, of which 7 were waited for; matrix products, arithmetic and copies ran while one was open for 14% of the time, Pallas kernels for 0%

profile of v11, /device:TPU:2, one launch (start us, length us, event | category | flops | bytes accessed | tf_op | source)
XLA Modules:
  0.0 229.4 jit_solution(7108056729250585597)
XLA Ops:
  6.5 0.7 all-gather.8.cloned.1.call-update
  7.3 0.9 reduce_window_sum.22
  8.5 1.3 fusion.27
  9.9 1.9 collective-permute-start.1
  11.9 19.4 %all-gather.2 = s32[8,8,2]{1,2,0:T(2,128)S(1)} all-gather(s32[1,8,2]{1,2,0:T(2,128)} %bitcast.147), channel_id=3, replica_groups=mesh['y'=4,'x'=4,'c'=2,'e'=4,'p'=2] {'e','p'}, dimensions={0}, use_global_device_ids=true | all-gather | bytes 576 | tf_op jit(solution)/shard_map/all_gather | solution.py:74
  31.2 1.7 pad_maximum_fusion.2
  34.0 3.4 %collective-permute-start.2 = (f32[4,129,128]{2,1,0:T(8,128)S(1)}, f32[4,129,128]{2,1,0:T(8,128)S(1)}, u32[]{:S(2)}, u32[]{:S(2)}) collective-permute-start(f32[4,129,128]{2,1,0:T(8,128)S(1)} %pad_maximum_fusion.4), channel_id=1, source_target_pairs={{0,16},{8,24},{16,32},{24,40},{32,48},{40,56},{48,64},{56,72},{64,... | collective-permute-start | bytes 792584 | tf_op jit(solution)/shard_map/ppermute | solution.py:25
  37.4 5.0 %collective-permute-done.2 = f32[4,129,128]{2,1,0:T(8,128)S(1)} collective-permute-done((f32[4,129,128]{2,1,0:T(8,128)S(1)}, f32[4,129,128]{2,1,0:T(8,128)S(1)}, u32[]{:S(2)}, u32[]{:S(2)}) %collective-permute-start.2) | collective-permute-done | bytes 264224 | tf_op jit(solution)/shard_map/ppermute | solution.py:25
  42.4 0.6 fusion.49
  43.1 0.8 pad_maximum_fusion.5
  43.8 4.0 %collective-permute-start.3 = (f32[4,129,128]{2,1,0:T(8,128)}, f32[4,129,128]{2,1,0:T(8,128)S(1)}, u32[]{:S(2)}, u32[]{:S(2)}) collective-permute-start(f32[4,129,128]{2,1,0:T(8,128)} %pad_maximum_fusion.5), channel_id=1, source_target_pairs={{0,32},{8,40},{16,48},{24,56},{32,64},{40,72},{48,80},{56,88},{64,... | collective-permute-start | bytes 792584 | tf_op jit(solution)/shard_map/ppermute | solution.py:25
  47.9 0.6 add.227
  48.5 0.7 ne.75
  49.2 0.7 div.36
  49.9 0.6 rem.35
  50.6 0.7 mul.246
  51.3 0.8 convolution_multiply_fusion
  52.7 0.7 multiply_add_fusion.1
  53.5 0.7 pad_maximum_fusion.6
  54.2 6.9 %collective-permute-start.4 = (f32[4,129,128]{2,1,0:T(8,128)}, f32[4,129,128]{2,1,0:T(8,128)}, u32[]{:S(2)}, u32[]{:S(2)}) collective-permute-start(f32[4,129,128]{2,1,0:T(8,128)} %pad_maximum_fusion.6), channel_id=1, source_target_pairs={{0,64},{8,72},{16,80},{24,88},{32,96},{40,104},{48,112},{56,120},{... | collective-permute-start | bytes 792584 | tf_op jit(solution)/shard_map/ppermute | solution.py:25
  61.1 0.7 fusion.42
  61.8 1.0 scatter_custom_fusion
  62.8 1.9 collective-permute-done.4
  64.7 1.0 multiply_add_fusion
  65.7 0.7 add_exponential_fusion
  66.4 6.0 %collective-permute-start.5 = (f32[4,129,128]{2,1,0:T(8,128)S(1)}, f32[4,129,128]{2,1,0:T(8,128)S(1)}, u32[]{:S(2)}, u32[]{:S(2)}) collective-permute-start(f32[4,129,128]{2,1,0:T(8,128)S(1)} %pad_maximum_fusion.7), channel_id=1, source_target_pairs={{0,128},{8,136},{16,144},{24,152},{32,160},{40,168},{48,176},{56,1... | collective-permute-start | bytes 792584 | tf_op jit(solution)/shard_map/ppermute | solution.py:25
  72.5 4.0 %collective-permute-done.5 = f32[4,129,128]{2,1,0:T(8,128)S(1)} collective-permute-done((f32[4,129,128]{2,1,0:T(8,128)S(1)}, f32[4,129,128]{2,1,0:T(8,128)S(1)}, u32[]{:S(2)}, u32[]{:S(2)}) %collective-permute-start.5) | collective-permute-done | bytes 264224 | tf_op jit(solution)/shard_map/ppermute | solution.py:25
  76.5 1.3 fusion.5
  77.8 1.2 fusion.18
  79.0 0.8 copy_bitcast_fusion
  79.8 1.7 gather_fusion
  81.5 4.0 %pad_maximum_fusion = bf16[2,4096,256]{2,1,0:T(8,128)(2,1)} fusion(bf16[2,4096,128]{2,1,0:T(8,128)(2,1)} %collective-permute-done, bf16[2,4096,128]{2,1,0:T(8,128)(2,1)S(1)} %pad_maximum_fusion.2), kind=kLoop, calls=%fused_computation.8 | loop fusion | flops 8388608 | bytes 8388608 | tf_op jit(solution)/shard_map/concatenate | solution.py:79
  85.5 4.6 %all-to-all-start = ((bf16[8,24,512]{2,1,0:T(8,128)(2,1)}), bf16[8,24,512]{2,1,0:T(8,128)(2,1)S(1)}, u32[]{:S(2)}, u32[]{:S(2)}) async-start(bf16[8,24,512]{2,1,0:T(8,128)(2,1)} %bitcast.21), calls=%async_computation | async-start | bytes 393216 | tf_op jit(solution)/shard_map/all_to_all | solution.py:132
  90.1 9.8 %all-to-all-done = bf16[8,24,512]{2,1,0:T(8,128)(2,1)S(1)} async-done(((bf16[8,24,512]{2,1,0:T(8,128)(2,1)}), bf16[8,24,512]{2,1,0:T(8,128)(2,1)S(1)}, u32[]{:S(2)}, u32[]{:S(2)}) %all-to-all-start) | async-done | bytes 196640 | tf_op jit(solution)/shard_map/all_to_all | solution.py:132
  99.9 2.0 broadcast_in_dim.58
  101.9 8.1 %all-to-all-start.1 = ((bf16[16,24,4096]{2,1,0:T(8,128)(2,1)}), bf16[16,24,4096]{2,1,0:T(8,128)(2,1)S(1)}, u32[]{:S(2)}, u32[]{:S(2)}) async-start(bf16[16,24,4096]{2,1,0:T(8,128)(2,1)} %broadcast_in_dim.58), calls=%async_computation.1 | async-start | bytes 6291456 | tf_op jit(solution)/shard_map/all_to_all | solution.py:140
  110.1 0.7 collective-permute-start.6
  110.8 39.1 %collective-permute-done.6 = bf16[256,4096]{1,0:T(8,128)(2,1)} collective-permute-done((bf16[256,4096]{1,0:T(8,128)(2,1)}, bf16[256,4096]{1,0:T(8,128)(2,1)}, u32[]{:S(2)}, u32[]{:S(2)}) %collective-permute-start.6) | collective-permute-done | bytes 2097184 | tf_op jit(solution)/shard_map/ppermute | solution.py:134
  149.8 4.5 %pad_maximum_fusion.1 = bf16[2,2,128,4096]{3,2,1,0:T(8,128)(2,1)} fusion(bf16[2,1,128,4096]{3,2,1,0:T(8,128)(2,1)} %bitcast.27, bf16[2,1,128,4096]{3,2,1,0:T(8,128)(2,1)} %bitcast.133), kind=kLoop, calls=%fused_computation.9 | loop fusion | flops 2097152 | bytes 8388608 | tf_op jit(solution)/shard_map/stack | solution.py:149
  154.4 4.8 %fusion = f32[384,512]{1,0:T(8,128)} fusion(bf16[384,4096]{1,0:T(8,128)(2,1)S(1)} %bitcast.129, bf16[2,4096,512]{2,1,0:T(8,128)(2,1)} %all-gather.6.cloned.1.call-done), kind=kOutput, calls=%fused_computation.5 | convolution fusion | flops 1610612736 | bytes 8126464 | tf_op jit(solution)/shard_map/dot_general | solution.py:153
  159.2 9.0 %convolution_convert_fusion = bf16[384,4096]{1,0:T(8,128)(2,1)} fusion(bf16[512,4096]{1,0:T(8,128)(2,1)} %bitcast.128, f32[384,512]{1,0:T(8,128)} %fusion, bf16[384,4096]{1,0:T(8,128)(2,1)S(1)} %bitcast.130, bf16[2,4096,512]{2,1,0:T(8,128)(2,1)} %all-gather.6.cloned.1.call-done), kind=kOutput, calls=%fused_computation.3 | convolution fusion | flops 3223977984 | bytes 15466496 | tf_op jit(solution)/shard_map/dot_general | solution.py:155
  168.3 37.0 %all_to_all.20 = bf16[16,24,4096]{2,1,0:T(8,128)(2,1)S(1)} all-to-all(bf16[16,24,4096]{2,1,0:T(8,128)(2,1)} %bitcast.131), channel_id=1, replica_groups=mesh['y'=4,'x'=4,'c'=2,'e'=4,'p'=2] {'y','x'}, dimensions={0} | all-to-all | bytes 6291456 | tf_op jit(solution)/shard_map/all_to_all | solution.py:156
  205.3 0.6 reduce_sum.41
  205.9 0.8 reshape.288
  206.7 3.4 %all-to-all-start.3 = ((bf16[8,3,4096]{2,1,0:T(4,128)(2,1)}), bf16[8,3,4096]{2,1,0:T(4,128)(2,1)S(1)}, u32[]{:S(2)}, u32[]{:S(2)}) async-start(bf16[8,3,4096]{2,1,0:T(4,128)(2,1)} %reshape.288), calls=%async_computation.3 | async-start | bytes 524288 | tf_op jit(solution)/shard_map/all_to_all | solution.py:160
  210.4 10.1 %all-to-all-done.3 = bf16[8,3,4096]{2,1,0:T(4,128)(2,1)S(1)} async-done(((bf16[8,3,4096]{2,1,0:T(4,128)(2,1)}), bf16[8,3,4096]{2,1,0:T(4,128)(2,1)S(1)}, u32[]{:S(2)}, u32[]{:S(2)}) %all-to-all-start.3) | async-done | bytes 196640 | tf_op jit(solution)/shard_map/all_to_all | solution.py:160
  220.7 0.6 gather_fusion.1
  221.5 1.0 multiply_reduce_fusion
  (54 shorter events, 3.1 us)
Async XLA Ops:
  6.5 2.0 copy-start
  6.5 83.6 %all-gather.8.cloned.1.call-start = ((), (), s32[]{:S(2)}) async-start(), calls=%async_computation.5 | async-start | bytes 3145728 | tf_op jit(solution)/shard_map/all_gather | solution.py:78
  7.3 44.0 %copy-start.1 = (bf16[64,512]{1,0:T(8,128)(2,1)S(1)}, bf16[64,512]{1,0:T(8,128)(2,1)}, u32[]{:S(2)}) copy-start(bf16[64,512]{1,0:T(8,128)(2,1)} %param.10) | copy-start | bytes 196612
  7.3 44.0 %copy-start.2 = (bf16[64,512]{1,0:T(8,128)(2,1)S(1)}, bf16[64,512]{1,0:T(8,128)(2,1)}, u32[]{:S(2)}) copy-start(bf16[64,512]{1,0:T(8,128)(2,1)} %param.11) | copy-start | bytes 196612
  7.3 147.1 %all-gather.6.cloned.1.call-start = ((), (), s32[]{:S(2)}) async-start(), calls=%async_computation.4 | async-start | bytes 12582912 | tf_op jit(solution)/shard_map/all_gather | solution.py:131
  9.9 23.9 %collective-permute-start.1 = (f32[4,129,128]{2,1,0:T(8,128)S(1)}, f32[4,129,128]{2,1,0:T(8,128)S(1)}, u32[]{:S(2)}, u32[]{:S(2)}) collective-permute-start(f32[4,129,128]{2,1,0:T(8,128)S(1)} %pad_maximum_fusion.3), channel_id=1, source_target_pairs={{0,8},{8,16},{16,24},{24,32},{32,40},{40,48},{48,56},{56,64},{64,7... | collective-permute-start | bytes 792584 | tf_op jit(solution)/shard_map/ppermute | solution.py:25
  33.0 48.5 %collective-permute-start = (bf16[2,4096,128]{2,1,0:T(8,128)(2,1)S(1)}, bf16[2,4096,128]{2,1,0:T(8,128)(2,1)}, u32[]{:S(2)}, u32[]{:S(2)}) collective-permute-start(bf16[2,4096,128]{2,1,0:T(8,128)(2,1)S(1)} %pad_maximum_fusion.2), channel_id=1, source_target_pairs={{0,1},{1,0},{2,3},{3,2},{4,5},{5,4},{6,7},{7,6},{8,9},{9,8},{10,11... | collective-permute-start | bytes 6291464 | tf_op jit(solution)/shard_map/ppermute | solution.py:79
  34.0 8.4 %collective-permute-start.2 = (f32[4,129,128]{2,1,0:T(8,128)S(1)}, f32[4,129,128]{2,1,0:T(8,128)S(1)}, u32[]{:S(2)}, u32[]{:S(2)}) collective-permute-start(f32[4,129,128]{2,1,0:T(8,128)S(1)} %pad_maximum_fusion.4), channel_id=1, source_target_pairs={{0,16},{8,24},{16,32},{24,40},{32,48},{40,56},{48,64},{56,72},{64,... | collective-permute-start | bytes 792584 | tf_op jit(solution)/shard_map/ppermute | solution.py:25
  43.8 8.4 %collective-permute-start.3 = (f32[4,129,128]{2,1,0:T(8,128)}, f32[4,129,128]{2,1,0:T(8,128)S(1)}, u32[]{:S(2)}, u32[]{:S(2)}) collective-permute-start(f32[4,129,128]{2,1,0:T(8,128)} %pad_maximum_fusion.5), channel_id=1, source_target_pairs={{0,32},{8,40},{16,48},{24,56},{32,64},{40,72},{48,80},{56,88},{64,... | collective-permute-start | bytes 792584 | tf_op jit(solution)/shard_map/ppermute | solution.py:25
  54.2 10.5 %collective-permute-start.4 = (f32[4,129,128]{2,1,0:T(8,128)}, f32[4,129,128]{2,1,0:T(8,128)}, u32[]{:S(2)}, u32[]{:S(2)}) collective-permute-start(f32[4,129,128]{2,1,0:T(8,128)} %pad_maximum_fusion.6), channel_id=1, source_target_pairs={{0,64},{8,72},{16,80},{24,88},{32,96},{40,104},{48,112},{56,120},{... | collective-permute-start | bytes 792584 | tf_op jit(solution)/shard_map/ppermute | solution.py:25
  66.4 10.1 %collective-permute-start.5 = (f32[4,129,128]{2,1,0:T(8,128)S(1)}, f32[4,129,128]{2,1,0:T(8,128)S(1)}, u32[]{:S(2)}, u32[]{:S(2)}) collective-permute-start(f32[4,129,128]{2,1,0:T(8,128)S(1)} %pad_maximum_fusion.7), channel_id=1, source_target_pairs={{0,128},{8,136},{16,144},{24,152},{32,160},{40,168},{48,176},{56,1... | collective-permute-start | bytes 792584 | tf_op jit(solution)/shard_map/ppermute | solution.py:25
  85.5 14.4 %all-to-all-start = ((bf16[8,24,512]{2,1,0:T(8,128)(2,1)}), bf16[8,24,512]{2,1,0:T(8,128)(2,1)S(1)}, u32[]{:S(2)}, u32[]{:S(2)}) async-start(bf16[8,24,512]{2,1,0:T(8,128)(2,1)} %bitcast.21), calls=%async_computation | async-start | bytes 393216 | tf_op jit(solution)/shard_map/all_to_all | solution.py:132
  101.9 47.9 %all-to-all-start.1 = ((bf16[16,24,4096]{2,1,0:T(8,128)(2,1)}), bf16[16,24,4096]{2,1,0:T(8,128)(2,1)S(1)}, u32[]{:S(2)}, u32[]{:S(2)}) async-start(bf16[16,24,4096]{2,1,0:T(8,128)(2,1)} %broadcast_in_dim.58), calls=%async_computation.1 | async-start | bytes 6291456 | tf_op jit(solution)/shard_map/all_to_all | solution.py:140
  110.1 39.8 %collective-permute-start.6 = (bf16[256,4096]{1,0:T(8,128)(2,1)}, bf16[256,4096]{1,0:T(8,128)(2,1)}, u32[]{:S(2)}, u32[]{:S(2)}) collective-permute-start(bf16[256,4096]{1,0:T(8,128)(2,1)} %bitcast.132), channel_id=1, source_target_pairs={{0,1},{1,0},{2,3},{3,2},{4,5},{5,4},{6,7},{7,6},{8,9},{9,8},{10,11... | collective-permute-start | bytes 6291464 | tf_op jit(solution)/shard_map/ppermute | solution.py:134
  168.3 41.9 %copy-start.3 = (f32[8,2]{0,1:T(2,128)S(1)}, f32[8,2]{0,1:T(2,128)}, u32[]{:S(2)}) copy-start(f32[8,2]{0,1:T(2,128)} %param.19) | copy-start | bytes 196
  206.7 13.8 %all-to-all-start.3 = ((bf16[8,3,4096]{2,1,0:T(4,128)(2,1)}), bf16[8,3,4096]{2,1,0:T(4,128)(2,1)S(1)}, u32[]{:S(2)}, u32[]{:S(2)}) async-start(bf16[8,3,4096]{2,1,0:T(4,128)(2,1)} %reshape.288), calls=%async_computation.3 | async-start | bytes 524288 | tf_op jit(solution)/shard_map/all_to_all | solution.py:160
Sparse Core Ops, SparseCore 0:
  9.2 18.8 all-gather.7
  85.6 23.2 all-gather.5

commit v12 on v11

--- a/solution.py
+++ b/solution.py
@@ -75,8 +75,9 @@
     partner = [(0, 1), (1, 0)]
     gate_up = jnp.stack([gate_weight[0], up_weight[0]])
     gate_up, ids_all = lax.optimization_barrier((gate_up, ids_all))
+    gate_up_core = lax.all_gather(gate_up, "c", axis=2, tiled=True)
     down_core = lax.all_gather(down_weight[0], "c", axis=0, tiled=True)
-    gate_up = jnp.concatenate([gate_up, lax.ppermute(gate_up, "p", partner)], axis=2)
+    gate_up_far = lax.ppermute(gate_up, "p", partner)
 
     tok_count = expert_ids.shape[0]
     top_count = expert_ids.shape[1]
@@ -127,8 +128,8 @@
     )
     padded = jnp.concatenate([normed, jnp.zeros((1, normed.shape[1]), normed.dtype)], axis=0)
     send_rows = padded[slot_token].reshape(dev_count, per_dev, -1)
-    gate_up, send_rows = lax.optimization_barrier((gate_up, send_rows))
-    gate_up = lax.all_gather(gate_up, "c", axis=2, tiled=True)
+    gate_up_far, send_rows = lax.optimization_barrier((gate_up_far, send_rows))
+    gate_up_far = lax.all_gather(gate_up_far, "c", axis=2, tiled=True)
     arrived = lax.all_to_all(send_rows, DEV_AXES, split_axis=0, concat_axis=0, tiled=True)
     down_core, arrived = lax.optimization_barrier((down_core, arrived))
     down_far = lax.ppermute(down_core, "p", partner)
@@ -145,14 +146,16 @@
         tiled=True,
     ).reshape(groups * per_dev, width)
     down_far, piece = lax.optimization_barrier((down_far, piece))
-    cores = down_far.shape[0] // down_weight.shape[1]
-    down_all = jnp.stack(
-        [down_core.reshape(cores, -1, width), down_far.reshape(cores, -1, width)], axis=1
-    ).reshape(-1, width)
-    gate_part = jnp.dot(piece, gate_up[0], preferred_element_type=jnp.float32)
-    up_part = jnp.dot(piece, gate_up[1], preferred_element_type=jnp.float32)
-    hidden_all = (jax.nn.silu(gate_part) * up_part).astype(jnp.bfloat16)
-    term = jnp.dot(hidden_all, down_all, preferred_element_type=jnp.float32).astype(jnp.bfloat16)
+
+    def hidden_of(weights):
+        gate_part = jnp.dot(piece, weights[0], preferred_element_type=jnp.float32)
+        up_part = jnp.dot(piece, weights[1], preferred_element_type=jnp.float32)
+        return (jax.nn.silu(gate_part) * up_part).astype(jnp.bfloat16)
+
+    term = (
+        jnp.dot(hidden_of(gate_up_core), down_core, preferred_element_type=jnp.float32)
+        + jnp.dot(hidden_of(gate_up_far), down_far, preferred_element_type=jnp.float32)
+    ).astype(jnp.bfloat16)
     parts = lax.all_to_all(
         term.reshape(groups, per_dev, width), TOK_AXES, split_axis=0, concat_axis=0, tiled=True
     )

time: 230 us -> 233 us (1.013)
  other arithmetic: 20.4 us -> 8.76 us
  matrix products: 18.5 us -> 27.6 us
  waiting for transfers between devices: 70.6 us -> 78.6 us
    dot_general x2 -> x4, matrix products: 13.9 us -> 24.5 us  [the longest x1 9.36 us: per_device(): jnp.dot(hidden_of(gate_up_far), down_far, preferred_element_type=jnp.floa...]
    ppermute x5, waiting for transfers between devices: 11 us -> 19.7 us  [shifted(): return lax.ppermute(value, SEQ_AXES, pairs)]
    another operation x1 -> x0, other arithmetic: 4.54 us -> none  [per_device(): jnp.stack([down_core.reshape(cores, -1, width), down_far.reshape(cores, -...]
    concatenate x1 -> x0, other arithmetic: 3.99 us -> none  [per_device(): jnp.concatenate([gate_up, lax.ppermute(gate_up, 'p', partner)], axis=2)]
  transfers between devices with their start and end apart: 12 -> 13, of which waited for: 7 -> 8; matrix products, arithmetic and copies ran while one was open for 14% -> 12% of each run, Pallas kernels for 0% -> 0%
where the time goes in v12:
time: 233 us; the launch traced here: 232 us
  waiting for transfers between devices  78.6 us (34%)
  blocking collectives  56 us (24%)
  starting transfers between devices  39.8 us (17%)
  matrix products  27.6 us (12%)
  between operations  13.5 us (6%)
  other arithmetic  8.76 us (4%)
  local copies, waits for them, and re-layouts  8.28 us (4%)
    ppermute x1, waiting for transfers between devices, per_device(): down_far = lax.ppermute(down_core, 'p', partner)  38.3 us
    all_to_all x1, blocking collectives, per_device(): lax.all_to_all(term.reshape(groups, per_dev, width), TOK_AXES, split_axis...  36.6 us
    ppermute x5, starting transfers between devices, shifted(): return lax.ppermute(value, SEQ_AXES, pairs)  21.9 us
    ppermute x5, waiting for transfers between devices, shifted(): return lax.ppermute(value, SEQ_AXES, pairs)  19.7 us
    all_gather x1, blocking collectives, per_device(): ids_all = lax.all_gather(expert_ids, DEV_AXES, axis=0, tiled=False)  19.4 us
    all_to_all x1, waiting for transfers between devices, per_device(): lax.all_to_all(summed.reshape(dev_count, half, width), DEV_AXES, split_ax...  10.1 us
    dot_general x1, matrix products, per_device(): jnp.dot(hidden_of(gate_up_far), down_far, preferred_element_type=jnp.floa...  9.36 us
    all_to_all x1, waiting for transfers between devices, per_device(): lax.all_to_all(send_rows, DEV_AXES, split_axis=0, concat_axis=0, tiled=True)  9.02 us
  transfers between devices with their start and end apart: 13, of which 8 were waited for; matrix products, arithmetic and copies ran while one was open for 12% of the time, Pallas kernels for 0%

profile of v12, /device:TPU:2, one launch (start us, length us, event | category | flops | bytes accessed | tf_op | source)
XLA Modules:
  0.0 232.5 jit_solution(4424800189352260367)
XLA Ops:
  6.5 0.7 all-gather.11.cloned.1.call-update
  7.3 19.4 %all-gather.2 = s32[8,8,2]{1,2,0:T(2,128)S(1)} all-gather(s32[1,8,2]{1,2,0:T(2,128)} %bitcast.157), channel_id=3, replica_groups=mesh['y'=4,'x'=4,'c'=2,'e'=4,'p'=2] {'e','p'}, dimensions={0}, use_global_device_ids=true | all-gather | bytes 576 | tf_op jit(solution)/shard_map/all_gather | solution.py:74
  26.7 1.7 pad_maximum_fusion
  28.6 0.2 reduce_window_sum.22
  28.8 0.2 exponential_reduce_fusion
  29.1 0.5 fusion.31
  29.7 1.9 collective-permute-start.1
  31.7 0.4 fusion.56
  32.3 5.3 %collective-permute-done.1 = f32[4,129,128]{2,1,0:T(8,128)S(1)} collective-permute-done((f32[4,129,128]{2,1,0:T(8,128)S(1)}, f32[4,129,128]{2,1,0:T(8,128)S(1)}, u32[]{:S(2)}, u32[]{:S(2)}) %collective-permute-start.1) | collective-permute-done | bytes 264224 | tf_op jit(solution)/shard_map/ppermute | solution.py:25
  37.7 3.4 %collective-permute-start.2 = (f32[4,129,128]{2,1,0:T(8,128)S(1)}, f32[4,129,128]{2,1,0:T(8,128)S(1)}, u32[]{:S(2)}, u32[]{:S(2)}) collective-permute-start(f32[4,129,128]{2,1,0:T(8,128)S(1)} %pad_maximum_fusion.2), channel_id=1, source_target_pairs={{0,16},{8,24},{16,32},{24,40},{32,48},{40,56},{48,64},{56,72},{64,... | collective-permute-start | bytes 792584 | tf_op jit(solution)/shard_map/ppermute | solution.py:25
  41.2 6.1 %collective-permute-done.2 = f32[4,129,128]{2,1,0:T(8,128)S(1)} collective-permute-done((f32[4,129,128]{2,1,0:T(8,128)S(1)}, f32[4,129,128]{2,1,0:T(8,128)S(1)}, u32[]{:S(2)}, u32[]{:S(2)}) %collective-permute-start.2) | collective-permute-done | bytes 264224 | tf_op jit(solution)/shard_map/ppermute | solution.py:25
  47.4 0.7 pad_maximum_fusion.3
  48.1 4.0 %collective-permute-start.3 = (f32[4,129,128]{2,1,0:T(8,128)}, f32[4,129,128]{2,1,0:T(8,128)S(1)}, u32[]{:S(2)}, u32[]{:S(2)}) collective-permute-start(f32[4,129,128]{2,1,0:T(8,128)} %pad_maximum_fusion.3), channel_id=1, source_target_pairs={{0,32},{8,40},{16,48},{24,56},{32,64},{40,72},{48,80},{56,88},{64,... | collective-permute-start | bytes 792584 | tf_op jit(solution)/shard_map/ppermute | solution.py:25
  52.3 0.6 add.233
  53.4 1.0 convolution_multiply_fusion
  54.4 2.5 %collective-permute-done.3 = f32[4,129,128]{2,1,0:T(8,128)S(1)} collective-permute-done((f32[4,129,128]{2,1,0:T(8,128)}, f32[4,129,128]{2,1,0:T(8,128)S(1)}, u32[]{:S(2)}, u32[]{:S(2)}) %collective-permute-start.3) | collective-permute-done | bytes 264224 | tf_op jit(solution)/shard_map/ppermute | solution.py:25
  56.9 0.7 pad_maximum_fusion.4
  57.6 6.5 %collective-permute-start.4 = (f32[4,129,128]{2,1,0:T(8,128)}, f32[4,129,128]{2,1,0:T(8,128)}, u32[]{:S(2)}, u32[]{:S(2)}) collective-permute-start(f32[4,129,128]{2,1,0:T(8,128)} %pad_maximum_fusion.4), channel_id=1, source_target_pairs={{0,64},{8,72},{16,80},{24,88},{32,96},{40,104},{48,112},{56,120},{... | collective-permute-start | bytes 792584 | tf_op jit(solution)/shard_map/ppermute | solution.py:25
  64.2 0.7 fusion.46
  64.9 1.0 scatter_custom_fusion
  65.9 1.9 collective-permute-done.4
  67.8 0.7 add_exponential_fusion
  68.6 1.0 multiply_add_fusion
  69.6 6.0 %collective-permute-start.5 = (f32[4,129,128]{2,1,0:T(8,128)S(1)}, f32[4,129,128]{2,1,0:T(8,128)S(1)}, u32[]{:S(2)}, u32[]{:S(2)}) collective-permute-start(f32[4,129,128]{2,1,0:T(8,128)S(1)} %pad_maximum_fusion.5), channel_id=1, source_target_pairs={{0,128},{8,136},{16,144},{24,152},{32,160},{40,168},{48,176},{56,1... | collective-permute-start | bytes 792584 | tf_op jit(solution)/shard_map/ppermute | solution.py:25
  75.7 4.0 %collective-permute-done.5 = f32[4,129,128]{2,1,0:T(8,128)S(1)} collective-permute-done((f32[4,129,128]{2,1,0:T(8,128)S(1)}, f32[4,129,128]{2,1,0:T(8,128)S(1)}, u32[]{:S(2)}, u32[]{:S(2)}) %collective-permute-start.5) | collective-permute-done | bytes 264224 | tf_op jit(solution)/shard_map/ppermute | solution.py:25
  79.7 1.4 fusion.6
  81.0 0.3 fusion.22
  81.5 1.7 gather_fusion
  83.2 4.8 %all-to-all-start = ((bf16[8,24,512]{2,1,0:T(8,128)(2,1)}), bf16[8,24,512]{2,1,0:T(8,128)(2,1)S(1)}, u32[]{:S(2)}, u32[]{:S(2)}) async-start(bf16[8,24,512]{2,1,0:T(8,128)(2,1)} %bitcast.21), calls=%async_computation | async-start | bytes 393216 | tf_op jit(solution)/shard_map/all_to_all | solution.py:133
  88.1 0.7 all-gather.9.cloned.1.call-update
  88.8 9.0 %all-to-all-done = bf16[8,24,512]{2,1,0:T(8,128)(2,1)S(1)} async-done(((bf16[8,24,512]{2,1,0:T(8,128)(2,1)}), bf16[8,24,512]{2,1,0:T(8,128)(2,1)S(1)}, u32[]{:S(2)}, u32[]{:S(2)}) %all-to-all-start) | async-done | bytes 196640 | tf_op jit(solution)/shard_map/all_to_all | solution.py:133
  97.8 2.0 broadcast_in_dim.58
  99.8 9.0 %all-to-all-start.1 = ((bf16[16,24,4096]{2,1,0:T(8,128)(2,1)}), bf16[16,24,4096]{2,1,0:T(8,128)(2,1)S(1)}, u32[]{:S(2)}, u32[]{:S(2)}) async-start(bf16[16,24,4096]{2,1,0:T(8,128)(2,1)} %broadcast_in_dim.58), calls=%async_computation.1 | async-start | bytes 6291456 | tf_op jit(solution)/shard_map/all_to_all | solution.py:141
  108.8 0.5 collective-permute-start.6
  109.3 38.3 %collective-permute-done.6 = bf16[256,4096]{1,0:T(8,128)(2,1)} collective-permute-done((bf16[256,4096]{1,0:T(8,128)(2,1)}, bf16[256,4096]{1,0:T(8,128)(2,1)}, u32[]{:S(2)}, u32[]{:S(2)}) %collective-permute-start.6) | collective-permute-done | bytes 2097184 | tf_op jit(solution)/shard_map/ppermute | solution.py:135
  147.6 3.3 %fusion.2 = f32[384,256]{1,0:T(8,128)} fusion(bf16[384,4096]{1,0:T(8,128)(2,1)S(1)} %bitcast.137, bf16[2,4096,256]{2,1,0:T(8,128)(2,1)} %all-gather.7.cloned.1.call-done), kind=kOutput, calls=%fused_computation.9 | convolution fusion | flops 805306368 | bytes 5636096 | tf_op jit(solution)/shard_map/dot_general | solution.py:152
  151.0 8.5 %fusion.18 = f32[384,4096]{1,0:T(8,128)} fusion(bf16[256,4096]{1,0:T(8,128)(2,1)} %bitcast.143, f32[384,256]{1,0:T(8,128)} %fusion.2, bf16[384,4096]{1,0:T(8,128)(2,1)S(1)} %bitcast.138, bf16[2,4096,256]{2,1,0:T(8,128)(2,1)} %all-gather.7.cloned.1.call-done), kind=kOutput, calls=%fused_computation.41 | convolution fusion | flops 1611202560 | bytes 14024704 | tf_op jit(solution)/shard_map/dot_general | solution.py:156
  159.4 3.3 %fusion = f32[384,256]{1,0:T(8,128)} fusion(bf16[384,4096]{1,0:T(8,128)(2,1)S(1)} %bitcast.139, bf16[2,4096,256]{2,1,0:T(8,128)(2,1)} %all-gather.9.cloned.1.call-done), kind=kOutput, calls=%fused_computation.5 | convolution fusion | flops 805306368 | bytes 5636096 | tf_op jit(solution)/shard_map/dot_general | solution.py:152
  162.7 9.4 %add_convert_fusion = bf16[384,4096]{1,0:T(8,128)(2,1)} fusion(f32[384,4096]{1,0:T(8,128)} %fusion.18, bf16[256,4096]{1,0:T(8,128)(2,1)} %collective-permute-done.6, f32[384,256]{1,0:T(8,128)} %fusion, bf16[384,4096]{1,0:T(8,128)(2,1)S(1)} %bitcast.140, bf16[2,4096,256]{2,1,0:T(8,128)(2,1)} %all-gather.9.cloned.1.call-done), kind=kOutput, calls=%fused_computation.3 | convolution fusion | flops 1614348288 | bytes 17170432 | tf_op jit(solution)/shard_map/dot_general | solution.py:157
  172.1 36.6 %all_to_all.20 = bf16[16,24,4096]{2,1,0:T(8,128)(2,1)S(1)} all-to-all(bf16[16,24,4096]{2,1,0:T(8,128)(2,1)} %bitcast.141), channel_id=1, replica_groups=mesh['y'=4,'x'=4,'c'=2,'e'=4,'p'=2] {'y','x'}, dimensions={0} | all-to-all | bytes 6291456 | tf_op jit(solution)/shard_map/all_to_all | solution.py:159
  208.7 0.6 reduce_sum.41
  209.3 0.8 reshape.284
  210.1 3.4 %all-to-all-start.3 = ((bf16[8,3,4096]{2,1,0:T(4,128)(2,1)}), bf16[8,3,4096]{2,1,0:T(4,128)(2,1)S(1)}, u32[]{:S(2)}, u32[]{:S(2)}) async-start(bf16[8,3,4096]{2,1,0:T(4,128)(2,1)} %reshape.284), calls=%async_computation.3 | async-start | bytes 524288 | tf_op jit(solution)/shard_map/all_to_all | solution.py:163
  213.6 0.2 add_reduce_fusion
  213.9 10.1 %all-to-all-done.3 = bf16[8,3,4096]{2,1,0:T(4,128)(2,1)S(1)} async-done(((bf16[8,3,4096]{2,1,0:T(4,128)(2,1)}), bf16[8,3,4096]{2,1,0:T(4,128)(2,1)S(1)}, u32[]{:S(2)}, u32[]{:S(2)}) %all-to-all-start.3) | async-done | bytes 196640 | tf_op jit(solution)/shard_map/all_to_all | solution.py:163
  224.1 0.6 gather_fusion.1
  224.7 0.2 reshape.286
  224.9 1.0 multiply_reduce_fusion
  (65 shorter events, 2.1 us)
Async XLA Ops:
  6.5 22.5 %copy-start = (bf16[64,512]{1,0:T(8,128)(2,1)S(1)}, bf16[64,512]{1,0:T(8,128)(2,1)}, u32[]{:S(2)}) copy-start(bf16[64,512]{1,0:T(8,128)(2,1)} %param.12) | copy-start | bytes 196612
  6.5 22.0 %copy-start.6 = (f32[64,4]{0,1:T(4,128)S(1)}, f32[64,4]{0,1:T(4,128)}, u32[]{:S(2)}) copy-start(f32[64,4]{0,1:T(4,128)} %param.13) | copy-start | bytes 3076
  6.5 22.5 %copy-start.4 = (bf16[64,512]{1,0:T(8,128)(2,1)S(1)}, bf16[64,512]{1,0:T(8,128)(2,1)}, u32[]{:S(2)}) copy-start(bf16[64,512]{1,0:T(8,128)(2,1)} %param.11) | copy-start | bytes 196612
  6.5 82.2 %all-gather.11.cloned.1.call-start = ((), (), s32[]{:S(2)}) async-start(), calls=%async_computation.6 | async-start | bytes 3145728 | tf_op jit(solution)/shard_map/all_gather | solution.py:79
  7.3 140.4 %all-gather.7.cloned.1.call-start = ((), (), s32[]{:S(2)}) async-start(), calls=%async_computation.4 | async-start | bytes 6291456 | tf_op jit(solution)/shard_map/all_gather | solution.py:78
  28.4 3.2 %copy-start.1 = (bf16[2,4096,128]{2,1,0:T(8,128)(2,1)}, bf16[2,4096,128]{2,1,0:T(8,128)(2,1)S(1)}, u32[]{:S(2)}) copy-start(bf16[2,4096,128]{2,1,0:T(8,128)(2,1)S(1)} %pad_maximum_fusion) | copy-start | bytes 6291460
  28.4 24.9 %copy-start.3 = (bf16[64,512]{1,0:T(8,128)(2,1)S(1)}, bf16[64,512]{1,0:T(8,128)(2,1)}, u32[]{:S(2)}) copy-start(bf16[64,512]{1,0:T(8,128)(2,1)} %param.10) | copy-start | bytes 196612
  28.5 54.7 %collective-permute-start = (bf16[2,4096,128]{2,1,0:T(8,128)(2,1)S(1)}, bf16[2,4096,128]{2,1,0:T(8,128)(2,1)}, u32[]{:S(2)}, u32[]{:S(2)}) collective-permute-start(bf16[2,4096,128]{2,1,0:T(8,128)(2,1)S(1)} %pad_maximum_fusion), channel_id=1, source_target_pairs={{0,1},{1,0},{2,3},{3,2},{4,5},{5,4},{6,7},{7,6},{8,9},{9,8},{10,11... | collective-permute-start | bytes 6291464 | tf_op jit(solution)/shard_map/ppermute | solution.py:80
  29.7 7.9 %collective-permute-start.1 = (f32[4,129,128]{2,1,0:T(8,128)S(1)}, f32[4,129,128]{2,1,0:T(8,128)S(1)}, u32[]{:S(2)}, u32[]{:S(2)}) collective-permute-start(f32[4,129,128]{2,1,0:T(8,128)S(1)} %pad_maximum_fusion.1), channel_id=1, source_target_pairs={{0,8},{8,16},{16,24},{24,32},{32,40},{40,48},{48,56},{56,64},{64,7... | collective-permute-start | bytes 792584 | tf_op jit(solution)/shard_map/ppermute | solution.py:25
  37.5 9.9 %copy-start.2 = (f32[4,129,128]{2,1,0:T(8,128)}, f32[4,129,128]{2,1,0:T(8,128)S(1)}, u32[]{:S(2)}) copy-start(f32[4,129,128]{2,1,0:T(8,128)S(1)} %collective-permute-done.1) | copy-start | bytes 792580
  37.7 9.6 %collective-permute-start.2 = (f32[4,129,128]{2,1,0:T(8,128)S(1)}, f32[4,129,128]{2,1,0:T(8,128)S(1)}, u32[]{:S(2)}, u32[]{:S(2)}) collective-permute-start(f32[4,129,128]{2,1,0:T(8,128)S(1)} %pad_maximum_fusion.2), channel_id=1, source_target_pairs={{0,16},{8,24},{16,32},{24,40},{32,48},{40,56},{48,64},{56,72},{64,... | collective-permute-start | bytes 792584 | tf_op jit(solution)/shard_map/ppermute | solution.py:25
  47.3 34.0 %copy-start.5 = (f32[512]{0:T(512)S(1)}, f32[512]{0:T(512)}, u32[]{:S(2)}) copy-start(f32[512]{0:T(512)} %param.14) | copy-start | bytes 6148
  48.1 8.7 %collective-permute-start.3 = (f32[4,129,128]{2,1,0:T(8,128)}, f32[4,129,128]{2,1,0:T(8,128)S(1)}, u32[]{:S(2)}, u32[]{:S(2)}) collective-permute-start(f32[4,129,128]{2,1,0:T(8,128)} %pad_maximum_fusion.3), channel_id=1, source_target_pairs={{0,32},{8,40},{16,48},{24,56},{32,64},{40,72},{48,80},{56,88},{64,... | collective-permute-start | bytes 792584 | tf_op jit(solution)/shard_map/ppermute | solution.py:25
  57.6 10.2 %collective-permute-start.4 = (f32[4,129,128]{2,1,0:T(8,128)}, f32[4,129,128]{2,1,0:T(8,128)}, u32[]{:S(2)}, u32[]{:S(2)}) collective-permute-start(f32[4,129,128]{2,1,0:T(8,128)} %pad_maximum_fusion.4), channel_id=1, source_target_pairs={{0,64},{8,72},{16,80},{24,88},{32,96},{40,104},{48,112},{56,120},{... | collective-permute-start | bytes 792584 | tf_op jit(solution)/shard_map/ppermute | solution.py:25
  69.6 10.1 %collective-permute-start.5 = (f32[4,129,128]{2,1,0:T(8,128)S(1)}, f32[4,129,128]{2,1,0:T(8,128)S(1)}, u32[]{:S(2)}, u32[]{:S(2)}) collective-permute-start(f32[4,129,128]{2,1,0:T(8,128)S(1)} %pad_maximum_fusion.5), channel_id=1, source_target_pairs={{0,128},{8,136},{16,144},{24,152},{32,160},{40,168},{48,176},{56,1... | collective-permute-start | bytes 792584 | tf_op jit(solution)/shard_map/ppermute | solution.py:25
  83.2 14.6 %all-to-all-start = ((bf16[8,24,512]{2,1,0:T(8,128)(2,1)}), bf16[8,24,512]{2,1,0:T(8,128)(2,1)S(1)}, u32[]{:S(2)}, u32[]{:S(2)}) async-start(bf16[8,24,512]{2,1,0:T(8,128)(2,1)} %bitcast.21), calls=%async_computation | async-start | bytes 393216 | tf_op jit(solution)/shard_map/all_to_all | solution.py:133
  88.0 71.4 %all-gather.9.cloned.1.call-start = ((), (), s32[]{:S(2)}) async-start(), calls=%async_computation.5 | async-start | bytes 6291456 | tf_op jit(solution)/shard_map/all_gather | solution.py:132
  99.8 47.8 %all-to-all-start.1 = ((bf16[16,24,4096]{2,1,0:T(8,128)(2,1)}), bf16[16,24,4096]{2,1,0:T(8,128)(2,1)S(1)}, u32[]{:S(2)}, u32[]{:S(2)}) async-start(bf16[16,24,4096]{2,1,0:T(8,128)(2,1)} %broadcast_in_dim.58), calls=%async_computation.1 | async-start | bytes 6291456 | tf_op jit(solution)/shard_map/all_to_all | solution.py:141
  108.8 38.8 %collective-permute-start.6 = (bf16[256,4096]{1,0:T(8,128)(2,1)}, bf16[256,4096]{1,0:T(8,128)(2,1)}, u32[]{:S(2)}, u32[]{:S(2)}) collective-permute-start(bf16[256,4096]{1,0:T(8,128)(2,1)} %bitcast.142), channel_id=1, source_target_pairs={{0,1},{1,0},{2,3},{3,2},{4,5},{5,4},{6,7},{7,6},{8,9},{9,8},{10,11... | collective-permute-start | bytes 6291464 | tf_op jit(solution)/shard_map/ppermute | solution.py:135
  208.7 4.8 %copy-start.7 = (f32[8,2]{0,1:T(2,128)S(1)}, f32[8,2]{0,1:T(2,128)}, u32[]{:S(2)}) copy-start(f32[8,2]{0,1:T(2,128)} %param.19) | copy-start | bytes 196
  210.1 13.8 %all-to-all-start.3 = ((bf16[8,3,4096]{2,1,0:T(4,128)(2,1)}), bf16[8,3,4096]{2,1,0:T(4,128)(2,1)S(1)}, u32[]{:S(2)}, u32[]{:S(2)}) async-start(bf16[8,3,4096]{2,1,0:T(4,128)(2,1)} %reshape.284), calls=%async_computation.3 | async-start | bytes 524288 | tf_op jit(solution)/shard_map/all_to_all | solution.py:163
Sparse Core Ops, SparseCore 0:
  9.2 18.8 all-gather.10
  31.7 18.5 all-gather.6
  90.6 21.4 all-gather.8

commit v13 on v12

--- a/solution.py
+++ b/solution.py
@@ -152,10 +152,9 @@
         up_part = jnp.dot(piece, weights[1], preferred_element_type=jnp.float32)
         return (jax.nn.silu(gate_part) * up_part).astype(jnp.bfloat16)
 
-    term = (
-        jnp.dot(hidden_of(gate_up_core), down_core, preferred_element_type=jnp.float32)
-        + jnp.dot(hidden_of(gate_up_far), down_far, preferred_element_type=jnp.float32)
-    ).astype(jnp.bfloat16)
+    hidden_all = jnp.concatenate([hidden_of(gate_up_core), hidden_of(gate_up_far)], axis=1)
+    down_all = jnp.concatenate([down_core, down_far], axis=0)
+    term = jnp.dot(hidden_all, down_all, preferred_element_type=jnp.float32).astype(jnp.bfloat16)
     parts = lax.all_to_all(
         term.reshape(groups, per_dev, width), TOK_AXES, split_axis=0, concat_axis=0, tiled=True
     )

time: 233 us -> 221 us (0.948)
  matrix products: 27.6 us -> 15.2 us
    dot_general x2 -> x3, matrix products: 17.8 us -> 9.5 us  [the longest x2 6.07 us: hidden_of(): gate_part = jnp.dot(piece, weights[0], preferred_element_type=jnp.float32)]
    dot_general x2, matrix products: 6.63 us -> 2.59 us  [hidden_of(): up_part = jnp.dot(piece, weights[1], preferred_element_type=jnp.float32)]
  transfers between devices with their start and end apart: 13 -> 13, of which waited for: 8 -> 8; matrix products, arithmetic and copies ran while one was open for 12% -> 9% of each run, Pallas kernels for 0% -> 0%
where the time goes in v13:
time: 221 us; the launch traced here: 220 us
  waiting for transfers between devices  79.8 us (36%)
  blocking collectives  55.8 us (25%)
  starting transfers between devices  39.8 us (18%)
  matrix products  15.2 us (7%)
  between operations  13.5 us (6%)
  local copies, waits for them, and re-layouts  8.15 us (4%)
  other arithmetic  8.09 us (4%)
    ppermute x1, waiting for transfers between devices, per_device(): down_far = lax.ppermute(down_core, 'p', partner)  38.3 us
    all_to_all x1, blocking collectives, per_device(): lax.all_to_all(term.reshape(groups, per_dev, width), TOK_AXES, split_axis...  36.4 us
    ppermute x5, starting transfers between devices, shifted(): return lax.ppermute(value, SEQ_AXES, pairs)  21.9 us
    ppermute x5, waiting for transfers between devices, shifted(): return lax.ppermute(value, SEQ_AXES, pairs)  20.8 us
    all_gather x1, blocking collectives, per_device(): ids_all = lax.all_gather(expert_ids, DEV_AXES, axis=0, tiled=False)  19.4 us
    all_to_all x1, waiting for transfers between devices, per_device(): lax.all_to_all(summed.reshape(dev_count, half, width), DEV_AXES, split_ax...  10.1 us
    all_to_all x1, waiting for transfers between devices, per_device(): lax.all_to_all(send_rows, DEV_AXES, split_axis=0, concat_axis=0, tiled=True)  9.76 us
    all_to_all x1, starting transfers between devices, per_device(): lax.all_to_all(jnp.broadcast_to(local_rows[None], (groups,) + local_rows....  8.97 us
  transfers between devices with their start and end apart: 13, of which 8 were waited for; matrix products, arithmetic and copies ran while one was open for 9% of the time, Pallas kernels for 0%

profile of v13, /device:TPU:2, one launch (start us, length us, event | category | flops | bytes accessed | tf_op | source)
XLA Modules:
  0.0 220.4 jit_solution(3225151371570642014)
XLA Ops:
  6.5 0.7 all-gather.11.cloned.1.call-update
  7.3 19.4 %all-gather.2 = s32[8,8,2]{1,2,0:T(2,128)S(1)} all-gather(s32[1,8,2]{1,2,0:T(2,128)} %bitcast.149), channel_id=3, replica_groups=mesh['y'=4,'x'=4,'c'=2,'e'=4,'p'=2] {'e','p'}, dimensions={0}, use_global_device_ids=true | all-gather | bytes 576 | tf_op jit(solution)/shard_map/all_gather | solution.py:74
  26.7 1.7 pad_maximum_fusion
  28.6 0.2 reduce_window_sum.22
  28.8 0.2 exponential_reduce_fusion
  29.1 0.5 fusion.34
  29.7 1.9 collective-permute-start.1
  31.8 0.4 fusion.58
  32.4 5.2 %collective-permute-done.1 = f32[4,129,128]{2,1,0:T(8,128)S(1)} collective-permute-done((f32[4,129,128]{2,1,0:T(8,128)S(1)}, f32[4,129,128]{2,1,0:T(8,128)S(1)}, u32[]{:S(2)}, u32[]{:S(2)}) %collective-permute-start.1) | collective-permute-done | bytes 264224 | tf_op jit(solution)/shard_map/ppermute | solution.py:25
  37.7 3.4 %collective-permute-start.2 = (f32[4,129,128]{2,1,0:T(8,128)S(1)}, f32[4,129,128]{2,1,0:T(8,128)S(1)}, u32[]{:S(2)}, u32[]{:S(2)}) collective-permute-start(f32[4,129,128]{2,1,0:T(8,128)S(1)} %pad_maximum_fusion.2), channel_id=1, source_target_pairs={{0,16},{8,24},{16,32},{24,40},{32,48},{40,56},{48,64},{56,72},{64,... | collective-permute-start | bytes 792584 | tf_op jit(solution)/shard_map/ppermute | solution.py:25
  41.2 6.1 %collective-permute-done.2 = f32[4,129,128]{2,1,0:T(8,128)S(1)} collective-permute-done((f32[4,129,128]{2,1,0:T(8,128)S(1)}, f32[4,129,128]{2,1,0:T(8,128)S(1)}, u32[]{:S(2)}, u32[]{:S(2)}) %collective-permute-start.2) | collective-permute-done | bytes 264224 | tf_op jit(solution)/shard_map/ppermute | solution.py:25
  47.4 0.7 pad_maximum_fusion.3
  48.1 4.0 %collective-permute-start.3 = (f32[4,129,128]{2,1,0:T(8,128)}, f32[4,129,128]{2,1,0:T(8,128)S(1)}, u32[]{:S(2)}, u32[]{:S(2)}) collective-permute-start(f32[4,129,128]{2,1,0:T(8,128)} %pad_maximum_fusion.3), channel_id=1, source_target_pairs={{0,32},{8,40},{16,48},{24,56},{32,64},{40,72},{48,80},{56,88},{64,... | collective-permute-start | bytes 792584 | tf_op jit(solution)/shard_map/ppermute | solution.py:25
  52.9 1.0 convolution_multiply_fusion
  53.9 3.0 %collective-permute-done.3 = f32[4,129,128]{2,1,0:T(8,128)S(1)} collective-permute-done((f32[4,129,128]{2,1,0:T(8,128)}, f32[4,129,128]{2,1,0:T(8,128)S(1)}, u32[]{:S(2)}, u32[]{:S(2)}) %collective-permute-start.3) | collective-permute-done | bytes 264224 | tf_op jit(solution)/shard_map/ppermute | solution.py:25
  56.9 0.7 pad_maximum_fusion.4
  57.6 6.5 %collective-permute-start.4 = (f32[4,129,128]{2,1,0:T(8,128)}, f32[4,129,128]{2,1,0:T(8,128)}, u32[]{:S(2)}, u32[]{:S(2)}) collective-permute-start(f32[4,129,128]{2,1,0:T(8,128)} %pad_maximum_fusion.4), channel_id=1, source_target_pairs={{0,64},{8,72},{16,80},{24,88},{32,96},{40,104},{48,112},{56,120},{... | collective-permute-start | bytes 792584 | tf_op jit(solution)/shard_map/ppermute | solution.py:25
  64.2 1.0 scatter_custom_fusion
  65.2 2.6 %collective-permute-done.4 = f32[4,129,128]{2,1,0:T(8,128)} collective-permute-done((f32[4,129,128]{2,1,0:T(8,128)}, f32[4,129,128]{2,1,0:T(8,128)}, u32[]{:S(2)}, u32[]{:S(2)}) %collective-permute-start.4) | collective-permute-done | bytes 264224 | tf_op jit(solution)/shard_map/ppermute | solution.py:25
  67.8 0.7 add_exponential_fusion
  68.6 1.0 multiply_add_fusion
  69.6 6.0 %collective-permute-start.5 = (f32[4,129,128]{2,1,0:T(8,128)S(1)}, f32[4,129,128]{2,1,0:T(8,128)S(1)}, u32[]{:S(2)}, u32[]{:S(2)}) collective-permute-start(f32[4,129,128]{2,1,0:T(8,128)S(1)} %pad_maximum_fusion.5), channel_id=1, source_target_pairs={{0,128},{8,136},{16,144},{24,152},{32,160},{40,168},{48,176},{56,1... | collective-permute-start | bytes 792584 | tf_op jit(solution)/shard_map/ppermute | solution.py:25
  75.6 4.0 %collective-permute-done.5 = f32[4,129,128]{2,1,0:T(8,128)S(1)} collective-permute-done((f32[4,129,128]{2,1,0:T(8,128)S(1)}, f32[4,129,128]{2,1,0:T(8,128)S(1)}, u32[]{:S(2)}, u32[]{:S(2)}) %collective-permute-start.5) | collective-permute-done | bytes 264224 | tf_op jit(solution)/shard_map/ppermute | solution.py:25
  79.6 1.4 fusion.12
  81.0 0.3 fusion.25
  81.5 1.7 gather_fusion
  83.2 4.8 %all-to-all-start = ((bf16[8,24,512]{2,1,0:T(8,128)(2,1)}), bf16[8,24,512]{2,1,0:T(8,128)(2,1)S(1)}, u32[]{:S(2)}, u32[]{:S(2)}) async-start(bf16[8,24,512]{2,1,0:T(8,128)(2,1)} %bitcast.21), calls=%async_computation | async-start | bytes 393216 | tf_op jit(solution)/shard_map/all_to_all | solution.py:133
  88.1 9.8 %all-to-all-done = bf16[8,24,512]{2,1,0:T(8,128)(2,1)S(1)} async-done(((bf16[8,24,512]{2,1,0:T(8,128)(2,1)}), bf16[8,24,512]{2,1,0:T(8,128)(2,1)S(1)}, u32[]{:S(2)}, u32[]{:S(2)}) %all-to-all-start) | async-done | bytes 196640 | tf_op jit(solution)/shard_map/all_to_all | solution.py:133
  97.8 2.1 broadcast_in_dim.58
  99.9 9.0 %all-to-all-start.1 = ((bf16[16,24,4096]{2,1,0:T(8,128)(2,1)}), bf16[16,24,4096]{2,1,0:T(8,128)(2,1)S(1)}, u32[]{:S(2)}, u32[]{:S(2)}) async-start(bf16[16,24,4096]{2,1,0:T(8,128)(2,1)} %broadcast_in_dim.58), calls=%async_computation.1 | async-start | bytes 6291456 | tf_op jit(solution)/shard_map/all_to_all | solution.py:141
  108.9 0.5 collective-permute-start.6
  109.4 38.3 %collective-permute-done.6 = bf16[256,4096]{1,0:T(8,128)(2,1)} collective-permute-done((bf16[256,4096]{1,0:T(8,128)(2,1)}, bf16[256,4096]{1,0:T(8,128)(2,1)}, u32[]{:S(2)}, u32[]{:S(2)}) %collective-permute-start.6) | collective-permute-done | bytes 2097184 | tf_op jit(solution)/shard_map/ppermute | solution.py:135
  147.7 3.0 %fusion.6 = f32[384,256]{0,1:T(8,128)S(1)} fusion(bf16[384,4096]{1,0:T(8,128)(2,1)S(1)} %bitcast.131, bf16[2,4096,256]{2,1,0:T(8,128)(2,1)} %all-gather.7.cloned.1.call-done), kind=kOutput, calls=%fused_computation.14 | convolution fusion | flops 805306368 | bytes 5636096 | tf_op jit(solution)/shard_map/dot_general | solution.py:151
  150.8 1.3 multiply_convert_fusion.1
  152.1 3.0 %fusion.4 = f32[384,256]{0,1:T(8,128)S(1)} fusion(bf16[384,4096]{1,0:T(8,128)(2,1)S(1)} %bitcast.133, bf16[2,4096,256]{2,1,0:T(8,128)(2,1)} %all-gather.9.cloned.1.call-done), kind=kOutput, calls=%fused_computation.10 | convolution fusion | flops 805306368 | bytes 5636096 | tf_op jit(solution)/shard_map/dot_general | solution.py:151
  155.2 1.3 multiply_convert_fusion
  156.5 0.3 copy-done.10
  156.8 3.4 %convolution_convert_fusion = bf16[384,4096]{1,0:T(8,128)(2,1)S(1)} fusion(bf16[256,4096]{1,0:T(8,128)(2,1)} %collective-permute-done.6, bf16[256,4096]{1,0:T(8,128)(2,1)S(1)} %bitcast.151, bf16[384,256]{0,1:T(8,128)(2,1)S(1)} %multiply_convert_fusion, bf16[384,256]{0,1:T(8,128)(2,1)S(1)} %multiply_convert_fusion.1), kind=kOutput, calls=%fused_computation.3 | convolution fusion | flops 1621360640 | bytes 7733248 | tf_op jit(solution)/shard_map/dot_general | solution.py:157
  160.2 36.4 %all_to_all.20 = bf16[16,24,4096]{2,1,0:T(8,128)(2,1)S(1)} all-to-all(bf16[16,24,4096]{2,1,0:T(8,128)(2,1)S(1)} %bitcast.135), channel_id=1, replica_groups=mesh['y'=4,'x'=4,'c'=2,'e'=4,'p'=2] {'y','x'}, dimensions={0} | all-to-all | bytes 6291456 | tf_op jit(solution)/shard_map/all_to_all | solution.py:158
  196.6 0.6 reduce_sum.41
  197.2 0.8 reshape.284
  198.0 3.4 %all-to-all-start.3 = ((bf16[8,3,4096]{2,1,0:T(4,128)(2,1)}), bf16[8,3,4096]{2,1,0:T(4,128)(2,1)S(1)}, u32[]{:S(2)}, u32[]{:S(2)}) async-start(bf16[8,3,4096]{2,1,0:T(4,128)(2,1)} %reshape.284), calls=%async_computation.3 | async-start | bytes 524288 | tf_op jit(solution)/shard_map/all_to_all | solution.py:162
  201.5 0.2 add_reduce_fusion
  201.7 10.1 %all-to-all-done.3 = bf16[8,3,4096]{2,1,0:T(4,128)(2,1)S(1)} async-done(((bf16[8,3,4096]{2,1,0:T(4,128)(2,1)}), bf16[8,3,4096]{2,1,0:T(4,128)(2,1)S(1)}, u32[]{:S(2)}, u32[]{:S(2)}) %all-to-all-start.3) | async-done | bytes 196640 | tf_op jit(solution)/shard_map/all_to_all | solution.py:162
  211.8 0.2 reshape.285
  212.0 0.6 gather_fusion.1
  212.6 0.2 reshape.286
  212.8 1.0 multiply_reduce_fusion
  (72 shorter events, 2.1 us)
Async XLA Ops:
  6.5 22.5 %copy-start = (bf16[64,512]{1,0:T(8,128)(2,1)S(1)}, bf16[64,512]{1,0:T(8,128)(2,1)}, u32[]{:S(2)}) copy-start(bf16[64,512]{1,0:T(8,128)(2,1)} %param.12) | copy-start | bytes 196612
  6.5 22.0 %copy-start.6 = (f32[64,4]{0,1:T(4,128)S(1)}, f32[64,4]{0,1:T(4,128)}, u32[]{:S(2)}) copy-start(f32[64,4]{0,1:T(4,128)} %param.13) | copy-start | bytes 3076
  6.5 22.5 %copy-start.4 = (bf16[64,512]{1,0:T(8,128)(2,1)S(1)}, bf16[64,512]{1,0:T(8,128)(2,1)}, u32[]{:S(2)}) copy-start(bf16[64,512]{1,0:T(8,128)(2,1)} %param.11) | copy-start | bytes 196612
  6.5 81.5 %all-gather.11.cloned.1.call-start = ((), (), s32[]{:S(2)}) async-start(), calls=%async_computation.6 | async-start | bytes 3145728 | tf_op jit(solution)/shard_map/all_gather | solution.py:79
  7.3 140.5 %all-gather.7.cloned.1.call-start = ((), (), s32[]{:S(2)}) async-start(), calls=%async_computation.4 | async-start | bytes 6291456 | tf_op jit(solution)/shard_map/all_gather | solution.py:78
  28.4 3.2 %copy-start.1 = (bf16[2,4096,128]{2,1,0:T(8,128)(2,1)}, bf16[2,4096,128]{2,1,0:T(8,128)(2,1)S(1)}, u32[]{:S(2)}) copy-start(bf16[2,4096,128]{2,1,0:T(8,128)(2,1)S(1)} %pad_maximum_fusion) | copy-start | bytes 6291460
  28.4 24.4 %copy-start.3 = (bf16[64,512]{1,0:T(8,128)(2,1)S(1)}, bf16[64,512]{1,0:T(8,128)(2,1)}, u32[]{:S(2)}) copy-start(bf16[64,512]{1,0:T(8,128)(2,1)} %param.10) | copy-start | bytes 196612
  28.5 54.7 %collective-permute-start = (bf16[2,4096,128]{2,1,0:T(8,128)(2,1)S(1)}, bf16[2,4096,128]{2,1,0:T(8,128)(2,1)}, u32[]{:S(2)}, u32[]{:S(2)}) collective-permute-start(bf16[2,4096,128]{2,1,0:T(8,128)(2,1)S(1)} %pad_maximum_fusion), channel_id=1, source_target_pairs={{0,1},{1,0},{2,3},{3,2},{4,5},{5,4},{6,7},{7,6},{8,9},{9,8},{10,11... | collective-permute-start | bytes 6291464 | tf_op jit(solution)/shard_map/ppermute | solution.py:80
  29.7 7.9 %collective-permute-start.1 = (f32[4,129,128]{2,1,0:T(8,128)S(1)}, f32[4,129,128]{2,1,0:T(8,128)S(1)}, u32[]{:S(2)}, u32[]{:S(2)}) collective-permute-start(f32[4,129,128]{2,1,0:T(8,128)S(1)} %pad_maximum_fusion.1), channel_id=1, source_target_pairs={{0,8},{8,16},{16,24},{24,32},{32,40},{40,48},{48,56},{56,64},{64,7... | collective-permute-start | bytes 792584 | tf_op jit(solution)/shard_map/ppermute | solution.py:25
  31.6 120.5 %all-gather.9.cloned.1.call-start = ((), (), s32[]{:S(2)}) async-start(), calls=%async_computation.5 | async-start | bytes 6291456 | tf_op jit(solution)/shard_map/all_gather | solution.py:132
  37.5 9.9 %copy-start.2 = (f32[4,129,128]{2,1,0:T(8,128)}, f32[4,129,128]{2,1,0:T(8,128)S(1)}, u32[]{:S(2)}) copy-start(f32[4,129,128]{2,1,0:T(8,128)S(1)} %collective-permute-done.1) | copy-start | bytes 792580
  37.7 9.6 %collective-permute-start.2 = (f32[4,129,128]{2,1,0:T(8,128)S(1)}, f32[4,129,128]{2,1,0:T(8,128)S(1)}, u32[]{:S(2)}, u32[]{:S(2)}) collective-permute-start(f32[4,129,128]{2,1,0:T(8,128)S(1)} %pad_maximum_fusion.2), channel_id=1, source_target_pairs={{0,16},{8,24},{16,32},{24,40},{32,48},{40,56},{48,64},{56,72},{64,... | collective-permute-start | bytes 792584 | tf_op jit(solution)/shard_map/ppermute | solution.py:25
  47.3 34.0 %copy-start.5 = (f32[512]{0:T(512)S(1)}, f32[512]{0:T(512)}, u32[]{:S(2)}) copy-start(f32[512]{0:T(512)} %param.14) | copy-start | bytes 6148
  48.1 8.7 %collective-permute-start.3 = (f32[4,129,128]{2,1,0:T(8,128)}, f32[4,129,128]{2,1,0:T(8,128)S(1)}, u32[]{:S(2)}, u32[]{:S(2)}) collective-permute-start(f32[4,129,128]{2,1,0:T(8,128)} %pad_maximum_fusion.3), channel_id=1, source_target_pairs={{0,32},{8,40},{16,48},{24,56},{32,64},{40,72},{48,80},{56,88},{64,... | collective-permute-start | bytes 792584 | tf_op jit(solution)/shard_map/ppermute | solution.py:25
  57.6 10.2 %collective-permute-start.4 = (f32[4,129,128]{2,1,0:T(8,128)}, f32[4,129,128]{2,1,0:T(8,128)}, u32[]{:S(2)}, u32[]{:S(2)}) collective-permute-start(f32[4,129,128]{2,1,0:T(8,128)} %pad_maximum_fusion.4), channel_id=1, source_target_pairs={{0,64},{8,72},{16,80},{24,88},{32,96},{40,104},{48,112},{56,120},{... | collective-permute-start | bytes 792584 | tf_op jit(solution)/shard_map/ppermute | solution.py:25
  69.6 10.1 %collective-permute-start.5 = (f32[4,129,128]{2,1,0:T(8,128)S(1)}, f32[4,129,128]{2,1,0:T(8,128)S(1)}, u32[]{:S(2)}, u32[]{:S(2)}) collective-permute-start(f32[4,129,128]{2,1,0:T(8,128)S(1)} %pad_maximum_fusion.5), channel_id=1, source_target_pairs={{0,128},{8,136},{16,144},{24,152},{32,160},{40,168},{48,176},{56,1... | collective-permute-start | bytes 792584 | tf_op jit(solution)/shard_map/ppermute | solution.py:25
  83.2 14.6 %all-to-all-start = ((bf16[8,24,512]{2,1,0:T(8,128)(2,1)}), bf16[8,24,512]{2,1,0:T(8,128)(2,1)S(1)}, u32[]{:S(2)}, u32[]{:S(2)}) async-start(bf16[8,24,512]{2,1,0:T(8,128)(2,1)} %bitcast.21), calls=%async_computation | async-start | bytes 393216 | tf_op jit(solution)/shard_map/all_to_all | solution.py:133
  99.9 47.8 %all-to-all-start.1 = ((bf16[16,24,4096]{2,1,0:T(8,128)(2,1)}), bf16[16,24,4096]{2,1,0:T(8,128)(2,1)S(1)}, u32[]{:S(2)}, u32[]{:S(2)}) async-start(bf16[16,24,4096]{2,1,0:T(8,128)(2,1)} %broadcast_in_dim.58), calls=%async_computation.1 | async-start | bytes 6291456 | tf_op jit(solution)/shard_map/all_to_all | solution.py:141
  108.9 38.8 %collective-permute-start.6 = (bf16[256,4096]{1,0:T(8,128)(2,1)}, bf16[256,4096]{1,0:T(8,128)(2,1)}, u32[]{:S(2)}, u32[]{:S(2)}) collective-permute-start(bf16[256,4096]{1,0:T(8,128)(2,1)} %bitcast.150), channel_id=1, source_target_pairs={{0,1},{1,0},{2,3},{3,2},{4,5},{5,4},{6,7},{7,6},{8,9},{9,8},{10,11... | collective-permute-start | bytes 6291464 | tf_op jit(solution)/shard_map/ppermute | solution.py:135
  147.7 3.0 %copy-start.8 = (bf16[2,4096,256]{2,1,0:T(8,128)(2,1)S(1)}, bf16[2,4096,256]{2,1,0:T(8,128)(2,1)}, u32[]{:S(2)}) copy-start(bf16[2,4096,256]{2,1,0:T(8,128)(2,1)} %all-gather.7.cloned.1.call-done) | copy-start | bytes 12582916
  152.1 3.1 %copy-start.9 = (bf16[2,4096,256]{2,1,0:T(8,128)(2,1)S(1)}, bf16[2,4096,256]{2,1,0:T(8,128)(2,1)}, u32[]{:S(2)}) copy-start(bf16[2,4096,256]{2,1,0:T(8,128)(2,1)} %all-gather.9.cloned.1.call-done) | copy-start | bytes 12582916
  155.2 1.6 copy-start.10
  196.6 4.8 %copy-start.7 = (f32[8,2]{0,1:T(2,128)S(1)}, f32[8,2]{0,1:T(2,128)}, u32[]{:S(2)}) copy-start(f32[8,2]{0,1:T(2,128)} %param.19) | copy-start | bytes 196
  198.0 13.8 %all-to-all-start.3 = ((bf16[8,3,4096]{2,1,0:T(4,128)(2,1)}), bf16[8,3,4096]{2,1,0:T(4,128)(2,1)S(1)}, u32[]{:S(2)}, u32[]{:S(2)}) async-start(bf16[8,3,4096]{2,1,0:T(4,128)(2,1)} %reshape.284), calls=%async_computation.3 | async-start | bytes 524288 | tf_op jit(solution)/shard_map/all_to_all | solution.py:162
Sparse Core Ops, SparseCore 0:
  9.2 18.8 all-gather.10
  31.7 18.5 all-gather.6
  83.3 19.0 all-gather.8

commit v14 on v13

--- a/solution.py
+++ b/solution.py
@@ -22,7 +22,7 @@
 
 def shifted(value, shift, count):
     pairs = [(i, i + shift) for i in range(count - shift)]
-    return lax.ppermute(value, SEQ_AXES, pairs)
+    return lax.ppermute(value.astype(jnp.bfloat16), SEQ_AXES, pairs).astype(value.dtype)
 
 
 def carried_in(log_total, local_state, count):

time: 221 us -> 211 us (0.955)
  waiting for transfers between devices: 79.8 us -> 75 us
  other arithmetic: 8.09 us -> 5.08 us
    ppermute x5, waiting for transfers between devices: 20.8 us -> 12.9 us  [shifted(): lax.ppermute(value.astype(jnp.bfloat16), SEQ_AXES, pairs)]
  transfers between devices with their start and end apart: 13 -> 13, of which waited for: 8 -> 9; matrix products, arithmetic and copies ran while one was open for 9% -> 7% of each run, Pallas kernels for 0% -> 0%
where the time goes in v14:
time: 211 us; the launch traced here: 210 us
  waiting for transfers between devices  75 us (36%)
  blocking collectives  56.5 us (27%)
  starting transfers between devices  38.8 us (18%)
  between operations  13.6 us (6%)
  matrix products  13.4 us (6%)
  local copies, waits for them, and re-layouts  8.16 us (4%)
  other arithmetic  5.08 us (2%)
    ppermute x1, waiting for transfers between devices, per_device(): down_far = lax.ppermute(down_core, 'p', partner)  39.6 us
    all_to_all x1, blocking collectives, per_device(): lax.all_to_all(term.reshape(groups, per_dev, width), TOK_AXES, split_axis...  37.1 us
    ppermute x5, starting transfers between devices, shifted(): lax.ppermute(value.astype(jnp.bfloat16), SEQ_AXES, pairs)  22.2 us
    all_gather x1, blocking collectives, per_device(): ids_all = lax.all_gather(expert_ids, DEV_AXES, axis=0, tiled=False)  19.4 us
    ppermute x5, waiting for transfers between devices, shifted(): lax.ppermute(value.astype(jnp.bfloat16), SEQ_AXES, pairs)  12.9 us
    all_to_all x1, waiting for transfers between devices, per_device(): lax.all_to_all(summed.reshape(dev_count, half, width), DEV_AXES, split_ax...  10.1 us
    all_to_all x1, waiting for transfers between devices, per_device(): lax.all_to_all(send_rows, DEV_AXES, split_axis=0, concat_axis=0, tiled=True)  9.66 us
    all_to_all x1, starting transfers between devices, per_device(): lax.all_to_all(jnp.broadcast_to(local_rows[None], (groups,) + local_rows....  9.03 us
  transfers between devices with their start and end apart: 13, of which 9 were waited for; matrix products, arithmetic and copies ran while one was open for 7% of the time, Pallas kernels for 0%

profile of v14, /device:TPU:2, one launch (start us, length us, event | category | flops | bytes accessed | tf_op | source)
XLA Modules:
  0.0 210.5 jit_solution(17799672735561193825)
XLA Ops:
  6.5 0.7 all-gather.11.cloned.1.call-update
  7.3 19.4 %all-gather.2 = s32[8,8,2]{1,2,0:T(2,128)S(1)} all-gather(s32[1,8,2]{1,2,0:T(2,128)} %bitcast.158), channel_id=3, replica_groups=mesh['y'=4,'x'=4,'c'=2,'e'=4,'p'=2] {'e','p'}, dimensions={0}, use_global_device_ids=true | all-gather | bytes 576 | tf_op jit(solution)/shard_map/all_gather | solution.py:74
  26.7 1.7 pad_maximum_fusion
  28.6 0.2 reduce_window_sum.22
  28.8 0.2 exponential_reduce_fusion
  29.1 0.5 fusion.64
  29.7 1.9 collective-permute-start.1
  31.8 0.4 fusion.65
  32.5 0.1 copy.55
  32.7 0.1 mul.252
  33.0 3.0 %collective-permute-done.1 = bf16[4,129,128]{2,1,0:T(8,128)(2,1)S(1)} collective-permute-done((bf16[4,129,128]{2,1,0:T(8,128)(2,1)S(1)}, bf16[4,129,128]{2,1,0:T(8,128)(2,1)S(1)}, u32[]{:S(2)}, u32[]{:S(2)}) %collective-permute-start.1) | collective-permute-done | bytes 132128 | tf_op jit(solution)/shard_map/ppermute | solution.py:25
  36.3 3.4 %collective-permute-start.2 = (bf16[4,129,128]{2,1,0:T(8,128)(2,1)S(1)}, bf16[4,129,128]{2,1,0:T(8,128)(2,1)S(1)}, u32[]{:S(2)}, u32[]{:S(2)}) collective-permute-start(bf16[4,129,128]{2,1,0:T(8,128)(2,1)S(1)} %pad_maximum_fusion.2), channel_id=1, source_target_pairs={{0,16},{8,24},{16,32},{24,40},{32,48},{40,56},{48,64},{56,72},{64,... | collective-permute-start | bytes 396296 | tf_op jit(solution)/shard_map/ppermute | solution.py:25
  39.8 1.0 scatter_custom_fusion
  40.8 2.4 %collective-permute-done.2 = bf16[4,129,128]{2,1,0:T(8,128)(2,1)S(1)} collective-permute-done((bf16[4,129,128]{2,1,0:T(8,128)(2,1)S(1)}, bf16[4,129,128]{2,1,0:T(8,128)(2,1)S(1)}, u32[]{:S(2)}, u32[]{:S(2)}) %collective-permute-start.2) | collective-permute-done | bytes 132128 | tf_op jit(solution)/shard_map/ppermute | solution.py:25
  43.3 5.2 %collective-permute-start.3 = (bf16[4,129,128]{2,1,0:T(8,128)(2,1)S(1)}, bf16[4,129,128]{2,1,0:T(8,128)(2,1)S(1)}, u32[]{:S(2)}, u32[]{:S(2)}) collective-permute-start(bf16[4,129,128]{2,1,0:T(8,128)(2,1)S(1)} %pad_maximum_fusion.3), channel_id=1, source_target_pairs={{0,32},{8,40},{16,48},{24,56},{32,64},{40,72},{48,80},{56,88},{64,... | collective-permute-start | bytes 396296 | tf_op jit(solution)/shard_map/ppermute | solution.py:25
  48.5 0.2 convolution_multiply_fusion
  48.7 2.4 %collective-permute-done.3 = bf16[4,129,128]{2,1,0:T(8,128)(2,1)S(1)} collective-permute-done((bf16[4,129,128]{2,1,0:T(8,128)(2,1)S(1)}, bf16[4,129,128]{2,1,0:T(8,128)(2,1)S(1)}, u32[]{:S(2)}, u32[]{:S(2)}) %collective-permute-start.3) | collective-permute-done | bytes 132128 | tf_op jit(solution)/shard_map/ppermute | solution.py:25
  51.2 5.7 %collective-permute-start.4 = (bf16[4,129,128]{2,1,0:T(8,128)(2,1)S(1)}, bf16[4,129,128]{2,1,0:T(8,128)(2,1)S(1)}, u32[]{:S(2)}, u32[]{:S(2)}) collective-permute-start(bf16[4,129,128]{2,1,0:T(8,128)(2,1)S(1)} %pad_maximum_fusion.4), channel_id=1, source_target_pairs={{0,64},{8,72},{16,80},{24,88},{32,96},{40,104},{48,112},{56,120},{... | collective-permute-start | bytes 396296 | tf_op jit(solution)/shard_map/ppermute | solution.py:25
  57.0 2.5 %collective-permute-done.4 = bf16[4,129,128]{2,1,0:T(8,128)(2,1)S(1)} collective-permute-done((bf16[4,129,128]{2,1,0:T(8,128)(2,1)S(1)}, bf16[4,129,128]{2,1,0:T(8,128)(2,1)S(1)}, u32[]{:S(2)}, u32[]{:S(2)}) %collective-permute-start.4) | collective-permute-done | bytes 132128 | tf_op jit(solution)/shard_map/ppermute | solution.py:25
  59.7 6.0 %collective-permute-start.5 = (bf16[4,129,128]{2,1,0:T(8,128)(2,1)S(1)}, bf16[4,129,128]{2,1,0:T(8,128)(2,1)S(1)}, u32[]{:S(2)}, u32[]{:S(2)}) collective-permute-start(bf16[4,129,128]{2,1,0:T(8,128)(2,1)S(1)} %pad_maximum_fusion.5), channel_id=1, source_target_pairs={{0,128},{8,136},{16,144},{24,152},{32,160},{40,168},{48,176},{56,1... | collective-permute-start | bytes 396296 | tf_op jit(solution)/shard_map/ppermute | solution.py:25
  65.7 2.6 %collective-permute-done.5 = bf16[4,129,128]{2,1,0:T(8,128)(2,1)S(1)} collective-permute-done((bf16[4,129,128]{2,1,0:T(8,128)(2,1)S(1)}, bf16[4,129,128]{2,1,0:T(8,128)(2,1)S(1)}, u32[]{:S(2)}, u32[]{:S(2)}) %collective-permute-start.5) | collective-permute-done | bytes 132128 | tf_op jit(solution)/shard_map/ppermute | solution.py:25
  68.2 0.3 fusion.11
  68.6 0.3 fusion.27
  68.9 0.1 copy_bitcast_fusion
  69.1 1.7 gather_fusion
  70.8 1.9 collective-permute-done
  72.7 3.4 %all-to-all-start = ((bf16[8,24,512]{2,1,0:T(8,128)(2,1)}), bf16[8,24,512]{2,1,0:T(8,128)(2,1)S(1)}, u32[]{:S(2)}, u32[]{:S(2)}) async-start(bf16[8,24,512]{2,1,0:T(8,128)(2,1)} %bitcast.21), calls=%async_computation | async-start | bytes 393216 | tf_op jit(solution)/shard_map/all_to_all | solution.py:133
  76.2 9.7 %all-to-all-done = bf16[8,24,512]{2,1,0:T(8,128)(2,1)S(1)} async-done(((bf16[8,24,512]{2,1,0:T(8,128)(2,1)}), bf16[8,24,512]{2,1,0:T(8,128)(2,1)S(1)}, u32[]{:S(2)}, u32[]{:S(2)}) %all-to-all-start) | async-done | bytes 196640 | tf_op jit(solution)/shard_map/all_to_all | solution.py:133
  85.8 2.1 broadcast_in_dim.61
  87.9 9.0 %all-to-all-start.1 = ((bf16[16,24,4096]{2,1,0:T(8,128)(2,1)}), bf16[16,24,4096]{2,1,0:T(8,128)(2,1)S(1)}, u32[]{:S(2)}, u32[]{:S(2)}) async-start(bf16[16,24,4096]{2,1,0:T(8,128)(2,1)} %broadcast_in_dim.61), calls=%async_computation.1 | async-start | bytes 6291456 | tf_op jit(solution)/shard_map/all_to_all | solution.py:141
  97.0 0.6 collective-permute-start.6
  97.5 39.6 %collective-permute-done.6 = bf16[256,4096]{1,0:T(8,128)(2,1)} collective-permute-done((bf16[256,4096]{1,0:T(8,128)(2,1)}, bf16[256,4096]{1,0:T(8,128)(2,1)}, u32[]{:S(2)}, u32[]{:S(2)}) %collective-permute-start.6) | collective-permute-done | bytes 2097184 | tf_op jit(solution)/shard_map/ppermute | solution.py:135
  137.1 3.0 %fusion.6 = f32[384,256]{0,1:T(8,128)S(1)} fusion(bf16[384,4096]{1,0:T(8,128)(2,1)S(1)} %bitcast.139, bf16[2,4096,256]{2,1,0:T(8,128)(2,1)} %all-gather.7.cloned.1.call-done), kind=kOutput, calls=%fused_computation.14 | convolution fusion | flops 805306368 | bytes 5636096 | tf_op jit(solution)/shard_map/dot_general | solution.py:151
  140.2 1.3 multiply_convert_fusion.1
  141.5 3.0 %fusion.4 = f32[384,256]{0,1:T(8,128)S(1)} fusion(bf16[384,4096]{1,0:T(8,128)(2,1)S(1)} %bitcast.141, bf16[2,4096,256]{2,1,0:T(8,128)(2,1)} %all-gather.9.cloned.1.call-done), kind=kOutput, calls=%fused_computation.10 | convolution fusion | flops 805306368 | bytes 5636096 | tf_op jit(solution)/shard_map/dot_general | solution.py:151
  144.6 1.3 multiply_convert_fusion
  145.9 0.3 copy-done.9
  146.2 3.4 %convolution_convert_fusion = bf16[384,4096]{1,0:T(8,128)(2,1)S(1)} fusion(bf16[256,4096]{1,0:T(8,128)(2,1)} %collective-permute-done.6, bf16[256,4096]{1,0:T(8,128)(2,1)S(1)} %bitcast.160, bf16[384,256]{0,1:T(8,128)(2,1)S(1)} %multiply_convert_fusion, bf16[384,256]{0,1:T(8,128)(2,1)S(1)} %multiply_convert_fusion.1), kind=kOutput, calls=%fused_computation.3 | convolution fusion | flops 1621360640 | bytes 7733248 | tf_op jit(solution)/shard_map/dot_general | solution.py:157
  149.6 37.1 %all_to_all.20 = bf16[16,24,4096]{2,1,0:T(8,128)(2,1)S(1)} all-to-all(bf16[16,24,4096]{2,1,0:T(8,128)(2,1)S(1)} %bitcast.143), channel_id=1, replica_groups=mesh['y'=4,'x'=4,'c'=2,'e'=4,'p'=2] {'y','x'}, dimensions={0} | all-to-all | bytes 6291456 | tf_op jit(solution)/shard_map/all_to_all | solution.py:158
  186.7 0.6 reduce_sum.41
  187.3 0.8 reshape.284
  188.1 3.4 %all-to-all-start.3 = ((bf16[8,3,4096]{2,1,0:T(4,128)(2,1)}), bf16[8,3,4096]{2,1,0:T(4,128)(2,1)S(1)}, u32[]{:S(2)}, u32[]{:S(2)}) async-start(bf16[8,3,4096]{2,1,0:T(4,128)(2,1)} %reshape.284), calls=%async_computation.3 | async-start | bytes 524288 | tf_op jit(solution)/shard_map/all_to_all | solution.py:162
  191.6 0.2 add_reduce_fusion
  191.8 10.1 %all-to-all-done.3 = bf16[8,3,4096]{2,1,0:T(4,128)(2,1)S(1)} async-done(((bf16[8,3,4096]{2,1,0:T(4,128)(2,1)}), bf16[8,3,4096]{2,1,0:T(4,128)(2,1)S(1)}, u32[]{:S(2)}, u32[]{:S(2)}) %all-to-all-start.3) | async-done | bytes 196640 | tf_op jit(solution)/shard_map/all_to_all | solution.py:162
  201.9 0.2 reshape.285
  202.1 0.6 gather_fusion.1
  202.7 0.2 reshape.286
  202.9 1.0 multiply_reduce_fusion
  (77 shorter events, 1.9 us)
Async XLA Ops:
  6.5 22.6 %copy-start = (bf16[64,512]{1,0:T(8,128)(2,1)S(1)}, bf16[64,512]{1,0:T(8,128)(2,1)}, u32[]{:S(2)}) copy-start(bf16[64,512]{1,0:T(8,128)(2,1)} %param.12) | copy-start | bytes 196612
  6.5 22.0 %copy-start.5 = (f32[64,4]{0,1:T(4,128)S(1)}, f32[64,4]{0,1:T(4,128)}, u32[]{:S(2)}) copy-start(f32[64,4]{0,1:T(4,128)} %param.13) | copy-start | bytes 3076
  6.5 22.6 %copy-start.2 = (bf16[64,512]{1,0:T(8,128)(2,1)S(1)}, bf16[64,512]{1,0:T(8,128)(2,1)}, u32[]{:S(2)}) copy-start(bf16[64,512]{1,0:T(8,128)(2,1)} %param.11) | copy-start | bytes 196612
  6.5 69.6 %all-gather.11.cloned.1.call-start = ((), (), s32[]{:S(2)}) async-start(), calls=%async_computation.6 | async-start | bytes 3145728 | tf_op jit(solution)/shard_map/all_gather | solution.py:79
  7.3 129.9 %all-gather.7.cloned.1.call-start = ((), (), s32[]{:S(2)}) async-start(), calls=%async_computation.4 | async-start | bytes 6291456 | tf_op jit(solution)/shard_map/all_gather | solution.py:78
  28.4 3.2 %copy-start.1 = (bf16[2,4096,128]{2,1,0:T(8,128)(2,1)}, bf16[2,4096,128]{2,1,0:T(8,128)(2,1)S(1)}, u32[]{:S(2)}) copy-start(bf16[2,4096,128]{2,1,0:T(8,128)(2,1)S(1)} %pad_maximum_fusion) | copy-start | bytes 6291460
  28.4 20.1 %copy-start.3 = (bf16[64,512]{1,0:T(8,128)(2,1)S(1)}, bf16[64,512]{1,0:T(8,128)(2,1)}, u32[]{:S(2)}) copy-start(bf16[64,512]{1,0:T(8,128)(2,1)} %param.10) | copy-start | bytes 196612
  28.5 44.2 %collective-permute-start = (bf16[2,4096,128]{2,1,0:T(8,128)(2,1)S(1)}, bf16[2,4096,128]{2,1,0:T(8,128)(2,1)}, u32[]{:S(2)}, u32[]{:S(2)}) collective-permute-start(bf16[2,4096,128]{2,1,0:T(8,128)(2,1)S(1)} %pad_maximum_fusion), channel_id=1, source_target_pairs={{0,1},{1,0},{2,3},{3,2},{4,5},{5,4},{6,7},{7,6},{8,9},{9,8},{10,11... | collective-permute-start | bytes 6291464 | tf_op jit(solution)/shard_map/ppermute | solution.py:80
  29.7 6.4 %collective-permute-start.1 = (bf16[4,129,128]{2,1,0:T(8,128)(2,1)S(1)}, bf16[4,129,128]{2,1,0:T(8,128)(2,1)S(1)}, u32[]{:S(2)}, u32[]{:S(2)}) collective-permute-start(bf16[4,129,128]{2,1,0:T(8,128)(2,1)S(1)} %pad_maximum_fusion.1), channel_id=1, source_target_pairs={{0,8},{8,16},{16,24},{24,32},{32,40},{40,48},{48,56},{56,64},{64,7... | collective-permute-start | bytes 396296 | tf_op jit(solution)/shard_map/ppermute | solution.py:25
  31.6 109.9 %all-gather.9.cloned.1.call-start = ((), (), s32[]{:S(2)}) async-start(), calls=%async_computation.5 | async-start | bytes 6291456 | tf_op jit(solution)/shard_map/all_gather | solution.py:132
  36.3 6.9 %collective-permute-start.2 = (bf16[4,129,128]{2,1,0:T(8,128)(2,1)S(1)}, bf16[4,129,128]{2,1,0:T(8,128)(2,1)S(1)}, u32[]{:S(2)}, u32[]{:S(2)}) collective-permute-start(bf16[4,129,128]{2,1,0:T(8,128)(2,1)S(1)} %pad_maximum_fusion.2), channel_id=1, source_target_pairs={{0,16},{8,24},{16,32},{24,40},{32,48},{40,56},{48,64},{56,72},{64,... | collective-permute-start | bytes 396296 | tf_op jit(solution)/shard_map/ppermute | solution.py:25
  43.3 25.6 %copy-start.4 = (f32[512]{0:T(512)S(1)}, f32[512]{0:T(512)}, u32[]{:S(2)}) copy-start(f32[512]{0:T(512)} %param.14) | copy-start | bytes 6148
  43.3 7.8 %collective-permute-start.3 = (bf16[4,129,128]{2,1,0:T(8,128)(2,1)S(1)}, bf16[4,129,128]{2,1,0:T(8,128)(2,1)S(1)}, u32[]{:S(2)}, u32[]{:S(2)}) collective-permute-start(bf16[4,129,128]{2,1,0:T(8,128)(2,1)S(1)} %pad_maximum_fusion.3), channel_id=1, source_target_pairs={{0,32},{8,40},{16,48},{24,56},{32,64},{40,72},{48,80},{56,88},{64,... | collective-permute-start | bytes 396296 | tf_op jit(solution)/shard_map/ppermute | solution.py:25
  51.2 8.3 %collective-permute-start.4 = (bf16[4,129,128]{2,1,0:T(8,128)(2,1)S(1)}, bf16[4,129,128]{2,1,0:T(8,128)(2,1)S(1)}, u32[]{:S(2)}, u32[]{:S(2)}) collective-permute-start(bf16[4,129,128]{2,1,0:T(8,128)(2,1)S(1)} %pad_maximum_fusion.4), channel_id=1, source_target_pairs={{0,64},{8,72},{16,80},{24,88},{32,96},{40,104},{48,112},{56,120},{... | collective-permute-start | bytes 396296 | tf_op jit(solution)/shard_map/ppermute | solution.py:25
  59.7 8.6 %collective-permute-start.5 = (bf16[4,129,128]{2,1,0:T(8,128)(2,1)S(1)}, bf16[4,129,128]{2,1,0:T(8,128)(2,1)S(1)}, u32[]{:S(2)}, u32[]{:S(2)}) collective-permute-start(bf16[4,129,128]{2,1,0:T(8,128)(2,1)S(1)} %pad_maximum_fusion.5), channel_id=1, source_target_pairs={{0,128},{8,136},{16,144},{24,152},{32,160},{40,168},{48,176},{56,1... | collective-permute-start | bytes 396296 | tf_op jit(solution)/shard_map/ppermute | solution.py:25
  72.7 13.1 %all-to-all-start = ((bf16[8,24,512]{2,1,0:T(8,128)(2,1)}), bf16[8,24,512]{2,1,0:T(8,128)(2,1)S(1)}, u32[]{:S(2)}, u32[]{:S(2)}) async-start(bf16[8,24,512]{2,1,0:T(8,128)(2,1)} %bitcast.21), calls=%async_computation | async-start | bytes 393216 | tf_op jit(solution)/shard_map/all_to_all | solution.py:133
  87.9 49.2 %all-to-all-start.1 = ((bf16[16,24,4096]{2,1,0:T(8,128)(2,1)}), bf16[16,24,4096]{2,1,0:T(8,128)(2,1)S(1)}, u32[]{:S(2)}, u32[]{:S(2)}) async-start(bf16[16,24,4096]{2,1,0:T(8,128)(2,1)} %broadcast_in_dim.61), calls=%async_computation.1 | async-start | bytes 6291456 | tf_op jit(solution)/shard_map/all_to_all | solution.py:141
  97.0 40.2 %collective-permute-start.6 = (bf16[256,4096]{1,0:T(8,128)(2,1)}, bf16[256,4096]{1,0:T(8,128)(2,1)}, u32[]{:S(2)}, u32[]{:S(2)}) collective-permute-start(bf16[256,4096]{1,0:T(8,128)(2,1)} %bitcast.159), channel_id=1, source_target_pairs={{0,1},{1,0},{2,3},{3,2},{4,5},{5,4},{6,7},{7,6},{8,9},{9,8},{10,11... | collective-permute-start | bytes 6291464 | tf_op jit(solution)/shard_map/ppermute | solution.py:135
  137.1 3.0 %copy-start.7 = (bf16[2,4096,256]{2,1,0:T(8,128)(2,1)S(1)}, bf16[2,4096,256]{2,1,0:T(8,128)(2,1)}, u32[]{:S(2)}) copy-start(bf16[2,4096,256]{2,1,0:T(8,128)(2,1)} %all-gather.7.cloned.1.call-done) | copy-start | bytes 12582916
  141.5 3.1 %copy-start.8 = (bf16[2,4096,256]{2,1,0:T(8,128)(2,1)S(1)}, bf16[2,4096,256]{2,1,0:T(8,128)(2,1)}, u32[]{:S(2)}) copy-start(bf16[2,4096,256]{2,1,0:T(8,128)(2,1)} %all-gather.9.cloned.1.call-done) | copy-start | bytes 12582916
  144.6 1.6 copy-start.9
  186.7 4.8 %copy-start.6 = (f32[8,2]{0,1:T(2,128)S(1)}, f32[8,2]{0,1:T(2,128)}, u32[]{:S(2)}) copy-start(f32[8,2]{0,1:T(2,128)} %param.19) | copy-start | bytes 196
  188.1 13.8 %all-to-all-start.3 = ((bf16[8,3,4096]{2,1,0:T(4,128)(2,1)}), bf16[8,3,4096]{2,1,0:T(4,128)(2,1)S(1)}, u32[]{:S(2)}, u32[]{:S(2)}) async-start(bf16[8,3,4096]{2,1,0:T(4,128)(2,1)} %reshape.284), calls=%async_computation.3 | async-start | bytes 524288 | tf_op jit(solution)/shard_map/all_to_all | solution.py:162
Sparse Core Ops, SparseCore 0:
  9.2 18.8 all-gather.10
  31.7 18.6 all-gather.6
  72.8 17.6 all-gather.8

commit v15 on v14

--- a/solution.py
+++ b/solution.py
@@ -147,18 +147,26 @@
     ).reshape(groups * per_dev, width)
     down_far, piece = lax.optimization_barrier((down_far, piece))
 
-    def hidden_of(weights):
-        gate_part = jnp.dot(piece, weights[0], preferred_element_type=jnp.float32)
-        up_part = jnp.dot(piece, weights[1], preferred_element_type=jnp.float32)
-        return (jax.nn.silu(gate_part) * up_part).astype(jnp.bfloat16)
-
-    hidden_all = jnp.concatenate([hidden_of(gate_up_core), hidden_of(gate_up_far)], axis=1)
     down_all = jnp.concatenate([down_core, down_far], axis=0)
-    term = jnp.dot(hidden_all, down_all, preferred_element_type=jnp.float32).astype(jnp.bfloat16)
-    parts = lax.all_to_all(
-        term.reshape(groups, per_dev, width), TOK_AXES, split_axis=0, concat_axis=0, tiled=True
-    )
-    summed = jnp.sum(parts.astype(jnp.float32), axis=0).astype(jnp.bfloat16)
+    rows = piece.reshape(groups, per_dev, width)
+    cut = per_dev // 2
+
+    def summed_of(chunk):
+        flat_rows = chunk.reshape(-1, width)
+
+        def hidden_of(weights):
+            gate_part = jnp.dot(flat_rows, weights[0], preferred_element_type=jnp.float32)
+            up_part = jnp.dot(flat_rows, weights[1], preferred_element_type=jnp.float32)
+            return (jax.nn.silu(gate_part) * up_part).astype(jnp.bfloat16)
+
+        hidden_all = jnp.concatenate([hidden_of(gate_up_core), hidden_of(gate_up_far)], axis=1)
+        term = jnp.dot(hidden_all, down_all, preferred_element_type=jnp.float32).astype(jnp.bfloat16)
+        parts = lax.all_to_all(
+            term.reshape(chunk.shape), TOK_AXES, split_axis=0, concat_axis=0, tiled=True
+        )
+        return jnp.sum(parts.astype(jnp.float32), axis=0).astype(jnp.bfloat16)
+
+    summed = jnp.concatenate([summed_of(rows[:, :cut]), summed_of(rows[:, cut:])], axis=0)
     returned = lax.all_to_all(
         summed.reshape(dev_count, half, width),
         DEV_AXES,

time: 211 us -> 244 us (1.16)
  blocking collectives: 56.5 us -> 19.4 us
  waiting for transfers between devices: 75 us -> 97 us
  local copies, waits for them, and re-layouts: 8.16 us -> 27.7 us
  starting transfers between devices: 38.8 us -> 53.5 us
  matrix products: 13.4 us -> 22.9 us
    all_to_all x1 -> x0, blocking collectives: 37.1 us -> none  [per_device(): lax.all_to_all(term.reshape(groups, per_dev, width), TOK_AXES, split_axis...]
    all_to_all x0 -> x2, waiting for transfers between devices: none -> 25.1 us  [summed_of(): lax.all_to_all(term.reshape(chunk.shape), TOK_AXES, split_axis=0, concat_...]
    all_to_all x0 -> x2, starting transfers between devices: none -> 14.7 us  [summed_of(): lax.all_to_all(term.reshape(chunk.shape), TOK_AXES, split_axis=0, concat_...]
    reshape x0 -> x4, local copies, waits for them, and re-layouts: none -> 10.1 us  [the longest x2 5.1 us: summed_of(): flat_rows = chunk.reshape(-1, width)]
    dot_general x5 -> x10, matrix products: 12.1 us -> 21.6 us  [the longest x4 8.41 us: hidden_of(): jnp.dot(flat_rows, weights[0], preferred_element_type=jnp.float32)]
    unnamed x21 -> x26, local copies, waits for them, and re-layouts: 0.4 us -> 4.29 us
    ppermute x1, waiting for transfers between devices: 39.6 us -> 36.4 us  [per_device(): down_far = lax.ppermute(down_core, 'p', partner)]
    concatenate x0 -> x1, local copies, waits for them, and re-layouts: none -> 3.14 us  [per_device(): down_all = jnp.concatenate([down_core, down_far], axis=0)]
  transfers between devices with their start and end apart: 13 -> 15, of which waited for: 9 -> 11; matrix products, arithmetic and copies ran while one was open for 7% -> 18% of each run, Pallas kernels for 0% -> 0%
where the time goes in v15:
time: 244 us; the launch traced here: 241 us
  waiting for transfers between devices  97 us (40%)
  starting transfers between devices  53.5 us (22%)
  local copies, waits for them, and re-layouts  27.7 us (11%)
  matrix products  22.9 us (9%)
  blocking collectives  19.4 us (8%)
  between operations  13.6 us (6%)
  other arithmetic  6.94 us (3%)
    ppermute x1, waiting for transfers between devices, per_device(): down_far = lax.ppermute(down_core, 'p', partner)  36.4 us
    all_to_all x2, waiting for transfers between devices, summed_of(): lax.all_to_all(term.reshape(chunk.shape), TOK_AXES, split_axis=0, concat_...  25.1 us
    ppermute x5, starting transfers between devices, shifted(): lax.ppermute(value.astype(jnp.bfloat16), SEQ_AXES, pairs)  22.2 us
    all_gather x1, blocking collectives, per_device(): ids_all = lax.all_gather(expert_ids, DEV_AXES, axis=0, tiled=False)  19.4 us
    all_to_all x2, starting transfers between devices, summed_of(): lax.all_to_all(term.reshape(chunk.shape), TOK_AXES, split_axis=0, concat_...  14.7 us
    ppermute x5, waiting for transfers between devices, shifted(): lax.ppermute(value.astype(jnp.bfloat16), SEQ_AXES, pairs)  13 us
    all_to_all x1, waiting for transfers between devices, per_device(): lax.all_to_all(summed.reshape(dev_count, half, width), DEV_AXES, split_ax...  10.1 us
    all_to_all x1, waiting for transfers between devices, per_device(): lax.all_to_all(send_rows, DEV_AXES, split_axis=0, concat_axis=0, tiled=True)  9.66 us
  transfers between devices with their start and end apart: 15, of which 11 were waited for; matrix products, arithmetic and copies ran while one was open for 18% of the time, Pallas kernels for 0%

profile of v15, /device:TPU:2, one launch (start us, length us, event | category | flops | bytes accessed | tf_op | source)
XLA Modules:
  0.0 241.0 jit_solution(7717841982705203926)
XLA Ops:
  6.5 0.7 all-gather.11.cloned.1.call-update
  7.3 19.4 %all-gather.2 = s32[8,8,2]{1,2,0:T(2,128)S(1)} all-gather(s32[1,8,2]{1,2,0:T(2,128)} %bitcast.177), channel_id=3, replica_groups=mesh['y'=4,'x'=4,'c'=2,'e'=4,'p'=2] {'e','p'}, dimensions={0}, use_global_device_ids=true | all-gather | bytes 576 | tf_op jit(solution)/shard_map/all_gather | solution.py:74
  26.7 1.8 pad_maximum_fusion
  29.7 1.9 collective-permute-start.1
  33.0 3.0 %collective-permute-done.1 = bf16[4,129,128]{2,1,0:T(8,128)(2,1)S(1)} collective-permute-done((bf16[4,129,128]{2,1,0:T(8,128)(2,1)S(1)}, bf16[4,129,128]{2,1,0:T(8,128)(2,1)S(1)}, u32[]{:S(2)}, u32[]{:S(2)}) %collective-permute-start.1) | collective-permute-done | bytes 132128 | tf_op jit(solution)/shard_map/ppermute | solution.py:25
  36.3 3.4 %collective-permute-start.2 = (bf16[4,129,128]{2,1,0:T(8,128)(2,1)S(1)}, bf16[4,129,128]{2,1,0:T(8,128)(2,1)S(1)}, u32[]{:S(2)}, u32[]{:S(2)}) collective-permute-start(bf16[4,129,128]{2,1,0:T(8,128)(2,1)S(1)} %pad_maximum_fusion.3), channel_id=1, source_target_pairs={{0,16},{8,24},{16,32},{24,40},{32,48},{40,56},{48,64},{56,72},{64,... | collective-permute-start | bytes 396296 | tf_op jit(solution)/shard_map/ppermute | solution.py:25
  39.8 1.0 scatter_custom_fusion
  40.8 2.4 %collective-permute-done.2 = bf16[4,129,128]{2,1,0:T(8,128)(2,1)S(1)} collective-permute-done((bf16[4,129,128]{2,1,0:T(8,128)(2,1)S(1)}, bf16[4,129,128]{2,1,0:T(8,128)(2,1)S(1)}, u32[]{:S(2)}, u32[]{:S(2)}) %collective-permute-start.2) | collective-permute-done | bytes 132128 | tf_op jit(solution)/shard_map/ppermute | solution.py:25
  43.4 5.2 %collective-permute-start.3 = (bf16[4,129,128]{2,1,0:T(8,128)(2,1)S(1)}, bf16[4,129,128]{2,1,0:T(8,128)(2,1)S(1)}, u32[]{:S(2)}, u32[]{:S(2)}) collective-permute-start(bf16[4,129,128]{2,1,0:T(8,128)(2,1)S(1)} %pad_maximum_fusion.4), channel_id=1, source_target_pairs={{0,32},{8,40},{16,48},{24,56},{32,64},{40,72},{48,80},{56,88},{64,... | collective-permute-start | bytes 396296 | tf_op jit(solution)/shard_map/ppermute | solution.py:25
  48.7 2.4 collective-permute-done.3
  51.3 5.7 %collective-permute-start.4 = (bf16[4,129,128]{2,1,0:T(8,128)(2,1)S(1)}, bf16[4,129,128]{2,1,0:T(8,128)(2,1)S(1)}, u32[]{:S(2)}, u32[]{:S(2)}) collective-permute-start(bf16[4,129,128]{2,1,0:T(8,128)(2,1)S(1)} %pad_maximum_fusion.5), channel_id=1, source_target_pairs={{0,64},{8,72},{16,80},{24,88},{32,96},{40,104},{48,112},{56,120},{... | collective-permute-start | bytes 396296 | tf_op jit(solution)/shard_map/ppermute | solution.py:25
  57.0 2.5 %collective-permute-done.4 = bf16[4,129,128]{2,1,0:T(8,128)(2,1)S(1)} collective-permute-done((bf16[4,129,128]{2,1,0:T(8,128)(2,1)S(1)}, bf16[4,129,128]{2,1,0:T(8,128)(2,1)S(1)}, u32[]{:S(2)}, u32[]{:S(2)}) %collective-permute-start.4) | collective-permute-done | bytes 132128 | tf_op jit(solution)/shard_map/ppermute | solution.py:25
  59.7 6.0 %collective-permute-start.5 = (bf16[4,129,128]{2,1,0:T(8,128)(2,1)S(1)}, bf16[4,129,128]{2,1,0:T(8,128)(2,1)S(1)}, u32[]{:S(2)}, u32[]{:S(2)}) collective-permute-start(bf16[4,129,128]{2,1,0:T(8,128)(2,1)S(1)} %pad_maximum_fusion.6), channel_id=1, source_target_pairs={{0,128},{8,136},{16,144},{24,152},{32,160},{40,168},{48,176},{56,1... | collective-permute-start | bytes 396296 | tf_op jit(solution)/shard_map/ppermute | solution.py:25
  65.7 2.6 %collective-permute-done.5 = bf16[4,129,128]{2,1,0:T(8,128)(2,1)S(1)} collective-permute-done((bf16[4,129,128]{2,1,0:T(8,128)(2,1)S(1)}, bf16[4,129,128]{2,1,0:T(8,128)(2,1)S(1)}, u32[]{:S(2)}, u32[]{:S(2)}) %collective-permute-start.5) | collective-permute-done | bytes 132128 | tf_op jit(solution)/shard_map/ppermute | solution.py:25
  69.1 1.7 gather_fusion
  70.7 2.0 collective-permute-done
  72.7 3.4 %all-to-all-start = ((bf16[8,24,512]{2,1,0:T(8,128)(2,1)}), bf16[8,24,512]{2,1,0:T(8,128)(2,1)S(1)}, u32[]{:S(2)}, u32[]{:S(2)}) async-start(bf16[8,24,512]{2,1,0:T(8,128)(2,1)} %bitcast.21), calls=%async_computation | async-start | bytes 393216 | tf_op jit(solution)/shard_map/all_to_all | solution.py:133
  76.1 9.7 %all-to-all-done = bf16[8,24,512]{2,1,0:T(8,128)(2,1)S(1)} async-done(((bf16[8,24,512]{2,1,0:T(8,128)(2,1)}), bf16[8,24,512]{2,1,0:T(8,128)(2,1)S(1)}, u32[]{:S(2)}, u32[]{:S(2)}) %all-to-all-start) | async-done | bytes 196640 | tf_op jit(solution)/shard_map/all_to_all | solution.py:133
  85.8 2.0 broadcast_in_dim.61
  87.8 9.0 %all-to-all-start.1 = ((bf16[16,24,4096]{2,1,0:T(8,128)(2,1)}), bf16[16,24,4096]{2,1,0:T(8,128)(2,1)S(1)}, u32[]{:S(2)}, u32[]{:S(2)}) async-start(bf16[16,24,4096]{2,1,0:T(8,128)(2,1)} %broadcast_in_dim.61), calls=%async_computation.1 | async-start | bytes 6291456 | tf_op jit(solution)/shard_map/all_to_all | solution.py:141
  96.9 0.7 collective-permute-start.6
  97.6 3.2 %constant_dynamic-update-slice_fusion.1 = bf16[512,4096]{1,0:T(8,128)(2,1)} fusion(bf16[256,4096]{1,0:T(8,128)(2,1)} %bitcast.162), kind=kLoop, calls=%fused_computation.98 | loop fusion | bytes 4194304
  100.8 36.4 %collective-permute-done.6 = bf16[256,4096]{1,0:T(8,128)(2,1)} collective-permute-done((bf16[256,4096]{1,0:T(8,128)(2,1)}, bf16[256,4096]{1,0:T(8,128)(2,1)}, u32[]{:S(2)}, u32[]{:S(2)}) %collective-permute-start.6) | collective-permute-done | bytes 2097184 | tf_op jit(solution)/shard_map/ppermute | solution.py:135
  137.2 2.5 %fusion.77 = (bf16[16,12,4096]{2,1,0:T(8,128)(2,1)}, bf16[16,12,4096]{2,1,0:T(8,128)(2,1)}) fusion(bf16[16,24,4096]{2,1,0:T(8,128)(2,1)S(1)} %all-to-all-done.1), kind=kLoop, calls=%fused_computation.142 | loop fusion | bytes 6291456 | tf_op jit(solution)/shard_map/slice | solution.py:169
  139.7 3.8 %reshape.298 = bf16[192,4096]{1,0:T(8,128)(2,1)} reshape(bf16[16,12,4096]{2,1,0:T(8,128)(2,1)} %get-tuple-element.34) | data formatting | bytes 3145728 | tf_op jit(solution)/shard_map/reshape | solution.py:155
  143.5 1.3 reshape.296
  144.8 2.8 %fusion = f32[192,256]{1,0:T(8,128)S(1)} fusion(bf16[192,4096]{1,0:T(8,128)(2,1)} %reshape.298, bf16[2,4096,256]{2,1,0:T(8,128)(2,1)} %all-gather.7.cloned.1.call-done), kind=kOutput, calls=%fused_computation.10 | convolution fusion | flops 402653184 | bytes 3866624 | tf_op jit(solution)/shard_map/dot_general | solution.py:158
  147.6 2.2 fusion.12
  149.8 3.1 %constant_dynamic-update-slice_fusion = bf16[512,4096]{1,0:T(8,128)(2,1)} fusion(bf16[512,4096]{1,0:T(8,128)(2,1)} %constant_dynamic-update-slice_fusion.1, bf16[256,4096]{1,0:T(8,128)(2,1)} %collective-permute-done.6), kind=kLoop, calls=%fused_computation.97 | loop fusion | bytes 4194304 | tf_op jit(solution)/shard_map/concatenate | solution.py:150
  152.9 2.3 fusion.4
  155.7 0.6 fusion.14
  156.3 3.2 %convolution_convert_fusion = bf16[192,4096]{1,0:T(8,128)(2,1)S(1)} fusion(bf16[512,4096]{1,0:T(8,128)(2,1)} %constant_dynamic-update-slice_fusion, bf16[192,256]{1,0:T(8,128)(2,1)S(1)} %fusion.14, bf16[192,256]{1,0:T(8,128)(2,1)S(1)} %fusion.12), kind=kOutput, calls=%fused_computation.3 | convolution fusion | flops 806486016 | bytes 5963776 | tf_op jit(solution)/shard_map/dot_general | solution.py:163
  159.5 1.5 reshape.299
  161.1 7.2 %all-to-all-start.3 = ((bf16[16,12,4096]{2,1,0:T(8,128)(2,1)}), bf16[16,12,4096]{2,1,0:T(8,128)(2,1)S(1)}, u32[]{:S(2)}, u32[]{:S(2)}) async-start(bf16[16,12,4096]{2,1,0:T(8,128)(2,1)} %reshape.299), calls=%async_computation.3 | async-start | bytes 4194304 | tf_op jit(solution)/shard_map/all_to_all | solution.py:164
  168.3 2.8 %fusion.1 = f32[192,256]{1,0:T(8,128)S(1)} fusion(bf16[192,4096]{1,0:T(8,128)(2,1)} %reshape.296, bf16[2,4096,256]{2,1,0:T(8,128)(2,1)} %all-gather.7.cloned.1.call-done), kind=kOutput, calls=%fused_computation.11 | convolution fusion | flops 402653184 | bytes 3866624 | tf_op jit(solution)/shard_map/dot_general | solution.py:158
  171.1 2.4 fusion.13
  174.5 0.6 fusion.15
  175.1 4.3 %convolution_convert_fusion.1 = bf16[192,4096]{1,0:T(8,128)(2,1)} fusion(bf16[512,4096]{1,0:T(8,128)(2,1)} %constant_dynamic-update-slice_fusion, bf16[192,256]{1,0:T(8,128)(2,1)S(1)} %fusion.15, bf16[192,256]{1,0:T(8,128)(2,1)S(1)} %fusion.13), kind=kOutput, calls=%fused_computation.4 | convolution fusion | flops 806486016 | bytes 5963776 | tf_op jit(solution)/shard_map/dot_general | solution.py:163
  179.4 3.4 %reshape.297 = bf16[16,12,4096]{2,1,0:T(8,128)(2,1)} reshape(bf16[192,4096]{1,0:T(8,128)(2,1)} %convolution_convert_fusion.1) | data formatting | bytes 3145728 | tf_op jit(solution)/shard_map/reshape | solution.py:165
  182.8 5.6 %all-to-all-done.3 = bf16[16,12,4096]{2,1,0:T(8,128)(2,1)S(1)} async-done(((bf16[16,12,4096]{2,1,0:T(8,128)(2,1)}), bf16[16,12,4096]{2,1,0:T(8,128)(2,1)S(1)}, u32[]{:S(2)}, u32[]{:S(2)}) %all-to-all-start.3) | async-done | bytes 1572896 | tf_op jit(solution)/shard_map/all_to_all | solution.py:164
  188.4 7.5 %all-to-all-start.2 = ((bf16[16,12,4096]{2,1,0:T(8,128)(2,1)}), bf16[16,12,4096]{2,1,0:T(8,128)(2,1)}, u32[]{:S(2)}, u32[]{:S(2)}) async-start(bf16[16,12,4096]{2,1,0:T(8,128)(2,1)} %reshape.297), calls=%async_computation.2 | async-start | bytes 4194304 | tf_op jit(solution)/shard_map/all_to_all | solution.py:164
  196.3 19.6 %all-to-all-done.2 = bf16[16,12,4096]{2,1,0:T(8,128)(2,1)} async-done(((bf16[16,12,4096]{2,1,0:T(8,128)(2,1)}), bf16[16,12,4096]{2,1,0:T(8,128)(2,1)}, u32[]{:S(2)}, u32[]{:S(2)}) %all-to-all-start.2) | async-done | bytes 1572896 | tf_op jit(solution)/shard_map/all_to_all | solution.py:164
  215.8 2.0 reduce_sum.53
  217.9 0.8 reshape.300
  218.7 3.4 %all-to-all-start.4 = ((bf16[8,3,4096]{2,1,0:T(4,128)(2,1)}), bf16[8,3,4096]{2,1,0:T(4,128)(2,1)S(1)}, u32[]{:S(2)}, u32[]{:S(2)}) async-start(bf16[8,3,4096]{2,1,0:T(4,128)(2,1)} %reshape.300), calls=%async_computation.4 | async-start | bytes 524288 | tf_op jit(solution)/shard_map/all_to_all | solution.py:170
  222.4 10.1 %all-to-all-done.4 = bf16[8,3,4096]{2,1,0:T(4,128)(2,1)S(1)} async-done(((bf16[8,3,4096]{2,1,0:T(4,128)(2,1)}), bf16[8,3,4096]{2,1,0:T(4,128)(2,1)S(1)}, u32[]{:S(2)}, u32[]{:S(2)}) %all-to-all-start.4) | async-done | bytes 196640 | tf_op jit(solution)/shard_map/all_to_all | solution.py:170
  232.7 0.6 gather_fusion.1
  233.5 1.0 multiply_reduce_fusion
  (98 shorter events, 6.8 us)
Async XLA Ops:
  6.5 22.6 %copy-start = (bf16[64,512]{1,0:T(8,128)(2,1)S(1)}, bf16[64,512]{1,0:T(8,128)(2,1)}, u32[]{:S(2)}) copy-start(bf16[64,512]{1,0:T(8,128)(2,1)} %param.12) | copy-start | bytes 196612
  6.5 69.6 %all-gather.11.cloned.1.call-start = ((), (), s32[]{:S(2)}) async-start(), calls=%async_computation.7 | async-start | bytes 3145728 | tf_op jit(solution)/shard_map/all_gather | solution.py:79
  7.3 137.6 %all-gather.7.cloned.1.call-start = ((), (), s32[]{:S(2)}) async-start(), calls=%async_computation.5 | async-start | bytes 6291456 | tf_op jit(solution)/shard_map/all_gather | solution.py:78
  26.7 1.9 copy-start.8
  26.7 2.4 %copy-start.5 = (bf16[64,512]{1,0:T(8,128)(2,1)S(1)}, bf16[64,512]{1,0:T(8,128)(2,1)}, u32[]{:S(2)}) copy-start(bf16[64,512]{1,0:T(8,128)(2,1)} %param.11) | copy-start | bytes 196612
  28.5 3.1 %copy-start.1 = (bf16[2,4096,128]{2,1,0:T(8,128)(2,1)}, bf16[2,4096,128]{2,1,0:T(8,128)(2,1)S(1)}, u32[]{:S(2)}) copy-start(bf16[2,4096,128]{2,1,0:T(8,128)(2,1)S(1)} %pad_maximum_fusion) | copy-start | bytes 6291460
  28.5 44.2 %collective-permute-start = (bf16[2,4096,128]{2,1,0:T(8,128)(2,1)S(1)}, bf16[2,4096,128]{2,1,0:T(8,128)(2,1)}, u32[]{:S(2)}, u32[]{:S(2)}) collective-permute-start(bf16[2,4096,128]{2,1,0:T(8,128)(2,1)S(1)} %pad_maximum_fusion), channel_id=1, source_target_pairs={{0,1},{1,0},{2,3},{3,2},{4,5},{5,4},{6,7},{7,6},{8,9},{9,8},{10,11... | collective-permute-start | bytes 6291464 | tf_op jit(solution)/shard_map/ppermute | solution.py:80
  29.7 6.4 %collective-permute-start.1 = (bf16[4,129,128]{2,1,0:T(8,128)(2,1)S(1)}, bf16[4,129,128]{2,1,0:T(8,128)(2,1)S(1)}, u32[]{:S(2)}, u32[]{:S(2)}) collective-permute-start(bf16[4,129,128]{2,1,0:T(8,128)(2,1)S(1)} %pad_maximum_fusion.2), channel_id=1, source_target_pairs={{0,8},{8,16},{16,24},{24,32},{32,40},{40,48},{48,56},{56,64},{64,7... | collective-permute-start | bytes 396296 | tf_op jit(solution)/shard_map/ppermute | solution.py:25
  31.6 16.9 %copy-start.6 = (bf16[64,512]{1,0:T(8,128)(2,1)S(1)}, bf16[64,512]{1,0:T(8,128)(2,1)}, u32[]{:S(2)}) copy-start(bf16[64,512]{1,0:T(8,128)(2,1)} %param.10) | copy-start | bytes 196612
  36.3 6.9 %collective-permute-start.2 = (bf16[4,129,128]{2,1,0:T(8,128)(2,1)S(1)}, bf16[4,129,128]{2,1,0:T(8,128)(2,1)S(1)}, u32[]{:S(2)}, u32[]{:S(2)}) collective-permute-start(bf16[4,129,128]{2,1,0:T(8,128)(2,1)S(1)} %pad_maximum_fusion.3), channel_id=1, source_target_pairs={{0,16},{8,24},{16,32},{24,40},{32,48},{40,56},{48,64},{56,72},{64,... | collective-permute-start | bytes 396296 | tf_op jit(solution)/shard_map/ppermute | solution.py:25
  43.4 7.8 %collective-permute-start.3 = (bf16[4,129,128]{2,1,0:T(8,128)(2,1)S(1)}, bf16[4,129,128]{2,1,0:T(8,128)(2,1)S(1)}, u32[]{:S(2)}, u32[]{:S(2)}) collective-permute-start(bf16[4,129,128]{2,1,0:T(8,128)(2,1)S(1)} %pad_maximum_fusion.4), channel_id=1, source_target_pairs={{0,32},{8,40},{16,48},{24,56},{32,64},{40,72},{48,80},{56,88},{64,... | collective-permute-start | bytes 396296 | tf_op jit(solution)/shard_map/ppermute | solution.py:25
  51.2 17.7 %copy-start.7 = (f32[512]{0:T(512)S(1)}, f32[512]{0:T(512)}, u32[]{:S(2)}) copy-start(f32[512]{0:T(512)} %param.14) | copy-start | bytes 6148
  51.3 8.3 %collective-permute-start.4 = (bf16[4,129,128]{2,1,0:T(8,128)(2,1)S(1)}, bf16[4,129,128]{2,1,0:T(8,128)(2,1)S(1)}, u32[]{:S(2)}, u32[]{:S(2)}) collective-permute-start(bf16[4,129,128]{2,1,0:T(8,128)(2,1)S(1)} %pad_maximum_fusion.5), channel_id=1, source_target_pairs={{0,64},{8,72},{16,80},{24,88},{32,96},{40,104},{48,112},{56,120},{... | collective-permute-start | bytes 396296 | tf_op jit(solution)/shard_map/ppermute | solution.py:25
  59.7 8.6 %collective-permute-start.5 = (bf16[4,129,128]{2,1,0:T(8,128)(2,1)S(1)}, bf16[4,129,128]{2,1,0:T(8,128)(2,1)S(1)}, u32[]{:S(2)}, u32[]{:S(2)}) collective-permute-start(bf16[4,129,128]{2,1,0:T(8,128)(2,1)S(1)} %pad_maximum_fusion.6), channel_id=1, source_target_pairs={{0,128},{8,136},{16,144},{24,152},{32,160},{40,168},{48,176},{56,1... | collective-permute-start | bytes 396296 | tf_op jit(solution)/shard_map/ppermute | solution.py:25
  72.7 13.1 %all-to-all-start = ((bf16[8,24,512]{2,1,0:T(8,128)(2,1)}), bf16[8,24,512]{2,1,0:T(8,128)(2,1)S(1)}, u32[]{:S(2)}, u32[]{:S(2)}) async-start(bf16[8,24,512]{2,1,0:T(8,128)(2,1)} %bitcast.21), calls=%async_computation | async-start | bytes 393216 | tf_op jit(solution)/shard_map/all_to_all | solution.py:133
  87.8 49.3 %all-to-all-start.1 = ((bf16[16,24,4096]{2,1,0:T(8,128)(2,1)}), bf16[16,24,4096]{2,1,0:T(8,128)(2,1)S(1)}, u32[]{:S(2)}, u32[]{:S(2)}) async-start(bf16[16,24,4096]{2,1,0:T(8,128)(2,1)} %broadcast_in_dim.61), calls=%async_computation.1 | async-start | bytes 6291456 | tf_op jit(solution)/shard_map/all_to_all | solution.py:141
  96.8 56.1 %all-gather.9.cloned.1.call-start = ((), (), s32[]{:S(2)}) async-start(), calls=%async_computation.6 | async-start | bytes 6291456 | tf_op jit(solution)/shard_map/all_gather | solution.py:132
  96.9 40.3 %collective-permute-start.6 = (bf16[256,4096]{1,0:T(8,128)(2,1)}, bf16[256,4096]{1,0:T(8,128)(2,1)}, u32[]{:S(2)}, u32[]{:S(2)}) collective-permute-start(bf16[256,4096]{1,0:T(8,128)(2,1)} %bitcast.161), channel_id=1, source_target_pairs={{0,1},{1,0},{2,3},{3,2},{4,5},{5,4},{6,7},{7,6},{8,9},{9,8},{10,11... | collective-permute-start | bytes 6291464 | tf_op jit(solution)/shard_map/ppermute | solution.py:135
  139.7 3.8 %copy-start.2 = (bf16[16,12,4096]{2,1,0:T(8,128)(2,1)S(1)}, bf16[16,12,4096]{2,1,0:T(8,128)(2,1)}, u32[]{:S(2)}) copy-start(bf16[16,12,4096]{2,1,0:T(8,128)(2,1)} %get-tuple-element.33) | copy-start | bytes 4718596
  144.8 2.8 %copy-start.4 = (bf16[192,4096]{1,0:T(8,128)(2,1)S(1)}, bf16[192,4096]{1,0:T(8,128)(2,1)}, u32[]{:S(2)}) copy-start(bf16[192,4096]{1,0:T(8,128)(2,1)} %reshape.298) | copy-start | bytes 4718596
  152.9 2.8 %copy-start.10 = (bf16[2,4096,256]{2,1,0:T(8,128)(2,1)S(1)}, bf16[2,4096,256]{2,1,0:T(8,128)(2,1)}, u32[]{:S(2)}) copy-start(bf16[2,4096,256]{2,1,0:T(8,128)(2,1)} %all-gather.9.cloned.1.call-done) | copy-start | bytes 12582916
  161.1 27.3 %all-to-all-start.3 = ((bf16[16,12,4096]{2,1,0:T(8,128)(2,1)}), bf16[16,12,4096]{2,1,0:T(8,128)(2,1)S(1)}, u32[]{:S(2)}, u32[]{:S(2)}) async-start(bf16[16,12,4096]{2,1,0:T(8,128)(2,1)} %reshape.299), calls=%async_computation.3 | async-start | bytes 4194304 | tf_op jit(solution)/shard_map/all_to_all | solution.py:164
  168.3 2.8 %copy-start.3 = (bf16[192,4096]{1,0:T(8,128)(2,1)S(1)}, bf16[192,4096]{1,0:T(8,128)(2,1)}, u32[]{:S(2)}) copy-start(bf16[192,4096]{1,0:T(8,128)(2,1)} %reshape.296) | copy-start | bytes 4718596
  171.1 2.8 %copy-start.11 = (bf16[2,4096,256]{2,1,0:T(8,128)(2,1)S(1)}, bf16[2,4096,256]{2,1,0:T(8,128)(2,1)}, u32[]{:S(2)}) copy-start(bf16[2,4096,256]{2,1,0:T(8,128)(2,1)} %all-gather.9.cloned.1.call-done) | copy-start | bytes 12582916
  188.4 27.5 %all-to-all-start.2 = ((bf16[16,12,4096]{2,1,0:T(8,128)(2,1)}), bf16[16,12,4096]{2,1,0:T(8,128)(2,1)}, u32[]{:S(2)}, u32[]{:S(2)}) async-start(bf16[16,12,4096]{2,1,0:T(8,128)(2,1)} %reshape.297), calls=%async_computation.2 | async-start | bytes 4194304 | tf_op jit(solution)/shard_map/all_to_all | solution.py:164
  196.2 25.9 %copy-start.9 = (f32[8,2]{0,1:T(2,128)S(1)}, f32[8,2]{0,1:T(2,128)}, u32[]{:S(2)}) copy-start(f32[8,2]{0,1:T(2,128)} %param.19) | copy-start | bytes 196
  218.7 13.8 %all-to-all-start.4 = ((bf16[8,3,4096]{2,1,0:T(4,128)(2,1)}), bf16[8,3,4096]{2,1,0:T(4,128)(2,1)S(1)}, u32[]{:S(2)}, u32[]{:S(2)}) async-start(bf16[8,3,4096]{2,1,0:T(4,128)(2,1)} %reshape.300), calls=%async_computation.4 | async-start | bytes 524288 | tf_op jit(solution)/shard_map/all_to_all | solution.py:170
Sparse Core Ops, SparseCore 0:
  9.2 18.8 all-gather.10
  31.8 18.6 all-gather.6
  99.4 14.4 all-gather.8

commit v16 on v14

--- a/solution.py
+++ b/solution.py
@@ -128,9 +128,9 @@
     )
     padded = jnp.concatenate([normed, jnp.zeros((1, normed.shape[1]), normed.dtype)], axis=0)
     send_rows = padded[slot_token].reshape(dev_count, per_dev, -1)
-    gate_up_far, send_rows = lax.optimization_barrier((gate_up_far, send_rows))
+    arrived = lax.all_to_all(send_rows, DEV_AXES, split_axis=0, concat_axis=0, tiled=True)
+    gate_up_far, arrived = lax.optimization_barrier((gate_up_far, arrived))
     gate_up_far = lax.all_gather(gate_up_far, "c", axis=2, tiled=True)
-    arrived = lax.all_to_all(send_rows, DEV_AXES, split_axis=0, concat_axis=0, tiled=True)
     down_core, arrived = lax.optimization_barrier((down_core, arrived))
     down_far = lax.ppermute(down_core, "p", partner)
     local_rows = jnp.transpose(arrived, (1, 0, 2)).reshape(per_dev, -1)

time: 211 us -> 208 us (0.986)
  blocking collectives: 56.5 us -> 70.1 us
  waiting for transfers between devices: 75 us -> 62.5 us
  starting transfers between devices: 38.8 us -> 35.8 us
    all_to_all x0 -> x1, blocking collectives: none -> 14.4 us  [per_device(): lax.all_to_all(send_rows, DEV_AXES, split_axis=0, concat_axis=0, tiled=True)]
    all_to_all x1 -> x0, waiting for transfers between devices: 9.66 us -> none  [per_device(): lax.all_to_all(send_rows, DEV_AXES, split_axis=0, concat_axis=0, tiled=True)]
    all_to_all x1 -> x0, starting transfers between devices: 3.4 us -> none  [per_device(): lax.all_to_all(send_rows, DEV_AXES, split_axis=0, concat_axis=0, tiled=True)]
  transfers between devices with their start and end apart: 13 -> 12, of which waited for: 9 -> 7; matrix products, arithmetic and copies ran while one was open for 7% -> 7% of each run, Pallas kernels for 0% -> 0%
where the time goes in v16:
time: 208 us
  blocking collectives  70.1 us (34%)
  waiting for transfers between devices  62.5 us (30%)
  starting transfers between devices  35.8 us (17%)
  between operations  13.6 us (7%)
  matrix products  13.4 us (6%)
  local copies, waits for them, and re-layouts  7.45 us (4%)
  other arithmetic  5.08 us (2%)
    ppermute x1, waiting for transfers between devices, per_device(): down_far = lax.ppermute(down_core, 'p', partner)  38.7 us
    all_to_all x1, blocking collectives, per_device(): lax.all_to_all(term.reshape(groups, per_dev, width), TOK_AXES, split_axis...  36.3 us
    ppermute x5, starting transfers between devices, shifted(): lax.ppermute(value.astype(jnp.bfloat16), SEQ_AXES, pairs)  22.2 us
    all_gather x1, blocking collectives, per_device(): ids_all = lax.all_gather(expert_ids, DEV_AXES, axis=0, tiled=False)  19.4 us
    all_to_all x1, blocking collectives, per_device(): lax.all_to_all(send_rows, DEV_AXES, split_axis=0, concat_axis=0, tiled=True)  14.4 us
    ppermute x5, waiting for transfers between devices, shifted(): lax.ppermute(value.astype(jnp.bfloat16), SEQ_AXES, pairs)  12.9 us
    all_to_all x1, waiting for transfers between devices, per_device(): lax.all_to_all(summed.reshape(dev_count, half, width), DEV_AXES, split_ax...  10.1 us
    all_to_all x1, starting transfers between devices, per_device(): lax.all_to_all(jnp.broadcast_to(local_rows[None], (groups,) + local_rows....  9.44 us
  transfers between devices with their start and end apart: 12, of which 7 were waited for; matrix products, arithmetic and copies ran while one was open for 7% of the time, Pallas kernels for 0%

profile of v16, /device:TPU:2, one launch (start us, length us, event | category | flops | bytes accessed | tf_op | source)
XLA Modules:
  0.0 207.9 jit_solution(6871030161930107329)
XLA Ops:
  6.5 0.7 all-gather.11.cloned.1.call-update
  7.3 19.4 %all-gather.2 = s32[8,8,2]{1,2,0:T(2,128)S(1)} all-gather(s32[1,8,2]{1,2,0:T(2,128)} %bitcast.159), channel_id=3, replica_groups=mesh['y'=4,'x'=4,'c'=2,'e'=4,'p'=2] {'e','p'}, dimensions={0}, use_global_device_ids=true | all-gather | bytes 576 | tf_op jit(solution)/shard_map/all_gather | solution.py:74
  26.7 1.7 pad_maximum_fusion
  28.5 0.1 collective-permute-start
  28.6 0.2 reduce_window_sum.22
  28.8 0.2 exponential_reduce_fusion
  29.1 0.5 fusion.64
  29.7 1.9 collective-permute-start.1
  31.8 0.4 fusion.65
  32.5 0.1 copy.55
  32.7 0.1 mul.252
  33.0 3.0 %collective-permute-done.1 = bf16[4,129,128]{2,1,0:T(8,128)(2,1)S(1)} collective-permute-done((bf16[4,129,128]{2,1,0:T(8,128)(2,1)S(1)}, bf16[4,129,128]{2,1,0:T(8,128)(2,1)S(1)}, u32[]{:S(2)}, u32[]{:S(2)}) %collective-permute-start.1) | collective-permute-done | bytes 132128 | tf_op jit(solution)/shard_map/ppermute | solution.py:25
  36.1 0.1 fusion.63
  36.3 3.4 %collective-permute-start.2 = (bf16[4,129,128]{2,1,0:T(8,128)(2,1)S(1)}, bf16[4,129,128]{2,1,0:T(8,128)(2,1)S(1)}, u32[]{:S(2)}, u32[]{:S(2)}) collective-permute-start(bf16[4,129,128]{2,1,0:T(8,128)(2,1)S(1)} %pad_maximum_fusion.2), channel_id=1, source_target_pairs={{0,16},{8,24},{16,32},{24,40},{32,48},{40,56},{48,64},{56,72},{64,... | collective-permute-start | bytes 396296 | tf_op jit(solution)/shard_map/ppermute | solution.py:25
  39.8 1.0 scatter_custom_fusion
  40.8 2.4 %collective-permute-done.2 = bf16[4,129,128]{2,1,0:T(8,128)(2,1)S(1)} collective-permute-done((bf16[4,129,128]{2,1,0:T(8,128)(2,1)S(1)}, bf16[4,129,128]{2,1,0:T(8,128)(2,1)S(1)}, u32[]{:S(2)}, u32[]{:S(2)}) %collective-permute-start.2) | collective-permute-done | bytes 132128 | tf_op jit(solution)/shard_map/ppermute | solution.py:25
  43.3 5.2 %collective-permute-start.3 = (bf16[4,129,128]{2,1,0:T(8,128)(2,1)S(1)}, bf16[4,129,128]{2,1,0:T(8,128)(2,1)S(1)}, u32[]{:S(2)}, u32[]{:S(2)}) collective-permute-start(bf16[4,129,128]{2,1,0:T(8,128)(2,1)S(1)} %pad_maximum_fusion.3), channel_id=1, source_target_pairs={{0,32},{8,40},{16,48},{24,56},{32,64},{40,72},{48,80},{56,88},{64,... | collective-permute-start | bytes 396296 | tf_op jit(solution)/shard_map/ppermute | solution.py:25
  48.5 0.2 convolution_multiply_fusion
  48.7 2.4 %collective-permute-done.3 = bf16[4,129,128]{2,1,0:T(8,128)(2,1)S(1)} collective-permute-done((bf16[4,129,128]{2,1,0:T(8,128)(2,1)S(1)}, bf16[4,129,128]{2,1,0:T(8,128)(2,1)S(1)}, u32[]{:S(2)}, u32[]{:S(2)}) %collective-permute-start.3) | collective-permute-done | bytes 132128 | tf_op jit(solution)/shard_map/ppermute | solution.py:25
  51.3 5.7 %collective-permute-start.4 = (bf16[4,129,128]{2,1,0:T(8,128)(2,1)S(1)}, bf16[4,129,128]{2,1,0:T(8,128)(2,1)S(1)}, u32[]{:S(2)}, u32[]{:S(2)}) collective-permute-start(bf16[4,129,128]{2,1,0:T(8,128)(2,1)S(1)} %pad_maximum_fusion.4), channel_id=1, source_target_pairs={{0,64},{8,72},{16,80},{24,88},{32,96},{40,104},{48,112},{56,120},{... | collective-permute-start | bytes 396296 | tf_op jit(solution)/shard_map/ppermute | solution.py:25
  57.0 2.5 %collective-permute-done.4 = bf16[4,129,128]{2,1,0:T(8,128)(2,1)S(1)} collective-permute-done((bf16[4,129,128]{2,1,0:T(8,128)(2,1)S(1)}, bf16[4,129,128]{2,1,0:T(8,128)(2,1)S(1)}, u32[]{:S(2)}, u32[]{:S(2)}) %collective-permute-start.4) | collective-permute-done | bytes 132128 | tf_op jit(solution)/shard_map/ppermute | solution.py:25
  59.7 6.0 %collective-permute-start.5 = (bf16[4,129,128]{2,1,0:T(8,128)(2,1)S(1)}, bf16[4,129,128]{2,1,0:T(8,128)(2,1)S(1)}, u32[]{:S(2)}, u32[]{:S(2)}) collective-permute-start(bf16[4,129,128]{2,1,0:T(8,128)(2,1)S(1)} %pad_maximum_fusion.5), channel_id=1, source_target_pairs={{0,128},{8,136},{16,144},{24,152},{32,160},{40,168},{48,176},{56,1... | collective-permute-start | bytes 396296 | tf_op jit(solution)/shard_map/ppermute | solution.py:25
  65.7 2.6 %collective-permute-done.5 = bf16[4,129,128]{2,1,0:T(8,128)(2,1)S(1)} collective-permute-done((bf16[4,129,128]{2,1,0:T(8,128)(2,1)S(1)}, bf16[4,129,128]{2,1,0:T(8,128)(2,1)S(1)}, u32[]{:S(2)}, u32[]{:S(2)}) %collective-permute-start.5) | collective-permute-done | bytes 132128 | tf_op jit(solution)/shard_map/ppermute | solution.py:25
  68.2 0.3 fusion.11
  68.6 0.3 fusion.27
  68.9 0.1 copy_bitcast_fusion
  69.1 1.0 gather_fusion
  70.1 14.4 %all_to_all.20 = bf16[8,24,512]{2,1,0:T(8,128)(2,1)S(1)} all-to-all(bf16[8,24,512]{2,1,0:T(8,128)(2,1)S(1)} %bitcast.144), channel_id=1, replica_groups=mesh['y'=4,'x'=4,'c'=2,'e'=4,'p'=2] {'e','p'}, dimensions={0} | all-to-all | bytes 393216 | tf_op jit(solution)/shard_map/all_to_all | solution.py:131
  84.5 2.1 %broadcast_in_dim.61 = bf16[16,24,4096]{2,1,0:T(8,128)(2,1)} broadcast(bf16[24,4096]{1,0:T(8,128)(2,1)S(1)} %bitcast.145), dimensions={1,2} | broadcast | bytes 3342336 | tf_op jit(solution)/shard_map/broadcast_in_dim | solution.py:142
  86.6 9.4 %all-to-all-start.1 = ((bf16[16,24,4096]{2,1,0:T(8,128)(2,1)}), bf16[16,24,4096]{2,1,0:T(8,128)(2,1)S(1)}, u32[]{:S(2)}, u32[]{:S(2)}) async-start(bf16[16,24,4096]{2,1,0:T(8,128)(2,1)} %broadcast_in_dim.61), calls=%async_computation.1 | async-start | bytes 6291456 | tf_op jit(solution)/shard_map/all_to_all | solution.py:141
  96.1 0.6 collective-permute-start.6
  96.6 38.7 %collective-permute-done.6 = bf16[256,4096]{1,0:T(8,128)(2,1)} collective-permute-done((bf16[256,4096]{1,0:T(8,128)(2,1)}, bf16[256,4096]{1,0:T(8,128)(2,1)}, u32[]{:S(2)}, u32[]{:S(2)}) %collective-permute-start.6) | collective-permute-done | bytes 2097184 | tf_op jit(solution)/shard_map/ppermute | solution.py:135
  135.3 3.0 %fusion.6 = f32[384,256]{0,1:T(8,128)S(1)} fusion(bf16[384,4096]{1,0:T(8,128)(2,1)S(1)} %bitcast.139, bf16[2,4096,256]{2,1,0:T(8,128)(2,1)} %all-gather.7.cloned.1.call-done), kind=kOutput, calls=%fused_computation.14 | convolution fusion | flops 805306368 | bytes 5636096 | tf_op jit(solution)/shard_map/dot_general | solution.py:151
  138.4 1.3 multiply_convert_fusion.1
  139.7 3.0 %fusion.4 = f32[384,256]{0,1:T(8,128)S(1)} fusion(bf16[384,4096]{1,0:T(8,128)(2,1)S(1)} %bitcast.141, bf16[2,4096,256]{2,1,0:T(8,128)(2,1)} %all-gather.9.cloned.1.call-done), kind=kOutput, calls=%fused_computation.10 | convolution fusion | flops 805306368 | bytes 5636096 | tf_op jit(solution)/shard_map/dot_general | solution.py:151
  142.8 1.3 multiply_convert_fusion
  144.1 0.3 copy-done.9
  144.4 3.4 %convolution_convert_fusion = bf16[384,4096]{1,0:T(8,128)(2,1)S(1)} fusion(bf16[256,4096]{1,0:T(8,128)(2,1)} %collective-permute-done.6, bf16[256,4096]{1,0:T(8,128)(2,1)S(1)} %bitcast.161, bf16[384,256]{0,1:T(8,128)(2,1)S(1)} %multiply_convert_fusion, bf16[384,256]{0,1:T(8,128)(2,1)S(1)} %multiply_convert_fusion.1), kind=kOutput, calls=%fused_computation.3 | convolution fusion | flops 1621360640 | bytes 7733248 | tf_op jit(solution)/shard_map/dot_general | solution.py:157
  147.8 36.3 %all_to_all.21 = bf16[16,24,4096]{2,1,0:T(8,128)(2,1)S(1)} all-to-all(bf16[16,24,4096]{2,1,0:T(8,128)(2,1)S(1)} %bitcast.143), channel_id=1, replica_groups=mesh['y'=4,'x'=4,'c'=2,'e'=4,'p'=2] {'y','x'}, dimensions={0} | all-to-all | bytes 6291456 | tf_op jit(solution)/shard_map/all_to_all | solution.py:158
  184.1 0.6 reduce_sum.41
  184.7 0.8 reshape.284
  185.5 3.4 %all-to-all-start.3 = ((bf16[8,3,4096]{2,1,0:T(4,128)(2,1)}), bf16[8,3,4096]{2,1,0:T(4,128)(2,1)S(1)}, u32[]{:S(2)}, u32[]{:S(2)}) async-start(bf16[8,3,4096]{2,1,0:T(4,128)(2,1)} %reshape.284), calls=%async_computation.3 | async-start | bytes 524288 | tf_op jit(solution)/shard_map/all_to_all | solution.py:162
  189.0 0.2 add_reduce_fusion
  189.3 10.1 %all-to-all-done.3 = bf16[8,3,4096]{2,1,0:T(4,128)(2,1)S(1)} async-done(((bf16[8,3,4096]{2,1,0:T(4,128)(2,1)}), bf16[8,3,4096]{2,1,0:T(4,128)(2,1)S(1)}, u32[]{:S(2)}, u32[]{:S(2)}) %all-to-all-start.3) | async-done | bytes 196640 | tf_op jit(solution)/shard_map/all_to_all | solution.py:162
  199.3 0.2 reshape.285
  199.5 0.6 gather_fusion.1
  200.1 0.2 reshape.286
  200.3 1.0 multiply_reduce_fusion
  (76 shorter events, 1.7 us)
Async XLA Ops:
  6.5 22.6 %copy-start = (bf16[64,512]{1,0:T(8,128)(2,1)S(1)}, bf16[64,512]{1,0:T(8,128)(2,1)}, u32[]{:S(2)}) copy-start(bf16[64,512]{1,0:T(8,128)(2,1)} %param.12) | copy-start | bytes 196612
  6.5 22.0 %copy-start.5 = (f32[64,4]{0,1:T(4,128)S(1)}, f32[64,4]{0,1:T(4,128)}, u32[]{:S(2)}) copy-start(f32[64,4]{0,1:T(4,128)} %param.13) | copy-start | bytes 3076
  6.5 22.6 %copy-start.2 = (bf16[64,512]{1,0:T(8,128)(2,1)S(1)}, bf16[64,512]{1,0:T(8,128)(2,1)}, u32[]{:S(2)}) copy-start(bf16[64,512]{1,0:T(8,128)(2,1)} %param.11) | copy-start | bytes 196612
  6.5 78.0 %all-gather.11.cloned.1.call-start = ((), (), s32[]{:S(2)}) async-start(), calls=%async_computation.6 | async-start | bytes 3145728 | tf_op jit(solution)/shard_map/all_gather | solution.py:79
  7.3 128.1 %all-gather.7.cloned.1.call-start = ((), (), s32[]{:S(2)}) async-start(), calls=%async_computation.4 | async-start | bytes 6291456 | tf_op jit(solution)/shard_map/all_gather | solution.py:78
  28.4 3.2 %copy-start.1 = (bf16[2,4096,128]{2,1,0:T(8,128)(2,1)}, bf16[2,4096,128]{2,1,0:T(8,128)(2,1)S(1)}, u32[]{:S(2)}) copy-start(bf16[2,4096,128]{2,1,0:T(8,128)(2,1)S(1)} %pad_maximum_fusion) | copy-start | bytes 6291460
  28.4 20.1 %copy-start.3 = (bf16[64,512]{1,0:T(8,128)(2,1)S(1)}, bf16[64,512]{1,0:T(8,128)(2,1)}, u32[]{:S(2)}) copy-start(bf16[64,512]{1,0:T(8,128)(2,1)} %param.10) | copy-start | bytes 196612
  28.5 56.0 %collective-permute-start = (bf16[2,4096,128]{2,1,0:T(8,128)(2,1)S(1)}, bf16[2,4096,128]{2,1,0:T(8,128)(2,1)}, u32[]{:S(2)}, u32[]{:S(2)}) collective-permute-start(bf16[2,4096,128]{2,1,0:T(8,128)(2,1)S(1)} %pad_maximum_fusion), channel_id=1, source_target_pairs={{0,1},{1,0},{2,3},{3,2},{4,5},{5,4},{6,7},{7,6},{8,9},{9,8},{10,11... | collective-permute-start | bytes 6291464 | tf_op jit(solution)/shard_map/ppermute | solution.py:80
  29.7 6.4 %collective-permute-start.1 = (bf16[4,129,128]{2,1,0:T(8,128)(2,1)S(1)}, bf16[4,129,128]{2,1,0:T(8,128)(2,1)S(1)}, u32[]{:S(2)}, u32[]{:S(2)}) collective-permute-start(bf16[4,129,128]{2,1,0:T(8,128)(2,1)S(1)} %pad_maximum_fusion.1), channel_id=1, source_target_pairs={{0,8},{8,16},{16,24},{24,32},{32,40},{40,48},{48,56},{56,64},{64,7... | collective-permute-start | bytes 396296 | tf_op jit(solution)/shard_map/ppermute | solution.py:25
  31.6 108.1 %all-gather.9.cloned.1.call-start = ((), (), s32[]{:S(2)}) async-start(), calls=%async_computation.5 | async-start | bytes 6291456 | tf_op jit(solution)/shard_map/all_gather | solution.py:133
  36.3 6.9 %collective-permute-start.2 = (bf16[4,129,128]{2,1,0:T(8,128)(2,1)S(1)}, bf16[4,129,128]{2,1,0:T(8,128)(2,1)S(1)}, u32[]{:S(2)}, u32[]{:S(2)}) collective-permute-start(bf16[4,129,128]{2,1,0:T(8,128)(2,1)S(1)} %pad_maximum_fusion.2), channel_id=1, source_target_pairs={{0,16},{8,24},{16,32},{24,40},{32,48},{40,56},{48,64},{56,72},{64,... | collective-permute-start | bytes 396296 | tf_op jit(solution)/shard_map/ppermute | solution.py:25
  43.3 25.6 %copy-start.4 = (f32[512]{0:T(512)S(1)}, f32[512]{0:T(512)}, u32[]{:S(2)}) copy-start(f32[512]{0:T(512)} %param.14) | copy-start | bytes 6148
  43.3 7.8 %collective-permute-start.3 = (bf16[4,129,128]{2,1,0:T(8,128)(2,1)S(1)}, bf16[4,129,128]{2,1,0:T(8,128)(2,1)S(1)}, u32[]{:S(2)}, u32[]{:S(2)}) collective-permute-start(bf16[4,129,128]{2,1,0:T(8,128)(2,1)S(1)} %pad_maximum_fusion.3), channel_id=1, source_target_pairs={{0,32},{8,40},{16,48},{24,56},{32,64},{40,72},{48,80},{56,88},{64,... | collective-permute-start | bytes 396296 | tf_op jit(solution)/shard_map/ppermute | solution.py:25
  51.3 8.3 %collective-permute-start.4 = (bf16[4,129,128]{2,1,0:T(8,128)(2,1)S(1)}, bf16[4,129,128]{2,1,0:T(8,128)(2,1)S(1)}, u32[]{:S(2)}, u32[]{:S(2)}) collective-permute-start(bf16[4,129,128]{2,1,0:T(8,128)(2,1)S(1)} %pad_maximum_fusion.4), channel_id=1, source_target_pairs={{0,64},{8,72},{16,80},{24,88},{32,96},{40,104},{48,112},{56,120},{... | collective-permute-start | bytes 396296 | tf_op jit(solution)/shard_map/ppermute | solution.py:25
  59.7 8.6 %collective-permute-start.5 = (bf16[4,129,128]{2,1,0:T(8,128)(2,1)S(1)}, bf16[4,129,128]{2,1,0:T(8,128)(2,1)S(1)}, u32[]{:S(2)}, u32[]{:S(2)}) collective-permute-start(bf16[4,129,128]{2,1,0:T(8,128)(2,1)S(1)} %pad_maximum_fusion.5), channel_id=1, source_target_pairs={{0,128},{8,136},{16,144},{24,152},{32,160},{40,168},{48,176},{56,1... | collective-permute-start | bytes 396296 | tf_op jit(solution)/shard_map/ppermute | solution.py:25
  86.6 48.7 %all-to-all-start.1 = ((bf16[16,24,4096]{2,1,0:T(8,128)(2,1)}), bf16[16,24,4096]{2,1,0:T(8,128)(2,1)S(1)}, u32[]{:S(2)}, u32[]{:S(2)}) async-start(bf16[16,24,4096]{2,1,0:T(8,128)(2,1)} %broadcast_in_dim.61), calls=%async_computation.1 | async-start | bytes 6291456 | tf_op jit(solution)/shard_map/all_to_all | solution.py:141
  96.1 39.3 %collective-permute-start.6 = (bf16[256,4096]{1,0:T(8,128)(2,1)}, bf16[256,4096]{1,0:T(8,128)(2,1)}, u32[]{:S(2)}, u32[]{:S(2)}) collective-permute-start(bf16[256,4096]{1,0:T(8,128)(2,1)} %bitcast.160), channel_id=1, source_target_pairs={{0,1},{1,0},{2,3},{3,2},{4,5},{5,4},{6,7},{7,6},{8,9},{9,8},{10,11... | collective-permute-start | bytes 6291464 | tf_op jit(solution)/shard_map/ppermute | solution.py:135
  135.3 3.0 %copy-start.7 = (bf16[2,4096,256]{2,1,0:T(8,128)(2,1)S(1)}, bf16[2,4096,256]{2,1,0:T(8,128)(2,1)}, u32[]{:S(2)}) copy-start(bf16[2,4096,256]{2,1,0:T(8,128)(2,1)} %all-gather.7.cloned.1.call-done) | copy-start | bytes 12582916
  139.7 3.1 %copy-start.8 = (bf16[2,4096,256]{2,1,0:T(8,128)(2,1)S(1)}, bf16[2,4096,256]{2,1,0:T(8,128)(2,1)}, u32[]{:S(2)}) copy-start(bf16[2,4096,256]{2,1,0:T(8,128)(2,1)} %all-gather.9.cloned.1.call-done) | copy-start | bytes 12582916
  142.8 1.6 copy-start.9
  184.1 4.8 %copy-start.6 = (f32[8,2]{0,1:T(2,128)S(1)}, f32[8,2]{0,1:T(2,128)}, u32[]{:S(2)}) copy-start(f32[8,2]{0,1:T(2,128)} %param.19) | copy-start | bytes 196
  185.5 13.8 %all-to-all-start.3 = ((bf16[8,3,4096]{2,1,0:T(4,128)(2,1)}), bf16[8,3,4096]{2,1,0:T(4,128)(2,1)S(1)}, u32[]{:S(2)}, u32[]{:S(2)}) async-start(bf16[8,3,4096]{2,1,0:T(4,128)(2,1)} %reshape.284), calls=%async_computation.3 | async-start | bytes 524288 | tf_op jit(solution)/shard_map/all_to_all | solution.py:162
Sparse Core Ops, SparseCore 0:
  9.2 18.8 all-gather.10
  31.7 18.6 all-gather.6
  84.6 16.6 all-gather.8

commit v17 on v16

--- a/solution.py
+++ b/solution.py
@@ -7,7 +7,7 @@
 
 PAIR = 2
 
-highest = lax.Precision.HIGHEST
+highest = lax.Precision.HIGH
 
 SEQ_AXES = ("y", "x", "c")
 TOK_AXES = ("y", "x")

time: 208 us -> 208 us (level)
  no operation moved by 1% of the time
where the time goes in v17:
time: 208 us
  blocking collectives  70.1 us (34%)
  waiting for transfers between devices  62.5 us (30%)
  starting transfers between devices  35.8 us (17%)
  between operations  13.6 us (7%)
  matrix products  13.2 us (6%)
  local copies, waits for them, and re-layouts  7.45 us (4%)
  other arithmetic  5.08 us (2%)
    ppermute x1, waiting for transfers between devices, per_device(): down_far = lax.ppermute(down_core, 'p', partner)  38.7 us
    all_to_all x1, blocking collectives, per_device(): lax.all_to_all(term.reshape(groups, per_dev, width), TOK_AXES, split_axis...  36.3 us
    ppermute x5, starting transfers between devices, shifted(): lax.ppermute(value.astype(jnp.bfloat16), SEQ_AXES, pairs)  22.2 us
    all_gather x1, blocking collectives, per_device(): ids_all = lax.all_gather(expert_ids, DEV_AXES, axis=0, tiled=False)  19.4 us
    all_to_all x1, blocking collectives, per_device(): lax.all_to_all(send_rows, DEV_AXES, split_axis=0, concat_axis=0, tiled=True)  14.4 us
    ppermute x5, waiting for transfers between devices, shifted(): lax.ppermute(value.astype(jnp.bfloat16), SEQ_AXES, pairs)  12.9 us
    all_to_all x1, waiting for transfers between devices, per_device(): lax.all_to_all(summed.reshape(dev_count, half, width), DEV_AXES, split_ax...  10.1 us
    all_to_all x1, starting transfers between devices, per_device(): lax.all_to_all(jnp.broadcast_to(local_rows[None], (groups,) + local_rows....  9.44 us
  transfers between devices with their start and end apart: 12, of which 7 were waited for; matrix products, arithmetic and copies ran while one was open for 7% of the time, Pallas kernels for 0%

profile of v17, /device:TPU:2, one launch (start us, length us, event | category | flops | bytes accessed | tf_op | source)
XLA Modules:
  0.0 207.7 jit_solution(422414869516971744)
XLA Ops:
  6.5 0.7 all-gather.11.cloned.1.call-update
  7.3 19.4 %all-gather.2 = s32[8,8,2]{1,2,0:T(2,128)S(1)} all-gather(s32[1,8,2]{1,2,0:T(2,128)} %bitcast.159), channel_id=3, replica_groups=mesh['y'=4,'x'=4,'c'=2,'e'=4,'p'=2] {'e','p'}, dimensions={0}, use_global_device_ids=true | all-gather | bytes 576 | tf_op jit(solution)/shard_map/all_gather | solution.py:74
  26.7 1.7 pad_maximum_fusion
  28.5 0.1 collective-permute-start
  28.6 0.2 reduce_window_sum.22
  28.8 0.2 exponential_reduce_fusion
  29.1 0.4 fusion.64
  29.6 1.9 collective-permute-start.1
  31.7 0.4 fusion.65
  32.5 0.1 copy.55
  32.6 0.1 mul.252
  33.0 3.0 %collective-permute-done.1 = bf16[4,129,128]{2,1,0:T(8,128)(2,1)S(1)} collective-permute-done((bf16[4,129,128]{2,1,0:T(8,128)(2,1)S(1)}, bf16[4,129,128]{2,1,0:T(8,128)(2,1)S(1)}, u32[]{:S(2)}, u32[]{:S(2)}) %collective-permute-start.1) | collective-permute-done | bytes 132128 | tf_op jit(solution)/shard_map/ppermute | solution.py:25
  36.1 0.1 fusion.63
  36.2 3.4 %collective-permute-start.2 = (bf16[4,129,128]{2,1,0:T(8,128)(2,1)S(1)}, bf16[4,129,128]{2,1,0:T(8,128)(2,1)S(1)}, u32[]{:S(2)}, u32[]{:S(2)}) collective-permute-start(bf16[4,129,128]{2,1,0:T(8,128)(2,1)S(1)} %pad_maximum_fusion.2), channel_id=1, source_target_pairs={{0,16},{8,24},{16,32},{24,40},{32,48},{40,56},{48,64},{56,72},{64,... | collective-permute-start | bytes 396296 | tf_op jit(solution)/shard_map/ppermute | solution.py:25
  39.7 1.0 scatter_custom_fusion
  40.7 2.4 %collective-permute-done.2 = bf16[4,129,128]{2,1,0:T(8,128)(2,1)S(1)} collective-permute-done((bf16[4,129,128]{2,1,0:T(8,128)(2,1)S(1)}, bf16[4,129,128]{2,1,0:T(8,128)(2,1)S(1)}, u32[]{:S(2)}, u32[]{:S(2)}) %collective-permute-start.2) | collective-permute-done | bytes 132128 | tf_op jit(solution)/shard_map/ppermute | solution.py:25
  43.3 5.2 %collective-permute-start.3 = (bf16[4,129,128]{2,1,0:T(8,128)(2,1)S(1)}, bf16[4,129,128]{2,1,0:T(8,128)(2,1)S(1)}, u32[]{:S(2)}, u32[]{:S(2)}) collective-permute-start(bf16[4,129,128]{2,1,0:T(8,128)(2,1)S(1)} %pad_maximum_fusion.3), channel_id=1, source_target_pairs={{0,32},{8,40},{16,48},{24,56},{32,64},{40,72},{48,80},{56,88},{64,... | collective-permute-start | bytes 396296 | tf_op jit(solution)/shard_map/ppermute | solution.py:25
  48.5 0.2 convolution_multiply_fusion
  48.6 2.4 %collective-permute-done.3 = bf16[4,129,128]{2,1,0:T(8,128)(2,1)S(1)} collective-permute-done((bf16[4,129,128]{2,1,0:T(8,128)(2,1)S(1)}, bf16[4,129,128]{2,1,0:T(8,128)(2,1)S(1)}, u32[]{:S(2)}, u32[]{:S(2)}) %collective-permute-start.3) | collective-permute-done | bytes 132128 | tf_op jit(solution)/shard_map/ppermute | solution.py:25
  51.2 5.7 %collective-permute-start.4 = (bf16[4,129,128]{2,1,0:T(8,128)(2,1)S(1)}, bf16[4,129,128]{2,1,0:T(8,128)(2,1)S(1)}, u32[]{:S(2)}, u32[]{:S(2)}) collective-permute-start(bf16[4,129,128]{2,1,0:T(8,128)(2,1)S(1)} %pad_maximum_fusion.4), channel_id=1, source_target_pairs={{0,64},{8,72},{16,80},{24,88},{32,96},{40,104},{48,112},{56,120},{... | collective-permute-start | bytes 396296 | tf_op jit(solution)/shard_map/ppermute | solution.py:25
  56.9 2.5 %collective-permute-done.4 = bf16[4,129,128]{2,1,0:T(8,128)(2,1)S(1)} collective-permute-done((bf16[4,129,128]{2,1,0:T(8,128)(2,1)S(1)}, bf16[4,129,128]{2,1,0:T(8,128)(2,1)S(1)}, u32[]{:S(2)}, u32[]{:S(2)}) %collective-permute-start.4) | collective-permute-done | bytes 132128 | tf_op jit(solution)/shard_map/ppermute | solution.py:25
  59.6 6.0 %collective-permute-start.5 = (bf16[4,129,128]{2,1,0:T(8,128)(2,1)S(1)}, bf16[4,129,128]{2,1,0:T(8,128)(2,1)S(1)}, u32[]{:S(2)}, u32[]{:S(2)}) collective-permute-start(bf16[4,129,128]{2,1,0:T(8,128)(2,1)S(1)} %pad_maximum_fusion.5), channel_id=1, source_target_pairs={{0,128},{8,136},{16,144},{24,152},{32,160},{40,168},{48,176},{56,1... | collective-permute-start | bytes 396296 | tf_op jit(solution)/shard_map/ppermute | solution.py:25
  65.6 2.6 %collective-permute-done.5 = bf16[4,129,128]{2,1,0:T(8,128)(2,1)S(1)} collective-permute-done((bf16[4,129,128]{2,1,0:T(8,128)(2,1)S(1)}, bf16[4,129,128]{2,1,0:T(8,128)(2,1)S(1)}, u32[]{:S(2)}, u32[]{:S(2)}) %collective-permute-start.5) | collective-permute-done | bytes 132128 | tf_op jit(solution)/shard_map/ppermute | solution.py:25
  68.2 0.3 fusion.11
  68.4 0.3 fusion.27
  68.7 0.1 copy_bitcast_fusion
  68.9 1.0 gather_fusion
  69.9 14.4 %all_to_all.20 = bf16[8,24,512]{2,1,0:T(8,128)(2,1)S(1)} all-to-all(bf16[8,24,512]{2,1,0:T(8,128)(2,1)S(1)} %bitcast.144), channel_id=1, replica_groups=mesh['y'=4,'x'=4,'c'=2,'e'=4,'p'=2] {'e','p'}, dimensions={0} | all-to-all | bytes 393216 | tf_op jit(solution)/shard_map/all_to_all | solution.py:131
  84.4 2.1 %broadcast_in_dim.61 = bf16[16,24,4096]{2,1,0:T(8,128)(2,1)} broadcast(bf16[24,4096]{1,0:T(8,128)(2,1)S(1)} %bitcast.145), dimensions={1,2} | broadcast | bytes 3342336 | tf_op jit(solution)/shard_map/broadcast_in_dim | solution.py:142
  86.5 9.4 %all-to-all-start.1 = ((bf16[16,24,4096]{2,1,0:T(8,128)(2,1)}), bf16[16,24,4096]{2,1,0:T(8,128)(2,1)S(1)}, u32[]{:S(2)}, u32[]{:S(2)}) async-start(bf16[16,24,4096]{2,1,0:T(8,128)(2,1)} %broadcast_in_dim.61), calls=%async_computation.1 | async-start | bytes 6291456 | tf_op jit(solution)/shard_map/all_to_all | solution.py:141
  95.9 0.6 collective-permute-start.6
  96.5 38.7 %collective-permute-done.6 = bf16[256,4096]{1,0:T(8,128)(2,1)} collective-permute-done((bf16[256,4096]{1,0:T(8,128)(2,1)}, bf16[256,4096]{1,0:T(8,128)(2,1)}, u32[]{:S(2)}, u32[]{:S(2)}) %collective-permute-start.6) | collective-permute-done | bytes 2097184 | tf_op jit(solution)/shard_map/ppermute | solution.py:135
  135.2 3.0 %fusion.6 = f32[384,256]{0,1:T(8,128)S(1)} fusion(bf16[384,4096]{1,0:T(8,128)(2,1)S(1)} %bitcast.139, bf16[2,4096,256]{2,1,0:T(8,128)(2,1)} %all-gather.7.cloned.1.call-done), kind=kOutput, calls=%fused_computation.14 | convolution fusion | flops 805306368 | bytes 5636096 | tf_op jit(solution)/shard_map/dot_general | solution.py:151
  138.2 1.3 multiply_convert_fusion.1
  139.6 3.0 %fusion.4 = f32[384,256]{0,1:T(8,128)S(1)} fusion(bf16[384,4096]{1,0:T(8,128)(2,1)S(1)} %bitcast.141, bf16[2,4096,256]{2,1,0:T(8,128)(2,1)} %all-gather.9.cloned.1.call-done), kind=kOutput, calls=%fused_computation.10 | convolution fusion | flops 805306368 | bytes 5636096 | tf_op jit(solution)/shard_map/dot_general | solution.py:151
  142.6 1.3 multiply_convert_fusion
  143.9 0.3 copy-done.9
  144.2 3.4 %convolution_convert_fusion = bf16[384,4096]{1,0:T(8,128)(2,1)S(1)} fusion(bf16[256,4096]{1,0:T(8,128)(2,1)} %collective-permute-done.6, bf16[256,4096]{1,0:T(8,128)(2,1)S(1)} %bitcast.161, bf16[384,256]{0,1:T(8,128)(2,1)S(1)} %multiply_convert_fusion, bf16[384,256]{0,1:T(8,128)(2,1)S(1)} %multiply_convert_fusion.1), kind=kOutput, calls=%fused_computation.3 | convolution fusion | flops 1621360640 | bytes 7733248 | tf_op jit(solution)/shard_map/dot_general | solution.py:157
  147.6 36.3 %all_to_all.21 = bf16[16,24,4096]{2,1,0:T(8,128)(2,1)S(1)} all-to-all(bf16[16,24,4096]{2,1,0:T(8,128)(2,1)S(1)} %bitcast.143), channel_id=1, replica_groups=mesh['y'=4,'x'=4,'c'=2,'e'=4,'p'=2] {'y','x'}, dimensions={0} | all-to-all | bytes 6291456 | tf_op jit(solution)/shard_map/all_to_all | solution.py:158
  184.0 0.6 reduce_sum.41
  184.5 0.8 reshape.284
  185.4 3.4 %all-to-all-start.3 = ((bf16[8,3,4096]{2,1,0:T(4,128)(2,1)}), bf16[8,3,4096]{2,1,0:T(4,128)(2,1)S(1)}, u32[]{:S(2)}, u32[]{:S(2)}) async-start(bf16[8,3,4096]{2,1,0:T(4,128)(2,1)} %reshape.284), calls=%async_computation.3 | async-start | bytes 524288 | tf_op jit(solution)/shard_map/all_to_all | solution.py:162
  188.9 0.2 add_reduce_fusion
  189.1 10.1 %all-to-all-done.3 = bf16[8,3,4096]{2,1,0:T(4,128)(2,1)S(1)} async-done(((bf16[8,3,4096]{2,1,0:T(4,128)(2,1)}), bf16[8,3,4096]{2,1,0:T(4,128)(2,1)S(1)}, u32[]{:S(2)}, u32[]{:S(2)}) %all-to-all-start.3) | async-done | bytes 196640 | tf_op jit(solution)/shard_map/all_to_all | solution.py:162
  199.2 0.2 reshape.285
  199.3 0.6 gather_fusion.1
  200.0 0.2 reshape.286
  200.2 1.0 multiply_reduce_fusion
  (76 shorter events, 1.7 us)
Async XLA Ops:
  6.5 22.6 %copy-start = (bf16[64,512]{1,0:T(8,128)(2,1)S(1)}, bf16[64,512]{1,0:T(8,128)(2,1)}, u32[]{:S(2)}) copy-start(bf16[64,512]{1,0:T(8,128)(2,1)} %param.12) | copy-start | bytes 196612
  6.5 22.0 %copy-start.5 = (f32[64,4]{0,1:T(4,128)S(1)}, f32[64,4]{0,1:T(4,128)}, u32[]{:S(2)}) copy-start(f32[64,4]{0,1:T(4,128)} %param.13) | copy-start | bytes 3076
  6.5 22.6 %copy-start.2 = (bf16[64,512]{1,0:T(8,128)(2,1)S(1)}, bf16[64,512]{1,0:T(8,128)(2,1)}, u32[]{:S(2)}) copy-start(bf16[64,512]{1,0:T(8,128)(2,1)} %param.11) | copy-start | bytes 196612
  6.5 77.8 %all-gather.11.cloned.1.call-start = ((), (), s32[]{:S(2)}) async-start(), calls=%async_computation.6 | async-start | bytes 3145728 | tf_op jit(solution)/shard_map/all_gather | solution.py:79
  7.3 127.9 %all-gather.7.cloned.1.call-start = ((), (), s32[]{:S(2)}) async-start(), calls=%async_computation.4 | async-start | bytes 6291456 | tf_op jit(solution)/shard_map/all_gather | solution.py:78
  28.4 3.1 %copy-start.1 = (bf16[2,4096,128]{2,1,0:T(8,128)(2,1)}, bf16[2,4096,128]{2,1,0:T(8,128)(2,1)S(1)}, u32[]{:S(2)}) copy-start(bf16[2,4096,128]{2,1,0:T(8,128)(2,1)S(1)} %pad_maximum_fusion) | copy-start | bytes 6291460
  28.4 20.0 %copy-start.3 = (bf16[64,512]{1,0:T(8,128)(2,1)S(1)}, bf16[64,512]{1,0:T(8,128)(2,1)}, u32[]{:S(2)}) copy-start(bf16[64,512]{1,0:T(8,128)(2,1)} %param.10) | copy-start | bytes 196612
  28.5 55.8 %collective-permute-start = (bf16[2,4096,128]{2,1,0:T(8,128)(2,1)S(1)}, bf16[2,4096,128]{2,1,0:T(8,128)(2,1)}, u32[]{:S(2)}, u32[]{:S(2)}) collective-permute-start(bf16[2,4096,128]{2,1,0:T(8,128)(2,1)S(1)} %pad_maximum_fusion), channel_id=1, source_target_pairs={{0,1},{1,0},{2,3},{3,2},{4,5},{5,4},{6,7},{7,6},{8,9},{9,8},{10,11... | collective-permute-start | bytes 6291464 | tf_op jit(solution)/shard_map/ppermute | solution.py:80
  29.6 6.4 %collective-permute-start.1 = (bf16[4,129,128]{2,1,0:T(8,128)(2,1)S(1)}, bf16[4,129,128]{2,1,0:T(8,128)(2,1)S(1)}, u32[]{:S(2)}, u32[]{:S(2)}) collective-permute-start(bf16[4,129,128]{2,1,0:T(8,128)(2,1)S(1)} %pad_maximum_fusion.1), channel_id=1, source_target_pairs={{0,8},{8,16},{16,24},{24,32},{32,40},{40,48},{48,56},{56,64},{64,7... | collective-permute-start | bytes 396296 | tf_op jit(solution)/shard_map/ppermute | solution.py:25
  31.6 108.0 %all-gather.9.cloned.1.call-start = ((), (), s32[]{:S(2)}) async-start(), calls=%async_computation.5 | async-start | bytes 6291456 | tf_op jit(solution)/shard_map/all_gather | solution.py:133
  36.2 6.9 %collective-permute-start.2 = (bf16[4,129,128]{2,1,0:T(8,128)(2,1)S(1)}, bf16[4,129,128]{2,1,0:T(8,128)(2,1)S(1)}, u32[]{:S(2)}, u32[]{:S(2)}) collective-permute-start(bf16[4,129,128]{2,1,0:T(8,128)(2,1)S(1)} %pad_maximum_fusion.2), channel_id=1, source_target_pairs={{0,16},{8,24},{16,32},{24,40},{32,48},{40,56},{48,64},{56,72},{64,... | collective-permute-start | bytes 396296 | tf_op jit(solution)/shard_map/ppermute | solution.py:25
  43.2 25.5 %copy-start.4 = (f32[512]{0:T(512)S(1)}, f32[512]{0:T(512)}, u32[]{:S(2)}) copy-start(f32[512]{0:T(512)} %param.14) | copy-start | bytes 6148
  43.3 7.8 %collective-permute-start.3 = (bf16[4,129,128]{2,1,0:T(8,128)(2,1)S(1)}, bf16[4,129,128]{2,1,0:T(8,128)(2,1)S(1)}, u32[]{:S(2)}, u32[]{:S(2)}) collective-permute-start(bf16[4,129,128]{2,1,0:T(8,128)(2,1)S(1)} %pad_maximum_fusion.3), channel_id=1, source_target_pairs={{0,32},{8,40},{16,48},{24,56},{32,64},{40,72},{48,80},{56,88},{64,... | collective-permute-start | bytes 396296 | tf_op jit(solution)/shard_map/ppermute | solution.py:25
  51.2 8.3 %collective-permute-start.4 = (bf16[4,129,128]{2,1,0:T(8,128)(2,1)S(1)}, bf16[4,129,128]{2,1,0:T(8,128)(2,1)S(1)}, u32[]{:S(2)}, u32[]{:S(2)}) collective-permute-start(bf16[4,129,128]{2,1,0:T(8,128)(2,1)S(1)} %pad_maximum_fusion.4), channel_id=1, source_target_pairs={{0,64},{8,72},{16,80},{24,88},{32,96},{40,104},{48,112},{56,120},{... | collective-permute-start | bytes 396296 | tf_op jit(solution)/shard_map/ppermute | solution.py:25
  59.6 8.6 %collective-permute-start.5 = (bf16[4,129,128]{2,1,0:T(8,128)(2,1)S(1)}, bf16[4,129,128]{2,1,0:T(8,128)(2,1)S(1)}, u32[]{:S(2)}, u32[]{:S(2)}) collective-permute-start(bf16[4,129,128]{2,1,0:T(8,128)(2,1)S(1)} %pad_maximum_fusion.5), channel_id=1, source_target_pairs={{0,128},{8,136},{16,144},{24,152},{32,160},{40,168},{48,176},{56,1... | collective-permute-start | bytes 396296 | tf_op jit(solution)/shard_map/ppermute | solution.py:25
  86.5 48.7 %all-to-all-start.1 = ((bf16[16,24,4096]{2,1,0:T(8,128)(2,1)}), bf16[16,24,4096]{2,1,0:T(8,128)(2,1)S(1)}, u32[]{:S(2)}, u32[]{:S(2)}) async-start(bf16[16,24,4096]{2,1,0:T(8,128)(2,1)} %broadcast_in_dim.61), calls=%async_computation.1 | async-start | bytes 6291456 | tf_op jit(solution)/shard_map/all_to_all | solution.py:141
  95.9 39.3 %collective-permute-start.6 = (bf16[256,4096]{1,0:T(8,128)(2,1)}, bf16[256,4096]{1,0:T(8,128)(2,1)}, u32[]{:S(2)}, u32[]{:S(2)}) collective-permute-start(bf16[256,4096]{1,0:T(8,128)(2,1)} %bitcast.160), channel_id=1, source_target_pairs={{0,1},{1,0},{2,3},{3,2},{4,5},{5,4},{6,7},{7,6},{8,9},{9,8},{10,11... | collective-permute-start | bytes 6291464 | tf_op jit(solution)/shard_map/ppermute | solution.py:135
  135.2 3.0 %copy-start.7 = (bf16[2,4096,256]{2,1,0:T(8,128)(2,1)S(1)}, bf16[2,4096,256]{2,1,0:T(8,128)(2,1)}, u32[]{:S(2)}) copy-start(bf16[2,4096,256]{2,1,0:T(8,128)(2,1)} %all-gather.7.cloned.1.call-done) | copy-start | bytes 12582916
  139.5 3.1 %copy-start.8 = (bf16[2,4096,256]{2,1,0:T(8,128)(2,1)S(1)}, bf16[2,4096,256]{2,1,0:T(8,128)(2,1)}, u32[]{:S(2)}) copy-start(bf16[2,4096,256]{2,1,0:T(8,128)(2,1)} %all-gather.9.cloned.1.call-done) | copy-start | bytes 12582916
  142.6 1.6 copy-start.9
  184.0 4.8 %copy-start.6 = (f32[8,2]{0,1:T(2,128)S(1)}, f32[8,2]{0,1:T(2,128)}, u32[]{:S(2)}) copy-start(f32[8,2]{0,1:T(2,128)} %param.19) | copy-start | bytes 196
  185.4 13.8 %all-to-all-start.3 = ((bf16[8,3,4096]{2,1,0:T(4,128)(2,1)}), bf16[8,3,4096]{2,1,0:T(4,128)(2,1)S(1)}, u32[]{:S(2)}, u32[]{:S(2)}) async-start(bf16[8,3,4096]{2,1,0:T(4,128)(2,1)} %reshape.284), calls=%async_computation.3 | async-start | bytes 524288 | tf_op jit(solution)/shard_map/all_to_all | solution.py:162
Sparse Core Ops, SparseCore 0:
  9.2 18.8 all-gather.10
  31.7 18.6 all-gather.6
  84.5 16.6 all-gather.8

commit v18 on v17

--- a/solution.py
+++ b/solution.py
@@ -126,8 +126,9 @@
         .at[slot_index.reshape(-1)]
         .set(token_local.reshape(-1))
     )
-    padded = jnp.concatenate([normed, jnp.zeros((1, normed.shape[1]), normed.dtype)], axis=0)
-    send_rows = padded[slot_token].reshape(dev_count, per_dev, -1)
+    send_rows = jnp.take(normed, slot_token, axis=0, mode="fill", fill_value=0).reshape(
+        dev_count, per_dev, -1
+    )
     arrived = lax.all_to_all(send_rows, DEV_AXES, split_axis=0, concat_axis=0, tiled=True)
     gate_up_far, arrived = lax.optimization_barrier((gate_up_far, arrived))
     gate_up_far = lax.all_gather(gate_up_far, "c", axis=2, tiled=True)

time: 208 us -> 211 us (1.014)
  transfers between devices with their start and end apart: 12 -> 12, of which waited for: 7 -> 7; matrix products, arithmetic and copies ran while one was open for 7% -> 9% of each run, Pallas kernels for 0% -> 0%
where the time goes in v18:
time: 211 us; the launch traced here: 210 us
  blocking collectives  70.1 us (33%)
  waiting for transfers between devices  60.7 us (29%)
  starting transfers between devices  36.2 us (17%)
  matrix products  14.7 us (7%)
  between operations  13.6 us (6%)
  local copies, waits for them, and re-layouts  8.09 us (4%)
  other arithmetic  6.81 us (3%)
    ppermute x1, waiting for transfers between devices, per_device(): down_far = lax.ppermute(down_core, 'p', partner)  38.6 us
    all_to_all x1, blocking collectives, per_device(): lax.all_to_all(term.reshape(groups, per_dev, width), TOK_AXES, split_axis...  36.3 us
    ppermute x5, starting transfers between devices, shifted(): lax.ppermute(value.astype(jnp.bfloat16), SEQ_AXES, pairs)  22.7 us
    all_gather x1, blocking collectives, per_device(): ids_all = lax.all_gather(expert_ids, DEV_AXES, axis=0, tiled=False)  19.4 us
    all_to_all x1, blocking collectives, per_device(): lax.all_to_all(send_rows, DEV_AXES, split_axis=0, concat_axis=0, tiled=True)  14.4 us
    ppermute x5, waiting for transfers between devices, shifted(): lax.ppermute(value.astype(jnp.bfloat16), SEQ_AXES, pairs)  11.2 us
    all_to_all x1, waiting for transfers between devices, per_device(): lax.all_to_all(summed.reshape(dev_count, half, width), DEV_AXES, split_ax...  10.1 us
    all_to_all x1, starting transfers between devices, per_device(): lax.all_to_all(jnp.broadcast_to(local_rows[None], (groups,) + local_rows....  9.37 us
  transfers between devices with their start and end apart: 12, of which 7 were waited for; matrix products, arithmetic and copies ran while one was open for 9% of the time, Pallas kernels for 0%

profile of v18, /device:TPU:2, one launch (start us, length us, event | category | flops | bytes accessed | tf_op | source)
XLA Modules:
  0.0 210.3 jit_solution(17192259952968818797)
XLA Ops:
  6.5 0.7 all-gather.11.cloned.1.call-update
  7.3 19.4 %all-gather.2 = s32[8,8,2]{1,2,0:T(2,128)S(1)} all-gather(s32[1,8,2]{1,2,0:T(2,128)} %bitcast.159), channel_id=3, replica_groups=mesh['y'=4,'x'=4,'c'=2,'e'=4,'p'=2] {'e','p'}, dimensions={0}, use_global_device_ids=true | all-gather | bytes 576 | tf_op jit(solution)/shard_map/all_gather | solution.py:74
  26.7 1.7 pad_maximum_fusion
  28.6 0.2 reduce_window_sum.23
  28.8 0.2 exponential_reduce_fusion
  29.1 0.4 fusion.64
  29.6 1.9 collective-permute-start.1
  31.7 0.4 fusion.65
  32.5 0.1 copy.63
  32.6 0.1 mul.215
  33.1 1.0 scatter_custom_fusion
  34.1 1.9 collective-permute-done.1
  36.2 3.4 %collective-permute-start.2 = (bf16[4,129,128]{2,1,0:T(8,128)(2,1)S(1)}, bf16[4,129,128]{2,1,0:T(8,128)(2,1)S(1)}, u32[]{:S(2)}, u32[]{:S(2)}) collective-permute-start(bf16[4,129,128]{2,1,0:T(8,128)(2,1)S(1)} %pad_maximum_fusion.2), channel_id=1, source_target_pairs={{0,16},{8,24},{16,32},{24,40},{32,48},{40,56},{48,64},{56,72},{64,... | collective-permute-start | bytes 396296 | tf_op jit(solution)/shard_map/ppermute | solution.py:25
  39.6 0.8 convolution_multiply_fusion
  40.4 3.0 %collective-permute-done.2 = bf16[4,129,128]{2,1,0:T(8,128)(2,1)S(1)} collective-permute-done((bf16[4,129,128]{2,1,0:T(8,128)(2,1)S(1)}, bf16[4,129,128]{2,1,0:T(8,128)(2,1)S(1)}, u32[]{:S(2)}, u32[]{:S(2)}) %collective-permute-start.2) | collective-permute-done | bytes 132128 | tf_op jit(solution)/shard_map/ppermute | solution.py:25
  43.5 4.9 %collective-permute-start.3 = (bf16[4,129,128]{2,1,0:T(8,128)(2,1)S(1)}, bf16[4,129,128]{2,1,0:T(8,128)(2,1)S(1)}, u32[]{:S(2)}, u32[]{:S(2)}) collective-permute-start(bf16[4,129,128]{2,1,0:T(8,128)(2,1)S(1)} %pad_maximum_fusion.3), channel_id=1, source_target_pairs={{0,32},{8,40},{16,48},{24,56},{32,64},{40,72},{48,80},{56,88},{64,... | collective-permute-start | bytes 396296 | tf_op jit(solution)/shard_map/ppermute | solution.py:25
  48.5 2.6 %collective-permute-done.3 = bf16[4,129,128]{2,1,0:T(8,128)(2,1)S(1)} collective-permute-done((bf16[4,129,128]{2,1,0:T(8,128)(2,1)S(1)}, bf16[4,129,128]{2,1,0:T(8,128)(2,1)S(1)}, u32[]{:S(2)}, u32[]{:S(2)}) %collective-permute-start.3) | collective-permute-done | bytes 132128 | tf_op jit(solution)/shard_map/ppermute | solution.py:25
  51.2 6.4 %collective-permute-start.4 = (bf16[4,129,128]{2,1,0:T(8,128)(2,1)S(1)}, bf16[4,129,128]{2,1,0:T(8,128)(2,1)}, u32[]{:S(2)}, u32[]{:S(2)}) collective-permute-start(bf16[4,129,128]{2,1,0:T(8,128)(2,1)S(1)} %pad_maximum_fusion.4), channel_id=1, source_target_pairs={{0,64},{8,72},{16,80},{24,88},{32,96},{40,104},{48,112},{56,120},{... | collective-permute-start | bytes 396296 | tf_op jit(solution)/shard_map/ppermute | solution.py:25
  57.5 0.7 broadcast_in_dim.65
  58.2 1.3 collective-permute-done.4
  59.5 0.9 convert_element_type.55
  60.5 6.1 %collective-permute-start.5 = (bf16[4,129,128]{2,1,0:T(8,128)(2,1)S(1)}, bf16[4,129,128]{2,1,0:T(8,128)(2,1)S(1)}, u32[]{:S(2)}, u32[]{:S(2)}) collective-permute-start(bf16[4,129,128]{2,1,0:T(8,128)(2,1)S(1)} %pad_maximum_fusion.5), channel_id=1, source_target_pairs={{0,128},{8,136},{16,144},{24,152},{32,160},{40,168},{48,176},{56,1... | collective-permute-start | bytes 396296 | tf_op jit(solution)/shard_map/ppermute | solution.py:25
  66.6 2.6 %collective-permute-done.5 = bf16[4,129,128]{2,1,0:T(8,128)(2,1)S(1)} collective-permute-done((bf16[4,129,128]{2,1,0:T(8,128)(2,1)S(1)}, bf16[4,129,128]{2,1,0:T(8,128)(2,1)S(1)}, u32[]{:S(2)}, u32[]{:S(2)}) %collective-permute-start.5) | collective-permute-done | bytes 132128 | tf_op jit(solution)/shard_map/ppermute | solution.py:25
  69.2 0.3 fusion.11
  69.5 1.2 fusion.27
  70.7 0.8 copy_bitcast_fusion
  71.5 1.0 gather_fusion
  72.6 14.4 %all_to_all.20 = bf16[8,24,512]{2,1,0:T(8,128)(2,1)S(1)} all-to-all(bf16[8,24,512]{2,1,0:T(8,128)(2,1)S(1)} %broadcast_select_fusion), channel_id=1, replica_groups=mesh['y'=4,'x'=4,'c'=2,'e'=4,'p'=2] {'e','p'}, dimensions={0} | all-to-all | bytes 393216 | tf_op jit(solution)/shard_map/all_to_all | solution.py:132
  87.1 2.1 broadcast_in_dim.74
  89.2 9.4 %all-to-all-start.1 = ((bf16[16,24,4096]{2,1,0:T(8,128)(2,1)}), bf16[16,24,4096]{2,1,0:T(8,128)(2,1)S(1)}, u32[]{:S(2)}, u32[]{:S(2)}) async-start(bf16[16,24,4096]{2,1,0:T(8,128)(2,1)} %broadcast_in_dim.74), calls=%async_computation.1 | async-start | bytes 6291456 | tf_op jit(solution)/shard_map/all_to_all | solution.py:142
  98.5 0.6 collective-permute-start.6
  99.1 38.6 %collective-permute-done.6 = bf16[256,4096]{1,0:T(8,128)(2,1)} collective-permute-done((bf16[256,4096]{1,0:T(8,128)(2,1)}, bf16[256,4096]{1,0:T(8,128)(2,1)}, u32[]{:S(2)}, u32[]{:S(2)}) %collective-permute-start.6) | collective-permute-done | bytes 2097184 | tf_op jit(solution)/shard_map/ppermute | solution.py:136
  137.8 3.0 %fusion.6 = f32[384,256]{0,1:T(8,128)S(1)} fusion(bf16[384,4096]{1,0:T(8,128)(2,1)S(1)} %bitcast.139, bf16[2,4096,256]{2,1,0:T(8,128)(2,1)} %all-gather.7.cloned.1.call-done), kind=kOutput, calls=%fused_computation.14 | convolution fusion | flops 805306368 | bytes 5636096 | tf_op jit(solution)/shard_map/dot_general | solution.py:152
  140.8 1.3 multiply_convert_fusion.1
  142.1 3.0 %fusion.4 = f32[384,256]{0,1:T(8,128)S(1)} fusion(bf16[384,4096]{1,0:T(8,128)(2,1)S(1)} %bitcast.141, bf16[2,4096,256]{2,1,0:T(8,128)(2,1)} %all-gather.9.cloned.1.call-done), kind=kOutput, calls=%fused_computation.10 | convolution fusion | flops 805306368 | bytes 5636096 | tf_op jit(solution)/shard_map/dot_general | solution.py:152
  145.2 1.3 multiply_convert_fusion
  146.5 0.3 copy-done.9
  146.8 3.4 %convolution_convert_fusion = bf16[384,4096]{1,0:T(8,128)(2,1)S(1)} fusion(bf16[256,4096]{1,0:T(8,128)(2,1)} %collective-permute-done.6, bf16[256,4096]{1,0:T(8,128)(2,1)S(1)} %bitcast.161, bf16[384,256]{0,1:T(8,128)(2,1)S(1)} %multiply_convert_fusion, bf16[384,256]{0,1:T(8,128)(2,1)S(1)} %multiply_convert_fusion.1), kind=kOutput, calls=%fused_computation.3 | convolution fusion | flops 1621360640 | bytes 7733248 | tf_op jit(solution)/shard_map/dot_general | solution.py:158
  150.2 36.3 %all_to_all.21 = bf16[16,24,4096]{2,1,0:T(8,128)(2,1)S(1)} all-to-all(bf16[16,24,4096]{2,1,0:T(8,128)(2,1)S(1)} %bitcast.143), channel_id=1, replica_groups=mesh['y'=4,'x'=4,'c'=2,'e'=4,'p'=2] {'y','x'}, dimensions={0} | all-to-all | bytes 6291456 | tf_op jit(solution)/shard_map/all_to_all | solution.py:159
  186.5 0.6 reduce_sum.41
  187.1 0.8 reshape.292
  187.9 3.4 %all-to-all-start.3 = ((bf16[8,3,4096]{2,1,0:T(4,128)(2,1)}), bf16[8,3,4096]{2,1,0:T(4,128)(2,1)S(1)}, u32[]{:S(2)}, u32[]{:S(2)}) async-start(bf16[8,3,4096]{2,1,0:T(4,128)(2,1)} %reshape.292), calls=%async_computation.3 | async-start | bytes 524288 | tf_op jit(solution)/shard_map/all_to_all | solution.py:163
  191.4 0.2 add_reduce_fusion
  191.6 10.1 %all-to-all-done.3 = bf16[8,3,4096]{2,1,0:T(4,128)(2,1)S(1)} async-done(((bf16[8,3,4096]{2,1,0:T(4,128)(2,1)}), bf16[8,3,4096]{2,1,0:T(4,128)(2,1)S(1)}, u32[]{:S(2)}, u32[]{:S(2)}) %all-to-all-start.3) | async-done | bytes 196640 | tf_op jit(solution)/shard_map/all_to_all | solution.py:163
  201.7 0.2 reshape.293
  201.9 0.6 gather_fusion.1
  202.5 0.2 reshape.294
  202.7 1.0 multiply_reduce_fusion
  (78 shorter events, 2.0 us)
Async XLA Ops:
  6.5 22.6 %copy-start = (bf16[64,512]{1,0:T(8,128)(2,1)S(1)}, bf16[64,512]{1,0:T(8,128)(2,1)}, u32[]{:S(2)}) copy-start(bf16[64,512]{1,0:T(8,128)(2,1)} %param.12) | copy-start | bytes 196612
  6.5 22.0 %copy-start.4 = (f32[64,4]{0,1:T(4,128)S(1)}, f32[64,4]{0,1:T(4,128)}, u32[]{:S(2)}) copy-start(f32[64,4]{0,1:T(4,128)} %param.13) | copy-start | bytes 3076
  6.5 22.6 %copy-start.2 = (bf16[64,512]{1,0:T(8,128)(2,1)S(1)}, bf16[64,512]{1,0:T(8,128)(2,1)}, u32[]{:S(2)}) copy-start(bf16[64,512]{1,0:T(8,128)(2,1)} %param.11) | copy-start | bytes 196612
  6.5 80.5 %all-gather.11.cloned.1.call-start = ((), (), s32[]{:S(2)}) async-start(), calls=%async_computation.6 | async-start | bytes 3145728 | tf_op jit(solution)/shard_map/all_gather | solution.py:79
  7.3 130.5 %all-gather.7.cloned.1.call-start = ((), (), s32[]{:S(2)}) async-start(), calls=%async_computation.4 | async-start | bytes 6291456 | tf_op jit(solution)/shard_map/all_gather | solution.py:78
  28.4 3.1 %copy-start.1 = (bf16[2,4096,128]{2,1,0:T(8,128)(2,1)}, bf16[2,4096,128]{2,1,0:T(8,128)(2,1)S(1)}, u32[]{:S(2)}) copy-start(bf16[2,4096,128]{2,1,0:T(8,128)(2,1)S(1)} %pad_maximum_fusion) | copy-start | bytes 6291460
  28.4 11.2 %copy-start.3 = (bf16[64,512]{1,0:T(8,128)(2,1)S(1)}, bf16[64,512]{1,0:T(8,128)(2,1)}, u32[]{:S(2)}) copy-start(bf16[64,512]{1,0:T(8,128)(2,1)} %param.10) | copy-start | bytes 196612
  28.5 58.5 %collective-permute-start = (bf16[2,4096,128]{2,1,0:T(8,128)(2,1)S(1)}, bf16[2,4096,128]{2,1,0:T(8,128)(2,1)}, u32[]{:S(2)}, u32[]{:S(2)}) collective-permute-start(bf16[2,4096,128]{2,1,0:T(8,128)(2,1)S(1)} %pad_maximum_fusion), channel_id=1, source_target_pairs={{0,1},{1,0},{2,3},{3,2},{4,5},{5,4},{6,7},{7,6},{8,9},{9,8},{10,11... | collective-permute-start | bytes 6291464 | tf_op jit(solution)/shard_map/ppermute | solution.py:80
  29.6 6.4 %collective-permute-start.1 = (bf16[4,129,128]{2,1,0:T(8,128)(2,1)S(1)}, bf16[4,129,128]{2,1,0:T(8,128)(2,1)S(1)}, u32[]{:S(2)}, u32[]{:S(2)}) collective-permute-start(bf16[4,129,128]{2,1,0:T(8,128)(2,1)S(1)} %pad_maximum_fusion.1), channel_id=1, source_target_pairs={{0,8},{8,16},{16,24},{24,32},{32,40},{40,48},{48,56},{56,64},{64,7... | collective-permute-start | bytes 396296 | tf_op jit(solution)/shard_map/ppermute | solution.py:25
  31.6 110.6 %all-gather.9.cloned.1.call-start = ((), (), s32[]{:S(2)}) async-start(), calls=%async_computation.5 | async-start | bytes 6291456 | tf_op jit(solution)/shard_map/all_gather | solution.py:134
  36.2 7.2 %collective-permute-start.2 = (bf16[4,129,128]{2,1,0:T(8,128)(2,1)S(1)}, bf16[4,129,128]{2,1,0:T(8,128)(2,1)S(1)}, u32[]{:S(2)}, u32[]{:S(2)}) collective-permute-start(bf16[4,129,128]{2,1,0:T(8,128)(2,1)S(1)} %pad_maximum_fusion.2), channel_id=1, source_target_pairs={{0,16},{8,24},{16,32},{24,40},{32,48},{40,56},{48,64},{56,72},{64,... | collective-permute-start | bytes 396296 | tf_op jit(solution)/shard_map/ppermute | solution.py:25
  43.5 7.5 %collective-permute-start.3 = (bf16[4,129,128]{2,1,0:T(8,128)(2,1)S(1)}, bf16[4,129,128]{2,1,0:T(8,128)(2,1)S(1)}, u32[]{:S(2)}, u32[]{:S(2)}) collective-permute-start(bf16[4,129,128]{2,1,0:T(8,128)(2,1)S(1)} %pad_maximum_fusion.3), channel_id=1, source_target_pairs={{0,32},{8,40},{16,48},{24,56},{32,64},{40,72},{48,80},{56,88},{64,... | collective-permute-start | bytes 396296 | tf_op jit(solution)/shard_map/ppermute | solution.py:25
  51.2 8.3 %collective-permute-start.4 = (bf16[4,129,128]{2,1,0:T(8,128)(2,1)S(1)}, bf16[4,129,128]{2,1,0:T(8,128)(2,1)}, u32[]{:S(2)}, u32[]{:S(2)}) collective-permute-start(bf16[4,129,128]{2,1,0:T(8,128)(2,1)S(1)} %pad_maximum_fusion.4), channel_id=1, source_target_pairs={{0,64},{8,72},{16,80},{24,88},{32,96},{40,104},{48,112},{56,120},{... | collective-permute-start | bytes 396296 | tf_op jit(solution)/shard_map/ppermute | solution.py:25
  59.5 13.0 %copy-start.5 = (pred[8,24]{1,0:T(8,128)(4,1)S(1)}, pred[8,24]{1,0:T(8,128)(4,1)}, u32[]{:S(2)}) copy-start(pred[8,24]{1,0:T(8,128)(4,1)} %broadcast_in_dim.65) | copy-start | bytes 580
  60.5 8.7 %collective-permute-start.5 = (bf16[4,129,128]{2,1,0:T(8,128)(2,1)S(1)}, bf16[4,129,128]{2,1,0:T(8,128)(2,1)S(1)}, u32[]{:S(2)}, u32[]{:S(2)}) collective-permute-start(bf16[4,129,128]{2,1,0:T(8,128)(2,1)S(1)} %pad_maximum_fusion.5), channel_id=1, source_target_pairs={{0,128},{8,136},{16,144},{24,152},{32,160},{40,168},{48,176},{56,1... | collective-permute-start | bytes 396296 | tf_op jit(solution)/shard_map/ppermute | solution.py:25
  89.2 48.6 %all-to-all-start.1 = ((bf16[16,24,4096]{2,1,0:T(8,128)(2,1)}), bf16[16,24,4096]{2,1,0:T(8,128)(2,1)S(1)}, u32[]{:S(2)}, u32[]{:S(2)}) async-start(bf16[16,24,4096]{2,1,0:T(8,128)(2,1)} %broadcast_in_dim.74), calls=%async_computation.1 | async-start | bytes 6291456 | tf_op jit(solution)/shard_map/all_to_all | solution.py:142
  98.5 39.2 %collective-permute-start.6 = (bf16[256,4096]{1,0:T(8,128)(2,1)}, bf16[256,4096]{1,0:T(8,128)(2,1)}, u32[]{:S(2)}, u32[]{:S(2)}) collective-permute-start(bf16[256,4096]{1,0:T(8,128)(2,1)} %bitcast.160), channel_id=1, source_target_pairs={{0,1},{1,0},{2,3},{3,2},{4,5},{5,4},{6,7},{7,6},{8,9},{9,8},{10,11... | collective-permute-start | bytes 6291464 | tf_op jit(solution)/shard_map/ppermute | solution.py:136
  137.8 3.0 %copy-start.7 = (bf16[2,4096,256]{2,1,0:T(8,128)(2,1)S(1)}, bf16[2,4096,256]{2,1,0:T(8,128)(2,1)}, u32[]{:S(2)}) copy-start(bf16[2,4096,256]{2,1,0:T(8,128)(2,1)} %all-gather.7.cloned.1.call-done) | copy-start | bytes 12582916
  142.1 3.1 %copy-start.8 = (bf16[2,4096,256]{2,1,0:T(8,128)(2,1)S(1)}, bf16[2,4096,256]{2,1,0:T(8,128)(2,1)}, u32[]{:S(2)}) copy-start(bf16[2,4096,256]{2,1,0:T(8,128)(2,1)} %all-gather.9.cloned.1.call-done) | copy-start | bytes 12582916
  145.2 1.6 copy-start.9
  186.5 4.8 %copy-start.6 = (f32[8,2]{0,1:T(2,128)S(1)}, f32[8,2]{0,1:T(2,128)}, u32[]{:S(2)}) copy-start(f32[8,2]{0,1:T(2,128)} %param.19) | copy-start | bytes 196
  187.9 13.8 %all-to-all-start.3 = ((bf16[8,3,4096]{2,1,0:T(4,128)(2,1)}), bf16[8,3,4096]{2,1,0:T(4,128)(2,1)S(1)}, u32[]{:S(2)}, u32[]{:S(2)}) async-start(bf16[8,3,4096]{2,1,0:T(4,128)(2,1)} %reshape.292), calls=%async_computation.3 | async-start | bytes 524288 | tf_op jit(solution)/shard_map/all_to_all | solution.py:163
Sparse Core Ops, SparseCore 0:
  9.2 18.8 all-gather.10
  31.7 18.6 all-gather.6
  87.1 16.5 all-gather.8

commit v19 on v17

--- a/solution.py
+++ b/solution.py
@@ -15,9 +15,9 @@
 
 
 def chain_join(earlier, later):
-    scale = jnp.exp(later[:, -1:, :])
-    state = scale * earlier[:, :-1, :] + later[:, :-1, :]
-    return jnp.concatenate([state, earlier[:, -1:, :] + later[:, -1:, :]], axis=1)
+    rows = jnp.arange(earlier.shape[1])[None, :, None]
+    scale = jnp.where(rows < earlier.shape[1] - 1, jnp.exp(later[:, -1:, :]), 1.0)
+    return scale * earlier + later
 
 
 def shifted(value, shift, count):

time: 208 us -> 209 us (level)
  no operation moved by 1% of the time
where the time goes in v19:
time: 209 us; the launch traced here: 208 us
  blocking collectives  70.3 us (34%)
  waiting for transfers between devices  63.1 us (30%)
  starting transfers between devices  35.2 us (17%)
  between operations  13.6 us (7%)
  matrix products  13.2 us (6%)
  local copies, waits for them, and re-layouts  7.5 us (4%)
  other arithmetic  5.23 us (3%)
    ppermute x1, waiting for transfers between devices, per_device(): down_far = lax.ppermute(down_core, 'p', partner)  39 us
    all_to_all x1, blocking collectives, per_device(): lax.all_to_all(term.reshape(groups, per_dev, width), TOK_AXES, split_axis...  36.5 us
    ppermute x5, starting transfers between devices, shifted(): lax.ppermute(value.astype(jnp.bfloat16), SEQ_AXES, pairs)  21.7 us
    all_gather x1, blocking collectives, per_device(): ids_all = lax.all_gather(expert_ids, DEV_AXES, axis=0, tiled=False)  19.4 us
    all_to_all x1, blocking collectives, per_device(): lax.all_to_all(send_rows, DEV_AXES, split_axis=0, concat_axis=0, tiled=True)  14.4 us
    ppermute x5, waiting for transfers between devices, shifted(): lax.ppermute(value.astype(jnp.bfloat16), SEQ_AXES, pairs)  13.3 us
    all_to_all x1, waiting for transfers between devices, per_device(): lax.all_to_all(summed.reshape(dev_count, half, width), DEV_AXES, split_ax...  10.1 us
    all_to_all x1, starting transfers between devices, per_device(): lax.all_to_all(jnp.broadcast_to(local_rows[None], (groups,) + local_rows....  9.37 us
  transfers between devices with their start and end apart: 12, of which 7 were waited for; matrix products, arithmetic and copies ran while one was open for 7% of the time, Pallas kernels for 0%

profile of v19, /device:TPU:2, one launch (start us, length us, event | category | flops | bytes accessed | tf_op | source)
XLA Modules:
  0.0 208.2 jit_solution(10181517242645386490)
XLA Ops:
  6.5 0.7 all-gather.11.cloned.1.call-update
  7.3 19.4 %all-gather.2 = s32[8,8,2]{1,2,0:T(2,128)S(1)} all-gather(s32[1,8,2]{1,2,0:T(2,128)} %bitcast.152), channel_id=3, replica_groups=mesh['y'=4,'x'=4,'c'=2,'e'=4,'p'=2] {'e','p'}, dimensions={0}, use_global_device_ids=true | all-gather | bytes 576 | tf_op jit(solution)/shard_map/all_gather | solution.py:74
  26.7 1.8 pad_maximum_fusion
  28.6 0.2 reduce_window_sum.22
  28.8 0.2 slice_reduce_fusion
  29.1 0.4 fusion.32
  29.6 1.9 collective-permute-start.1
  31.7 0.4 fusion.59
  32.6 0.1 mul.183
  33.1 1.0 scatter_custom_fusion
  34.1 0.2 convolution_multiply_fusion
  34.3 1.6 collective-permute-done.1
  36.0 0.1 fusion.58
  36.1 3.4 %collective-permute-start.2 = (bf16[4,129,128]{2,1,0:T(8,128)(2,1)S(1)}, bf16[4,129,128]{2,1,0:T(8,128)(2,1)S(1)}, u32[]{:S(2)}, u32[]{:S(2)}) collective-permute-start(bf16[4,129,128]{2,1,0:T(8,128)(2,1)S(1)} %get-tuple-element.25), channel_id=1, source_target_pairs={{0,16},{8,24},{16,32},{24,40},{32,48},{40,56},{48,64},{56,72},{64,... | collective-permute-start | bytes 396296 | tf_op jit(solution)/shard_map/ppermute | solution.py:25
  39.6 4.0 %collective-permute-done.2 = bf16[4,129,128]{2,1,0:T(8,128)(2,1)S(1)} collective-permute-done((bf16[4,129,128]{2,1,0:T(8,128)(2,1)S(1)}, bf16[4,129,128]{2,1,0:T(8,128)(2,1)S(1)}, u32[]{:S(2)}, u32[]{:S(2)}) %collective-permute-start.2) | collective-permute-done | bytes 132128 | tf_op jit(solution)/shard_map/ppermute | solution.py:25
  43.6 0.2 fusion.56
  43.7 4.7 %collective-permute-start.3 = (bf16[4,129,128]{2,1,0:T(8,128)(2,1)S(1)}, bf16[4,129,128]{2,1,0:T(8,128)(2,1)S(1)}, u32[]{:S(2)}, u32[]{:S(2)}) collective-permute-start(bf16[4,129,128]{2,1,0:T(8,128)(2,1)S(1)} %get-tuple-element.23), channel_id=1, source_target_pairs={{0,32},{8,40},{16,48},{24,56},{32,64},{40,72},{48,80},{56,88},{64,... | collective-permute-start | bytes 396296 | tf_op jit(solution)/shard_map/ppermute | solution.py:25
  48.5 2.6 %collective-permute-done.3 = bf16[4,129,128]{2,1,0:T(8,128)(2,1)S(1)} collective-permute-done((bf16[4,129,128]{2,1,0:T(8,128)(2,1)S(1)}, bf16[4,129,128]{2,1,0:T(8,128)(2,1)S(1)}, u32[]{:S(2)}, u32[]{:S(2)}) %collective-permute-start.3) | collective-permute-done | bytes 132128 | tf_op jit(solution)/shard_map/ppermute | solution.py:25
  51.0 0.2 fusion.54
  51.2 5.7 %collective-permute-start.4 = (bf16[4,129,128]{2,1,0:T(8,128)(2,1)S(1)}, bf16[4,129,128]{2,1,0:T(8,128)(2,1)S(1)}, u32[]{:S(2)}, u32[]{:S(2)}) collective-permute-start(bf16[4,129,128]{2,1,0:T(8,128)(2,1)S(1)} %get-tuple-element.21), channel_id=1, source_target_pairs={{0,64},{8,72},{16,80},{24,88},{32,96},{40,104},{48,112},{56,120},{... | collective-permute-start | bytes 396296 | tf_op jit(solution)/shard_map/ppermute | solution.py:25
  56.9 2.5 %collective-permute-done.4 = bf16[4,129,128]{2,1,0:T(8,128)(2,1)S(1)} collective-permute-done((bf16[4,129,128]{2,1,0:T(8,128)(2,1)S(1)}, bf16[4,129,128]{2,1,0:T(8,128)(2,1)S(1)}, u32[]{:S(2)}, u32[]{:S(2)}) %collective-permute-start.4) | collective-permute-done | bytes 132128 | tf_op jit(solution)/shard_map/ppermute | solution.py:25
  59.5 0.2 fusion.17
  59.6 6.0 %collective-permute-start.5 = (bf16[4,129,128]{2,1,0:T(8,128)(2,1)S(1)}, bf16[4,129,128]{2,1,0:T(8,128)(2,1)S(1)}, u32[]{:S(2)}, u32[]{:S(2)}) collective-permute-start(bf16[4,129,128]{2,1,0:T(8,128)(2,1)S(1)} %get-tuple-element.27), channel_id=1, source_target_pairs={{0,128},{8,136},{16,144},{24,152},{32,160},{40,168},{48,176},{56,1... | collective-permute-start | bytes 396296 | tf_op jit(solution)/shard_map/ppermute | solution.py:25
  65.6 2.6 %collective-permute-done.5 = bf16[4,129,128]{2,1,0:T(8,128)(2,1)S(1)} collective-permute-done((bf16[4,129,128]{2,1,0:T(8,128)(2,1)S(1)}, bf16[4,129,128]{2,1,0:T(8,128)(2,1)S(1)}, u32[]{:S(2)}, u32[]{:S(2)}) %collective-permute-start.5) | collective-permute-done | bytes 132128 | tf_op jit(solution)/shard_map/ppermute | solution.py:25
  68.2 0.3 fusion.18
  68.5 0.3 fusion.27
  68.9 1.0 gather_fusion
  69.9 14.4 %all_to_all.20 = bf16[8,24,512]{2,1,0:T(8,128)(2,1)S(1)} all-to-all(bf16[8,24,512]{2,1,0:T(8,128)(2,1)S(1)} %bitcast.137), channel_id=1, replica_groups=mesh['y'=4,'x'=4,'c'=2,'e'=4,'p'=2] {'e','p'}, dimensions={0} | all-to-all | bytes 393216 | tf_op jit(solution)/shard_map/all_to_all | solution.py:131
  84.4 2.1 %broadcast_in_dim.194 = bf16[16,24,4096]{2,1,0:T(8,128)(2,1)} broadcast(bf16[24,4096]{1,0:T(8,128)(2,1)S(1)} %bitcast.138), dimensions={1,2} | broadcast | bytes 3342336 | tf_op jit(solution)/shard_map/broadcast_in_dim | solution.py:142
  86.5 9.4 %all-to-all-start.1 = ((bf16[16,24,4096]{2,1,0:T(8,128)(2,1)}), bf16[16,24,4096]{2,1,0:T(8,128)(2,1)S(1)}, u32[]{:S(2)}, u32[]{:S(2)}) async-start(bf16[16,24,4096]{2,1,0:T(8,128)(2,1)} %broadcast_in_dim.194), calls=%async_computation.1 | async-start | bytes 6291456 | tf_op jit(solution)/shard_map/all_to_all | solution.py:141
  95.9 0.6 collective-permute-start.6
  96.4 39.0 %collective-permute-done.6 = bf16[256,4096]{1,0:T(8,128)(2,1)} collective-permute-done((bf16[256,4096]{1,0:T(8,128)(2,1)}, bf16[256,4096]{1,0:T(8,128)(2,1)}, u32[]{:S(2)}, u32[]{:S(2)}) %collective-permute-start.6) | collective-permute-done | bytes 2097184 | tf_op jit(solution)/shard_map/ppermute | solution.py:135
  135.4 3.0 %fusion.6 = f32[384,256]{0,1:T(8,128)S(1)} fusion(bf16[384,4096]{1,0:T(8,128)(2,1)S(1)} %bitcast.132, bf16[2,4096,256]{2,1,0:T(8,128)(2,1)} %all-gather.7.cloned.1.call-done), kind=kOutput, calls=%fused_computation.14 | convolution fusion | flops 805306368 | bytes 5636096 | tf_op jit(solution)/shard_map/dot_general | solution.py:151
  138.5 1.3 multiply_convert_fusion.1
  139.8 3.0 %fusion.4 = f32[384,256]{0,1:T(8,128)S(1)} fusion(bf16[384,4096]{1,0:T(8,128)(2,1)S(1)} %bitcast.134, bf16[2,4096,256]{2,1,0:T(8,128)(2,1)} %all-gather.9.cloned.1.call-done), kind=kOutput, calls=%fused_computation.10 | convolution fusion | flops 805306368 | bytes 5636096 | tf_op jit(solution)/shard_map/dot_general | solution.py:151
  142.9 1.3 multiply_convert_fusion
  144.2 0.3 copy-done.9
  144.4 3.4 %convolution_convert_fusion = bf16[384,4096]{1,0:T(8,128)(2,1)S(1)} fusion(bf16[256,4096]{1,0:T(8,128)(2,1)} %collective-permute-done.6, bf16[256,4096]{1,0:T(8,128)(2,1)S(1)} %bitcast.154, bf16[384,256]{0,1:T(8,128)(2,1)S(1)} %multiply_convert_fusion, bf16[384,256]{0,1:T(8,128)(2,1)S(1)} %multiply_convert_fusion.1), kind=kOutput, calls=%fused_computation.3 | convolution fusion | flops 1621360640 | bytes 7733248 | tf_op jit(solution)/shard_map/dot_general | solution.py:157
  147.9 36.5 %all_to_all.21 = bf16[16,24,4096]{2,1,0:T(8,128)(2,1)S(1)} all-to-all(bf16[16,24,4096]{2,1,0:T(8,128)(2,1)S(1)} %bitcast.136), channel_id=1, replica_groups=mesh['y'=4,'x'=4,'c'=2,'e'=4,'p'=2] {'y','x'}, dimensions={0} | all-to-all | bytes 6291456 | tf_op jit(solution)/shard_map/all_to_all | solution.py:158
  184.4 0.6 reduce_sum.41
  185.0 0.8 reshape.290
  185.8 3.4 %all-to-all-start.3 = ((bf16[8,3,4096]{2,1,0:T(4,128)(2,1)}), bf16[8,3,4096]{2,1,0:T(4,128)(2,1)S(1)}, u32[]{:S(2)}, u32[]{:S(2)}) async-start(bf16[8,3,4096]{2,1,0:T(4,128)(2,1)} %reshape.290), calls=%async_computation.3 | async-start | bytes 524288 | tf_op jit(solution)/shard_map/all_to_all | solution.py:162
  189.3 0.2 add_reduce_fusion
  189.5 10.1 %all-to-all-done.3 = bf16[8,3,4096]{2,1,0:T(4,128)(2,1)S(1)} async-done(((bf16[8,3,4096]{2,1,0:T(4,128)(2,1)}), bf16[8,3,4096]{2,1,0:T(4,128)(2,1)S(1)}, u32[]{:S(2)}, u32[]{:S(2)}) %all-to-all-start.3) | async-done | bytes 196640 | tf_op jit(solution)/shard_map/all_to_all | solution.py:162
  199.6 0.2 reshape.291
  199.8 0.6 gather_fusion.1
  200.4 0.2 reshape.292
  200.6 1.0 multiply_reduce_fusion
  (69 shorter events, 1.7 us)
Async XLA Ops:
  6.5 22.6 %copy-start = (bf16[64,512]{1,0:T(8,128)(2,1)S(1)}, bf16[64,512]{1,0:T(8,128)(2,1)}, u32[]{:S(2)}) copy-start(bf16[64,512]{1,0:T(8,128)(2,1)} %param.12) | copy-start | bytes 196612
  6.5 22.0 %copy-start.5 = (f32[64,4]{0,1:T(4,128)S(1)}, f32[64,4]{0,1:T(4,128)}, u32[]{:S(2)}) copy-start(f32[64,4]{0,1:T(4,128)} %param.13) | copy-start | bytes 3076
  6.5 22.6 %copy-start.2 = (bf16[64,512]{1,0:T(8,128)(2,1)S(1)}, bf16[64,512]{1,0:T(8,128)(2,1)}, u32[]{:S(2)}) copy-start(bf16[64,512]{1,0:T(8,128)(2,1)} %param.11) | copy-start | bytes 196612
  6.5 77.9 %all-gather.11.cloned.1.call-start = ((), (), s32[]{:S(2)}) async-start(), calls=%async_computation.6 | async-start | bytes 3145728 | tf_op jit(solution)/shard_map/all_gather | solution.py:79
  7.3 128.1 %all-gather.7.cloned.1.call-start = ((), (), s32[]{:S(2)}) async-start(), calls=%async_computation.4 | async-start | bytes 6291456 | tf_op jit(solution)/shard_map/all_gather | solution.py:78
  26.7 7.4 %copy-start.3 = (bf16[64,512]{1,0:T(8,128)(2,1)S(1)}, bf16[64,512]{1,0:T(8,128)(2,1)}, u32[]{:S(2)}) copy-start(bf16[64,512]{1,0:T(8,128)(2,1)} %param.10) | copy-start | bytes 196612
  28.5 3.1 %copy-start.1 = (bf16[2,4096,128]{2,1,0:T(8,128)(2,1)}, bf16[2,4096,128]{2,1,0:T(8,128)(2,1)S(1)}, u32[]{:S(2)}) copy-start(bf16[2,4096,128]{2,1,0:T(8,128)(2,1)S(1)} %pad_maximum_fusion) | copy-start | bytes 6291460
  28.5 55.9 %collective-permute-start = (bf16[2,4096,128]{2,1,0:T(8,128)(2,1)S(1)}, bf16[2,4096,128]{2,1,0:T(8,128)(2,1)}, u32[]{:S(2)}, u32[]{:S(2)}) collective-permute-start(bf16[2,4096,128]{2,1,0:T(8,128)(2,1)S(1)} %pad_maximum_fusion), channel_id=1, source_target_pairs={{0,1},{1,0},{2,3},{3,2},{4,5},{5,4},{6,7},{7,6},{8,9},{9,8},{10,11... | collective-permute-start | bytes 6291464 | tf_op jit(solution)/shard_map/ppermute | solution.py:80
  29.6 6.4 %collective-permute-start.1 = (bf16[4,129,128]{2,1,0:T(8,128)(2,1)S(1)}, bf16[4,129,128]{2,1,0:T(8,128)(2,1)S(1)}, u32[]{:S(2)}, u32[]{:S(2)}) collective-permute-start(bf16[4,129,128]{2,1,0:T(8,128)(2,1)S(1)} %fusion.22), channel_id=1, source_target_pairs={{0,8},{8,16},{16,24},{24,32},{32,40},{40,48},{48,56},{56,64},{64,7... | collective-permute-start | bytes 396296 | tf_op jit(solution)/shard_map/ppermute | solution.py:25
  31.6 108.2 %all-gather.9.cloned.1.call-start = ((), (), s32[]{:S(2)}) async-start(), calls=%async_computation.5 | async-start | bytes 6291456 | tf_op jit(solution)/shard_map/all_gather | solution.py:133
  34.3 34.5 %copy-start.4 = (f32[512]{0:T(512)S(1)}, f32[512]{0:T(512)}, u32[]{:S(2)}) copy-start(f32[512]{0:T(512)} %param.14) | copy-start | bytes 6148
  36.1 7.4 %collective-permute-start.2 = (bf16[4,129,128]{2,1,0:T(8,128)(2,1)S(1)}, bf16[4,129,128]{2,1,0:T(8,128)(2,1)S(1)}, u32[]{:S(2)}, u32[]{:S(2)}) collective-permute-start(bf16[4,129,128]{2,1,0:T(8,128)(2,1)S(1)} %get-tuple-element.25), channel_id=1, source_target_pairs={{0,16},{8,24},{16,32},{24,40},{32,48},{40,56},{48,64},{56,72},{64,... | collective-permute-start | bytes 396296 | tf_op jit(solution)/shard_map/ppermute | solution.py:25
  43.7 7.3 %collective-permute-start.3 = (bf16[4,129,128]{2,1,0:T(8,128)(2,1)S(1)}, bf16[4,129,128]{2,1,0:T(8,128)(2,1)S(1)}, u32[]{:S(2)}, u32[]{:S(2)}) collective-permute-start(bf16[4,129,128]{2,1,0:T(8,128)(2,1)S(1)} %get-tuple-element.23), channel_id=1, source_target_pairs={{0,32},{8,40},{16,48},{24,56},{32,64},{40,72},{48,80},{56,88},{64,... | collective-permute-start | bytes 396296 | tf_op jit(solution)/shard_map/ppermute | solution.py:25
  51.2 8.3 %collective-permute-start.4 = (bf16[4,129,128]{2,1,0:T(8,128)(2,1)S(1)}, bf16[4,129,128]{2,1,0:T(8,128)(2,1)S(1)}, u32[]{:S(2)}, u32[]{:S(2)}) collective-permute-start(bf16[4,129,128]{2,1,0:T(8,128)(2,1)S(1)} %get-tuple-element.21), channel_id=1, source_target_pairs={{0,64},{8,72},{16,80},{24,88},{32,96},{40,104},{48,112},{56,120},{... | collective-permute-start | bytes 396296 | tf_op jit(solution)/shard_map/ppermute | solution.py:25
  59.6 8.6 %collective-permute-start.5 = (bf16[4,129,128]{2,1,0:T(8,128)(2,1)S(1)}, bf16[4,129,128]{2,1,0:T(8,128)(2,1)S(1)}, u32[]{:S(2)}, u32[]{:S(2)}) collective-permute-start(bf16[4,129,128]{2,1,0:T(8,128)(2,1)S(1)} %get-tuple-element.27), channel_id=1, source_target_pairs={{0,128},{8,136},{16,144},{24,152},{32,160},{40,168},{48,176},{56,1... | collective-permute-start | bytes 396296 | tf_op jit(solution)/shard_map/ppermute | solution.py:25
  86.5 48.9 %all-to-all-start.1 = ((bf16[16,24,4096]{2,1,0:T(8,128)(2,1)}), bf16[16,24,4096]{2,1,0:T(8,128)(2,1)S(1)}, u32[]{:S(2)}, u32[]{:S(2)}) async-start(bf16[16,24,4096]{2,1,0:T(8,128)(2,1)} %broadcast_in_dim.194), calls=%async_computation.1 | async-start | bytes 6291456 | tf_op jit(solution)/shard_map/all_to_all | solution.py:141
  95.9 39.5 %collective-permute-start.6 = (bf16[256,4096]{1,0:T(8,128)(2,1)}, bf16[256,4096]{1,0:T(8,128)(2,1)}, u32[]{:S(2)}, u32[]{:S(2)}) collective-permute-start(bf16[256,4096]{1,0:T(8,128)(2,1)} %bitcast.153), channel_id=1, source_target_pairs={{0,1},{1,0},{2,3},{3,2},{4,5},{5,4},{6,7},{7,6},{8,9},{9,8},{10,11... | collective-permute-start | bytes 6291464 | tf_op jit(solution)/shard_map/ppermute | solution.py:135
  135.4 3.0 %copy-start.7 = (bf16[2,4096,256]{2,1,0:T(8,128)(2,1)S(1)}, bf16[2,4096,256]{2,1,0:T(8,128)(2,1)}, u32[]{:S(2)}) copy-start(bf16[2,4096,256]{2,1,0:T(8,128)(2,1)} %all-gather.7.cloned.1.call-done) | copy-start | bytes 12582916
  139.8 3.1 %copy-start.8 = (bf16[2,4096,256]{2,1,0:T(8,128)(2,1)S(1)}, bf16[2,4096,256]{2,1,0:T(8,128)(2,1)}, u32[]{:S(2)}) copy-start(bf16[2,4096,256]{2,1,0:T(8,128)(2,1)} %all-gather.9.cloned.1.call-done) | copy-start | bytes 12582916
  142.9 1.6 copy-start.9
  184.4 4.8 %copy-start.6 = (f32[8,2]{0,1:T(2,128)S(1)}, f32[8,2]{0,1:T(2,128)}, u32[]{:S(2)}) copy-start(f32[8,2]{0,1:T(2,128)} %param.19) | copy-start | bytes 196
  185.8 13.8 %all-to-all-start.3 = ((bf16[8,3,4096]{2,1,0:T(4,128)(2,1)}), bf16[8,3,4096]{2,1,0:T(4,128)(2,1)S(1)}, u32[]{:S(2)}, u32[]{:S(2)}) async-start(bf16[8,3,4096]{2,1,0:T(4,128)(2,1)} %reshape.290), calls=%async_computation.3 | async-start | bytes 524288 | tf_op jit(solution)/shard_map/all_to_all | solution.py:162
Sparse Core Ops, SparseCore 0:
  9.2 18.8 all-gather.10
  31.7 18.6 all-gather.6
  84.5 16.5 all-gather.8
